TPU v7x, 256 devices: a whole 4x4x8 slice. The times are simulated.
256 devices in a mesh: dp: 16 (over z_lo, x), seq: 16 (over y, z_hi, core).
Axes of the slice: x: 4, y: 4, z: 8 (z_hi: 2, z_lo: 4; z = z_hi * 4 + z_lo), core: 2. Of those that a mesh axis runs over, the one named last changes fastest.
Arguments:
- codes: int32 [16, 32768], P('dp', 'seq'), may hold values from 0 to 3
- embed: bfloat16 [4, 256], replicated, may hold values from -6 to 6
- first_weight_taps: bfloat16 [3, 256, 256], replicated, may hold values from -0.21875 to 0.21875
- second_weight_taps: bfloat16 [3, 256, 256], replicated, may hold values from -0.21875 to 0.21875
- cotangent: bfloat16 [16, 32768, 256], P('dp', 'seq'), may hold values from -6 to 6
Outputs:
- block_out: bfloat16 [16, 32768, 256], P('dp', 'seq')
- first_weight_gradient: float32 [3, 256, 256], replicated
- second_weight_gradient: float32 [3, 256, 256], replicated
All inputs are finite; a program needn't handle non-finite values.
Results may differ from a plain program's by a relative error of at most 0.0085.
Values may be sent and summed in bfloat16 or wider, within the bound.
No kernel may reach another device: no remote copies, remote signals or barrier semaphores. Data moves between devices by JAX's collectives and lax.ppermute only.
A program may use at most 64 MiB of HBM per device.

v0:
```python
import jax
import jax.numpy as jnp
from jax import lax
from jax.sharding import PartitionSpec as P

FIRST_DILATION = 4
SECOND_DILATION = 16


def with_halo(cells, sides, width):
    for axis, dim in sides:
        count = lax.axis_size(axis)
        ends = count - 1
        head = lax.slice_in_dim(cells, 0, width, axis=dim)
        tail = lax.slice_in_dim(cells, cells.shape[dim] - width, cells.shape[dim], axis=dim)
        cells = jnp.concatenate(
            [
                lax.ppermute(tail, axis, [(i, (i + 1) % count) for i in range(ends)]),
                cells,
                lax.ppermute(head, axis, [((i + 1) % count, i) for i in range(ends)]),
            ],
            axis=dim,
        )
    return cells


def pad_rows(value, dilation):
    return with_halo(value, (("seq", 1),), dilation)


def stack_rows(padded, dilation, order):
    count_rows = padded.shape[1] - 2 * dilation
    return jnp.concatenate(
        [padded[:, k * dilation : k * dilation + count_rows] for k in order], axis=-1
    )


def product(stacked, matrix):
    shape_in = stacked.shape
    result = jnp.dot(stacked.reshape(-1, shape_in[-1]), matrix, preferred_element_type=jnp.float32)
    return result.reshape(shape_in[:-1] + (matrix.shape[1],))


def weight_term(stacked, grad):
    channels = grad.shape[-1]
    term = jnp.dot(
        stacked.reshape(-1, 3 * channels).T,
        grad.reshape(-1, channels),
        preferred_element_type=jnp.float32,
    )
    return term.reshape(3, channels, channels)


def layer_forward_pass(value, weight, dilation):
    channels = weight.shape[2]
    stacked = stack_rows(pad_rows(value, dilation), dilation, (0, 1, 2))
    flat = weight.reshape(-1, channels)
    reversed_taps = weight[::-1, ::-1, ::-1].reshape(-1, channels)
    both = product(stacked, jnp.concatenate([flat, reversed_taps], axis=1))
    return (both[..., :channels] + both[..., channels:], stacked)


def input_backward_pass(grad, weight, dilation):
    channels = weight.shape[2]
    stacked = stack_rows(pad_rows(grad, dilation), dilation, (2, 1, 0))
    flat_t = jnp.transpose(weight, (0, 2, 1)).reshape(-1, channels)
    reversed_t = jnp.transpose(weight[::-1, ::-1, ::-1], (0, 2, 1)).reshape(-1, channels)
    both = product(stacked, jnp.concatenate([flat_t, reversed_t], axis=1))
    return both[..., :channels] + both[..., channels:]


def strand_total(stacked, grad):
    term = weight_term(stacked, grad)
    return term + term[::-1, ::-1, ::-1]


def local(codes, embed, first_weight_taps, second_weight_taps, cotangent):
    onehot = (codes[..., None] == jnp.arange(4, dtype=jnp.int32)).astype(jnp.bfloat16)
    nucleotide_features = product(onehot, embed).astype(jnp.bfloat16)
    first_activation, first_shift_stack = layer_forward_pass(
        nucleotide_features, first_weight_taps, FIRST_DILATION
    )
    gelu_one, back_one = jax.vjp(jax.nn.gelu, first_activation)
    hidden_state = gelu_one.astype(jnp.bfloat16)
    second_activation, second_shift_stack = layer_forward_pass(
        hidden_state, second_weight_taps, SECOND_DILATION
    )
    gelu_two, back_two = jax.vjp(jax.nn.gelu, second_activation)
    block_out = (hidden_state.astype(jnp.float32) + gelu_two).astype(jnp.bfloat16)
    cotangent_wide_float = cotangent.astype(jnp.float32)
    second_activation_gradient = back_two(cotangent_wide_float)[0].astype(jnp.bfloat16)
    input_contribution = input_backward_pass(
        second_activation_gradient, second_weight_taps, SECOND_DILATION
    )
    second_weight_gradient = strand_total(second_shift_stack, second_activation_gradient)
    second_weight_gradient = lax.psum(second_weight_gradient, ("dp", "seq"))
    hidden_gradient = cotangent_wide_float + input_contribution
    first_activation_gradient = back_one(hidden_gradient)[0].astype(jnp.bfloat16)
    first_weight_gradient = strand_total(first_shift_stack, first_activation_gradient)
    first_weight_gradient = lax.psum(first_weight_gradient, ("dp", "seq"))
    return (block_out, first_weight_gradient, second_weight_gradient)


def solution(mesh):
    in_specs = (P("dp", "seq"), P(), P(), P(), P("dp", "seq", None))
    out_specs = (P("dp", "seq", None), P(), P())
    return jax.shard_map(local, mesh=mesh, in_specs=in_specs, out_specs=out_specs, check_vma=False)
```

profile of v0, /device:TPU:1, one launch (start us, length us, event | category | flops | bytes accessed | tf_op | source)
XLA Modules:
  0.0 364.1 jit_solution(2068877500604701353)
XLA Ops:
  7.9 1.2 fusion.14
  9.1 5.1 %collective-permute-start.1 = (bf16[1,4,256]{2,1,0:T(4,128)(2,1)S(1)}, bf16[1,4,256]{2,1,0:T(4,128)(2,1)S(1)}, u32[]{:S(2)}, u32[]{:S(2)}) collective-permute-start(bf16[1,4,256]{2,1,0:T(4,128)(2,1)S(1)} %get-tuple-element.12), channel_id=1, source_target_pairs={{1,0},{2,1},{3,2},{4,3},{5,4},{6,5},{7,6},{8,7},{9,8},{10,9},{11,1... | collective-permute-start | bytes 6152 | tf_op jit(solution)/shard_map/ppermute | solution.py:20
  14.2 7.0 %collective-permute-start = (bf16[1,4,256]{2,1,0:T(4,128)(2,1)S(1)}, bf16[1,4,256]{2,1,0:T(4,128)(2,1)S(1)}, u32[]{:S(2)}, u32[]{:S(2)}) collective-permute-start(bf16[1,4,256]{2,1,0:T(4,128)(2,1)S(1)} %get-tuple-element.11), channel_id=1, source_target_pairs={{0,1},{1,2},{2,3},{3,4},{4,5},{5,6},{6,7},{7,8},{8,9},{9,10},{10,1... | collective-permute-start | bytes 6152 | tf_op jit(solution)/shard_map/ppermute | solution.py:18
  21.2 5.3 %rev.14 = bf16[3,256,256]{2,1,0:T(8,128)(2,1)S(1)} reverse(bf16[3,256,256]{2,1,0:T(8,128)(2,1)} %param.8), dimensions={0,1,2} | reverse | bytes 786432 | tf_op jit(solution)/shard_map/rev | solution.py:58
  27.5 1.3 rev.13
  29.7 1.8 convolution_bitcast_fusion.2
  32.4 1.2 copy-done.1
  34.2 1.9 collective-permute-start.3
  36.1 7.6 %collective-permute-start.2 = (bf16[1,16,256]{2,1,0:T(8,128)(2,1)}, bf16[1,16,256]{2,1,0:T(8,128)(2,1)}, u32[]{:S(2)}, u32[]{:S(2)}) collective-permute-start(bf16[1,16,256]{2,1,0:T(8,128)(2,1)} %get-tuple-element.9), channel_id=1, source_target_pairs={{0,1},{1,2},{2,3},{3,4},{4,5},{5,6},{6,7},{7,8},{8,9},{9,10},{10,1... | collective-permute-start | bytes 24584 | tf_op jit(solution)/shard_map/ppermute | solution.py:18
  43.7 4.4 %fusion.37 = bf16[768,2048]{0,1:T(8,128)(2,1)S(1)} fusion(bf16[1,4,256]{2,1,0:T(4,128)(2,1)S(1)} %collective-permute-done.1, bf16[1,2048,256]{2,1,0:T(8,128)(2,1)} %copy-done.6, bf16[1,4,256]{2,1,0:T(4,128)(2,1)} %copy-done.18), kind=kLoop, calls=%fused_computation.57 | loop fusion | flops 15728640 | bytes 4198400 | tf_op jit(solution)/shard_map/dot_general | solution.py:46
  48.1 3.0 copy.14
  51.1 6.2 %convolution_bitcast_fusion.1 = f32[1,2048,512]{2,1,0:T(8,128)S(1)} fusion(bf16[1,16,256]{2,1,0:T(8,128)(2,1)S(1)} %collective-permute-done.3, bf16[1,2048,256]{2,1,0:T(8,128)(2,1)} %copy-done.4, bf16[1,16,256]{2,1,0:T(8,128)(2,1)} %collective-permute-done.2, bf16[768,256]{1,0:T(8,128)(2,1)} %bitcast.50, bf16[768,256]{1,0:T(8,128)(2,1)S(1)} %bitcast.48), kind=kOutput, calls=%fused_computation.1 | convolution fusion | flops 1627914240 | bytes 6045696 | tf_op jit(solution)/shard_map/dot_general | solution.py:40
  57.4 3.3 fusion.28
  60.7 2.6 collective-permute-start.5
  63.3 2.1 collective-permute-start.4
  65.4 7.9 %fusion.39 = bf16[768,2048]{0,1:T(8,128)(2,1)S(1)} fusion(bf16[1,16,256]{2,1,0:T(8,128)(2,1)S(1)} %collective-permute-done.3, bf16[1,2048,256]{2,1,0:T(8,128)(2,1)S(1)} %copy-done.5, bf16[1,16,256]{2,1,0:T(8,128)(2,1)} %collective-permute-done.2), kind=kLoop, calls=%fused_computation.58 | loop fusion | flops 15728640 | bytes 4210688 | tf_op jit(solution)/shard_map/dot_general | solution.py:46
  73.3 3.0 copy.17
  76.3 3.2 fusion.32
  79.5 1.1 rev.16
  81.6 1.8 convolution_bitcast_fusion
  85.0 2.2 fusion.34
  87.2 1.1 rev.15
  89.3 264.9 %all-reduce.3.cloned.1.call-done = (f32[3,256,256]{2,1,0:T(8,128)}, f32[3,256,256]{2,1,0:T(8,128)}) async-done(((f32[3,256,256]{2,1,0:T(8,128)}, f32[3,256,256]{2,1,0:T(8,128)}), (f32[3,256,256]{2,1,0:T(8,128)}, f32[3,256,256]{2,1,0:T(8,128)})) %all-reduce.3.cloned.1.call-update) | async-done | bytes 1572880 | tf_op jit(solution)/shard_map/psum | solution.py:100
  354.2 2.1 copy.20
  (54 shorter events, 8.4 us)
Async XLA Ops:
  7.2 19.3 %copy-start.8 = (bf16[3,256,256]{2,1,0:T(8,128)(2,1)S(1)}, bf16[3,256,256]{2,1,0:T(8,128)(2,1)}, u32[]{:S(2)}) copy-start(bf16[3,256,256]{2,1,0:T(8,128)(2,1)} %param.8) | copy-start | bytes 1179652
  7.2 20.3 %copy-start.15 = (bf16[3,256,256]{2,1,0:T(8,128)(2,1)S(1)}, bf16[3,256,256]{2,1,0:T(8,128)(2,1)}, u32[]{:S(2)}) copy-start(bf16[3,256,256]{2,1,0:T(8,128)(2,1)} %param.7) | copy-start | bytes 1179652
  7.2 347.0 %all-reduce.3.cloned.1.call-start = ((), (), s32[]{:S(2)}) async-start(), calls=%async_computation | async-start | bytes 3145728 | tf_op jit(solution)/shard_map/psum | solution.py:100
  9.0 22.5 %copy-start.6 = (bf16[1,2048,256]{2,1,0:T(8,128)(2,1)}, bf16[1,2048,256]{2,1,0:T(8,128)(2,1)S(1)}, u32[]{:S(2)}) copy-start(bf16[1,2048,256]{2,1,0:T(8,128)(2,1)S(1)} %fusion.14) | copy-start | bytes 3145732
  9.1 20.6 %collective-permute-start.1 = (bf16[1,4,256]{2,1,0:T(4,128)(2,1)S(1)}, bf16[1,4,256]{2,1,0:T(4,128)(2,1)S(1)}, u32[]{:S(2)}, u32[]{:S(2)}) collective-permute-start(bf16[1,4,256]{2,1,0:T(4,128)(2,1)S(1)} %get-tuple-element.12), channel_id=1, source_target_pairs={{1,0},{2,1},{3,2},{4,3},{5,4},{6,5},{7,6},{8,7},{9,8},{10,9},{11,1... | collective-permute-start | bytes 6152 | tf_op jit(solution)/shard_map/ppermute | solution.py:20
  14.2 15.5 %collective-permute-start = (bf16[1,4,256]{2,1,0:T(4,128)(2,1)S(1)}, bf16[1,4,256]{2,1,0:T(4,128)(2,1)S(1)}, u32[]{:S(2)}, u32[]{:S(2)}) collective-permute-start(bf16[1,4,256]{2,1,0:T(4,128)(2,1)S(1)} %get-tuple-element.11), channel_id=1, source_target_pairs={{0,1},{1,2},{2,3},{3,4},{4,5},{5,6},{6,7},{7,8},{8,9},{9,10},{10,1... | collective-permute-start | bytes 6152 | tf_op jit(solution)/shard_map/ppermute | solution.py:18
  26.5 5.1 %copy-start.9 = (bf16[3,256,256]{2,1,0:T(8,128)(2,1)}, bf16[3,256,256]{2,1,0:T(8,128)(2,1)S(1)}, u32[]{:S(2)}) copy-start(bf16[3,256,256]{2,1,0:T(8,128)(2,1)S(1)} %rev.14) | copy-start | bytes 1179652
  31.6 2.0 copy-start.1
  33.6 2.6 copy-start.4
  34.2 16.9 %collective-permute-start.3 = (bf16[1,16,256]{2,1,0:T(8,128)(2,1)}, bf16[1,16,256]{2,1,0:T(8,128)(2,1)S(1)}, u32[]{:S(2)}, u32[]{:S(2)}) collective-permute-start(bf16[1,16,256]{2,1,0:T(8,128)(2,1)} %get-tuple-element.10), channel_id=1, source_target_pairs={{1,0},{2,1},{3,2},{4,3},{5,4},{6,5},{7,6},{8,7},{9,8},{10,9},{11,1... | collective-permute-start | bytes 24584 | tf_op jit(solution)/shard_map/ppermute | solution.py:20
  36.1 15.0 %collective-permute-start.2 = (bf16[1,16,256]{2,1,0:T(8,128)(2,1)}, bf16[1,16,256]{2,1,0:T(8,128)(2,1)}, u32[]{:S(2)}, u32[]{:S(2)}) collective-permute-start(bf16[1,16,256]{2,1,0:T(8,128)(2,1)} %get-tuple-element.9), channel_id=1, source_target_pairs={{0,1},{1,2},{2,3},{3,4},{4,5},{5,6},{6,7},{7,8},{8,9},{9,10},{10,1... | collective-permute-start | bytes 24584 | tf_op jit(solution)/shard_map/ppermute | solution.py:18
  51.1 6.3 %copy-start.2 = (f32[1,2048,512]{2,1,0:T(8,128)S(1)}, f32[1,2048,512]{2,1,0:T(8,128)}, u32[]{:S(2)}) copy-start(f32[1,2048,512]{2,1,0:T(8,128)} %copy-done.1) | copy-start | bytes 12582916
  51.1 6.3 %copy-start.12 = (bf16[1,2048,256]{2,1,0:T(8,128)(2,1)S(1)}, bf16[1,2048,256]{2,1,0:T(8,128)(2,1)}, u32[]{:S(2)}) copy-start(bf16[1,2048,256]{2,1,0:T(8,128)(2,1)} %param.9) | copy-start | bytes 3145732
  57.4 8.1 %copy-start.5 = (bf16[1,2048,256]{2,1,0:T(8,128)(2,1)S(1)}, bf16[1,2048,256]{2,1,0:T(8,128)(2,1)}, u32[]{:S(2)}) copy-start(bf16[1,2048,256]{2,1,0:T(8,128)(2,1)} %copy-done.4) | copy-start | bytes 3145732
  60.7 2.6 copy-start.10
  60.7 20.9 %collective-permute-start.5 = (bf16[1,16,256]{2,1,0:T(8,128)(2,1)S(1)}, bf16[1,16,256]{2,1,0:T(8,128)(2,1)S(1)}, u32[]{:S(2)}, u32[]{:S(2)}) collective-permute-start(bf16[1,16,256]{2,1,0:T(8,128)(2,1)S(1)} %get-tuple-element.8), channel_id=1, source_target_pairs={{0,1},{1,2},{2,3},{3,4},{4,5},{5,6},{6,7},{7,8},{8,9},{9,10},{10,1... | collective-permute-start | bytes 24584 | tf_op jit(solution)/shard_map/ppermute | solution.py:18
  63.3 18.3 %collective-permute-start.4 = (bf16[1,16,256]{2,1,0:T(8,128)(2,1)S(1)}, bf16[1,16,256]{2,1,0:T(8,128)(2,1)S(1)}, u32[]{:S(2)}, u32[]{:S(2)}) collective-permute-start(bf16[1,16,256]{2,1,0:T(8,128)(2,1)S(1)} %get-tuple-element.7), channel_id=1, source_target_pairs={{1,0},{2,1},{3,2},{4,3},{5,4},{6,5},{7,6},{8,7},{9,8},{10,9},{11,1... | collective-permute-start | bytes 24584 | tf_op jit(solution)/shard_map/ppermute | solution.py:20
  79.5 2.1 copy-start.11
  79.5 2.1 copy-start.16
  79.5 2.1 copy-start.17
  81.6 2.2 copy-start.3
  81.6 3.2 copy-start.7
  81.6 3.4 copy-start.13
  354.2 2.1 copy-start.14
  (2 other events, 2.6 us)
Sparse Core Ops, SparseCore 0:
  89.4 264.7 all-reduce.2
where the time goes:
time: 366 us; the launch traced here: 364 us
  waiting for transfers between devices  265 us (72%)
  starting transfers between devices  26.3 us (7%)
  local copies, waits for them, and re-layouts  23.7 us (6%)
  other arithmetic  18.3 us (5%)
  matrix products  16.4 us (4%)
  between operations  14.4 us (4%)
    psum x1, waiting for transfers between devices, local(): first_weight_gradient = lax.psum(first_weight_gradient, ('dp', 'seq'))  265 us
    ppermute x3, starting transfers between devices, with_halo(): lax.ppermute(tail, axis, [(i, (i + 1) % count) for i in range(ends)])  17.2 us
    dot_general x2, other arithmetic, weight_term(): jnp.dot(stacked.reshape(-1, 3 * channels).T, grad.reshape(-1, channels),...  12.3 us
    dot_general x4, matrix products, product(): jnp.dot(stacked.reshape(-1, shape_in[-1]), matrix, preferred_element_type...  11.1 us
    ppermute x3, starting transfers between devices, with_halo(): lax.ppermute(head, axis, [((i + 1) % count, i) for i in range(ends)])  9.12 us
    unnamed x41, local copies, waits for them, and re-layouts  7.38 us
  transfers between devices with their start and end apart: 7, of which 1 were waited for; matrix products, arithmetic and copies ran while one was open for 9% of the time, Pallas kernels for 0%

commit v1 on v0

--- a/solution.py
+++ b/solution.py
@@ -74,6 +74,47 @@
     return term + term[::-1, ::-1, ::-1]
 
 
+def exchange_steps():
+    steps = []
+    for axis, bit in (("seq", 1), ("dp", 1), ("dp", 2), ("seq", 4), ("seq", 8), ("dp", 4), ("dp", 8), ("seq", 2)):
+        if bit < lax.axis_size(axis):
+            steps.append((axis, bit))
+    return steps
+
+
+def butterfly_sum(rows):
+    kept = []
+    for axis, bit in exchange_steps():
+        count = lax.axis_size(axis)
+        pairs = [(i, i ^ bit) for i in range(count)]
+        half = rows.shape[0] // 2
+        upper = (lax.axis_index(axis) & bit) != 0
+        low, high = rows[:half], rows[half:]
+        mine = jnp.where(upper, high, low)
+        other = jnp.where(upper, low, high)
+        rows = mine + lax.ppermute(other, axis, pairs)
+        kept.append((axis, bit, upper))
+    for axis, bit, upper in reversed(kept):
+        count = lax.axis_size(axis)
+        pairs = [(i, i ^ bit) for i in range(count)]
+        got = lax.ppermute(rows, axis, pairs)
+        rows = jnp.where(upper, jnp.concatenate([got, rows]), jnp.concatenate([rows, got]))
+    return rows
+
+
+def symmetric_sum(first, second):
+    shape = first.shape
+    flat_rows = shape[0] * shape[1]
+    half = flat_rows // 2
+    halves = [g.reshape(flat_rows, shape[2])[:half] for g in (first, second)]
+    total = butterfly_sum(jnp.concatenate(halves, axis=0))
+    outs = []
+    for i in range(2):
+        part = total[i * half : (i + 1) * half]
+        outs.append(jnp.concatenate([part, part[::-1, ::-1]], axis=0).reshape(shape))
+    return outs
+
+
 def local(codes, embed, first_weight_taps, second_weight_taps, cotangent):
     onehot = (codes[..., None] == jnp.arange(4, dtype=jnp.int32)).astype(jnp.bfloat16)
     nucleotide_features = product(onehot, embed).astype(jnp.bfloat16)
@@ -93,11 +134,12 @@
         second_activation_gradient, second_weight_taps, SECOND_DILATION
     )
     second_weight_gradient = strand_total(second_shift_stack, second_activation_gradient)
-    second_weight_gradient = lax.psum(second_weight_gradient, ("dp", "seq"))
     hidden_gradient = cotangent_wide_float + input_contribution
     first_activation_gradient = back_one(hidden_gradient)[0].astype(jnp.bfloat16)
     first_weight_gradient = strand_total(first_shift_stack, first_activation_gradient)
-    first_weight_gradient = lax.psum(first_weight_gradient, ("dp", "seq"))
+    second_weight_gradient, first_weight_gradient = symmetric_sum(
+        second_weight_gradient, first_weight_gradient
+    )
     return (block_out, first_weight_gradient, second_weight_gradient)
 
 

time: 366 us -> 169 us (0.46)
  waiting for transfers between devices: 265 us -> 40.5 us
  starting transfers between devices: 26.3 us -> 73.3 us
  between operations: 14.4 us -> 1.08 us
    psum x1 -> x0, waiting for transfers between devices: 265 us -> none  [local(): first_weight_gradient = lax.psum(first_weight_gradient, ('dp', 'seq'))]
    ppermute x0 -> x16, starting transfers between devices: none -> 46.8 us  [the longest x8 29.3 us: butterfly_sum(): got = lax.ppermute(rows, axis, pairs)]
    ppermute x0 -> x16, waiting for transfers between devices: none -> 35.1 us  [the longest x8 18 us: butterfly_sum(): rows = mine + lax.ppermute(other, axis, pairs)]
    ppermute x3, waiting for transfers between devices: 0.01 us -> 5.39 us  [with_halo(): lax.ppermute(head, axis, [((i + 1) % count, i) for i in range(ends)])]
    unnamed x41 -> x33, local copies, waits for them, and re-layouts: 7.38 us -> 4.42 us
  transfers between devices with their start and end apart: 7 -> 22, of which waited for: 1 -> 17; matrix products, arithmetic and copies ran while one was open for 9% -> 11% of each run, Pallas kernels for 0% -> 0%
where the time goes in v1:
time: 169 us; the launch traced here: 168 us
  starting transfers between devices  73.3 us (43%)
  waiting for transfers between devices  40.5 us (24%)
  local copies, waits for them, and re-layouts  21.9 us (13%)
  other arithmetic  16.9 us (10%)
  matrix products  14.2 us (8%)
    ppermute x8, starting transfers between devices, butterfly_sum(): got = lax.ppermute(rows, axis, pairs)  29.3 us
    ppermute x8, waiting for transfers between devices, butterfly_sum(): rows = mine + lax.ppermute(other, axis, pairs)  18 us
    ppermute x8, starting transfers between devices, butterfly_sum(): rows = mine + lax.ppermute(other, axis, pairs)  17.5 us
    ppermute x3, starting transfers between devices, with_halo(): lax.ppermute(tail, axis, [(i, (i + 1) % count) for i in range(ends)])  17.4 us
    ppermute x8, waiting for transfers between devices, butterfly_sum(): got = lax.ppermute(rows, axis, pairs)  17.1 us
    dot_general x4, matrix products, product(): jnp.dot(stacked.reshape(-1, shape_in[-1]), matrix, preferred_element_type...  11 us
    dot_general x2, other arithmetic, weight_term(): jnp.dot(stacked.reshape(-1, 3 * channels).T, grad.reshape(-1, channels),...  11 us
    ppermute x3, starting transfers between devices, with_halo(): lax.ppermute(head, axis, [((i + 1) % count, i) for i in range(ends)])  9.16 us
  transfers between devices with their start and end apart: 22, of which 17 were waited for; matrix products, arithmetic and copies ran while one was open for 11% of the time, Pallas kernels for 0%

profile of v1, /device:TPU:1, one launch (start us, length us, event | category | flops | bytes accessed | tf_op | source)
XLA Modules:
  0.0 167.8 jit_solution(3840570076031280519)
XLA Ops:
  2.5 5.1 %collective-permute-start.1 = (bf16[1,4,256]{2,1,0:T(4,128)(2,1)S(1)}, bf16[1,4,256]{2,1,0:T(4,128)(2,1)S(1)}, u32[]{:S(2)}, u32[]{:S(2)}) collective-permute-start(bf16[1,4,256]{2,1,0:T(4,128)(2,1)S(1)} %get-tuple-element.10), channel_id=1, source_target_pairs={{1,0},{2,1},{3,2},{4,3},{5,4},{6,5},{7,6},{8,7},{9,8},{10,9},{11,1... | collective-permute-start | bytes 6152 | tf_op jit(solution)/shard_map/ppermute | solution.py:20
  7.6 7.0 %collective-permute-start = (bf16[1,4,256]{2,1,0:T(4,128)(2,1)S(1)}, bf16[1,4,256]{2,1,0:T(4,128)(2,1)S(1)}, u32[]{:S(2)}, u32[]{:S(2)}) collective-permute-start(bf16[1,4,256]{2,1,0:T(4,128)(2,1)S(1)} %get-tuple-element.9), channel_id=1, source_target_pairs={{0,1},{1,2},{2,3},{3,4},{4,5},{5,6},{6,7},{7,8},{8,9},{9,10},{10,1... | collective-permute-start | bytes 6152 | tf_op jit(solution)/shard_map/ppermute | solution.py:18
  14.7 5.3 %rev.20 = bf16[3,256,256]{2,1,0:T(8,128)(2,1)S(1)} reverse(bf16[3,256,256]{2,1,0:T(8,128)(2,1)} %param.8), dimensions={0,1,2} | reverse | bytes 786432 | tf_op jit(solution)/shard_map/rev | solution.py:58
  29.6 7.7 %collective-permute-start.2 = (bf16[1,16,256]{2,1,0:T(8,128)(2,1)}, bf16[1,16,256]{2,1,0:T(8,128)(2,1)}, u32[]{:S(2)}, u32[]{:S(2)}) collective-permute-start(bf16[1,16,256]{2,1,0:T(8,128)(2,1)} %get-tuple-element.7), channel_id=1, source_target_pairs={{0,1},{1,2},{2,3},{3,4},{4,5},{5,6},{6,7},{7,8},{8,9},{9,10},{10,1... | collective-permute-start | bytes 24584 | tf_op jit(solution)/shard_map/ppermute | solution.py:18
  37.3 4.4 %fusion.37 = bf16[768,2048]{0,1:T(8,128)(2,1)S(1)} fusion(bf16[1,4,256]{2,1,0:T(4,128)(2,1)S(1)} %collective-permute-done.1, bf16[1,2048,256]{2,1,0:T(8,128)(2,1)} %copy-done.5, bf16[1,4,256]{2,1,0:T(4,128)(2,1)} %copy-done.15), kind=kLoop, calls=%fused_computation.57 | loop fusion | flops 15728640 | bytes 4198400 | tf_op jit(solution)/shard_map/dot_general | solution.py:46
  41.7 3.0 %copy.14 = bf16[768,2048]{1,0:T(8,128)(2,1)} copy(bf16[768,2048]{0,1:T(8,128)(2,1)S(1)} %fusion.37) | data formatting | bytes 6291456 | tf_op jit(solution)/shard_map/dot_general | solution.py:46
  44.7 6.6 %fusion.39 = bf16[768,2048]{0,1:T(8,128)(2,1)S(1)} fusion(bf16[1,16,256]{2,1,0:T(8,128)(2,1)S(1)} %collective-permute-done.3, bf16[1,2048,256]{2,1,0:T(8,128)(2,1)} %copy-done.4, bf16[1,16,256]{2,1,0:T(8,128)(2,1)} %collective-permute-done.2), kind=kLoop, calls=%fused_computation.58 | loop fusion | flops 15728640 | bytes 4210688 | tf_op jit(solution)/shard_map/dot_general | solution.py:46
  51.3 3.0 %copy.17 = bf16[768,2048]{1,0:T(8,128)(2,1)} copy(bf16[768,2048]{0,1:T(8,128)(2,1)S(1)} %fusion.39) | data formatting | bytes 6291456 | tf_op jit(solution)/shard_map/dot_general | solution.py:46
  54.2 6.2 %convolution_bitcast_fusion.1 = f32[1,2048,512]{2,1,0:T(8,128)S(1)} fusion(bf16[1,16,256]{2,1,0:T(8,128)(2,1)S(1)} %collective-permute-done.3, bf16[1,2048,256]{2,1,0:T(8,128)(2,1)} %copy-done.4, bf16[1,16,256]{2,1,0:T(8,128)(2,1)} %collective-permute-done.2, bf16[768,256]{1,0:T(8,128)(2,1)} %bitcast.58, bf16[768,256]{1,0:T(8,128)(2,1)S(1)} %bitcast.56), kind=kOutput, calls=%fused_computation.1 | convolution fusion | flops 1627914240 | bytes 6045696 | tf_op jit(solution)/shard_map/dot_general | solution.py:40
  60.5 3.3 %fusion.28 = (bf16[1,2048,256]{2,1,0:T(8,128)(2,1)S(1)}, bf16[1,2048,256]{2,1,0:T(8,128)(2,1)}) fusion(bf16[1,2048,256]{2,1,0:T(8,128)(2,1)S(1)} %copy-done.10, f32[1,2048,512]{2,1,0:T(8,128)S(1)} %convolution_bitcast_fusion.1, f32[1,2048,512]{2,1,0:T(8,128)S(1)} %copy-done.2), kind=kLoop, calls=%fused_computation.43 | loop fusion | flops 18874368 | bytes 11534336 | tf_op jit(solution)/shard_map/convert_element_type | solution.py:132
  63.8 2.6 %collective-permute-start.5 = (bf16[1,16,256]{2,1,0:T(8,128)(2,1)S(1)}, bf16[1,16,256]{2,1,0:T(8,128)(2,1)S(1)}, u32[]{:S(2)}, u32[]{:S(2)}) collective-permute-start(bf16[1,16,256]{2,1,0:T(8,128)(2,1)S(1)} %get-tuple-element.6), channel_id=1, source_target_pairs={{0,1},{1,2},{2,3},{3,4},{4,5},{5,6},{6,7},{7,8},{8,9},{9,10},{10,1... | collective-permute-start | bytes 24584 | tf_op jit(solution)/shard_map/ppermute | solution.py:18
  70.8 5.4 %collective-permute-done.4 = bf16[1,16,256]{2,1,0:T(8,128)(2,1)S(1)} collective-permute-done((bf16[1,16,256]{2,1,0:T(8,128)(2,1)S(1)}, bf16[1,16,256]{2,1,0:T(8,128)(2,1)S(1)}, u32[]{:S(2)}, u32[]{:S(2)}) %collective-permute-start.4) | collective-permute-done | bytes 8224 | tf_op jit(solution)/shard_map/ppermute | solution.py:20
  86.3 5.1 %collective-permute-done.7 = f32[192,256]{1,0:T(8,128)S(1)} collective-permute-done((f32[192,256]{1,0:T(8,128)S(1)}, f32[192,256]{1,0:T(8,128)S(1)}, u32[]{:S(2)}, u32[]{:S(2)}) %collective-permute-start.7) | collective-permute-done | bytes 196640 | tf_op jit(solution)/shard_map/ppermute | solution.py:95
  91.5 2.8 %collective-permute-start.8 = (f32[96,256]{1,0:T(8,128)S(1)}, f32[96,256]{1,0:T(8,128)S(1)}, u32[]{:S(2)}, u32[]{:S(2)}) collective-permute-start(f32[96,256]{1,0:T(8,128)S(1)} %slice_select_fusion.2), channel_id=1, source_target_pairs={{0,32},{16,48},{32,0},{48,16},{64,96},{80,112},{96,64},{112,80},{1... | collective-permute-start | bytes 294920 | tf_op jit(solution)/shard_map/ppermute | solution.py:95
  94.3 2.2 %collective-permute-done.8 = f32[96,256]{1,0:T(8,128)S(1)} collective-permute-done((f32[96,256]{1,0:T(8,128)S(1)}, f32[96,256]{1,0:T(8,128)S(1)}, u32[]{:S(2)}, u32[]{:S(2)}) %collective-permute-start.8) | collective-permute-done | bytes 98336 | tf_op jit(solution)/shard_map/ppermute | solution.py:95
  96.6 3.4 %collective-permute-start.9 = (f32[48,256]{1,0:T(8,128)S(1)}, f32[48,256]{1,0:T(8,128)S(1)}, u32[]{:S(2)}, u32[]{:S(2)}) collective-permute-start(f32[48,256]{1,0:T(8,128)S(1)} %slice_select_fusion.3), channel_id=1, source_target_pairs={{0,4},{1,5},{2,6},{3,7},{4,0},{5,1},{6,2},{7,3},{8,12},{9,13},{10,... | collective-permute-start | bytes 147464 | tf_op jit(solution)/shard_map/ppermute | solution.py:95
  101.5 3.2 %collective-permute-start.10 = (f32[24,256]{1,0:T(8,128)S(1)}, f32[24,256]{1,0:T(8,128)S(1)}, u32[]{:S(2)}, u32[]{:S(2)}) collective-permute-start(f32[24,256]{1,0:T(8,128)S(1)} %slice_select_fusion.4), channel_id=1, source_target_pairs={{0,8},{1,9},{2,10},{3,11},{4,12},{5,13},{6,14},{7,15},{8,0},{9,1},... | collective-permute-start | bytes 73736 | tf_op jit(solution)/shard_map/ppermute | solution.py:95
  112.3 4.6 %collective-permute-start.13 = (f32[3,256]{1,0:T(4,128)S(1)}, f32[3,256]{1,0:T(4,128)S(1)}, u32[]{:S(2)}, u32[]{:S(2)}) collective-permute-start(f32[3,256]{1,0:T(4,128)S(1)} %slice_select_fusion.7), channel_id=1, source_target_pairs={{0,2},{1,3},{2,0},{3,1},{4,6},{5,7},{6,4},{7,5},{8,10},{9,11},{10,... | collective-permute-start | bytes 9224 | tf_op jit(solution)/shard_map/ppermute | solution.py:95
  118.8 4.5 %collective-permute-start.14 = (f32[3,256]{1,0:T(4,128)S(1)}, f32[3,256]{1,0:T(4,128)S(1)}, u32[]{:S(2)}, u32[]{:S(2)}) collective-permute-start(f32[3,256]{1,0:T(4,128)S(1)} %select_add_fusion.7), channel_id=1, source_target_pairs={{0,2},{1,3},{2,0},{3,1},{4,6},{5,7},{6,4},{7,5},{8,10},{9,11},{10,... | collective-permute-start | bytes 9224 | tf_op jit(solution)/shard_map/ppermute | solution.py:100
  131.7 2.5 %collective-permute-start.17 = (f32[24,256]{1,0:T(8,128)S(1)}, f32[24,256]{1,0:T(8,128)S(1)}, u32[]{:S(2)}, u32[]{:S(2)}) collective-permute-start(f32[24,256]{1,0:T(8,128)S(1)} %maximum_select_fusion.5), channel_id=1, source_target_pairs={{0,8},{1,9},{2,10},{3,11},{4,12},{5,13},{6,14},{7,15},{8,0},{9,1},... | collective-permute-start | bytes 73736 | tf_op jit(solution)/shard_map/ppermute | solution.py:100
  138.9 2.8 %collective-permute-start.19 = (f32[96,256]{1,0:T(8,128)S(1)}, f32[96,256]{1,0:T(8,128)S(1)}, u32[]{:S(2)}, u32[]{:S(2)}) collective-permute-start(f32[96,256]{1,0:T(8,128)S(1)} %maximum_select_fusion.3), channel_id=1, source_target_pairs={{0,32},{16,48},{32,0},{48,16},{64,96},{80,112},{96,64},{112,80},{1... | collective-permute-start | bytes 294920 | tf_op jit(solution)/shard_map/ppermute | solution.py:100
  141.7 2.2 %collective-permute-done.19 = f32[96,256]{1,0:T(8,128)S(1)} collective-permute-done((f32[96,256]{1,0:T(8,128)S(1)}, f32[96,256]{1,0:T(8,128)S(1)}, u32[]{:S(2)}, u32[]{:S(2)}) %collective-permute-start.19) | collective-permute-done | bytes 98336 | tf_op jit(solution)/shard_map/ppermute | solution.py:100
  145.3 3.3 %collective-permute-done.20 = f32[192,256]{1,0:T(8,128)S(1)} collective-permute-done((f32[192,256]{1,0:T(8,128)S(1)}, f32[192,256]{1,0:T(8,128)S(1)}, u32[]{:S(2)}, u32[]{:S(2)}) %collective-permute-start.20) | collective-permute-done | bytes 196640 | tf_op jit(solution)/shard_map/ppermute | solution.py:100
  148.6 15.4 %collective-permute-start.21 = (f32[384,256]{1,0:T(8,128)S(1)}, f32[384,256]{1,0:T(8,128)S(1)}, u32[]{:S(2)}, u32[]{:S(2)}) collective-permute-start(f32[384,256]{1,0:T(8,128)S(1)} %maximum_select_fusion.1), channel_id=1, source_target_pairs={{0,1},{1,0},{2,3},{3,2},{4,5},{5,4},{6,7},{7,6},{8,9},{9,8},{10,11... | collective-permute-start | bytes 1179656 | tf_op jit(solution)/shard_map/ppermute | solution.py:100
  (103 shorter events, 55.1 us)
Async XLA Ops:
  0.7 20.3 %copy-start.12 = (bf16[3,256,256]{2,1,0:T(8,128)(2,1)S(1)}, bf16[3,256,256]{2,1,0:T(8,128)(2,1)}, u32[]{:S(2)}) copy-start(bf16[3,256,256]{2,1,0:T(8,128)(2,1)} %param.7) | copy-start | bytes 1179652
  2.5 22.5 %copy-start.5 = (bf16[1,2048,256]{2,1,0:T(8,128)(2,1)}, bf16[1,2048,256]{2,1,0:T(8,128)(2,1)S(1)}, u32[]{:S(2)}) copy-start(bf16[1,2048,256]{2,1,0:T(8,128)(2,1)S(1)} %fusion.14) | copy-start | bytes 3145732
  2.5 20.7 %collective-permute-start.1 = (bf16[1,4,256]{2,1,0:T(4,128)(2,1)S(1)}, bf16[1,4,256]{2,1,0:T(4,128)(2,1)S(1)}, u32[]{:S(2)}, u32[]{:S(2)}) collective-permute-start(bf16[1,4,256]{2,1,0:T(4,128)(2,1)S(1)} %get-tuple-element.10), channel_id=1, source_target_pairs={{1,0},{2,1},{3,2},{4,3},{5,4},{6,5},{7,6},{8,7},{9,8},{10,9},{11,1... | collective-permute-start | bytes 6152 | tf_op jit(solution)/shard_map/ppermute | solution.py:20
  7.6 15.5 %collective-permute-start = (bf16[1,4,256]{2,1,0:T(4,128)(2,1)S(1)}, bf16[1,4,256]{2,1,0:T(4,128)(2,1)S(1)}, u32[]{:S(2)}, u32[]{:S(2)}) collective-permute-start(bf16[1,4,256]{2,1,0:T(4,128)(2,1)S(1)} %get-tuple-element.9), channel_id=1, source_target_pairs={{0,1},{1,2},{2,3},{3,4},{4,5},{5,6},{6,7},{7,8},{8,9},{9,10},{10,1... | collective-permute-start | bytes 6152 | tf_op jit(solution)/shard_map/ppermute | solution.py:18
  27.6 17.0 %collective-permute-start.3 = (bf16[1,16,256]{2,1,0:T(8,128)(2,1)}, bf16[1,16,256]{2,1,0:T(8,128)(2,1)S(1)}, u32[]{:S(2)}, u32[]{:S(2)}) collective-permute-start(bf16[1,16,256]{2,1,0:T(8,128)(2,1)} %get-tuple-element.8), channel_id=1, source_target_pairs={{1,0},{2,1},{3,2},{4,3},{5,4},{6,5},{7,6},{8,7},{9,8},{10,9},{11,1... | collective-permute-start | bytes 24584 | tf_op jit(solution)/shard_map/ppermute | solution.py:20
  29.6 15.1 %collective-permute-start.2 = (bf16[1,16,256]{2,1,0:T(8,128)(2,1)}, bf16[1,16,256]{2,1,0:T(8,128)(2,1)}, u32[]{:S(2)}, u32[]{:S(2)}) collective-permute-start(bf16[1,16,256]{2,1,0:T(8,128)(2,1)} %get-tuple-element.7), channel_id=1, source_target_pairs={{0,1},{1,2},{2,3},{3,4},{4,5},{5,6},{6,7},{7,8},{8,9},{9,10},{10,1... | collective-permute-start | bytes 24584 | tf_op jit(solution)/shard_map/ppermute | solution.py:18
  63.8 7.0 %collective-permute-start.5 = (bf16[1,16,256]{2,1,0:T(8,128)(2,1)S(1)}, bf16[1,16,256]{2,1,0:T(8,128)(2,1)S(1)}, u32[]{:S(2)}, u32[]{:S(2)}) collective-permute-start(bf16[1,16,256]{2,1,0:T(8,128)(2,1)S(1)} %get-tuple-element.6), channel_id=1, source_target_pairs={{0,1},{1,2},{2,3},{3,4},{4,5},{5,6},{6,7},{7,8},{8,9},{9,10},{10,1... | collective-permute-start | bytes 24584 | tf_op jit(solution)/shard_map/ppermute | solution.py:18
  66.4 9.8 %collective-permute-start.4 = (bf16[1,16,256]{2,1,0:T(8,128)(2,1)S(1)}, bf16[1,16,256]{2,1,0:T(8,128)(2,1)S(1)}, u32[]{:S(2)}, u32[]{:S(2)}) collective-permute-start(bf16[1,16,256]{2,1,0:T(8,128)(2,1)S(1)} %get-tuple-element.5), channel_id=1, source_target_pairs={{1,0},{2,1},{3,2},{4,3},{5,4},{6,5},{7,6},{8,7},{9,8},{10,9},{11,1... | collective-permute-start | bytes 24584 | tf_op jit(solution)/shard_map/ppermute | solution.py:20
  83.1 1.8 %collective-permute-start.6 = (f32[384,256]{1,0:T(8,128)S(1)}, f32[384,256]{1,0:T(8,128)S(1)}, u32[]{:S(2)}, u32[]{:S(2)}) collective-permute-start(f32[384,256]{1,0:T(8,128)S(1)} %slice_select_fusion), channel_id=1, source_target_pairs={{0,1},{1,0},{2,3},{3,2},{4,5},{5,4},{6,7},{7,6},{8,9},{9,8},{10,11... | collective-permute-start | bytes 1179656 | tf_op jit(solution)/shard_map/ppermute | solution.py:95
  85.0 6.4 %collective-permute-start.7 = (f32[192,256]{1,0:T(8,128)S(1)}, f32[192,256]{1,0:T(8,128)S(1)}, u32[]{:S(2)}, u32[]{:S(2)}) collective-permute-start(f32[192,256]{1,0:T(8,128)S(1)} %slice_select_fusion.1), channel_id=1, source_target_pairs={{0,16},{16,0},{32,48},{48,32},{64,80},{80,64},{96,112},{112,96},{1... | collective-permute-start | bytes 589832 | tf_op jit(solution)/shard_map/ppermute | solution.py:95
  91.5 5.1 %collective-permute-start.8 = (f32[96,256]{1,0:T(8,128)S(1)}, f32[96,256]{1,0:T(8,128)S(1)}, u32[]{:S(2)}, u32[]{:S(2)}) collective-permute-start(f32[96,256]{1,0:T(8,128)S(1)} %slice_select_fusion.2), channel_id=1, source_target_pairs={{0,32},{16,48},{32,0},{48,16},{64,96},{80,112},{96,64},{112,80},{1... | collective-permute-start | bytes 294920 | tf_op jit(solution)/shard_map/ppermute | solution.py:95
  96.6 4.9 %collective-permute-start.9 = (f32[48,256]{1,0:T(8,128)S(1)}, f32[48,256]{1,0:T(8,128)S(1)}, u32[]{:S(2)}, u32[]{:S(2)}) collective-permute-start(f32[48,256]{1,0:T(8,128)S(1)} %slice_select_fusion.3), channel_id=1, source_target_pairs={{0,4},{1,5},{2,6},{3,7},{4,0},{5,1},{6,2},{7,3},{8,12},{9,13},{10,... | collective-permute-start | bytes 147464 | tf_op jit(solution)/shard_map/ppermute | solution.py:95
  101.5 4.4 %collective-permute-start.10 = (f32[24,256]{1,0:T(8,128)S(1)}, f32[24,256]{1,0:T(8,128)S(1)}, u32[]{:S(2)}, u32[]{:S(2)}) collective-permute-start(f32[24,256]{1,0:T(8,128)S(1)} %slice_select_fusion.4), channel_id=1, source_target_pairs={{0,8},{1,9},{2,10},{3,11},{4,12},{5,13},{6,14},{7,15},{8,0},{9,1},... | collective-permute-start | bytes 73736 | tf_op jit(solution)/shard_map/ppermute | solution.py:95
  105.9 3.0 %collective-permute-start.11 = (f32[12,256]{1,0:T(8,128)S(1)}, f32[12,256]{1,0:T(8,128)S(1)}, u32[]{:S(2)}, u32[]{:S(2)}) collective-permute-start(f32[12,256]{1,0:T(8,128)S(1)} %slice_select_fusion.5), channel_id=1, source_target_pairs={{0,64},{16,80},{32,96},{48,112},{64,0},{80,16},{96,32},{112,48},{1... | collective-permute-start | bytes 36872 | tf_op jit(solution)/shard_map/ppermute | solution.py:95
  108.8 3.5 %collective-permute-start.12 = (f32[6,256]{1,0:T(8,128)S(1)}, f32[6,256]{1,0:T(8,128)S(1)}, u32[]{:S(2)}, u32[]{:S(2)}) collective-permute-start(f32[6,256]{1,0:T(8,128)S(1)} %slice_select_fusion.6), channel_id=1, source_target_pairs={{0,128},{16,144},{32,160},{48,176},{64,192},{80,208},{96,224},{112... | collective-permute-start | bytes 18440 | tf_op jit(solution)/shard_map/ppermute | solution.py:95
  112.3 6.5 %collective-permute-start.13 = (f32[3,256]{1,0:T(4,128)S(1)}, f32[3,256]{1,0:T(4,128)S(1)}, u32[]{:S(2)}, u32[]{:S(2)}) collective-permute-start(f32[3,256]{1,0:T(4,128)S(1)} %slice_select_fusion.7), channel_id=1, source_target_pairs={{0,2},{1,3},{2,0},{3,1},{4,6},{5,7},{6,4},{7,5},{8,10},{9,11},{10,... | collective-permute-start | bytes 9224 | tf_op jit(solution)/shard_map/ppermute | solution.py:95
  118.8 6.4 %collective-permute-start.14 = (f32[3,256]{1,0:T(4,128)S(1)}, f32[3,256]{1,0:T(4,128)S(1)}, u32[]{:S(2)}, u32[]{:S(2)}) collective-permute-start(f32[3,256]{1,0:T(4,128)S(1)} %select_add_fusion.7), channel_id=1, source_target_pairs={{0,2},{1,3},{2,0},{3,1},{4,6},{5,7},{6,4},{7,5},{8,10},{9,11},{10,... | collective-permute-start | bytes 9224 | tf_op jit(solution)/shard_map/ppermute | solution.py:100
  125.2 3.5 %collective-permute-start.15 = (f32[6,256]{1,0:T(8,128)S(1)}, f32[6,256]{1,0:T(8,128)S(1)}, u32[]{:S(2)}, u32[]{:S(2)}) collective-permute-start(f32[6,256]{1,0:T(8,128)S(1)} %maximum_select_fusion.7), channel_id=1, source_target_pairs={{0,128},{16,144},{32,160},{48,176},{64,192},{80,208},{96,224},{112... | collective-permute-start | bytes 18440 | tf_op jit(solution)/shard_map/ppermute | solution.py:100
  128.7 3.0 %collective-permute-start.16 = (f32[12,256]{1,0:T(8,128)S(1)}, f32[12,256]{1,0:T(8,128)S(1)}, u32[]{:S(2)}, u32[]{:S(2)}) collective-permute-start(f32[12,256]{1,0:T(8,128)S(1)} %maximum_select_fusion.6), channel_id=1, source_target_pairs={{0,64},{16,80},{32,96},{48,112},{64,0},{80,16},{96,32},{112,48},{1... | collective-permute-start | bytes 36872 | tf_op jit(solution)/shard_map/ppermute | solution.py:100
  131.7 4.3 %collective-permute-start.17 = (f32[24,256]{1,0:T(8,128)S(1)}, f32[24,256]{1,0:T(8,128)S(1)}, u32[]{:S(2)}, u32[]{:S(2)}) collective-permute-start(f32[24,256]{1,0:T(8,128)S(1)} %maximum_select_fusion.5), channel_id=1, source_target_pairs={{0,8},{1,9},{2,10},{3,11},{4,12},{5,13},{6,14},{7,15},{8,0},{9,1},... | collective-permute-start | bytes 73736 | tf_op jit(solution)/shard_map/ppermute | solution.py:100
  135.9 2.9 %collective-permute-start.18 = (f32[48,256]{1,0:T(8,128)S(1)}, f32[48,256]{1,0:T(8,128)S(1)}, u32[]{:S(2)}, u32[]{:S(2)}) collective-permute-start(f32[48,256]{1,0:T(8,128)S(1)} %maximum_select_fusion.4), channel_id=1, source_target_pairs={{0,4},{1,5},{2,6},{3,7},{4,0},{5,1},{6,2},{7,3},{8,12},{9,13},{10,... | collective-permute-start | bytes 147464 | tf_op jit(solution)/shard_map/ppermute | solution.py:100
  138.9 5.1 %collective-permute-start.19 = (f32[96,256]{1,0:T(8,128)S(1)}, f32[96,256]{1,0:T(8,128)S(1)}, u32[]{:S(2)}, u32[]{:S(2)}) collective-permute-start(f32[96,256]{1,0:T(8,128)S(1)} %maximum_select_fusion.3), channel_id=1, source_target_pairs={{0,32},{16,48},{32,0},{48,16},{64,96},{80,112},{96,64},{112,80},{1... | collective-permute-start | bytes 294920 | tf_op jit(solution)/shard_map/ppermute | solution.py:100
  144.0 4.6 %collective-permute-start.20 = (f32[192,256]{1,0:T(8,128)S(1)}, f32[192,256]{1,0:T(8,128)S(1)}, u32[]{:S(2)}, u32[]{:S(2)}) collective-permute-start(f32[192,256]{1,0:T(8,128)S(1)} %maximum_select_fusion.2), channel_id=1, source_target_pairs={{0,16},{16,0},{32,48},{48,32},{64,80},{80,64},{96,112},{112,96},{1... | collective-permute-start | bytes 589832 | tf_op jit(solution)/shard_map/ppermute | solution.py:100
  148.6 16.7 %collective-permute-start.21 = (f32[384,256]{1,0:T(8,128)S(1)}, f32[384,256]{1,0:T(8,128)S(1)}, u32[]{:S(2)}, u32[]{:S(2)}) collective-permute-start(f32[384,256]{1,0:T(8,128)S(1)} %maximum_select_fusion.1), channel_id=1, source_target_pairs={{0,1},{1,0},{2,3},{3,2},{4,5},{5,4},{6,7},{7,6},{8,9},{9,8},{10,11... | collective-permute-start | bytes 1179656 | tf_op jit(solution)/shard_map/ppermute | solution.py:100
  (14 other events, 71.8 us)

commit v2 on v0

--- a/solution.py
+++ b/solution.py
@@ -74,6 +74,54 @@
     return term + term[::-1, ::-1, ::-1]
 
 
+def exchange_groups():
+    groups = []
+    for axis, shift, radix in (("dp", 0, 4), ("seq", 2, 4), ("dp", 2, 4), ("seq", 0, 4)):
+        if (radix << shift) <= lax.axis_size(axis):
+            groups.append((axis, shift, radix))
+    return groups
+
+
+def partner_pairs(axis, shift, offset):
+    count = lax.axis_size(axis)
+    return [(i, i ^ (offset << shift)) for i in range(count)]
+
+
+def butterfly_sum(rows):
+    kept = []
+    for axis, shift, radix in exchange_groups():
+        place = (lax.axis_index(axis) >> shift) & (radix - 1)
+        width = rows.shape[0] // radix
+        total = lax.dynamic_slice_in_dim(rows, place * width, width)
+        for offset in range(1, radix):
+            sent = lax.dynamic_slice_in_dim(rows, (place ^ offset) * width, width)
+            total = total + lax.ppermute(sent, axis, partner_pairs(axis, shift, offset))
+        rows = total
+        kept.append((axis, shift, radix, place))
+    for axis, shift, radix, place in reversed(kept):
+        width = rows.shape[0]
+        full = jnp.zeros((width * radix,) + rows.shape[1:], rows.dtype)
+        full = lax.dynamic_update_slice_in_dim(full, rows, place * width, 0)
+        for offset in range(1, radix):
+            got = lax.ppermute(rows, axis, partner_pairs(axis, shift, offset))
+            full = lax.dynamic_update_slice_in_dim(full, got, (place ^ offset) * width, 0)
+        rows = full
+    return rows
+
+
+def symmetric_sum(first, second):
+    shape = first.shape
+    flat_rows = shape[0] * shape[1]
+    half = flat_rows // 2
+    halves = [g.reshape(flat_rows, shape[2])[:half] for g in (first, second)]
+    total = butterfly_sum(jnp.concatenate(halves, axis=0))
+    outs = []
+    for i in range(2):
+        part = total[i * half : (i + 1) * half]
+        outs.append(jnp.concatenate([part, part[::-1, ::-1]], axis=0).reshape(shape))
+    return outs
+
+
 def local(codes, embed, first_weight_taps, second_weight_taps, cotangent):
     onehot = (codes[..., None] == jnp.arange(4, dtype=jnp.int32)).astype(jnp.bfloat16)
     nucleotide_features = product(onehot, embed).astype(jnp.bfloat16)
@@ -93,11 +141,12 @@
         second_activation_gradient, second_weight_taps, SECOND_DILATION
     )
     second_weight_gradient = strand_total(second_shift_stack, second_activation_gradient)
-    second_weight_gradient = lax.psum(second_weight_gradient, ("dp", "seq"))
     hidden_gradient = cotangent_wide_float + input_contribution
     first_activation_gradient = back_one(hidden_gradient)[0].astype(jnp.bfloat16)
     first_weight_gradient = strand_total(first_shift_stack, first_activation_gradient)
-    first_weight_gradient = lax.psum(first_weight_gradient, ("dp", "seq"))
+    second_weight_gradient, first_weight_gradient = symmetric_sum(
+        second_weight_gradient, first_weight_gradient
+    )
     return (block_out, first_weight_gradient, second_weight_gradient)
 
 

time: 366 us -> 161 us (0.44)
  waiting for transfers between devices: 265 us -> 34.3 us
  starting transfers between devices: 26.3 us -> 68.4 us
  between operations: 14.4 us -> 1.18 us
    psum x1 -> x0, waiting for transfers between devices: 265 us -> none  [local(): first_weight_gradient = lax.psum(first_weight_gradient, ('dp', 'seq'))]
    ppermute x0 -> x24, starting transfers between devices: none -> 41.9 us  [the longest x12 23.4 us: butterfly_sum(): total = total + lax.ppermute(sent, axis, partner_pairs(axis, shift, offset))]
    ppermute x0 -> x24, waiting for transfers between devices: none -> 29 us  [the longest x12 17.6 us: butterfly_sum(): got = lax.ppermute(rows, axis, partner_pairs(axis, shift, offset))]
    ppermute x3, waiting for transfers between devices: 0.01 us -> 5.35 us  [with_halo(): lax.ppermute(head, axis, [((i + 1) % count, i) for i in range(ends)])]
    unnamed x41 -> x33, local copies, waits for them, and re-layouts: 7.38 us -> 4.42 us
  transfers between devices with their start and end apart: 7 -> 30, of which waited for: 1 -> 17; matrix products, arithmetic and copies ran while one was open for 9% -> 12% of each run, Pallas kernels for 0% -> 0%
where the time goes in v2:
time: 161 us; the launch traced here: 158 us
  starting transfers between devices  68.4 us (42%)
  waiting for transfers between devices  34.3 us (21%)
  local copies, waits for them, and re-layouts  23.2 us (14%)
  other arithmetic  16.7 us (10%)
  matrix products  14.2 us (9%)
    ppermute x12, starting transfers between devices, butterfly_sum(): total = total + lax.ppermute(sent, axis, partner_pairs(axis, shift, offset))  23.4 us
    ppermute x12, starting transfers between devices, butterfly_sum(): got = lax.ppermute(rows, axis, partner_pairs(axis, shift, offset))  18.5 us
    ppermute x12, waiting for transfers between devices, butterfly_sum(): got = lax.ppermute(rows, axis, partner_pairs(axis, shift, offset))  17.6 us
    ppermute x3, starting transfers between devices, with_halo(): lax.ppermute(tail, axis, [(i, (i + 1) % count) for i in range(ends)])  17.4 us
    ppermute x12, waiting for transfers between devices, butterfly_sum(): total = total + lax.ppermute(sent, axis, partner_pairs(axis, shift, offset))  11.4 us
    dot_general x4, matrix products, product(): jnp.dot(stacked.reshape(-1, shape_in[-1]), matrix, preferred_element_type...  11 us
    dot_general x2, other arithmetic, weight_term(): jnp.dot(stacked.reshape(-1, 3 * channels).T, grad.reshape(-1, channels),...  10.8 us
    ppermute x3, starting transfers between devices, with_halo(): lax.ppermute(head, axis, [((i + 1) % count, i) for i in range(ends)])  9.16 us
  transfers between devices with their start and end apart: 30, of which 17 were waited for; matrix products, arithmetic and copies ran while one was open for 12% of the time, Pallas kernels for 0%

profile of v2, /device:TPU:1, one launch (start us, length us, event | category | flops | bytes accessed | tf_op | source)
XLA Modules:
  0.0 158.0 jit_solution(14648152525572654912)
XLA Ops:
  2.5 5.1 %collective-permute-start.1 = (bf16[1,4,256]{2,1,0:T(4,128)(2,1)S(1)}, bf16[1,4,256]{2,1,0:T(4,128)(2,1)S(1)}, u32[]{:S(2)}, u32[]{:S(2)}) collective-permute-start(bf16[1,4,256]{2,1,0:T(4,128)(2,1)S(1)} %get-tuple-element.10), channel_id=1, source_target_pairs={{1,0},{2,1},{3,2},{4,3},{5,4},{6,5},{7,6},{8,7},{9,8},{10,9},{11,1... | collective-permute-start | bytes 6152 | tf_op jit(solution)/shard_map/ppermute | solution.py:20
  7.6 7.0 %collective-permute-start = (bf16[1,4,256]{2,1,0:T(4,128)(2,1)S(1)}, bf16[1,4,256]{2,1,0:T(4,128)(2,1)S(1)}, u32[]{:S(2)}, u32[]{:S(2)}) collective-permute-start(bf16[1,4,256]{2,1,0:T(4,128)(2,1)S(1)} %get-tuple-element.9), channel_id=1, source_target_pairs={{0,1},{1,2},{2,3},{3,4},{4,5},{5,6},{6,7},{7,8},{8,9},{9,10},{10,1... | collective-permute-start | bytes 6152 | tf_op jit(solution)/shard_map/ppermute | solution.py:18
  14.7 5.3 %rev.20 = bf16[3,256,256]{2,1,0:T(8,128)(2,1)S(1)} reverse(bf16[3,256,256]{2,1,0:T(8,128)(2,1)} %param.8), dimensions={0,1,2} | reverse | bytes 786432 | tf_op jit(solution)/shard_map/rev | solution.py:58
  29.6 7.7 %collective-permute-start.2 = (bf16[1,16,256]{2,1,0:T(8,128)(2,1)}, bf16[1,16,256]{2,1,0:T(8,128)(2,1)}, u32[]{:S(2)}, u32[]{:S(2)}) collective-permute-start(bf16[1,16,256]{2,1,0:T(8,128)(2,1)} %get-tuple-element.7), channel_id=1, source_target_pairs={{0,1},{1,2},{2,3},{3,4},{4,5},{5,6},{6,7},{7,8},{8,9},{9,10},{10,1... | collective-permute-start | bytes 24584 | tf_op jit(solution)/shard_map/ppermute | solution.py:18
  37.4 4.3 %fusion.37 = bf16[768,2048]{0,1:T(8,128)(2,1)S(1)} fusion(bf16[1,4,256]{2,1,0:T(4,128)(2,1)S(1)} %collective-permute-done.1, bf16[1,2048,256]{2,1,0:T(8,128)(2,1)} %copy-done.5, bf16[1,4,256]{2,1,0:T(4,128)(2,1)} %copy-done.15), kind=kLoop, calls=%fused_computation.65 | loop fusion | flops 15728640 | bytes 4198400 | tf_op jit(solution)/shard_map/dot_general | solution.py:46
  41.6 3.0 %copy.15 = bf16[768,2048]{1,0:T(8,128)(2,1)} copy(bf16[768,2048]{0,1:T(8,128)(2,1)S(1)} %fusion.37) | data formatting | bytes 6291456 | tf_op jit(solution)/shard_map/dot_general | solution.py:46
  44.6 6.6 %fusion.39 = bf16[768,2048]{0,1:T(8,128)(2,1)S(1)} fusion(bf16[1,16,256]{2,1,0:T(8,128)(2,1)S(1)} %collective-permute-done.3, bf16[1,2048,256]{2,1,0:T(8,128)(2,1)} %copy-done.4, bf16[1,16,256]{2,1,0:T(8,128)(2,1)} %collective-permute-done.2), kind=kLoop, calls=%fused_computation.66 | loop fusion | flops 15728640 | bytes 4210688 | tf_op jit(solution)/shard_map/dot_general | solution.py:46
  51.2 3.0 %copy.14 = bf16[768,2048]{1,0:T(8,128)(2,1)} copy(bf16[768,2048]{0,1:T(8,128)(2,1)S(1)} %fusion.39) | data formatting | bytes 6291456 | tf_op jit(solution)/shard_map/dot_general | solution.py:46
  54.1 6.2 %convolution_bitcast_fusion.1 = f32[1,2048,512]{2,1,0:T(8,128)S(1)} fusion(bf16[1,16,256]{2,1,0:T(8,128)(2,1)S(1)} %collective-permute-done.3, bf16[1,2048,256]{2,1,0:T(8,128)(2,1)} %copy-done.4, bf16[1,16,256]{2,1,0:T(8,128)(2,1)} %collective-permute-done.2, bf16[768,256]{1,0:T(8,128)(2,1)} %bitcast.56, bf16[768,256]{1,0:T(8,128)(2,1)S(1)} %bitcast.54), kind=kOutput, calls=%fused_computation.1 | convolution fusion | flops 1627914240 | bytes 6045696 | tf_op jit(solution)/shard_map/dot_general | solution.py:40
  60.4 3.3 %fusion.28 = (bf16[1,2048,256]{2,1,0:T(8,128)(2,1)S(1)}, bf16[1,2048,256]{2,1,0:T(8,128)(2,1)}) fusion(bf16[1,2048,256]{2,1,0:T(8,128)(2,1)S(1)} %copy-done.10, f32[1,2048,512]{2,1,0:T(8,128)S(1)} %convolution_bitcast_fusion.1, f32[1,2048,512]{2,1,0:T(8,128)S(1)} %copy-done.2), kind=kLoop, calls=%fused_computation.43 | loop fusion | flops 18874368 | bytes 11534336 | tf_op jit(solution)/shard_map/convert_element_type | solution.py:139
  63.7 2.6 %collective-permute-start.5 = (bf16[1,16,256]{2,1,0:T(8,128)(2,1)S(1)}, bf16[1,16,256]{2,1,0:T(8,128)(2,1)S(1)}, u32[]{:S(2)}, u32[]{:S(2)}) collective-permute-start(bf16[1,16,256]{2,1,0:T(8,128)(2,1)S(1)} %get-tuple-element.6), channel_id=1, source_target_pairs={{0,1},{1,2},{2,3},{3,4},{4,5},{5,6},{6,7},{7,8},{8,9},{9,10},{10,1... | collective-permute-start | bytes 24584 | tf_op jit(solution)/shard_map/ppermute | solution.py:18
  66.3 2.1 %collective-permute-start.4 = (bf16[1,16,256]{2,1,0:T(8,128)(2,1)S(1)}, bf16[1,16,256]{2,1,0:T(8,128)(2,1)S(1)}, u32[]{:S(2)}, u32[]{:S(2)}) collective-permute-start(bf16[1,16,256]{2,1,0:T(8,128)(2,1)S(1)} %get-tuple-element.5), channel_id=1, source_target_pairs={{1,0},{2,1},{3,2},{4,3},{5,4},{6,5},{7,6},{8,7},{9,8},{10,9},{11,1... | collective-permute-start | bytes 24584 | tf_op jit(solution)/shard_map/ppermute | solution.py:20
  70.8 5.3 %collective-permute-done.4 = bf16[1,16,256]{2,1,0:T(8,128)(2,1)S(1)} collective-permute-done((bf16[1,16,256]{2,1,0:T(8,128)(2,1)S(1)}, bf16[1,16,256]{2,1,0:T(8,128)(2,1)S(1)}, u32[]{:S(2)}, u32[]{:S(2)}) %collective-permute-start.4) | collective-permute-done | bytes 8224 | tf_op jit(solution)/shard_map/ppermute | solution.py:20
  79.5 2.2 %fusion.32 = f32[3,256,256]{2,1,0:T(8,128)S(1)} fusion(bf16[3,256,2048]{2,1,0:T(8,128)(2,1)S(1)} %bitcast.50, f32[1,2048,512]{2,1,0:T(8,128)S(1)} %convolution_bitcast_fusion, bf16[1,2048,256]{2,1,0:T(8,128)(2,1)S(1)} %copy-done.11, f32[1,2048,512]{2,1,0:T(8,128)S(1)} %copy-done.3), kind=kOutput, calls=%fused_computation.60 | convolution fusion | flops 817889280 | bytes 13369344 | tf_op jit(solution)/shard_map/dot_general | solution.py:46
  83.2 2.6 %collective-permute-start.8 = (f32[192,256]{1,0:T(8,128)S(1)}, f32[192,256]{1,0:T(8,128)S(1)}, u32[]{:S(2)}, u32[]{:S(2)}) collective-permute-start(f32[192,256]{1,0:T(8,128)S(1)} %get-tuple-element.15), channel_id=1, source_target_pairs={{0,48},{16,32},{32,16},{48,0},{64,112},{80,96},{96,80},{112,64},{1... | collective-permute-start | bytes 589832 | tf_op jit(solution)/shard_map/ppermute | solution.py:98
  86.5 3.9 %collective-permute-done.8 = f32[192,256]{1,0:T(8,128)S(1)} collective-permute-done((f32[192,256]{1,0:T(8,128)S(1)}, f32[192,256]{1,0:T(8,128)S(1)}, u32[]{:S(2)}, u32[]{:S(2)}) %collective-permute-start.8) | collective-permute-done | bytes 196640 | tf_op jit(solution)/shard_map/ppermute | solution.py:98
  93.6 3.7 %collective-permute-start.10 = (f32[48,256]{1,0:T(8,128)S(1)}, f32[48,256]{1,0:T(8,128)S(1)}, u32[]{:S(2)}, u32[]{:S(2)}) collective-permute-start(f32[48,256]{1,0:T(8,128)S(1)} %get-tuple-element.18), channel_id=1, source_target_pairs={{0,8},{1,9},{2,10},{3,11},{4,12},{5,13},{6,14},{7,15},{8,0},{9,1},... | collective-permute-start | bytes 147464 | tf_op jit(solution)/shard_map/ppermute | solution.py:98
  105.8 3.5 %collective-permute-start.17 = (f32[3,256]{1,0:T(4,128)S(1)}, f32[3,256]{1,0:T(4,128)S(1)}, u32[]{:S(2)}, u32[]{:S(2)}) collective-permute-start(f32[3,256]{1,0:T(4,128)S(1)} %get-tuple-element.23), channel_id=1, source_target_pairs={{0,3},{1,2},{2,1},{3,0},{4,7},{5,6},{6,5},{7,4},{8,11},{9,10},{10,... | collective-permute-start | bytes 9224 | tf_op jit(solution)/shard_map/ppermute | solution.py:98
  109.3 7.5 %collective-permute-start.16 = (f32[3,256]{1,0:T(4,128)S(1)}, f32[3,256]{1,0:T(4,128)S(1)}, u32[]{:S(2)}, u32[]{:S(2)}) collective-permute-start(f32[3,256]{1,0:T(4,128)S(1)} %get-tuple-element.24), channel_id=1, source_target_pairs={{0,2},{1,3},{2,0},{3,1},{4,6},{5,7},{6,4},{7,5},{8,10},{9,11},{10,... | collective-permute-start | bytes 9224 | tf_op jit(solution)/shard_map/ppermute | solution.py:98
  119.6 4.1 %collective-permute-start.19 = (f32[3,256]{1,0:T(4,128)S(1)}, f32[3,256]{1,0:T(4,128)S(1)}, u32[]{:S(2)}, u32[]{:S(2)}) collective-permute-start(f32[3,256]{1,0:T(4,128)S(1)} %fusion.60), channel_id=1, source_target_pairs={{0,2},{1,3},{2,0},{3,1},{4,6},{5,7},{6,4},{7,5},{8,10},{9,11},{10,... | collective-permute-start | bytes 9224 | tf_op jit(solution)/shard_map/ppermute | solution.py:106
  126.0 4.9 %collective-permute-done.20 = f32[3,256]{1,0:T(4,128)S(1)} collective-permute-done((f32[3,256]{1,0:T(4,128)S(1)}, f32[3,256]{1,0:T(4,128)S(1)}, u32[]{:S(2)}, u32[]{:S(2)}) %collective-permute-start.20) | collective-permute-done | bytes 3104 | tf_op jit(solution)/shard_map/ppermute | solution.py:106
  138.2 2.3 %collective-permute-start.25 = (f32[48,256]{1,0:T(8,128)S(1)}, f32[48,256]{1,0:T(8,128)S(1)}, u32[]{:S(2)}, u32[]{:S(2)}) collective-permute-start(f32[48,256]{1,0:T(8,128)S(1)} %dynamic_update_slice.55), channel_id=1, source_target_pairs={{0,8},{1,9},{2,10},{3,11},{4,12},{5,13},{6,14},{7,15},{8,0},{9,1},... | collective-permute-start | bytes 147464 | tf_op jit(solution)/shard_map/ppermute | solution.py:106
  145.9 2.5 %collective-permute-start.28 = (f32[192,256]{1,0:T(8,128)S(1)}, f32[192,256]{1,0:T(8,128)S(1)}, u32[]{:S(2)}, u32[]{:S(2)}) collective-permute-start(f32[192,256]{1,0:T(8,128)S(1)} %constant_dynamic-update-slice_fusion.4), channel_id=1, source_target_pairs={{0,32},{16,48},{32,0},{48,16},{64,96},{80,112},{96,64},{112,80},{1... | collective-permute-start | bytes 589832 | tf_op jit(solution)/shard_map/ppermute | solution.py:106
  149.3 4.3 %collective-permute-done.28 = f32[192,256]{1,0:T(8,128)S(1)} collective-permute-done((f32[192,256]{1,0:T(8,128)S(1)}, f32[192,256]{1,0:T(8,128)S(1)}, u32[]{:S(2)}, u32[]{:S(2)}) %collective-permute-start.28) | collective-permute-done | bytes 196640 | tf_op jit(solution)/shard_map/ppermute | solution.py:106
  (125 shorter events, 53.7 us)
Async XLA Ops:
  2.5 20.7 %collective-permute-start.1 = (bf16[1,4,256]{2,1,0:T(4,128)(2,1)S(1)}, bf16[1,4,256]{2,1,0:T(4,128)(2,1)S(1)}, u32[]{:S(2)}, u32[]{:S(2)}) collective-permute-start(bf16[1,4,256]{2,1,0:T(4,128)(2,1)S(1)} %get-tuple-element.10), channel_id=1, source_target_pairs={{1,0},{2,1},{3,2},{4,3},{5,4},{6,5},{7,6},{8,7},{9,8},{10,9},{11,1... | collective-permute-start | bytes 6152 | tf_op jit(solution)/shard_map/ppermute | solution.py:20
  7.6 15.5 %collective-permute-start = (bf16[1,4,256]{2,1,0:T(4,128)(2,1)S(1)}, bf16[1,4,256]{2,1,0:T(4,128)(2,1)S(1)}, u32[]{:S(2)}, u32[]{:S(2)}) collective-permute-start(bf16[1,4,256]{2,1,0:T(4,128)(2,1)S(1)} %get-tuple-element.9), channel_id=1, source_target_pairs={{0,1},{1,2},{2,3},{3,4},{4,5},{5,6},{6,7},{7,8},{8,9},{9,10},{10,1... | collective-permute-start | bytes 6152 | tf_op jit(solution)/shard_map/ppermute | solution.py:18
  27.7 16.9 %collective-permute-start.3 = (bf16[1,16,256]{2,1,0:T(8,128)(2,1)}, bf16[1,16,256]{2,1,0:T(8,128)(2,1)S(1)}, u32[]{:S(2)}, u32[]{:S(2)}) collective-permute-start(bf16[1,16,256]{2,1,0:T(8,128)(2,1)} %get-tuple-element.8), channel_id=1, source_target_pairs={{1,0},{2,1},{3,2},{4,3},{5,4},{6,5},{7,6},{8,7},{9,8},{10,9},{11,1... | collective-permute-start | bytes 24584 | tf_op jit(solution)/shard_map/ppermute | solution.py:20
  29.6 15.0 %collective-permute-start.2 = (bf16[1,16,256]{2,1,0:T(8,128)(2,1)}, bf16[1,16,256]{2,1,0:T(8,128)(2,1)}, u32[]{:S(2)}, u32[]{:S(2)}) collective-permute-start(bf16[1,16,256]{2,1,0:T(8,128)(2,1)} %get-tuple-element.7), channel_id=1, source_target_pairs={{0,1},{1,2},{2,3},{3,4},{4,5},{5,6},{6,7},{7,8},{8,9},{9,10},{10,1... | collective-permute-start | bytes 24584 | tf_op jit(solution)/shard_map/ppermute | solution.py:18
  63.7 7.1 %collective-permute-start.5 = (bf16[1,16,256]{2,1,0:T(8,128)(2,1)S(1)}, bf16[1,16,256]{2,1,0:T(8,128)(2,1)S(1)}, u32[]{:S(2)}, u32[]{:S(2)}) collective-permute-start(bf16[1,16,256]{2,1,0:T(8,128)(2,1)S(1)} %get-tuple-element.6), channel_id=1, source_target_pairs={{0,1},{1,2},{2,3},{3,4},{4,5},{5,6},{6,7},{7,8},{8,9},{9,10},{10,1... | collective-permute-start | bytes 24584 | tf_op jit(solution)/shard_map/ppermute | solution.py:18
  66.3 9.8 %collective-permute-start.4 = (bf16[1,16,256]{2,1,0:T(8,128)(2,1)S(1)}, bf16[1,16,256]{2,1,0:T(8,128)(2,1)S(1)}, u32[]{:S(2)}, u32[]{:S(2)}) collective-permute-start(bf16[1,16,256]{2,1,0:T(8,128)(2,1)S(1)} %get-tuple-element.5), channel_id=1, source_target_pairs={{1,0},{2,1},{3,2},{4,3},{5,4},{6,5},{7,6},{8,7},{9,8},{10,9},{11,1... | collective-permute-start | bytes 24584 | tf_op jit(solution)/shard_map/ppermute | solution.py:20
  83.2 7.3 %collective-permute-start.8 = (f32[192,256]{1,0:T(8,128)S(1)}, f32[192,256]{1,0:T(8,128)S(1)}, u32[]{:S(2)}, u32[]{:S(2)}) collective-permute-start(f32[192,256]{1,0:T(8,128)S(1)} %get-tuple-element.15), channel_id=1, source_target_pairs={{0,48},{16,32},{32,16},{48,0},{64,112},{80,96},{96,80},{112,64},{1... | collective-permute-start | bytes 589832 | tf_op jit(solution)/shard_map/ppermute | solution.py:98
  85.8 6.0 %collective-permute-start.7 = (f32[192,256]{1,0:T(8,128)S(1)}, f32[192,256]{1,0:T(8,128)S(1)}, u32[]{:S(2)}, u32[]{:S(2)}) collective-permute-start(f32[192,256]{1,0:T(8,128)S(1)} %get-tuple-element.14), channel_id=1, source_target_pairs={{0,32},{16,48},{32,0},{48,16},{64,96},{80,112},{96,64},{112,80},{1... | collective-permute-start | bytes 589832 | tf_op jit(solution)/shard_map/ppermute | solution.py:98
  86.3 5.5 %collective-permute-start.6 = (f32[192,256]{1,0:T(8,128)S(1)}, f32[192,256]{1,0:T(8,128)S(1)}, u32[]{:S(2)}, u32[]{:S(2)}) collective-permute-start(f32[192,256]{1,0:T(8,128)S(1)} %get-tuple-element.13), channel_id=1, source_target_pairs={{0,16},{16,0},{32,48},{48,32},{64,80},{80,64},{96,112},{112,96},{1... | collective-permute-start | bytes 589832 | tf_op jit(solution)/shard_map/ppermute | solution.py:98
  91.9 5.4 %collective-permute-start.11 = (f32[48,256]{1,0:T(8,128)S(1)}, f32[48,256]{1,0:T(8,128)S(1)}, u32[]{:S(2)}, u32[]{:S(2)}) collective-permute-start(f32[48,256]{1,0:T(8,128)S(1)} %get-tuple-element.17), channel_id=1, source_target_pairs={{0,12},{1,13},{2,14},{3,15},{4,8},{5,9},{6,10},{7,11},{8,4},{9,5},... | collective-permute-start | bytes 147464 | tf_op jit(solution)/shard_map/ppermute | solution.py:98
  93.6 5.2 %collective-permute-start.10 = (f32[48,256]{1,0:T(8,128)S(1)}, f32[48,256]{1,0:T(8,128)S(1)}, u32[]{:S(2)}, u32[]{:S(2)}) collective-permute-start(f32[48,256]{1,0:T(8,128)S(1)} %get-tuple-element.18), channel_id=1, source_target_pairs={{0,8},{1,9},{2,10},{3,11},{4,12},{5,13},{6,14},{7,15},{8,0},{9,1},... | collective-permute-start | bytes 147464 | tf_op jit(solution)/shard_map/ppermute | solution.py:98
  100.3 4.5 %collective-permute-start.14 = (f32[12,256]{1,0:T(8,128)S(1)}, f32[12,256]{1,0:T(8,128)S(1)}, u32[]{:S(2)}, u32[]{:S(2)}) collective-permute-start(f32[12,256]{1,0:T(8,128)S(1)} %get-tuple-element.20), channel_id=1, source_target_pairs={{0,192},{16,208},{32,224},{48,240},{64,128},{80,144},{96,160},{112... | collective-permute-start | bytes 36872 | tf_op jit(solution)/shard_map/ppermute | solution.py:98
  105.8 11.0 %collective-permute-start.17 = (f32[3,256]{1,0:T(4,128)S(1)}, f32[3,256]{1,0:T(4,128)S(1)}, u32[]{:S(2)}, u32[]{:S(2)}) collective-permute-start(f32[3,256]{1,0:T(4,128)S(1)} %get-tuple-element.23), channel_id=1, source_target_pairs={{0,3},{1,2},{2,1},{3,0},{4,7},{5,6},{6,5},{7,4},{8,11},{9,10},{10,... | collective-permute-start | bytes 9224 | tf_op jit(solution)/shard_map/ppermute | solution.py:98
  109.3 8.8 %collective-permute-start.16 = (f32[3,256]{1,0:T(4,128)S(1)}, f32[3,256]{1,0:T(4,128)S(1)}, u32[]{:S(2)}, u32[]{:S(2)}) collective-permute-start(f32[3,256]{1,0:T(4,128)S(1)} %get-tuple-element.24), channel_id=1, source_target_pairs={{0,2},{1,3},{2,0},{3,1},{4,6},{5,7},{6,4},{7,5},{8,10},{9,11},{10,... | collective-permute-start | bytes 9224 | tf_op jit(solution)/shard_map/ppermute | solution.py:98
  118.2 7.2 %collective-permute-start.18 = (f32[3,256]{1,0:T(4,128)S(1)}, f32[3,256]{1,0:T(4,128)S(1)}, u32[]{:S(2)}, u32[]{:S(2)}) collective-permute-start(f32[3,256]{1,0:T(4,128)S(1)} %fusion.60), channel_id=1, source_target_pairs={{0,1},{1,0},{2,3},{3,2},{4,5},{5,4},{6,7},{7,6},{8,9},{9,8},{10,11... | collective-permute-start | bytes 9224 | tf_op jit(solution)/shard_map/ppermute | solution.py:106
  119.6 6.4 %collective-permute-start.19 = (f32[3,256]{1,0:T(4,128)S(1)}, f32[3,256]{1,0:T(4,128)S(1)}, u32[]{:S(2)}, u32[]{:S(2)}) collective-permute-start(f32[3,256]{1,0:T(4,128)S(1)} %fusion.60), channel_id=1, source_target_pairs={{0,2},{1,3},{2,0},{3,1},{4,6},{5,7},{6,4},{7,5},{8,10},{9,11},{10,... | collective-permute-start | bytes 9224 | tf_op jit(solution)/shard_map/ppermute | solution.py:106
  123.7 7.3 %collective-permute-start.20 = (f32[3,256]{1,0:T(4,128)S(1)}, f32[3,256]{1,0:T(4,128)S(1)}, u32[]{:S(2)}, u32[]{:S(2)}) collective-permute-start(f32[3,256]{1,0:T(4,128)S(1)} %fusion.60), channel_id=1, source_target_pairs={{0,3},{1,2},{2,1},{3,0},{4,7},{5,6},{6,5},{7,4},{8,11},{9,10},{10,... | collective-permute-start | bytes 9224 | tf_op jit(solution)/shard_map/ppermute | solution.py:106
  133.0 4.4 %collective-permute-start.23 = (f32[12,256]{1,0:T(8,128)S(1)}, f32[12,256]{1,0:T(8,128)S(1)}, u32[]{:S(2)}, u32[]{:S(2)}) collective-permute-start(f32[12,256]{1,0:T(8,128)S(1)} %dynamic_update_slice.51), channel_id=1, source_target_pairs={{0,192},{16,208},{32,224},{48,240},{64,128},{80,144},{96,160},{112... | collective-permute-start | bytes 36872 | tf_op jit(solution)/shard_map/ppermute | solution.py:106
  137.4 4.0 %collective-permute-start.24 = (f32[48,256]{1,0:T(8,128)S(1)}, f32[48,256]{1,0:T(8,128)S(1)}, u32[]{:S(2)}, u32[]{:S(2)}) collective-permute-start(f32[48,256]{1,0:T(8,128)S(1)} %dynamic_update_slice.55), channel_id=1, source_target_pairs={{0,4},{1,5},{2,6},{3,7},{4,0},{5,1},{6,2},{7,3},{8,12},{9,13},{10,... | collective-permute-start | bytes 147464 | tf_op jit(solution)/shard_map/ppermute | solution.py:106
  138.2 4.4 %collective-permute-start.25 = (f32[48,256]{1,0:T(8,128)S(1)}, f32[48,256]{1,0:T(8,128)S(1)}, u32[]{:S(2)}, u32[]{:S(2)}) collective-permute-start(f32[48,256]{1,0:T(8,128)S(1)} %dynamic_update_slice.55), channel_id=1, source_target_pairs={{0,8},{1,9},{2,10},{3,11},{4,12},{5,13},{6,14},{7,15},{8,0},{9,1},... | collective-permute-start | bytes 147464 | tf_op jit(solution)/shard_map/ppermute | solution.py:106
  140.6 4.2 %collective-permute-start.26 = (f32[48,256]{1,0:T(8,128)S(1)}, f32[48,256]{1,0:T(8,128)S(1)}, u32[]{:S(2)}, u32[]{:S(2)}) collective-permute-start(f32[48,256]{1,0:T(8,128)S(1)} %dynamic_update_slice.55), channel_id=1, source_target_pairs={{0,12},{1,13},{2,14},{3,15},{4,8},{5,9},{6,10},{7,11},{8,4},{9,5},... | collective-permute-start | bytes 147464 | tf_op jit(solution)/shard_map/ppermute | solution.py:106
  144.8 4.5 %collective-permute-start.27 = (f32[192,256]{1,0:T(8,128)S(1)}, f32[192,256]{1,0:T(8,128)S(1)}, u32[]{:S(2)}, u32[]{:S(2)}) collective-permute-start(f32[192,256]{1,0:T(8,128)S(1)} %constant_dynamic-update-slice_fusion.4), channel_id=1, source_target_pairs={{0,16},{16,0},{32,48},{48,32},{64,80},{80,64},{96,112},{112,96},{1... | collective-permute-start | bytes 589832 | tf_op jit(solution)/shard_map/ppermute | solution.py:106
  145.9 7.7 %collective-permute-start.28 = (f32[192,256]{1,0:T(8,128)S(1)}, f32[192,256]{1,0:T(8,128)S(1)}, u32[]{:S(2)}, u32[]{:S(2)}) collective-permute-start(f32[192,256]{1,0:T(8,128)S(1)} %constant_dynamic-update-slice_fusion.4), channel_id=1, source_target_pairs={{0,32},{16,48},{32,0},{48,16},{64,96},{80,112},{96,64},{112,80},{1... | collective-permute-start | bytes 589832 | tf_op jit(solution)/shard_map/ppermute | solution.py:106
  148.3 7.3 %collective-permute-start.29 = (f32[192,256]{1,0:T(8,128)S(1)}, f32[192,256]{1,0:T(8,128)S(1)}, u32[]{:S(2)}, u32[]{:S(2)}) collective-permute-start(f32[192,256]{1,0:T(8,128)S(1)} %constant_dynamic-update-slice_fusion.4), channel_id=1, source_target_pairs={{0,48},{16,32},{32,16},{48,0},{64,112},{80,96},{96,80},{112,64},{1... | collective-permute-start | bytes 589832 | tf_op jit(solution)/shard_map/ppermute | solution.py:106
  (22 other events, 135.5 us)

commit v3 on v2

--- a/solution.py
+++ b/solution.py
@@ -122,31 +122,94 @@
     return outs
 
 
+def neighbour_halo(cells, width, dim):
+    count = lax.axis_size("seq")
+    head = lax.slice_in_dim(cells, 0, width, axis=dim)
+    tail = lax.slice_in_dim(cells, cells.shape[dim] - width, cells.shape[dim], axis=dim)
+    from_left = lax.ppermute(tail, "seq", [(i, i + 1) for i in range(count - 1)])
+    from_right = lax.ppermute(head, "seq", [(i + 1, i) for i in range(count - 1)])
+    return from_left, from_right
+
+
+def inside_window(rows, reach):
+    panel = rows - 2 * reach
+    place = lax.axis_index("seq") * panel + jnp.arange(rows, dtype=jnp.int32) - reach
+    return (place >= 0) & (place < lax.axis_size("seq") * panel)
+
+
+def anti_diagonal(channels):
+    i = jnp.arange(channels, dtype=jnp.int32)
+    return (i[:, None] + i[None, :] == channels - 1).astype(jnp.bfloat16)
+
+
+def mirrored_taps(weight):
+    anti = anti_diagonal(weight.shape[1])
+    flipped = weight[::-1]
+    left = jnp.einsum("ab,kbc->kac", anti, flipped, preferred_element_type=jnp.float32).astype(weight.dtype)
+    return jnp.einsum("kab,bc->kac", left, anti, preferred_element_type=jnp.float32).astype(weight.dtype)
+
+
+def both_strands(stacked, matrix, mirrored):
+    channels = matrix.shape[2]
+    both = product(stacked, jnp.concatenate([matrix.reshape(-1, channels), mirrored.reshape(-1, channels)], axis=1))
+    return both[..., :channels] + both[..., channels:]
+
+
+def taps_of(padded, dilation, rows, order):
+    return jnp.concatenate(
+        [lax.slice_in_dim(padded, k * dilation, k * dilation + rows, axis=1) for k in order], axis=-1
+    )
+
+
 def local(codes, embed, first_weight_taps, second_weight_taps, cotangent):
-    onehot = (codes[..., None] == jnp.arange(4, dtype=jnp.int32)).astype(jnp.bfloat16)
-    nucleotide_features = product(onehot, embed).astype(jnp.bfloat16)
-    first_activation, first_shift_stack = layer_forward_pass(
-        nucleotide_features, first_weight_taps, FIRST_DILATION
-    )
-    gelu_one, back_one = jax.vjp(jax.nn.gelu, first_activation)
-    hidden_state = gelu_one.astype(jnp.bfloat16)
-    second_activation, second_shift_stack = layer_forward_pass(
-        hidden_state, second_weight_taps, SECOND_DILATION
-    )
+    one, two = FIRST_DILATION, SECOND_DILATION
+    panel = codes.shape[1]
+    reach_hidden = 2 * two
+    reach_codes = reach_hidden + one
+    code_left, code_right = neighbour_halo(codes, reach_codes, 1)
+    cot_left, cot_right = neighbour_halo(cotangent, two, 1)
+    codes_wide = jnp.concatenate([code_left, codes, code_right], axis=1)
+    cot_wide = jnp.concatenate([cot_left, cotangent, cot_right], axis=1)
+
+    first_mirror = mirrored_taps(first_weight_taps)
+    second_mirror = mirrored_taps(second_weight_taps)
+
+    onehot = (codes_wide[..., None] == jnp.arange(4, dtype=jnp.int32)).astype(jnp.bfloat16)
+    features = product(onehot, embed).astype(jnp.bfloat16)
+    rows_codes = panel + 2 * reach_codes
+    features = jnp.where(inside_window(rows_codes, reach_codes)[None, :, None], features, jnp.zeros_like(features))
+
+    rows_hidden = panel + 2 * reach_hidden
+    first_stack = taps_of(features, one, rows_hidden, (0, 1, 2))
+    first_activation = both_strands(first_stack, first_weight_taps, first_mirror)
+    hidden = jax.nn.gelu(first_activation).astype(jnp.bfloat16)
+    hidden = jnp.where(inside_window(rows_hidden, reach_hidden)[None, :, None], hidden, jnp.zeros_like(hidden))
+
+    rows_two = panel + 2 * two
+    second_stack = taps_of(hidden, two, rows_two, (0, 1, 2))
+    second_activation = both_strands(second_stack, second_weight_taps, second_mirror)
     gelu_two, back_two = jax.vjp(jax.nn.gelu, second_activation)
-    block_out = (hidden_state.astype(jnp.float32) + gelu_two).astype(jnp.bfloat16)
-    cotangent_wide_float = cotangent.astype(jnp.float32)
-    second_activation_gradient = back_two(cotangent_wide_float)[0].astype(jnp.bfloat16)
-    input_contribution = input_backward_pass(
-        second_activation_gradient, second_weight_taps, SECOND_DILATION
-    )
-    second_weight_gradient = strand_total(second_shift_stack, second_activation_gradient)
-    hidden_gradient = cotangent_wide_float + input_contribution
-    first_activation_gradient = back_one(hidden_gradient)[0].astype(jnp.bfloat16)
-    first_weight_gradient = strand_total(first_shift_stack, first_activation_gradient)
-    second_weight_gradient, first_weight_gradient = symmetric_sum(
-        second_weight_gradient, first_weight_gradient
-    )
+
+    hidden_own = lax.slice_in_dim(hidden, reach_hidden, reach_hidden + panel, axis=1)
+    block_out = (hidden_own.astype(jnp.float32) + lax.slice_in_dim(gelu_two, two, two + panel, axis=1)).astype(jnp.bfloat16)
+
+    second_grad_wide = back_two(cot_wide.astype(jnp.float32))[0].astype(jnp.bfloat16)
+    grad_stack = taps_of(second_grad_wide, two, panel, (2, 1, 0))
+    flat_t = jnp.transpose(second_weight_taps, (0, 2, 1))
+    mirror_t = jnp.transpose(second_mirror, (0, 2, 1))
+    input_contribution = both_strands(grad_stack, flat_t, mirror_t)
+    hidden_gradient = cotangent.astype(jnp.float32) + input_contribution
+
+    first_own = lax.slice_in_dim(first_activation, reach_hidden, reach_hidden + panel, axis=1)
+    _, back_one = jax.vjp(jax.nn.gelu, first_own)
+    first_grad = back_one(hidden_gradient)[0].astype(jnp.bfloat16)
+
+    second_grad_own = lax.slice_in_dim(second_grad_wide, two, two + panel, axis=1)
+    second_weight_gradient = strand_total(lax.slice_in_dim(second_stack, two, two + panel, axis=1), second_grad_own)
+    first_weight_gradient = strand_total(
+        lax.slice_in_dim(first_stack, reach_hidden, reach_hidden + panel, axis=1), first_grad
+    )
+    second_weight_gradient, first_weight_gradient = symmetric_sum(second_weight_gradient, first_weight_gradient)
     return (block_out, first_weight_gradient, second_weight_gradient)
 
 

time: 161 us -> 168 us (1.043)
  local copies, waits for them, and re-layouts: 23.2 us -> 40.3 us
  starting transfers between devices: 68.4 us -> 56.7 us
  matrix products: 14.2 us -> 17.2 us
  waiting for transfers between devices: 34.3 us -> 31.8 us
  other arithmetic: 16.7 us -> 18.9 us
    rev x2, local copies, waits for them, and re-layouts: 2.16 us -> 14.4 us  [strand_total(): return term + term[::-1, ::-1, ::-1]]
    dot_general x2 -> x0, other arithmetic: 10.8 us -> none  [weight_term(): jnp.dot(stacked.reshape(-1, 3 * channels).T, grad.reshape(-1, channels),...]
    ppermute x6 -> x4, starting transfers between devices: 26.5 us -> 16.4 us  [the longest x2 9.4 us: neighbour_halo(): lax.ppermute(tail, 'seq', [(i, i + 1) for i in range(count - 1)])]
    dot_general x2 -> x4, local copies, waits for them, and re-layouts: 5.93 us -> 13.2 us  [weight_term(): jnp.dot(stacked.reshape(-1, 3 * channels).T, grad.reshape(-1, channels),...]
    rev x2 -> x0, local copies, waits for them, and re-layouts: 6.64 us -> none  [layer_forward_pass(): reversed_taps = weight[::-1, ::-1, ::-1].reshape(-1, channels)]
    ppermute x12, waiting for transfers between devices: 11.4 us -> 16.5 us  [butterfly_sum(): total = total + lax.ppermute(sent, axis, partner_pairs(axis, shift, offset))]
    ppermute x6 -> x4, waiting for transfers between devices: 5.36 us -> 1.15 us  [the longest x2 1.14 us: neighbour_halo(): lax.ppermute(head, 'seq', [(i + 1, i) for i in range(count - 1)])]
    ppermute x12, waiting for transfers between devices: 17.6 us -> 14.1 us  [butterfly_sum(): got = lax.ppermute(rows, axis, partner_pairs(axis, shift, offset))]
  transfers between devices with their start and end apart: 30 -> 28, of which waited for: 17 -> 15; matrix products, arithmetic and copies ran while one was open for 12% -> 22% of each run, Pallas kernels for 0% -> 0%
where the time goes in v3:
time: 168 us; the launch traced here: 166 us
  starting transfers between devices  56.7 us (34%)
  local copies, waits for them, and re-layouts  40.3 us (24%)
  waiting for transfers between devices  31.8 us (19%)
  other arithmetic  18.9 us (11%)
  matrix products  17.2 us (10%)
    ppermute x12, starting transfers between devices, butterfly_sum(): total = total + lax.ppermute(sent, axis, partner_pairs(axis, shift, offset))  22.7 us
    ppermute x12, starting transfers between devices, butterfly_sum(): got = lax.ppermute(rows, axis, partner_pairs(axis, shift, offset))  17.6 us
    ppermute x12, waiting for transfers between devices, butterfly_sum(): total = total + lax.ppermute(sent, axis, partner_pairs(axis, shift, offset))  16.5 us
    rev x2, local copies, waits for them, and re-layouts, strand_total(): return term + term[::-1, ::-1, ::-1]  14.4 us
    ppermute x12, waiting for transfers between devices, butterfly_sum(): got = lax.ppermute(rows, axis, partner_pairs(axis, shift, offset))  14.1 us
    dot_general x4, local copies, waits for them, and re-layouts, weight_term(): jnp.dot(stacked.reshape(-1, 3 * channels).T, grad.reshape(-1, channels),...  13.2 us
    ppermute x2, starting transfers between devices, neighbour_halo(): lax.ppermute(tail, 'seq', [(i, i + 1) for i in range(count - 1)])  9.4 us
    dot_general x4, matrix products, product(): jnp.dot(stacked.reshape(-1, shape_in[-1]), matrix, preferred_element_type...  9.39 us
  transfers between devices with their start and end apart: 28, of which 15 were waited for; matrix products, arithmetic and copies ran while one was open for 22% of the time, Pallas kernels for 0%

profile of v3, /device:TPU:1, one launch (start us, length us, event | category | flops | bytes accessed | tf_op | source)
XLA Modules:
  0.0 166.1 jit_solution(14410378752120531768)
XLA Ops:
  1.4 5.1 %collective-permute-start.3 = (bf16[1,16,256]{2,1,0:T(8,128)(2,1)S(1)}, bf16[1,16,256]{2,1,0:T(8,128)(2,1)S(1)}, u32[]{:S(2)}, u32[]{:S(2)}) collective-permute-start(bf16[1,16,256]{2,1,0:T(8,128)(2,1)S(1)} %get-tuple-element.17), channel_id=1, source_target_pairs={{1,0},{2,1},{3,2},{4,3},{5,4},{6,5},{7,6},{8,7},{9,8},{10,9},{11,1... | collective-permute-start | bytes 24584 | tf_op jit(solution)/shard_map/ppermute | solution.py:130
  6.5 7.0 %collective-permute-start.2 = (bf16[1,16,256]{2,1,0:T(8,128)(2,1)S(1)}, bf16[1,16,256]{2,1,0:T(8,128)(2,1)S(1)}, u32[]{:S(2)}, u32[]{:S(2)}) collective-permute-start(bf16[1,16,256]{2,1,0:T(8,128)(2,1)S(1)} %get-tuple-element.16), channel_id=1, source_target_pairs={{0,1},{1,2},{2,3},{3,4},{4,5},{5,6},{6,7},{7,8},{8,9},{9,10},{10,1... | collective-permute-start | bytes 24584 | tf_op jit(solution)/shard_map/ppermute | solution.py:129
  36.4 3.8 %convolution_bitcast_fusion = f32[1,2080,512]{2,1,0:T(8,128)} fusion(bf16[768,256]{1,0:T(8,128)(2,1)S(1)} %bitcast.77, bf16[768,256]{1,0:T(8,128)(2,1)S(1)} %bitcast.73, bf16[1,2080,256]{2,1,0:T(8,128)(2,1)S(1)} %get-tuple-element.11, bf16[1,2080,256]{2,1,0:T(8,128)(2,1)S(1)} %get-tuple-element.12, bf16[1,2080,256]{2,1,0:T(8,128)(2,1)S(1)} %get-tuple-element.10), kind=kOutput, calls=%fused_computation | convolution fusion | flops 1646936064 | bytes 8241152 | tf_op jit(solution)/shard_map/dot_general | solution.py:40
  40.3 4.7 %copy.14 = bf16[768,2048]{1,0:T(8,128)(2,1)} copy(bf16[768,2048]{0,1:T(8,128)(2,1)} %slice_bitcast_fusion.1) | data formatting | bytes 6291456 | tf_op jit(solution)/shard_map/dot_general | solution.py:46
  44.9 4.7 %copy.15 = bf16[768,2048]{1,0:T(8,128)(2,1)} copy(bf16[768,2048]{0,1:T(8,128)(2,1)} %slice_bitcast_fusion) | data formatting | bytes 6291456 | tf_op jit(solution)/shard_map/dot_general | solution.py:46
  49.7 3.4 %fusion.18 = (bf16[1,2080,256]{2,1,0:T(8,128)(2,1)S(1)}, f32[1,2080,256]{2,1,0:T(8,128)S(1)}) fusion(bf16[1,16,256]{2,1,0:T(8,128)(2,1)S(1)} %collective-permute-done.3, bf16[1,2048,256]{2,1,0:T(8,128)(2,1)} %param.9, bf16[1,16,256]{2,1,0:T(8,128)(2,1)S(1)} %collective-permute-done.2, f32[1,2080,512]{2,1,0:T(8,128)} %convolution_bitcast_fusion), kind=kLoop, calls=%fused_computation.35 | loop fusion | flops 14376960 | bytes 8519680 | tf_op jit(solution)/shard_map/convert_element_type | solution.py:196
  58.0 7.2 %rev.20 = f32[3,256,256]{2,1,0:T(8,128)} reverse(f32[3,256,256]{2,1,0:T(8,128)} %fusion.41), dimensions={0,1,2} | reverse | bytes 1572864 | tf_op jit(solution)/shard_map/rev | solution.py:74
  67.6 3.1 %convolution_bitcast_fusion.2 = f32[1,2048,512]{2,1,0:T(8,128)S(1)} fusion(bf16[1,2048,256]{2,1,0:T(8,128)(2,1)S(1)} %copy-done.9, bf16[1,2048,256]{2,1,0:T(8,128)(2,1)S(1)} %copy-done.10, bf16[1,2048,256]{2,1,0:T(8,128)(2,1)S(1)} %copy-done.8, bf16[768,256]{1,0:T(8,128)(2,1)} %bitcast.75, bf16[768,256]{1,0:T(8,128)(2,1)} %bitcast.74), kind=kOutput, calls=%fused_computation.5 | convolution fusion | flops 1621622784 | bytes 8126464 | tf_op jit(solution)/shard_map/dot_general | solution.py:40
  70.7 3.1 %fusion.39 = f32[3,256,256]{2,1,0:T(8,128)} fusion(bf16[3,256,2048]{2,1,0:T(8,128)(2,1)S(1)} %bitcast.67, f32[1,2048,512]{2,1,0:T(8,128)S(1)} %convolution_bitcast_fusion.2, f32[1,2112,256]{2,1,0:T(8,128)S(1)} %copy-done.6, bf16[1,2048,256]{2,1,0:T(8,128)(2,1)S(1)} %copy-done.7), kind=kOutput, calls=%fused_computation.72 | convolution fusion | flops 817364992 | bytes 11272192 | tf_op jit(solution)/shard_map/dot_general | solution.py:46
  73.8 7.2 %rev.21 = f32[3,256,256]{2,1,0:T(8,128)} reverse(f32[3,256,256]{2,1,0:T(8,128)} %fusion.39), dimensions={0,1,2} | reverse | bytes 1572864 | tf_op jit(solution)/shard_map/rev | solution.py:74
  83.5 2.5 %collective-permute-start.6 = (f32[192,256]{1,0:T(8,128)}, f32[192,256]{1,0:T(8,128)S(1)}, u32[]{:S(2)}, u32[]{:S(2)}) collective-permute-start(f32[192,256]{1,0:T(8,128)} %get-tuple-element.22), channel_id=1, source_target_pairs={{0,48},{16,32},{32,16},{48,0},{64,112},{80,96},{96,80},{112,64},{1... | collective-permute-start | bytes 589832 | tf_op jit(solution)/shard_map/ppermute | solution.py:98
  86.8 7.7 %collective-permute-done.6 = f32[192,256]{1,0:T(8,128)S(1)} collective-permute-done((f32[192,256]{1,0:T(8,128)}, f32[192,256]{1,0:T(8,128)S(1)}, u32[]{:S(2)}, u32[]{:S(2)}) %collective-permute-start.6) | collective-permute-done | bytes 196640 | tf_op jit(solution)/shard_map/ppermute | solution.py:98
  97.0 3.1 %collective-permute-start.7 = (f32[48,256]{1,0:T(8,128)S(1)}, f32[48,256]{1,0:T(8,128)}, u32[]{:S(2)}, u32[]{:S(2)}) collective-permute-start(f32[48,256]{1,0:T(8,128)S(1)} %get-tuple-element.23), channel_id=1, source_target_pairs={{0,4},{1,5},{2,6},{3,7},{4,0},{5,1},{6,2},{7,3},{8,12},{9,13},{10,... | collective-permute-start | bytes 147464 | tf_op jit(solution)/shard_map/ppermute | solution.py:98
  103.2 2.6 %collective-permute-start.12 = (f32[12,256]{1,0:T(8,128)S(1)}, f32[12,256]{1,0:T(8,128)S(1)}, u32[]{:S(2)}, u32[]{:S(2)}) collective-permute-start(f32[12,256]{1,0:T(8,128)S(1)} %get-tuple-element.27), channel_id=1, source_target_pairs={{0,192},{16,208},{32,224},{48,240},{64,128},{80,144},{96,160},{112... | collective-permute-start | bytes 36872 | tf_op jit(solution)/shard_map/ppermute | solution.py:98
  109.3 10.0 %collective-permute-start.15 = (f32[3,256]{1,0:T(4,128)S(1)}, f32[3,256]{1,0:T(4,128)S(1)}, u32[]{:S(2)}, u32[]{:S(2)}) collective-permute-start(f32[3,256]{1,0:T(4,128)S(1)} %get-tuple-element.30), channel_id=1, source_target_pairs={{0,3},{1,2},{2,1},{3,0},{4,7},{5,6},{6,5},{7,4},{8,11},{9,10},{10,... | collective-permute-start | bytes 9224 | tf_op jit(solution)/shard_map/ppermute | solution.py:98
  119.3 2.4 %collective-permute-start.14 = (f32[3,256]{1,0:T(4,128)S(1)}, f32[3,256]{1,0:T(4,128)S(1)}, u32[]{:S(2)}, u32[]{:S(2)}) collective-permute-start(f32[3,256]{1,0:T(4,128)S(1)} %get-tuple-element.31), channel_id=1, source_target_pairs={{0,2},{1,3},{2,0},{3,1},{4,6},{5,7},{6,4},{7,5},{8,10},{9,11},{10,... | collective-permute-start | bytes 9224 | tf_op jit(solution)/shard_map/ppermute | solution.py:98
  121.8 3.9 %collective-permute-done.14 = f32[3,256]{1,0:T(4,128)S(1)} collective-permute-done((f32[3,256]{1,0:T(4,128)S(1)}, f32[3,256]{1,0:T(4,128)S(1)}, u32[]{:S(2)}, u32[]{:S(2)}) %collective-permute-start.14) | collective-permute-done | bytes 3104 | tf_op jit(solution)/shard_map/ppermute | solution.py:98
  125.8 2.5 %collective-permute-start.17 = (f32[3,256]{1,0:T(4,128)S(1)}, f32[3,256]{1,0:T(4,128)S(1)}, u32[]{:S(2)}, u32[]{:S(2)}) collective-permute-start(f32[3,256]{1,0:T(4,128)S(1)} %fusion.78), channel_id=1, source_target_pairs={{0,2},{1,3},{2,0},{3,1},{4,6},{5,7},{6,4},{7,5},{8,10},{9,11},{10,... | collective-permute-start | bytes 9224 | tf_op jit(solution)/shard_map/ppermute | solution.py:106
  128.3 3.5 %collective-permute-start.18 = (f32[3,256]{1,0:T(4,128)S(1)}, f32[3,256]{1,0:T(4,128)S(1)}, u32[]{:S(2)}, u32[]{:S(2)}) collective-permute-start(f32[3,256]{1,0:T(4,128)S(1)} %fusion.78), channel_id=1, source_target_pairs={{0,3},{1,2},{2,1},{3,0},{4,7},{5,6},{6,5},{7,4},{8,11},{9,10},{10,... | collective-permute-start | bytes 9224 | tf_op jit(solution)/shard_map/ppermute | solution.py:106
  132.4 3.3 %collective-permute-done.18 = f32[3,256]{1,0:T(4,128)S(1)} collective-permute-done((f32[3,256]{1,0:T(4,128)S(1)}, f32[3,256]{1,0:T(4,128)S(1)}, u32[]{:S(2)}, u32[]{:S(2)}) %collective-permute-start.18) | collective-permute-done | bytes 3104 | tf_op jit(solution)/shard_map/ppermute | solution.py:106
  149.5 2.9 %fusion.35 = bf16[1,2048,256]{2,1,0:T(8,128)(2,1)} fusion(f32[1,2080,256]{2,1,0:T(8,128)} %add_multiply_fusion, f32[1,2080,256]{2,1,0:T(8,128)S(1)} %get-tuple-element.4, bf16[1,2112,256]{2,1,0:T(8,128)(2,1)S(1)} %get-tuple-element.5), kind=kLoop, calls=%fused_computation.55 | loop fusion | flops 2097152 | bytes 6291456 | tf_op jit(solution)/shard_map/convert_element_type | solution.py:194
  152.5 2.4 %collective-permute-start.26 = (f32[192,256]{1,0:T(8,128)S(1)}, f32[192,256]{1,0:T(8,128)S(1)}, u32[]{:S(2)}, u32[]{:S(2)}) collective-permute-start(f32[192,256]{1,0:T(8,128)S(1)} %constant_dynamic-update-slice_fusion.4), channel_id=1, source_target_pairs={{0,32},{16,48},{32,0},{48,16},{64,96},{80,112},{96,64},{112,80},{1... | collective-permute-start | bytes 589832 | tf_op jit(solution)/shard_map/ppermute | solution.py:106
  155.3 4.5 %collective-permute-done.26 = f32[192,256]{1,0:T(8,128)S(1)} collective-permute-done((f32[192,256]{1,0:T(8,128)S(1)}, f32[192,256]{1,0:T(8,128)S(1)}, u32[]{:S(2)}, u32[]{:S(2)}) %collective-permute-start.26) | collective-permute-done | bytes 196640 | tf_op jit(solution)/shard_map/ppermute | solution.py:106
  159.8 3.9 %collective-permute-done.27 = f32[192,256]{1,0:T(8,128)S(1)} collective-permute-done((f32[192,256]{1,0:T(8,128)S(1)}, f32[192,256]{1,0:T(8,128)S(1)}, u32[]{:S(2)}, u32[]{:S(2)}) %collective-permute-start.27) | collective-permute-done | bytes 196640 | tf_op jit(solution)/shard_map/ppermute | solution.py:106
  (133 shorter events, 60.4 us)
Async XLA Ops:
  1.4 48.3 %collective-permute-start.3 = (bf16[1,16,256]{2,1,0:T(8,128)(2,1)S(1)}, bf16[1,16,256]{2,1,0:T(8,128)(2,1)S(1)}, u32[]{:S(2)}, u32[]{:S(2)}) collective-permute-start(bf16[1,16,256]{2,1,0:T(8,128)(2,1)S(1)} %get-tuple-element.17), channel_id=1, source_target_pairs={{1,0},{2,1},{3,2},{4,3},{5,4},{6,5},{7,6},{8,7},{9,8},{10,9},{11,1... | collective-permute-start | bytes 24584 | tf_op jit(solution)/shard_map/ppermute | solution.py:130
  6.5 43.2 %collective-permute-start.2 = (bf16[1,16,256]{2,1,0:T(8,128)(2,1)S(1)}, bf16[1,16,256]{2,1,0:T(8,128)(2,1)S(1)}, u32[]{:S(2)}, u32[]{:S(2)}) collective-permute-start(bf16[1,16,256]{2,1,0:T(8,128)(2,1)S(1)} %get-tuple-element.16), channel_id=1, source_target_pairs={{0,1},{1,2},{2,3},{3,4},{4,5},{5,6},{6,7},{7,8},{8,9},{9,10},{10,1... | collective-permute-start | bytes 24584 | tf_op jit(solution)/shard_map/ppermute | solution.py:129
  14.3 10.3 %collective-permute-start = (s32[1,36]{1,0:T(1,128)S(1)}, s32[1,36]{1,0:T(1,128)S(1)}, u32[]{:S(2)}, u32[]{:S(2)}) collective-permute-start(s32[1,36]{1,0:T(1,128)S(1)} %get-tuple-element.33), channel_id=1, source_target_pairs={{0,1},{1,2},{2,3},{3,4},{4,5},{5,6},{6,7},{7,8},{8,9},{9,10},{10,1... | collective-permute-start | bytes 440 | tf_op jit(solution)/shard_map/ppermute | solution.py:129
  16.7 9.0 %collective-permute-start.1 = (s32[1,36]{1,0:T(1,128)S(1)}, s32[1,36]{1,0:T(1,128)S(1)}, u32[]{:S(2)}, u32[]{:S(2)}) collective-permute-start(s32[1,36]{1,0:T(1,128)S(1)} %get-tuple-element.32), channel_id=1, source_target_pairs={{1,0},{2,1},{3,2},{4,3},{5,4},{6,5},{7,6},{8,7},{9,8},{10,9},{11,1... | collective-permute-start | bytes 440 | tf_op jit(solution)/shard_map/ppermute | solution.py:130
  83.5 11.0 %collective-permute-start.6 = (f32[192,256]{1,0:T(8,128)}, f32[192,256]{1,0:T(8,128)S(1)}, u32[]{:S(2)}, u32[]{:S(2)}) collective-permute-start(f32[192,256]{1,0:T(8,128)} %get-tuple-element.22), channel_id=1, source_target_pairs={{0,48},{16,32},{32,16},{48,0},{64,112},{80,96},{96,80},{112,64},{1... | collective-permute-start | bytes 589832 | tf_op jit(solution)/shard_map/ppermute | solution.py:98
  86.0 8.5 %collective-permute-start.5 = (f32[192,256]{1,0:T(8,128)}, f32[192,256]{1,0:T(8,128)}, u32[]{:S(2)}, u32[]{:S(2)}) collective-permute-start(f32[192,256]{1,0:T(8,128)} %get-tuple-element.21), channel_id=1, source_target_pairs={{0,32},{16,48},{32,0},{48,16},{64,96},{80,112},{96,64},{112,80},{1... | collective-permute-start | bytes 589832 | tf_op jit(solution)/shard_map/ppermute | solution.py:98
  86.5 9.0 %collective-permute-start.4 = (f32[192,256]{1,0:T(8,128)}, f32[192,256]{1,0:T(8,128)}, u32[]{:S(2)}, u32[]{:S(2)}) collective-permute-start(f32[192,256]{1,0:T(8,128)} %get-tuple-element.20), channel_id=1, source_target_pairs={{0,16},{16,0},{32,48},{48,32},{64,80},{80,64},{96,112},{112,96},{1... | collective-permute-start | bytes 589832 | tf_op jit(solution)/shard_map/ppermute | solution.py:98
  96.8 4.9 %collective-permute-start.9 = (f32[48,256]{1,0:T(8,128)S(1)}, f32[48,256]{1,0:T(8,128)}, u32[]{:S(2)}, u32[]{:S(2)}) collective-permute-start(f32[48,256]{1,0:T(8,128)S(1)} %get-tuple-element.24), channel_id=1, source_target_pairs={{0,12},{1,13},{2,14},{3,15},{4,8},{5,9},{6,10},{7,11},{8,4},{9,5},... | collective-permute-start | bytes 147464 | tf_op jit(solution)/shard_map/ppermute | solution.py:98
  96.9 4.8 %collective-permute-start.8 = (f32[48,256]{1,0:T(8,128)S(1)}, f32[48,256]{1,0:T(8,128)}, u32[]{:S(2)}, u32[]{:S(2)}) collective-permute-start(f32[48,256]{1,0:T(8,128)S(1)} %get-tuple-element.25), channel_id=1, source_target_pairs={{0,8},{1,9},{2,10},{3,11},{4,12},{5,13},{6,14},{7,15},{8,0},{9,1},... | collective-permute-start | bytes 147464 | tf_op jit(solution)/shard_map/ppermute | solution.py:98
  97.0 5.2 %collective-permute-start.7 = (f32[48,256]{1,0:T(8,128)S(1)}, f32[48,256]{1,0:T(8,128)}, u32[]{:S(2)}, u32[]{:S(2)}) collective-permute-start(f32[48,256]{1,0:T(8,128)S(1)} %get-tuple-element.23), channel_id=1, source_target_pairs={{0,4},{1,5},{2,6},{3,7},{4,0},{5,1},{6,2},{7,3},{8,12},{9,13},{10,... | collective-permute-start | bytes 147464 | tf_op jit(solution)/shard_map/ppermute | solution.py:98
  103.2 4.9 %collective-permute-start.12 = (f32[12,256]{1,0:T(8,128)S(1)}, f32[12,256]{1,0:T(8,128)S(1)}, u32[]{:S(2)}, u32[]{:S(2)}) collective-permute-start(f32[12,256]{1,0:T(8,128)S(1)} %get-tuple-element.27), channel_id=1, source_target_pairs={{0,192},{16,208},{32,224},{48,240},{64,128},{80,144},{96,160},{112... | collective-permute-start | bytes 36872 | tf_op jit(solution)/shard_map/ppermute | solution.py:98
  109.3 12.5 %collective-permute-start.15 = (f32[3,256]{1,0:T(4,128)S(1)}, f32[3,256]{1,0:T(4,128)S(1)}, u32[]{:S(2)}, u32[]{:S(2)}) collective-permute-start(f32[3,256]{1,0:T(4,128)S(1)} %get-tuple-element.30), channel_id=1, source_target_pairs={{0,3},{1,2},{2,1},{3,0},{4,7},{5,6},{6,5},{7,4},{8,11},{9,10},{10,... | collective-permute-start | bytes 9224 | tf_op jit(solution)/shard_map/ppermute | solution.py:98
  119.3 6.4 %collective-permute-start.14 = (f32[3,256]{1,0:T(4,128)S(1)}, f32[3,256]{1,0:T(4,128)S(1)}, u32[]{:S(2)}, u32[]{:S(2)}) collective-permute-start(f32[3,256]{1,0:T(4,128)S(1)} %get-tuple-element.31), channel_id=1, source_target_pairs={{0,2},{1,3},{2,0},{3,1},{4,6},{5,7},{6,4},{7,5},{8,10},{9,11},{10,... | collective-permute-start | bytes 9224 | tf_op jit(solution)/shard_map/ppermute | solution.py:98
  125.7 6.2 %collective-permute-start.16 = (f32[3,256]{1,0:T(4,128)S(1)}, f32[3,256]{1,0:T(4,128)S(1)}, u32[]{:S(2)}, u32[]{:S(2)}) collective-permute-start(f32[3,256]{1,0:T(4,128)S(1)} %fusion.78), channel_id=1, source_target_pairs={{0,1},{1,0},{2,3},{3,2},{4,5},{5,4},{6,7},{7,6},{8,9},{9,8},{10,11... | collective-permute-start | bytes 9224 | tf_op jit(solution)/shard_map/ppermute | solution.py:106
  125.8 6.5 %collective-permute-start.17 = (f32[3,256]{1,0:T(4,128)S(1)}, f32[3,256]{1,0:T(4,128)S(1)}, u32[]{:S(2)}, u32[]{:S(2)}) collective-permute-start(f32[3,256]{1,0:T(4,128)S(1)} %fusion.78), channel_id=1, source_target_pairs={{0,2},{1,3},{2,0},{3,1},{4,6},{5,7},{6,4},{7,5},{8,10},{9,11},{10,... | collective-permute-start | bytes 9224 | tf_op jit(solution)/shard_map/ppermute | solution.py:106
  128.3 7.3 %collective-permute-start.18 = (f32[3,256]{1,0:T(4,128)S(1)}, f32[3,256]{1,0:T(4,128)S(1)}, u32[]{:S(2)}, u32[]{:S(2)}) collective-permute-start(f32[3,256]{1,0:T(4,128)S(1)} %fusion.78), channel_id=1, source_target_pairs={{0,3},{1,2},{2,1},{3,0},{4,7},{5,6},{6,5},{7,4},{8,11},{9,10},{10,... | collective-permute-start | bytes 9224 | tf_op jit(solution)/shard_map/ppermute | solution.py:106
  135.7 5.8 %collective-permute-start.19 = (f32[12,256]{1,0:T(8,128)S(1)}, f32[12,256]{1,0:T(8,128)S(1)}, u32[]{:S(2)}, u32[]{:S(2)}) collective-permute-start(f32[12,256]{1,0:T(8,128)S(1)} %dynamic_update_slice.51), channel_id=1, source_target_pairs={{0,64},{16,80},{32,96},{48,112},{64,0},{80,16},{96,32},{112,48},{1... | collective-permute-start | bytes 36872 | tf_op jit(solution)/shard_map/ppermute | solution.py:106
  137.1 4.7 %collective-permute-start.20 = (f32[12,256]{1,0:T(8,128)S(1)}, f32[12,256]{1,0:T(8,128)S(1)}, u32[]{:S(2)}, u32[]{:S(2)}) collective-permute-start(f32[12,256]{1,0:T(8,128)S(1)} %dynamic_update_slice.51), channel_id=1, source_target_pairs={{0,128},{16,144},{32,160},{48,176},{64,192},{80,208},{96,224},{112... | collective-permute-start | bytes 36872 | tf_op jit(solution)/shard_map/ppermute | solution.py:106
  137.7 4.4 %collective-permute-start.21 = (f32[12,256]{1,0:T(8,128)S(1)}, f32[12,256]{1,0:T(8,128)S(1)}, u32[]{:S(2)}, u32[]{:S(2)}) collective-permute-start(f32[12,256]{1,0:T(8,128)S(1)} %dynamic_update_slice.51), channel_id=1, source_target_pairs={{0,192},{16,208},{32,224},{48,240},{64,128},{80,144},{96,160},{112... | collective-permute-start | bytes 36872 | tf_op jit(solution)/shard_map/ppermute | solution.py:106
  142.3 4.5 %collective-permute-start.23 = (f32[48,256]{1,0:T(8,128)S(1)}, f32[48,256]{1,0:T(8,128)S(1)}, u32[]{:S(2)}, u32[]{:S(2)}) collective-permute-start(f32[48,256]{1,0:T(8,128)S(1)} %dynamic_update_slice.55), channel_id=1, source_target_pairs={{0,8},{1,9},{2,10},{3,11},{4,12},{5,13},{6,14},{7,15},{8,0},{9,1},... | collective-permute-start | bytes 147464 | tf_op jit(solution)/shard_map/ppermute | solution.py:106
  144.3 4.2 %collective-permute-start.24 = (f32[48,256]{1,0:T(8,128)S(1)}, f32[48,256]{1,0:T(8,128)S(1)}, u32[]{:S(2)}, u32[]{:S(2)}) collective-permute-start(f32[48,256]{1,0:T(8,128)S(1)} %dynamic_update_slice.55), channel_id=1, source_target_pairs={{0,12},{1,13},{2,14},{3,15},{4,8},{5,9},{6,10},{7,11},{8,4},{9,5},... | collective-permute-start | bytes 147464 | tf_op jit(solution)/shard_map/ppermute | solution.py:106
  148.4 6.9 %collective-permute-start.25 = (f32[192,256]{1,0:T(8,128)S(1)}, f32[192,256]{1,0:T(8,128)S(1)}, u32[]{:S(2)}, u32[]{:S(2)}) collective-permute-start(f32[192,256]{1,0:T(8,128)S(1)} %constant_dynamic-update-slice_fusion.4), channel_id=1, source_target_pairs={{0,16},{16,0},{32,48},{48,32},{64,80},{80,64},{96,112},{112,96},{1... | collective-permute-start | bytes 589832 | tf_op jit(solution)/shard_map/ppermute | solution.py:106
  152.5 7.3 %collective-permute-start.26 = (f32[192,256]{1,0:T(8,128)S(1)}, f32[192,256]{1,0:T(8,128)S(1)}, u32[]{:S(2)}, u32[]{:S(2)}) collective-permute-start(f32[192,256]{1,0:T(8,128)S(1)} %constant_dynamic-update-slice_fusion.4), channel_id=1, source_target_pairs={{0,32},{16,48},{32,0},{48,16},{64,96},{80,112},{96,64},{112,80},{1... | collective-permute-start | bytes 589832 | tf_op jit(solution)/shard_map/ppermute | solution.py:106
  154.9 8.8 %collective-permute-start.27 = (f32[192,256]{1,0:T(8,128)S(1)}, f32[192,256]{1,0:T(8,128)S(1)}, u32[]{:S(2)}, u32[]{:S(2)}) collective-permute-start(f32[192,256]{1,0:T(8,128)S(1)} %constant_dynamic-update-slice_fusion.4), channel_id=1, source_target_pairs={{0,48},{16,32},{32,16},{48,0},{64,112},{80,96},{96,80},{112,64},{1... | collective-permute-start | bytes 589832 | tf_op jit(solution)/shard_map/ppermute | solution.py:106
  (21 other events, 101.0 us)

commit v4 on v3

--- a/solution.py
+++ b/solution.py
@@ -109,6 +109,28 @@
     return rows
 
 
+def folded_term(stacked, grad):
+    channels = grad.shape[-1]
+    term = jnp.dot(
+        grad.reshape(-1, channels).T,
+        stacked.reshape(-1, 3 * channels),
+        preferred_element_type=jnp.float32,
+    )
+    half = channels // 2
+    return term[:half] + term[half:][::-1, ::-1]
+
+
+def unfolded_sums(first, second):
+    half, width = first.shape
+    total = butterfly_sum(jnp.concatenate([first, second], axis=0))
+    outs = []
+    for i in range(2):
+        part = total[i * half : (i + 1) * half]
+        full = jnp.concatenate([part, part[::-1, ::-1]], axis=0)
+        outs.append(jnp.transpose(full.reshape(2 * half, 3, width // 3), (1, 2, 0)))
+    return outs
+
+
 def symmetric_sum(first, second):
     shape = first.shape
     flat_rows = shape[0] * shape[1]
@@ -205,11 +227,11 @@
     first_grad = back_one(hidden_gradient)[0].astype(jnp.bfloat16)
 
     second_grad_own = lax.slice_in_dim(second_grad_wide, two, two + panel, axis=1)
-    second_weight_gradient = strand_total(lax.slice_in_dim(second_stack, two, two + panel, axis=1), second_grad_own)
-    first_weight_gradient = strand_total(
+    second_weight_gradient = folded_term(lax.slice_in_dim(second_stack, two, two + panel, axis=1), second_grad_own)
+    first_weight_gradient = folded_term(
         lax.slice_in_dim(first_stack, reach_hidden, reach_hidden + panel, axis=1), first_grad
     )
-    second_weight_gradient, first_weight_gradient = symmetric_sum(second_weight_gradient, first_weight_gradient)
+    second_weight_gradient, first_weight_gradient = unfolded_sums(second_weight_gradient, first_weight_gradient)
     return (block_out, first_weight_gradient, second_weight_gradient)
 
 

time: 168 us -> 235 us (1.40)
  the two profiles are of different devices: /device:TPU:1 before, /device:TPU:32 now
where the time goes in v4:
time: 235 us; the launch traced here: 233 us
  local copies, waits for them, and re-layouts  78.1 us (33%)
  waiting for transfers between devices  70.5 us (30%)
  starting transfers between devices  52.5 us (22%)
  other arithmetic  17.7 us (8%)
  matrix products  13.4 us (6%)
    ppermute x12, waiting for transfers between devices, butterfly_sum(): got = lax.ppermute(rows, axis, partner_pairs(axis, shift, offset))  44.5 us
    dynamic_update_slice x12, local copies, waits for them, and re-layouts, butterfly_sum(): lax.dynamic_update_slice_in_dim(full, got, (place ^ offset) * width, 0)  38.3 us
    ppermute x12, waiting for transfers between devices, butterfly_sum(): total = total + lax.ppermute(sent, axis, partner_pairs(axis, shift, offset))  25.9 us
    ppermute x12, starting transfers between devices, butterfly_sum(): total = total + lax.ppermute(sent, axis, partner_pairs(axis, shift, offset))  21.5 us
    ppermute x12, starting transfers between devices, butterfly_sum(): got = lax.ppermute(rows, axis, partner_pairs(axis, shift, offset))  17.6 us
    dynamic_update_slice x4, local copies, waits for them, and re-layouts, butterfly_sum(): full = lax.dynamic_update_slice_in_dim(full, rows, place * width, 0)  12.2 us
    ppermute x2, starting transfers between devices, neighbour_halo(): lax.ppermute(tail, 'seq', [(i, i + 1) for i in range(count - 1)])  10.8 us
    dot_general x4, matrix products, product(): jnp.dot(stacked.reshape(-1, shape_in[-1]), matrix, preferred_element_type...  8.41 us
  transfers between devices with their start and end apart: 28, of which 14 were waited for; matrix products, arithmetic and copies ran while one was open for 27% of the time, Pallas kernels for 0%

profile of v4, /device:TPU:32, one launch (start us, length us, event | category | flops | bytes accessed | tf_op | source)
XLA Modules:
  0.0 233.2 jit_solution(2424162777290847282)
XLA Ops:
  6.5 7.8 %collective-permute-start.2 = (bf16[1,16,256]{2,1,0:T(8,128)(2,1)S(1)}, bf16[1,16,256]{2,1,0:T(8,128)(2,1)S(1)}, u32[]{:S(2)}, u32[]{:S(2)}) collective-permute-start(bf16[1,16,256]{2,1,0:T(8,128)(2,1)S(1)} %get-tuple-element.16), channel_id=1, source_target_pairs={{0,1},{1,2},{2,3},{3,4},{4,5},{5,6},{6,7},{7,8},{8,9},{9,10},{10,1... | collective-permute-start | bytes 24584 | tf_op jit(solution)/shard_map/ppermute | solution.py:151
  37.1 4.1 %rev.20 = f32[128,768]{1,0:T(8,128)} reverse(f32[128,768]{1,0:T(8,128)} %slice.137), dimensions={0,1} | reverse | bytes 786432 | tf_op jit(solution)/shard_map/rev | solution.py:120
  41.2 4.1 %convolution_bitcast_fusion.2 = f32[1,2048,512]{2,1,0:T(8,128)S(1)} fusion(bf16[1,2048,256]{2,1,0:T(8,128)(2,1)} %get-tuple-element.14, bf16[1,2048,256]{2,1,0:T(8,128)(2,1)} %get-tuple-element.15, bf16[1,2048,256]{2,1,0:T(8,128)(2,1)} %get-tuple-element.13, bf16[768,256]{1,0:T(8,128)(2,1)} %bitcast.65, bf16[768,256]{1,0:T(8,128)(2,1)} %bitcast.64), kind=kOutput, calls=%fused_computation.5 | convolution fusion | flops 1621622784 | bytes 8126464 | tf_op jit(solution)/shard_map/dot_general | solution.py:40
  49.0 4.1 %rev.21 = f32[128,768]{1,0:T(8,128)} reverse(f32[128,768]{1,0:T(8,128)} %slice.145), dimensions={0,1} | reverse | bytes 786432 | tf_op jit(solution)/shard_map/rev | solution.py:120
  60.8 3.1 %collective-permute-done.4 = f32[64,768]{1,0:T(8,128)S(1)} collective-permute-done((f32[64,768]{1,0:T(8,128)}, f32[64,768]{1,0:T(8,128)S(1)}, u32[]{:S(2)}, u32[]{:S(2)}) %collective-permute-start.4) | collective-permute-done | bytes 196640 | tf_op jit(solution)/shard_map/ppermute | solution.py:98
  64.0 6.6 %collective-permute-done.5 = f32[64,768]{1,0:T(8,128)} collective-permute-done((f32[64,768]{1,0:T(8,128)}, f32[64,768]{1,0:T(8,128)}, u32[]{:S(2)}, u32[]{:S(2)}) %collective-permute-start.5) | collective-permute-done | bytes 196640 | tf_op jit(solution)/shard_map/ppermute | solution.py:98
  94.0 4.9 %collective-permute-start.15 = (f32[1,768]{1,0:T(1,128)S(1)}, f32[1,768]{1,0:T(1,128)S(1)}, u32[]{:S(2)}, u32[]{:S(2)}) collective-permute-start(f32[1,768]{1,0:T(1,128)S(1)} %get-tuple-element.30), channel_id=1, source_target_pairs={{0,3},{1,2},{2,1},{3,0},{4,7},{5,6},{6,5},{7,4},{8,11},{9,10},{10,... | collective-permute-start | bytes 9224 | tf_op jit(solution)/shard_map/ppermute | solution.py:98
  101.1 5.4 %collective-permute-done.14 = f32[1,768]{1,0:T(1,128)S(1)} collective-permute-done((f32[1,768]{1,0:T(1,128)S(1)}, f32[1,768]{1,0:T(1,128)S(1)}, u32[]{:S(2)}, u32[]{:S(2)}) %collective-permute-start.14) | collective-permute-done | bytes 3104 | tf_op jit(solution)/shard_map/ppermute | solution.py:98
  107.8 4.5 %collective-permute-start.18 = (f32[1,768]{1,0:T(1,128)S(1)}, f32[1,768]{1,0:T(1,128)S(1)}, u32[]{:S(2)}, u32[]{:S(2)}) collective-permute-start(f32[1,768]{1,0:T(1,128)S(1)} %fusion.78), channel_id=1, source_target_pairs={{0,3},{1,2},{2,1},{3,0},{4,7},{5,6},{6,5},{7,4},{8,11},{9,10},{10,... | collective-permute-start | bytes 9224 | tf_op jit(solution)/shard_map/ppermute | solution.py:106
  129.7 3.3 %dynamic_update_slice.52 = f32[16,768]{0,1:T(8,128)} dynamic-update-slice(f32[16,768]{0,1:T(8,128)} %broadcast_in_dim.48, f32[4,768]{0,1:T(8,128)} %dynamic_update_slice.51, s32[]{:T(128)S(6)} %select_n.86, s32[]{:T(128)} %constant.26.clone.1) | dynamic-update-slice | bytes 24580 | tf_op jit(solution)/shard_map/dynamic_update_slice | solution.py:104
  133.0 11.3 %collective-permute-done.19 = f32[4,768]{0,1:T(8,128)} collective-permute-done((f32[4,768]{0,1:T(8,128)}, f32[4,768]{0,1:T(8,128)}, u32[]{:S(2)}, u32[]{:S(2)}) %collective-permute-start.19) | collective-permute-done | bytes 12320 | tf_op jit(solution)/shard_map/ppermute | solution.py:106
  147.2 7.4 %collective-permute-done.20 = f32[4,768]{0,1:T(8,128)} collective-permute-done((f32[4,768]{0,1:T(8,128)}, f32[4,768]{0,1:T(8,128)}, u32[]{:S(2)}, u32[]{:S(2)}) %collective-permute-start.20) | collective-permute-done | bytes 12320 | tf_op jit(solution)/shard_map/ppermute | solution.py:106
  154.6 3.3 %dynamic_update_slice.54 = f32[16,768]{0,1:T(8,128)} dynamic-update-slice(f32[16,768]{0,1:T(8,128)} %dynamic_update_slice.53, f32[4,768]{0,1:T(8,128)} %collective-permute-done.20, s32[]{:T(128)S(6)} %select_n.88, s32[]{:T(128)} %constant.26.clone.1) | dynamic-update-slice | bytes 24580 | tf_op jit(solution)/shard_map/dynamic_update_slice | solution.py:107
  157.9 5.9 %collective-permute-done.21 = f32[4,768]{0,1:T(8,128)} collective-permute-done((f32[4,768]{0,1:T(8,128)}, f32[4,768]{0,1:T(8,128)}, u32[]{:S(2)}, u32[]{:S(2)}) %collective-permute-start.21) | collective-permute-done | bytes 12320 | tf_op jit(solution)/shard_map/ppermute | solution.py:106
  163.8 3.3 %dynamic_update_slice.55 = f32[16,768]{0,1:T(8,128)} dynamic-update-slice(f32[16,768]{0,1:T(8,128)} %dynamic_update_slice.54, f32[4,768]{0,1:T(8,128)} %collective-permute-done.21, s32[]{:T(128)S(6)} %select_n.89, s32[]{:T(128)} %constant.26.clone.1) | dynamic-update-slice | bytes 24580 | tf_op jit(solution)/shard_map/dynamic_update_slice | solution.py:107
  176.8 11.4 %collective-permute-done.22 = f32[16,768]{0,1:T(8,128)} collective-permute-done((f32[16,768]{0,1:T(8,128)}, f32[16,768]{0,1:T(8,128)}, u32[]{:S(2)}, u32[]{:S(2)}) %collective-permute-start.22) | collective-permute-done | bytes 49184 | tf_op jit(solution)/shard_map/ppermute | solution.py:106
  188.1 3.3 %dynamic_update_slice.57 = f32[64,768]{0,1:T(8,128)} dynamic-update-slice(f32[64,768]{0,1:T(8,128)} %dynamic_update_slice.56, f32[16,768]{0,1:T(8,128)} %collective-permute-done.22, s32[]{:T(128)S(6)} %select_n.83, s32[]{:T(128)} %constant.26.clone.1) | dynamic-update-slice | bytes 98308 | tf_op jit(solution)/shard_map/dynamic_update_slice | solution.py:107
  191.4 3.3 %dynamic_update_slice.58 = f32[64,768]{0,1:T(8,128)} dynamic-update-slice(f32[64,768]{0,1:T(8,128)} %dynamic_update_slice.57, f32[16,768]{0,1:T(8,128)} %collective-permute-done.23, s32[]{:T(128)S(6)} %select_n.84, s32[]{:T(128)} %constant.26.clone.1) | dynamic-update-slice | bytes 98308 | tf_op jit(solution)/shard_map/dynamic_update_slice | solution.py:107
  194.8 3.3 %dynamic_update_slice.59 = f32[64,768]{0,1:T(8,128)} dynamic-update-slice(f32[64,768]{0,1:T(8,128)} %dynamic_update_slice.58, f32[16,768]{0,1:T(8,128)} %collective-permute-done.24, s32[]{:T(128)S(6)} %select_n.85, s32[]{:T(128)} %constant.26.clone.1) | dynamic-update-slice | bytes 98308 | tf_op jit(solution)/shard_map/dynamic_update_slice | solution.py:107
  205.3 4.2 %dynamic_update_slice.60 = f32[256,768]{0,1:T(8,128)S(1)} dynamic-update-slice(f32[256,768]{0,1:T(8,128)S(1)} %broadcast_in_dim.46, f32[64,768]{0,1:T(8,128)} %dynamic_update_slice.59, s32[]{:T(128)S(6)} %select_n.78, s32[]{:T(128)} %constant.26.clone.1) | dynamic-update-slice | bytes 393220 | tf_op jit(solution)/shard_map/dynamic_update_slice | solution.py:104
  209.5 8.5 %collective-permute-done.25 = f32[64,768]{0,1:T(8,128)} collective-permute-done((f32[64,768]{0,1:T(8,128)}, f32[64,768]{0,1:T(8,128)}, u32[]{:S(2)}, u32[]{:S(2)}) %collective-permute-start.25) | collective-permute-done | bytes 196640 | tf_op jit(solution)/shard_map/ppermute | solution.py:106
  218.0 4.7 %dynamic_update_slice.61 = f32[256,768]{0,1:T(8,128)S(1)} dynamic-update-slice(f32[256,768]{0,1:T(8,128)S(1)} %dynamic_update_slice.60, f32[64,768]{0,1:T(8,128)} %collective-permute-done.25, s32[]{:T(128)S(6)} %select_n.79, s32[]{:T(128)} %constant.26.clone.1) | dynamic-update-slice | bytes 393220 | tf_op jit(solution)/shard_map/dynamic_update_slice | solution.py:107
  222.7 3.5 %dynamic_update_slice.62 = f32[256,768]{0,1:T(8,128)S(1)} dynamic-update-slice(f32[256,768]{0,1:T(8,128)S(1)} %dynamic_update_slice.61, f32[64,768]{0,1:T(8,128)} %collective-permute-done.26, s32[]{:T(128)S(6)} %select_n.80, s32[]{:T(128)} %constant.26.clone.1) | dynamic-update-slice | bytes 393220 | tf_op jit(solution)/shard_map/dynamic_update_slice | solution.py:107
  226.2 4.1 %dynamic_update_slice.63 = f32[256,768]{0,1:T(8,128)S(1)} dynamic-update-slice(f32[256,768]{0,1:T(8,128)S(1)} %dynamic_update_slice.62, f32[64,768]{0,1:T(8,128)} %collective-permute-done.27, s32[]{:T(128)S(6)} %select_n.81, s32[]{:T(128)} %constant.26.clone.1) | dynamic-update-slice | bytes 393220 | tf_op jit(solution)/shard_map/dynamic_update_slice | solution.py:107
  (125 shorter events, 106.8 us)
Async XLA Ops:
  1.5 19.1 %collective-permute-start.1 = (s32[1,36]{1,0:T(1,128)S(1)}, s32[1,36]{1,0:T(1,128)S(1)}, u32[]{:S(2)}, u32[]{:S(2)}) collective-permute-start(s32[1,36]{1,0:T(1,128)S(1)} %get-tuple-element.32), channel_id=1, source_target_pairs={{1,0},{2,1},{3,2},{4,3},{5,4},{6,5},{7,6},{8,7},{9,8},{10,9},{11,1... | collective-permute-start | bytes 440 | tf_op jit(solution)/shard_map/ppermute | solution.py:152
  2.8 17.8 %collective-permute-start = (s32[1,36]{1,0:T(1,128)S(1)}, s32[1,36]{1,0:T(1,128)S(1)}, u32[]{:S(2)}, u32[]{:S(2)}) collective-permute-start(s32[1,36]{1,0:T(1,128)S(1)} %get-tuple-element.33), channel_id=1, source_target_pairs={{0,1},{1,2},{2,3},{3,4},{4,5},{5,6},{6,7},{7,8},{8,9},{9,10},{10,1... | collective-permute-start | bytes 440 | tf_op jit(solution)/shard_map/ppermute | solution.py:151
  6.5 24.5 %collective-permute-start.2 = (bf16[1,16,256]{2,1,0:T(8,128)(2,1)S(1)}, bf16[1,16,256]{2,1,0:T(8,128)(2,1)S(1)}, u32[]{:S(2)}, u32[]{:S(2)}) collective-permute-start(bf16[1,16,256]{2,1,0:T(8,128)(2,1)S(1)} %get-tuple-element.16), channel_id=1, source_target_pairs={{0,1},{1,2},{2,3},{3,4},{4,5},{5,6},{6,7},{7,8},{8,9},{9,10},{10,1... | collective-permute-start | bytes 24584 | tf_op jit(solution)/shard_map/ppermute | solution.py:151
  14.3 16.7 %collective-permute-start.3 = (bf16[1,16,256]{2,1,0:T(8,128)(2,1)S(1)}, bf16[1,16,256]{2,1,0:T(8,128)(2,1)S(1)}, u32[]{:S(2)}, u32[]{:S(2)}) collective-permute-start(bf16[1,16,256]{2,1,0:T(8,128)(2,1)S(1)} %get-tuple-element.17), channel_id=1, source_target_pairs={{1,0},{2,1},{3,2},{4,3},{5,4},{6,5},{7,6},{8,7},{9,8},{10,9},{11,1... | collective-permute-start | bytes 24584 | tf_op jit(solution)/shard_map/ppermute | solution.py:152
  56.1 7.8 %collective-permute-start.4 = (f32[64,768]{1,0:T(8,128)}, f32[64,768]{1,0:T(8,128)S(1)}, u32[]{:S(2)}, u32[]{:S(2)}) collective-permute-start(f32[64,768]{1,0:T(8,128)} %get-tuple-element.20), channel_id=1, source_target_pairs={{0,16},{16,0},{32,48},{48,32},{64,80},{80,64},{96,112},{112,96},{1... | collective-permute-start | bytes 589832 | tf_op jit(solution)/shard_map/ppermute | solution.py:98
  57.6 13.0 %collective-permute-start.5 = (f32[64,768]{1,0:T(8,128)}, f32[64,768]{1,0:T(8,128)}, u32[]{:S(2)}, u32[]{:S(2)}) collective-permute-start(f32[64,768]{1,0:T(8,128)} %get-tuple-element.21), channel_id=1, source_target_pairs={{0,32},{16,48},{32,0},{48,16},{64,96},{80,112},{96,64},{112,80},{1... | collective-permute-start | bytes 589832 | tf_op jit(solution)/shard_map/ppermute | solution.py:98
  60.4 13.1 %collective-permute-start.6 = (f32[64,768]{1,0:T(8,128)}, f32[64,768]{1,0:T(8,128)}, u32[]{:S(2)}, u32[]{:S(2)}) collective-permute-start(f32[64,768]{1,0:T(8,128)} %get-tuple-element.22), channel_id=1, source_target_pairs={{0,48},{16,32},{32,16},{48,0},{64,112},{80,96},{96,80},{112,64},{1... | collective-permute-start | bytes 589832 | tf_op jit(solution)/shard_map/ppermute | solution.py:98
  75.4 6.2 %collective-permute-start.7 = (f32[16,768]{1,0:T(8,128)}, f32[16,768]{1,0:T(8,128)}, u32[]{:S(2)}, u32[]{:S(2)}) collective-permute-start(f32[16,768]{1,0:T(8,128)} %get-tuple-element.23), channel_id=1, source_target_pairs={{0,4},{1,5},{2,6},{3,7},{4,0},{5,1},{6,2},{7,3},{8,12},{9,13},{10,... | collective-permute-start | bytes 147464 | tf_op jit(solution)/shard_map/ppermute | solution.py:98
  80.6 5.7 %collective-permute-start.8 = (f32[16,768]{1,0:T(8,128)S(1)}, f32[16,768]{1,0:T(8,128)}, u32[]{:S(2)}, u32[]{:S(2)}) collective-permute-start(f32[16,768]{1,0:T(8,128)S(1)} %get-tuple-element.25), channel_id=1, source_target_pairs={{0,8},{1,9},{2,10},{3,11},{4,12},{5,13},{6,14},{7,15},{8,0},{9,1},... | collective-permute-start | bytes 147464 | tf_op jit(solution)/shard_map/ppermute | solution.py:98
  93.9 6.1 %collective-permute-start.13 = (f32[1,768]{1,0:T(1,128)S(1)}, f32[1,768]{1,0:T(1,128)S(1)}, u32[]{:S(2)}, u32[]{:S(2)}) collective-permute-start(f32[1,768]{1,0:T(1,128)S(1)} %get-tuple-element.29), channel_id=1, source_target_pairs={{0,1},{1,0},{2,3},{3,2},{4,5},{5,4},{6,7},{7,6},{8,9},{9,8},{10,11... | collective-permute-start | bytes 9224 | tf_op jit(solution)/shard_map/ppermute | solution.py:98
  94.0 7.0 %collective-permute-start.15 = (f32[1,768]{1,0:T(1,128)S(1)}, f32[1,768]{1,0:T(1,128)S(1)}, u32[]{:S(2)}, u32[]{:S(2)}) collective-permute-start(f32[1,768]{1,0:T(1,128)S(1)} %get-tuple-element.30), channel_id=1, source_target_pairs={{0,3},{1,2},{2,1},{3,0},{4,7},{5,6},{6,5},{7,4},{8,11},{9,10},{10,... | collective-permute-start | bytes 9224 | tf_op jit(solution)/shard_map/ppermute | solution.py:98
  99.0 7.5 %collective-permute-start.14 = (f32[1,768]{1,0:T(1,128)S(1)}, f32[1,768]{1,0:T(1,128)S(1)}, u32[]{:S(2)}, u32[]{:S(2)}) collective-permute-start(f32[1,768]{1,0:T(1,128)S(1)} %get-tuple-element.31), channel_id=1, source_target_pairs={{0,2},{1,3},{2,0},{3,1},{4,6},{5,7},{6,4},{7,5},{8,10},{9,11},{10,... | collective-permute-start | bytes 9224 | tf_op jit(solution)/shard_map/ppermute | solution.py:98
  106.5 9.4 %collective-permute-start.16 = (f32[1,768]{1,0:T(1,128)S(1)}, f32[1,768]{1,0:T(1,128)S(1)}, u32[]{:S(2)}, u32[]{:S(2)}) collective-permute-start(f32[1,768]{1,0:T(1,128)S(1)} %fusion.78), channel_id=1, source_target_pairs={{0,1},{1,0},{2,3},{3,2},{4,5},{5,4},{6,7},{7,6},{8,9},{9,8},{10,11... | collective-permute-start | bytes 9224 | tf_op jit(solution)/shard_map/ppermute | solution.py:106
  106.6 12.5 %collective-permute-start.17 = (f32[1,768]{1,0:T(1,128)S(1)}, f32[1,768]{1,0:T(1,128)S(1)}, u32[]{:S(2)}, u32[]{:S(2)}) collective-permute-start(f32[1,768]{1,0:T(1,128)S(1)} %fusion.78), channel_id=1, source_target_pairs={{0,2},{1,3},{2,0},{3,1},{4,6},{5,7},{6,4},{7,5},{8,10},{9,11},{10,... | collective-permute-start | bytes 9224 | tf_op jit(solution)/shard_map/ppermute | solution.py:106
  107.8 14.5 %collective-permute-start.18 = (f32[1,768]{1,0:T(1,128)S(1)}, f32[1,768]{1,0:T(1,128)S(1)}, u32[]{:S(2)}, u32[]{:S(2)}) collective-permute-start(f32[1,768]{1,0:T(1,128)S(1)} %fusion.78), channel_id=1, source_target_pairs={{0,3},{1,2},{2,1},{3,0},{4,7},{5,6},{6,5},{7,4},{8,11},{9,10},{10,... | collective-permute-start | bytes 9224 | tf_op jit(solution)/shard_map/ppermute | solution.py:106
  125.4 18.9 %collective-permute-start.19 = (f32[4,768]{0,1:T(8,128)}, f32[4,768]{0,1:T(8,128)}, u32[]{:S(2)}, u32[]{:S(2)}) collective-permute-start(f32[4,768]{0,1:T(8,128)} %dynamic_update_slice.51), channel_id=1, source_target_pairs={{0,64},{16,80},{32,96},{48,112},{64,0},{80,16},{96,32},{112,48},{1... | collective-permute-start | bytes 36872 | tf_op jit(solution)/shard_map/ppermute | solution.py:106
  127.3 27.3 %collective-permute-start.20 = (f32[4,768]{0,1:T(8,128)}, f32[4,768]{0,1:T(8,128)}, u32[]{:S(2)}, u32[]{:S(2)}) collective-permute-start(f32[4,768]{0,1:T(8,128)} %dynamic_update_slice.51), channel_id=1, source_target_pairs={{0,128},{16,144},{32,160},{48,176},{64,192},{80,208},{96,224},{112... | collective-permute-start | bytes 36872 | tf_op jit(solution)/shard_map/ppermute | solution.py:106
  127.9 35.9 %collective-permute-start.21 = (f32[4,768]{0,1:T(8,128)}, f32[4,768]{0,1:T(8,128)}, u32[]{:S(2)}, u32[]{:S(2)}) collective-permute-start(f32[4,768]{0,1:T(8,128)} %dynamic_update_slice.51), channel_id=1, source_target_pairs={{0,192},{16,208},{32,224},{48,240},{64,128},{80,144},{96,160},{112... | collective-permute-start | bytes 36872 | tf_op jit(solution)/shard_map/ppermute | solution.py:106
  167.1 27.6 %collective-permute-start.24 = (f32[16,768]{0,1:T(8,128)}, f32[16,768]{0,1:T(8,128)}, u32[]{:S(2)}, u32[]{:S(2)}) collective-permute-start(f32[16,768]{0,1:T(8,128)} %dynamic_update_slice.55), channel_id=1, source_target_pairs={{0,12},{1,13},{2,14},{3,15},{4,8},{5,9},{6,10},{7,11},{8,4},{9,5},... | collective-permute-start | bytes 147464 | tf_op jit(solution)/shard_map/ppermute | solution.py:106
  168.2 23.3 %collective-permute-start.23 = (f32[16,768]{0,1:T(8,128)}, f32[16,768]{0,1:T(8,128)}, u32[]{:S(2)}, u32[]{:S(2)}) collective-permute-start(f32[16,768]{0,1:T(8,128)} %dynamic_update_slice.55), channel_id=1, source_target_pairs={{0,8},{1,9},{2,10},{3,11},{4,12},{5,13},{6,14},{7,15},{8,0},{9,1},... | collective-permute-start | bytes 147464 | tf_op jit(solution)/shard_map/ppermute | solution.py:106
  168.6 19.5 %collective-permute-start.22 = (f32[16,768]{0,1:T(8,128)}, f32[16,768]{0,1:T(8,128)}, u32[]{:S(2)}, u32[]{:S(2)}) collective-permute-start(f32[16,768]{0,1:T(8,128)} %dynamic_update_slice.55), channel_id=1, source_target_pairs={{0,4},{1,5},{2,6},{3,7},{4,0},{5,1},{6,2},{7,3},{8,12},{9,13},{10,... | collective-permute-start | bytes 147464 | tf_op jit(solution)/shard_map/ppermute | solution.py:106
  198.1 28.1 %collective-permute-start.27 = (f32[64,768]{0,1:T(8,128)}, f32[64,768]{0,1:T(8,128)}, u32[]{:S(2)}, u32[]{:S(2)}) collective-permute-start(f32[64,768]{0,1:T(8,128)} %dynamic_update_slice.59), channel_id=1, source_target_pairs={{0,48},{16,32},{32,16},{48,0},{64,112},{80,96},{96,80},{112,64},{1... | collective-permute-start | bytes 589832 | tf_op jit(solution)/shard_map/ppermute | solution.py:106
  198.5 24.1 %collective-permute-start.26 = (f32[64,768]{0,1:T(8,128)}, f32[64,768]{0,1:T(8,128)}, u32[]{:S(2)}, u32[]{:S(2)}) collective-permute-start(f32[64,768]{0,1:T(8,128)} %dynamic_update_slice.59), channel_id=1, source_target_pairs={{0,32},{16,48},{32,0},{48,16},{64,96},{80,112},{96,64},{112,80},{1... | collective-permute-start | bytes 589832 | tf_op jit(solution)/shard_map/ppermute | solution.py:106
  199.1 18.9 %collective-permute-start.25 = (f32[64,768]{0,1:T(8,128)}, f32[64,768]{0,1:T(8,128)}, u32[]{:S(2)}, u32[]{:S(2)}) collective-permute-start(f32[64,768]{0,1:T(8,128)} %dynamic_update_slice.59), channel_id=1, source_target_pairs={{0,16},{16,0},{32,48},{48,32},{64,80},{80,64},{96,112},{112,96},{1... | collective-permute-start | bytes 589832 | tf_op jit(solution)/shard_map/ppermute | solution.py:106
  (17 other events, 103.5 us)

commit v5 on v4

--- a/solution.py
+++ b/solution.py
@@ -122,10 +122,12 @@
 
 def unfolded_sums(first, second):
     half, width = first.shape
-    total = butterfly_sum(jnp.concatenate([first, second], axis=0))
+    lanes = width // 3
+    rows = half * 3
+    total = butterfly_sum(jnp.concatenate([first.reshape(rows, lanes), second.reshape(rows, lanes)], axis=0))
     outs = []
     for i in range(2):
-        part = total[i * half : (i + 1) * half]
+        part = total[i * rows : (i + 1) * rows].reshape(half, width)
         full = jnp.concatenate([part, part[::-1, ::-1]], axis=0)
         outs.append(jnp.transpose(full.reshape(2 * half, 3, width // 3), (1, 2, 0)))
     return outs

time: 235 us -> 160 us (0.68)
  the two profiles are of different devices: /device:TPU:32 before, /device:TPU:1 now
where the time goes in v5:
time: 160 us; the launch traced here: 158 us
  starting transfers between devices  56.5 us (35%)
  local copies, waits for them, and re-layouts  36 us (22%)
  waiting for transfers between devices  32 us (20%)
  other arithmetic  17.8 us (11%)
  matrix products  14.4 us (9%)
    ppermute x12, starting transfers between devices, butterfly_sum(): total = total + lax.ppermute(sent, axis, partner_pairs(axis, shift, offset))  22.5 us
    ppermute x12, starting transfers between devices, butterfly_sum(): got = lax.ppermute(rows, axis, partner_pairs(axis, shift, offset))  17.6 us
    ppermute x12, waiting for transfers between devices, butterfly_sum(): total = total + lax.ppermute(sent, axis, partner_pairs(axis, shift, offset))  16.8 us
    ppermute x12, waiting for transfers between devices, butterfly_sum(): got = lax.ppermute(rows, axis, partner_pairs(axis, shift, offset))  14.2 us
    unnamed x30, local copies, waits for them, and re-layouts  9.59 us
    ppermute x2, starting transfers between devices, neighbour_halo(): lax.ppermute(tail, 'seq', [(i, i + 1) for i in range(count - 1)])  9.4 us
    dot_general x4, matrix products, product(): jnp.dot(stacked.reshape(-1, shape_in[-1]), matrix, preferred_element_type...  8.46 us
    rev x2, local copies, waits for them, and re-layouts, folded_term(): return term[:half] + term[half:][::-1, ::-1]  8.2 us
  transfers between devices with their start and end apart: 28, of which 15 were waited for; matrix products, arithmetic and copies ran while one was open for 14% of the time, Pallas kernels for 0%

profile of v5, /device:TPU:1, one launch (start us, length us, event | category | flops | bytes accessed | tf_op | source)
XLA Modules:
  0.0 157.9 jit_solution(7051842418489672207)
XLA Ops:
  1.4 5.1 %collective-permute-start.3 = (bf16[1,16,256]{2,1,0:T(8,128)(2,1)S(1)}, bf16[1,16,256]{2,1,0:T(8,128)(2,1)S(1)}, u32[]{:S(2)}, u32[]{:S(2)}) collective-permute-start(bf16[1,16,256]{2,1,0:T(8,128)(2,1)S(1)} %get-tuple-element.26), channel_id=1, source_target_pairs={{1,0},{2,1},{3,2},{4,3},{5,4},{6,5},{7,6},{8,7},{9,8},{10,9},{11,1... | collective-permute-start | bytes 24584 | tf_op jit(solution)/shard_map/ppermute | solution.py:154
  6.5 7.0 %collective-permute-start.2 = (bf16[1,16,256]{2,1,0:T(8,128)(2,1)S(1)}, bf16[1,16,256]{2,1,0:T(8,128)(2,1)S(1)}, u32[]{:S(2)}, u32[]{:S(2)}) collective-permute-start(bf16[1,16,256]{2,1,0:T(8,128)(2,1)S(1)} %get-tuple-element.25), channel_id=1, source_target_pairs={{0,1},{1,2},{2,3},{3,4},{4,5},{5,6},{6,7},{7,8},{8,9},{9,10},{10,1... | collective-permute-start | bytes 24584 | tf_op jit(solution)/shard_map/ppermute | solution.py:153
  14.2 2.4 %collective-permute-start = (s32[1,36]{1,0:T(1,128)S(1)}, s32[1,36]{1,0:T(1,128)S(1)}, u32[]{:S(2)}, u32[]{:S(2)}) collective-permute-start(s32[1,36]{1,0:T(1,128)S(1)} %get-tuple-element.42), channel_id=1, source_target_pairs={{0,1},{1,2},{2,3},{3,4},{4,5},{5,6},{6,7},{7,8},{8,9},{9,10},{10,1... | collective-permute-start | bytes 440 | tf_op jit(solution)/shard_map/ppermute | solution.py:153
  20.1 2.1 %copy.20 = bf16[3,256,256]{1,2,0:T(8,128)(2,1)} copy(bf16[3,256,256]{2,1,0:T(8,128)(2,1)} %param.8) | data formatting | bytes 786432 | tf_op args[3]
  30.7 2.4 %fusion.40 = (bf16[1,2112,256]{2,1,0:T(8,128)(2,1)S(1)}, f32[1,2112,256]{2,1,0:T(8,128)}) fusion(pred[2112]{0:T(1024)(128)(4,1)S(1)} %fusion.67, f32[1,2112,512]{2,1,0:T(8,128)S(1)} %convolution_bitcast_fusion.1), kind=kLoop, calls=%fused_computation.65 | loop fusion | flops 5947392 | bytes 7571520 | tf_op jit(solution)/shard_map/jit(_where)/select_n | solution.py:210
  42.4 4.1 %rev.20 = f32[128,768]{1,0:T(8,128)} reverse(f32[128,768]{1,0:T(8,128)} %slice.137), dimensions={0,1} | reverse | bytes 786432 | tf_op jit(solution)/shard_map/rev | solution.py:120
  52.0 4.1 %convolution_bitcast_fusion.2 = f32[1,2048,512]{2,1,0:T(8,128)S(1)} fusion(bf16[1,2048,256]{2,1,0:T(8,128)(2,1)} %get-tuple-element.23, bf16[1,2048,256]{2,1,0:T(8,128)(2,1)} %get-tuple-element.24, bf16[1,2048,256]{2,1,0:T(8,128)(2,1)} %get-tuple-element.22, bf16[768,256]{1,0:T(8,128)(2,1)} %bitcast.65, bf16[768,256]{1,0:T(8,128)(2,1)} %bitcast.64), kind=kOutput, calls=%fused_computation.5 | convolution fusion | flops 1621622784 | bytes 8126464 | tf_op jit(solution)/shard_map/dot_general | solution.py:40
  56.2 2.0 %fusion.4 = f32[256,768]{1,0:T(8,128)S(1)} fusion(bf16[1,2112,768]{2,1,0:T(8,128)(2,1)S(1)} %copy-done.1, f32[1,2048,512]{2,1,0:T(8,128)S(1)} %convolution_bitcast_fusion.2, f32[1,2112,256]{2,1,0:T(8,128)S(1)} %copy-done.2, bf16[1,2048,256]{2,1,0:T(8,128)(2,1)S(1)} %copy-done.4), kind=kOutput, calls=%fused_computation.12 | convolution fusion | flops 817364992 | bytes 11272192 | tf_op jit(solution)/shard_map/dot_general | solution.py:114
  59.8 4.1 %rev.21 = f32[128,768]{1,0:T(8,128)} reverse(f32[128,768]{1,0:T(8,128)} %slice.145), dimensions={0,1} | reverse | bytes 786432 | tf_op jit(solution)/shard_map/rev | solution.py:120
  71.4 2.5 %collective-permute-start.6 = (f32[192,256]{1,0:T(8,128)}, f32[192,256]{1,0:T(8,128)S(1)}, u32[]{:S(2)}, u32[]{:S(2)}) collective-permute-start(f32[192,256]{1,0:T(8,128)} %get-tuple-element.30), channel_id=1, source_target_pairs={{0,48},{16,32},{32,16},{48,0},{64,112},{80,96},{96,80},{112,64},{1... | collective-permute-start | bytes 589832 | tf_op jit(solution)/shard_map/ppermute | solution.py:98
  74.6 7.8 %collective-permute-done.6 = f32[192,256]{1,0:T(8,128)S(1)} collective-permute-done((f32[192,256]{1,0:T(8,128)}, f32[192,256]{1,0:T(8,128)S(1)}, u32[]{:S(2)}, u32[]{:S(2)}) %collective-permute-start.6) | collective-permute-done | bytes 196640 | tf_op jit(solution)/shard_map/ppermute | solution.py:98
  85.4 3.2 %collective-permute-start.7 = (f32[48,256]{1,0:T(8,128)S(1)}, f32[48,256]{1,0:T(8,128)}, u32[]{:S(2)}, u32[]{:S(2)}) collective-permute-start(f32[48,256]{1,0:T(8,128)S(1)} %get-tuple-element.32), channel_id=1, source_target_pairs={{0,4},{1,5},{2,6},{3,7},{4,0},{5,1},{6,2},{7,3},{8,12},{9,13},{10,... | collective-permute-start | bytes 147464 | tf_op jit(solution)/shard_map/ppermute | solution.py:98
  91.6 2.7 %collective-permute-start.12 = (f32[12,256]{1,0:T(8,128)S(1)}, f32[12,256]{1,0:T(8,128)S(1)}, u32[]{:S(2)}, u32[]{:S(2)}) collective-permute-start(f32[12,256]{1,0:T(8,128)S(1)} %get-tuple-element.36), channel_id=1, source_target_pairs={{0,192},{16,208},{32,224},{48,240},{64,128},{80,144},{96,160},{112... | collective-permute-start | bytes 36872 | tf_op jit(solution)/shard_map/ppermute | solution.py:98
  97.8 10.0 %collective-permute-start.15 = (f32[3,256]{1,0:T(4,128)S(1)}, f32[3,256]{1,0:T(4,128)S(1)}, u32[]{:S(2)}, u32[]{:S(2)}) collective-permute-start(f32[3,256]{1,0:T(4,128)S(1)} %get-tuple-element.39), channel_id=1, source_target_pairs={{0,3},{1,2},{2,1},{3,0},{4,7},{5,6},{6,5},{7,4},{8,11},{9,10},{10,... | collective-permute-start | bytes 9224 | tf_op jit(solution)/shard_map/ppermute | solution.py:98
  107.9 2.3 %collective-permute-start.14 = (f32[3,256]{1,0:T(4,128)S(1)}, f32[3,256]{1,0:T(4,128)S(1)}, u32[]{:S(2)}, u32[]{:S(2)}) collective-permute-start(f32[3,256]{1,0:T(4,128)S(1)} %get-tuple-element.40), channel_id=1, source_target_pairs={{0,2},{1,3},{2,0},{3,1},{4,6},{5,7},{6,4},{7,5},{8,10},{9,11},{10,... | collective-permute-start | bytes 9224 | tf_op jit(solution)/shard_map/ppermute | solution.py:98
  110.2 4.0 %collective-permute-done.14 = f32[3,256]{1,0:T(4,128)S(1)} collective-permute-done((f32[3,256]{1,0:T(4,128)S(1)}, f32[3,256]{1,0:T(4,128)S(1)}, u32[]{:S(2)}, u32[]{:S(2)}) %collective-permute-start.14) | collective-permute-done | bytes 3104 | tf_op jit(solution)/shard_map/ppermute | solution.py:98
  114.3 2.4 %collective-permute-start.17 = (f32[3,256]{1,0:T(4,128)S(1)}, f32[3,256]{1,0:T(4,128)S(1)}, u32[]{:S(2)}, u32[]{:S(2)}) collective-permute-start(f32[3,256]{1,0:T(4,128)S(1)} %fusion.71), channel_id=1, source_target_pairs={{0,2},{1,3},{2,0},{3,1},{4,6},{5,7},{6,4},{7,5},{8,10},{9,11},{10,... | collective-permute-start | bytes 9224 | tf_op jit(solution)/shard_map/ppermute | solution.py:106
  116.8 3.6 %collective-permute-start.18 = (f32[3,256]{1,0:T(4,128)S(1)}, f32[3,256]{1,0:T(4,128)S(1)}, u32[]{:S(2)}, u32[]{:S(2)}) collective-permute-start(f32[3,256]{1,0:T(4,128)S(1)} %fusion.71), channel_id=1, source_target_pairs={{0,3},{1,2},{2,1},{3,0},{4,7},{5,6},{6,5},{7,4},{8,11},{9,10},{10,... | collective-permute-start | bytes 9224 | tf_op jit(solution)/shard_map/ppermute | solution.py:106
  120.9 3.2 %collective-permute-done.18 = f32[3,256]{1,0:T(4,128)S(1)} collective-permute-done((f32[3,256]{1,0:T(4,128)S(1)}, f32[3,256]{1,0:T(4,128)S(1)}, u32[]{:S(2)}, u32[]{:S(2)}) %collective-permute-start.18) | collective-permute-done | bytes 3104 | tf_op jit(solution)/shard_map/ppermute | solution.py:106
  130.7 2.0 %collective-permute-start.23 = (f32[48,256]{1,0:T(8,128)S(1)}, f32[48,256]{1,0:T(8,128)S(1)}, u32[]{:S(2)}, u32[]{:S(2)}) collective-permute-start(f32[48,256]{1,0:T(8,128)S(1)} %dynamic_update_slice.55), channel_id=1, source_target_pairs={{0,8},{1,9},{2,10},{3,11},{4,12},{5,13},{6,14},{7,15},{8,0},{9,1},... | collective-permute-start | bytes 147464 | tf_op jit(solution)/shard_map/ppermute | solution.py:106
  138.0 3.1 %fusion.37 = bf16[1,2048,256]{2,1,0:T(8,128)(2,1)} fusion(f32[1,2080,256]{2,1,0:T(8,128)} %add_multiply_fusion, f32[1,2080,256]{2,1,0:T(8,128)S(1)} %get-tuple-element.13, bf16[1,2112,256]{2,1,0:T(8,128)(2,1)S(1)} %get-tuple-element.14), kind=kLoop, calls=%fused_computation.57 | loop fusion | flops 2097152 | bytes 6291456 | tf_op jit(solution)/shard_map/convert_element_type | solution.py:218
  141.1 2.4 %collective-permute-start.26 = (f32[192,256]{1,0:T(8,128)S(1)}, f32[192,256]{1,0:T(8,128)S(1)}, u32[]{:S(2)}, u32[]{:S(2)}) collective-permute-start(f32[192,256]{1,0:T(8,128)S(1)} %constant_dynamic-update-slice_fusion.6), channel_id=1, source_target_pairs={{0,32},{16,48},{32,0},{48,16},{64,96},{80,112},{96,64},{112,80},{1... | collective-permute-start | bytes 589832 | tf_op jit(solution)/shard_map/ppermute | solution.py:106
  143.9 4.6 %collective-permute-done.26 = f32[192,256]{1,0:T(8,128)S(1)} collective-permute-done((f32[192,256]{1,0:T(8,128)S(1)}, f32[192,256]{1,0:T(8,128)S(1)}, u32[]{:S(2)}, u32[]{:S(2)}) %collective-permute-start.26) | collective-permute-done | bytes 196640 | tf_op jit(solution)/shard_map/ppermute | solution.py:106
  148.6 3.9 %collective-permute-done.27 = f32[192,256]{1,0:T(8,128)S(1)} collective-permute-done((f32[192,256]{1,0:T(8,128)S(1)}, f32[192,256]{1,0:T(8,128)S(1)}, u32[]{:S(2)}, u32[]{:S(2)}) %collective-permute-start.27) | collective-permute-done | bytes 196640 | tf_op jit(solution)/shard_map/ppermute | solution.py:106
  (136 shorter events, 65.6 us)
Async XLA Ops:
  1.4 34.9 %collective-permute-start.3 = (bf16[1,16,256]{2,1,0:T(8,128)(2,1)S(1)}, bf16[1,16,256]{2,1,0:T(8,128)(2,1)S(1)}, u32[]{:S(2)}, u32[]{:S(2)}) collective-permute-start(bf16[1,16,256]{2,1,0:T(8,128)(2,1)S(1)} %get-tuple-element.26), channel_id=1, source_target_pairs={{1,0},{2,1},{3,2},{4,3},{5,4},{6,5},{7,6},{8,7},{9,8},{10,9},{11,1... | collective-permute-start | bytes 24584 | tf_op jit(solution)/shard_map/ppermute | solution.py:154
  6.5 29.9 %collective-permute-start.2 = (bf16[1,16,256]{2,1,0:T(8,128)(2,1)S(1)}, bf16[1,16,256]{2,1,0:T(8,128)(2,1)S(1)}, u32[]{:S(2)}, u32[]{:S(2)}) collective-permute-start(bf16[1,16,256]{2,1,0:T(8,128)(2,1)S(1)} %get-tuple-element.25), channel_id=1, source_target_pairs={{0,1},{1,2},{2,3},{3,4},{4,5},{5,6},{6,7},{7,8},{8,9},{9,10},{10,1... | collective-permute-start | bytes 24584 | tf_op jit(solution)/shard_map/ppermute | solution.py:153
  14.2 10.4 %collective-permute-start = (s32[1,36]{1,0:T(1,128)S(1)}, s32[1,36]{1,0:T(1,128)S(1)}, u32[]{:S(2)}, u32[]{:S(2)}) collective-permute-start(s32[1,36]{1,0:T(1,128)S(1)} %get-tuple-element.42), channel_id=1, source_target_pairs={{0,1},{1,2},{2,3},{3,4},{4,5},{5,6},{6,7},{7,8},{8,9},{9,10},{10,1... | collective-permute-start | bytes 440 | tf_op jit(solution)/shard_map/ppermute | solution.py:153
  16.7 9.0 %collective-permute-start.1 = (s32[1,36]{1,0:T(1,128)S(1)}, s32[1,36]{1,0:T(1,128)S(1)}, u32[]{:S(2)}, u32[]{:S(2)}) collective-permute-start(s32[1,36]{1,0:T(1,128)S(1)} %get-tuple-element.41), channel_id=1, source_target_pairs={{1,0},{2,1},{3,2},{4,3},{5,4},{6,5},{7,6},{8,7},{9,8},{10,9},{11,1... | collective-permute-start | bytes 440 | tf_op jit(solution)/shard_map/ppermute | solution.py:154
  71.4 11.0 %collective-permute-start.6 = (f32[192,256]{1,0:T(8,128)}, f32[192,256]{1,0:T(8,128)S(1)}, u32[]{:S(2)}, u32[]{:S(2)}) collective-permute-start(f32[192,256]{1,0:T(8,128)} %get-tuple-element.30), channel_id=1, source_target_pairs={{0,48},{16,32},{32,16},{48,0},{64,112},{80,96},{96,80},{112,64},{1... | collective-permute-start | bytes 589832 | tf_op jit(solution)/shard_map/ppermute | solution.py:98
  73.9 8.6 %collective-permute-start.5 = (f32[192,256]{1,0:T(8,128)}, f32[192,256]{1,0:T(8,128)}, u32[]{:S(2)}, u32[]{:S(2)}) collective-permute-start(f32[192,256]{1,0:T(8,128)} %get-tuple-element.31), channel_id=1, source_target_pairs={{0,32},{16,48},{32,0},{48,16},{64,96},{80,112},{96,64},{112,80},{1... | collective-permute-start | bytes 589832 | tf_op jit(solution)/shard_map/ppermute | solution.py:98
  74.4 9.1 %collective-permute-start.4 = (f32[192,256]{1,0:T(8,128)}, f32[192,256]{1,0:T(8,128)}, u32[]{:S(2)}, u32[]{:S(2)}) collective-permute-start(f32[192,256]{1,0:T(8,128)} %get-tuple-element.29), channel_id=1, source_target_pairs={{0,16},{16,0},{32,48},{48,32},{64,80},{80,64},{96,112},{112,96},{1... | collective-permute-start | bytes 589832 | tf_op jit(solution)/shard_map/ppermute | solution.py:98
  85.4 5.0 %collective-permute-start.9 = (f32[48,256]{1,0:T(8,128)}, f32[48,256]{1,0:T(8,128)}, u32[]{:S(2)}, u32[]{:S(2)}) collective-permute-start(f32[48,256]{1,0:T(8,128)} %get-tuple-element.33), channel_id=1, source_target_pairs={{0,12},{1,13},{2,14},{3,15},{4,8},{5,9},{6,10},{7,11},{8,4},{9,5},... | collective-permute-start | bytes 147464 | tf_op jit(solution)/shard_map/ppermute | solution.py:98
  85.4 5.0 %collective-permute-start.8 = (f32[48,256]{1,0:T(8,128)S(1)}, f32[48,256]{1,0:T(8,128)}, u32[]{:S(2)}, u32[]{:S(2)}) collective-permute-start(f32[48,256]{1,0:T(8,128)S(1)} %get-tuple-element.34), channel_id=1, source_target_pairs={{0,8},{1,9},{2,10},{3,11},{4,12},{5,13},{6,14},{7,15},{8,0},{9,1},... | collective-permute-start | bytes 147464 | tf_op jit(solution)/shard_map/ppermute | solution.py:98
  85.4 5.4 %collective-permute-start.7 = (f32[48,256]{1,0:T(8,128)S(1)}, f32[48,256]{1,0:T(8,128)}, u32[]{:S(2)}, u32[]{:S(2)}) collective-permute-start(f32[48,256]{1,0:T(8,128)S(1)} %get-tuple-element.32), channel_id=1, source_target_pairs={{0,4},{1,5},{2,6},{3,7},{4,0},{5,1},{6,2},{7,3},{8,12},{9,13},{10,... | collective-permute-start | bytes 147464 | tf_op jit(solution)/shard_map/ppermute | solution.py:98
  91.6 4.9 %collective-permute-start.12 = (f32[12,256]{1,0:T(8,128)S(1)}, f32[12,256]{1,0:T(8,128)S(1)}, u32[]{:S(2)}, u32[]{:S(2)}) collective-permute-start(f32[12,256]{1,0:T(8,128)S(1)} %get-tuple-element.36), channel_id=1, source_target_pairs={{0,192},{16,208},{32,224},{48,240},{64,128},{80,144},{96,160},{112... | collective-permute-start | bytes 36872 | tf_op jit(solution)/shard_map/ppermute | solution.py:98
  97.8 12.4 %collective-permute-start.15 = (f32[3,256]{1,0:T(4,128)S(1)}, f32[3,256]{1,0:T(4,128)S(1)}, u32[]{:S(2)}, u32[]{:S(2)}) collective-permute-start(f32[3,256]{1,0:T(4,128)S(1)} %get-tuple-element.39), channel_id=1, source_target_pairs={{0,3},{1,2},{2,1},{3,0},{4,7},{5,6},{6,5},{7,4},{8,11},{9,10},{10,... | collective-permute-start | bytes 9224 | tf_op jit(solution)/shard_map/ppermute | solution.py:98
  107.9 6.4 %collective-permute-start.14 = (f32[3,256]{1,0:T(4,128)S(1)}, f32[3,256]{1,0:T(4,128)S(1)}, u32[]{:S(2)}, u32[]{:S(2)}) collective-permute-start(f32[3,256]{1,0:T(4,128)S(1)} %get-tuple-element.40), channel_id=1, source_target_pairs={{0,2},{1,3},{2,0},{3,1},{4,6},{5,7},{6,4},{7,5},{8,10},{9,11},{10,... | collective-permute-start | bytes 9224 | tf_op jit(solution)/shard_map/ppermute | solution.py:98
  114.2 6.2 %collective-permute-start.16 = (f32[3,256]{1,0:T(4,128)S(1)}, f32[3,256]{1,0:T(4,128)S(1)}, u32[]{:S(2)}, u32[]{:S(2)}) collective-permute-start(f32[3,256]{1,0:T(4,128)S(1)} %fusion.71), channel_id=1, source_target_pairs={{0,1},{1,0},{2,3},{3,2},{4,5},{5,4},{6,7},{7,6},{8,9},{9,8},{10,11... | collective-permute-start | bytes 9224 | tf_op jit(solution)/shard_map/ppermute | solution.py:106
  114.3 6.5 %collective-permute-start.17 = (f32[3,256]{1,0:T(4,128)S(1)}, f32[3,256]{1,0:T(4,128)S(1)}, u32[]{:S(2)}, u32[]{:S(2)}) collective-permute-start(f32[3,256]{1,0:T(4,128)S(1)} %fusion.71), channel_id=1, source_target_pairs={{0,2},{1,3},{2,0},{3,1},{4,6},{5,7},{6,4},{7,5},{8,10},{9,11},{10,... | collective-permute-start | bytes 9224 | tf_op jit(solution)/shard_map/ppermute | solution.py:106
  116.8 7.3 %collective-permute-start.18 = (f32[3,256]{1,0:T(4,128)S(1)}, f32[3,256]{1,0:T(4,128)S(1)}, u32[]{:S(2)}, u32[]{:S(2)}) collective-permute-start(f32[3,256]{1,0:T(4,128)S(1)} %fusion.71), channel_id=1, source_target_pairs={{0,3},{1,2},{2,1},{3,0},{4,7},{5,6},{6,5},{7,4},{8,11},{9,10},{10,... | collective-permute-start | bytes 9224 | tf_op jit(solution)/shard_map/ppermute | solution.py:106
  124.1 5.8 %collective-permute-start.19 = (f32[12,256]{1,0:T(8,128)S(1)}, f32[12,256]{1,0:T(8,128)S(1)}, u32[]{:S(2)}, u32[]{:S(2)}) collective-permute-start(f32[12,256]{1,0:T(8,128)S(1)} %dynamic_update_slice.51), channel_id=1, source_target_pairs={{0,64},{16,80},{32,96},{48,112},{64,0},{80,16},{96,32},{112,48},{1... | collective-permute-start | bytes 36872 | tf_op jit(solution)/shard_map/ppermute | solution.py:106
  125.5 4.7 %collective-permute-start.20 = (f32[12,256]{1,0:T(8,128)S(1)}, f32[12,256]{1,0:T(8,128)S(1)}, u32[]{:S(2)}, u32[]{:S(2)}) collective-permute-start(f32[12,256]{1,0:T(8,128)S(1)} %dynamic_update_slice.51), channel_id=1, source_target_pairs={{0,128},{16,144},{32,160},{48,176},{64,192},{80,208},{96,224},{112... | collective-permute-start | bytes 36872 | tf_op jit(solution)/shard_map/ppermute | solution.py:106
  126.1 4.4 %collective-permute-start.21 = (f32[12,256]{1,0:T(8,128)S(1)}, f32[12,256]{1,0:T(8,128)S(1)}, u32[]{:S(2)}, u32[]{:S(2)}) collective-permute-start(f32[12,256]{1,0:T(8,128)S(1)} %dynamic_update_slice.51), channel_id=1, source_target_pairs={{0,192},{16,208},{32,224},{48,240},{64,128},{80,144},{96,160},{112... | collective-permute-start | bytes 36872 | tf_op jit(solution)/shard_map/ppermute | solution.py:106
  130.7 4.5 %collective-permute-start.23 = (f32[48,256]{1,0:T(8,128)S(1)}, f32[48,256]{1,0:T(8,128)S(1)}, u32[]{:S(2)}, u32[]{:S(2)}) collective-permute-start(f32[48,256]{1,0:T(8,128)S(1)} %dynamic_update_slice.55), channel_id=1, source_target_pairs={{0,8},{1,9},{2,10},{3,11},{4,12},{5,13},{6,14},{7,15},{8,0},{9,1},... | collective-permute-start | bytes 147464 | tf_op jit(solution)/shard_map/ppermute | solution.py:106
  132.7 4.2 %collective-permute-start.24 = (f32[48,256]{1,0:T(8,128)S(1)}, f32[48,256]{1,0:T(8,128)S(1)}, u32[]{:S(2)}, u32[]{:S(2)}) collective-permute-start(f32[48,256]{1,0:T(8,128)S(1)} %dynamic_update_slice.55), channel_id=1, source_target_pairs={{0,12},{1,13},{2,14},{3,15},{4,8},{5,9},{6,10},{7,11},{8,4},{9,5},... | collective-permute-start | bytes 147464 | tf_op jit(solution)/shard_map/ppermute | solution.py:106
  136.8 7.0 %collective-permute-start.25 = (f32[192,256]{1,0:T(8,128)S(1)}, f32[192,256]{1,0:T(8,128)S(1)}, u32[]{:S(2)}, u32[]{:S(2)}) collective-permute-start(f32[192,256]{1,0:T(8,128)S(1)} %constant_dynamic-update-slice_fusion.6), channel_id=1, source_target_pairs={{0,16},{16,0},{32,48},{48,32},{64,80},{80,64},{96,112},{112,96},{1... | collective-permute-start | bytes 589832 | tf_op jit(solution)/shard_map/ppermute | solution.py:106
  141.1 7.5 %collective-permute-start.26 = (f32[192,256]{1,0:T(8,128)S(1)}, f32[192,256]{1,0:T(8,128)S(1)}, u32[]{:S(2)}, u32[]{:S(2)}) collective-permute-start(f32[192,256]{1,0:T(8,128)S(1)} %constant_dynamic-update-slice_fusion.6), channel_id=1, source_target_pairs={{0,32},{16,48},{32,0},{48,16},{64,96},{80,112},{96,64},{112,80},{1... | collective-permute-start | bytes 589832 | tf_op jit(solution)/shard_map/ppermute | solution.py:106
  143.5 8.9 %collective-permute-start.27 = (f32[192,256]{1,0:T(8,128)S(1)}, f32[192,256]{1,0:T(8,128)S(1)}, u32[]{:S(2)}, u32[]{:S(2)}) collective-permute-start(f32[192,256]{1,0:T(8,128)S(1)} %constant_dynamic-update-slice_fusion.6), channel_id=1, source_target_pairs={{0,48},{16,32},{32,16},{48,0},{64,112},{80,96},{96,80},{112,64},{1... | collective-permute-start | bytes 589832 | tf_op jit(solution)/shard_map/ppermute | solution.py:106
  (17 other events, 91.8 us)

commit v6 on v5

--- a/solution.py
+++ b/solution.py
@@ -87,9 +87,10 @@
     return [(i, i ^ (offset << shift)) for i in range(count)]
 
 
-def butterfly_sum(rows):
+def butterfly_sum(rows, scattered=2):
     kept = []
-    for axis, shift, radix in exchange_groups():
+    groups = exchange_groups()
+    for axis, shift, radix in groups[:scattered]:
         place = (lax.axis_index(axis) >> shift) & (radix - 1)
         width = rows.shape[0] // radix
         total = lax.dynamic_slice_in_dim(rows, place * width, width)
@@ -98,6 +99,14 @@
             total = total + lax.ppermute(sent, axis, partner_pairs(axis, shift, offset))
         rows = total
         kept.append((axis, shift, radix, place))
+    for axis, shift, radix in groups[scattered:]:
+        place = (lax.axis_index(axis) >> shift) & (radix - 1)
+        pieces = [rows] + [lax.ppermute(rows, axis, partner_pairs(axis, shift, offset)) for offset in range(1, radix)]
+        stacked = jnp.stack(pieces)
+        total = stacked[place]
+        for position in range(1, radix):
+            total = total + stacked[place ^ position]
+        rows = total
     for axis, shift, radix, place in reversed(kept):
         width = rows.shape[0]
         full = jnp.zeros((width * radix,) + rows.shape[1:], rows.dtype)

time: 160 us -> 147 us (0.919)
  starting transfers between devices: 56.5 us -> 47 us
  other arithmetic: 17.8 us -> 14.8 us
  waiting for transfers between devices: 32 us -> 34.1 us
    ppermute x0 -> x6, starting transfers between devices: none -> 16.2 us  [butterfly_sum(): lax.ppermute(rows, axis, partner_pairs(axis, shift, offset))]
    ppermute x12 -> x6, starting transfers between devices: 22.5 us -> 6.51 us  [butterfly_sum(): total = total + lax.ppermute(sent, axis, partner_pairs(axis, shift, offset))]
    ppermute x12 -> x6, starting transfers between devices: 17.6 us -> 7.89 us  [butterfly_sum(): got = lax.ppermute(rows, axis, partner_pairs(axis, shift, offset))]
    ppermute x0 -> x6, waiting for transfers between devices: none -> 7.58 us  [butterfly_sum(): lax.ppermute(rows, axis, partner_pairs(axis, shift, offset))]
    ppermute x12 -> x6, waiting for transfers between devices: 16.8 us -> 10.2 us  [butterfly_sum(): total = total + lax.ppermute(sent, axis, partner_pairs(axis, shift, offset))]
    convert_element_type x1, other arithmetic: 3.08 us -> 1.41 us  [local(): (hidden_own.astype(jnp.float32) + lax.slice_in_dim(gelu_two, two, two + p...]
    ppermute x12 -> x6, waiting for transfers between devices: 14.2 us -> 15.2 us  [butterfly_sum(): got = lax.ppermute(rows, axis, partner_pairs(axis, shift, offset))]
  transfers between devices with their start and end apart: 28 -> 22, of which waited for: 15 -> 13; matrix products, arithmetic and copies ran while one was open for 14% -> 13% of each run, Pallas kernels for 0% -> 0%
where the time goes in v6:
time: 147 us; the launch traced here: 146 us
  starting transfers between devices  47 us (32%)
  local copies, waits for them, and re-layouts  34.8 us (24%)
  waiting for transfers between devices  34.1 us (23%)
  other arithmetic  14.8 us (10%)
  matrix products  14.4 us (10%)
    ppermute x6, starting transfers between devices, butterfly_sum(): lax.ppermute(rows, axis, partner_pairs(axis, shift, offset))  16.2 us
    ppermute x6, waiting for transfers between devices, butterfly_sum(): got = lax.ppermute(rows, axis, partner_pairs(axis, shift, offset))  15.2 us
    ppermute x6, waiting for transfers between devices, butterfly_sum(): total = total + lax.ppermute(sent, axis, partner_pairs(axis, shift, offset))  10.2 us
    unnamed x30, local copies, waits for them, and re-layouts  9.57 us
    ppermute x2, starting transfers between devices, neighbour_halo(): lax.ppermute(tail, 'seq', [(i, i + 1) for i in range(count - 1)])  9.4 us
    dot_general x4, matrix products, product(): jnp.dot(stacked.reshape(-1, shape_in[-1]), matrix, preferred_element_type...  8.46 us
    rev x2, local copies, waits for them, and re-layouts, folded_term(): return term[:half] + term[half:][::-1, ::-1]  8.25 us
    ppermute x6, starting transfers between devices, butterfly_sum(): got = lax.ppermute(rows, axis, partner_pairs(axis, shift, offset))  7.89 us
  transfers between devices with their start and end apart: 22, of which 13 were waited for; matrix products, arithmetic and copies ran while one was open for 13% of the time, Pallas kernels for 0%

profile of v6, /device:TPU:1, one launch (start us, length us, event | category | flops | bytes accessed | tf_op | source)
XLA Modules:
  0.0 146.2 jit_solution(8232592266105417744)
XLA Ops:
  1.4 5.1 %collective-permute-start.3 = (bf16[1,16,256]{2,1,0:T(8,128)(2,1)S(1)}, bf16[1,16,256]{2,1,0:T(8,128)(2,1)S(1)}, u32[]{:S(2)}, u32[]{:S(2)}) collective-permute-start(bf16[1,16,256]{2,1,0:T(8,128)(2,1)S(1)} %get-tuple-element.28), channel_id=1, source_target_pairs={{1,0},{2,1},{3,2},{4,3},{5,4},{6,5},{7,6},{8,7},{9,8},{10,9},{11,1... | collective-permute-start | bytes 24584 | tf_op jit(solution)/shard_map/ppermute | solution.py:163
  6.5 7.0 %collective-permute-start.2 = (bf16[1,16,256]{2,1,0:T(8,128)(2,1)S(1)}, bf16[1,16,256]{2,1,0:T(8,128)(2,1)S(1)}, u32[]{:S(2)}, u32[]{:S(2)}) collective-permute-start(bf16[1,16,256]{2,1,0:T(8,128)(2,1)S(1)} %get-tuple-element.27), channel_id=1, source_target_pairs={{0,1},{1,2},{2,3},{3,4},{4,5},{5,6},{6,7},{7,8},{8,9},{9,10},{10,1... | collective-permute-start | bytes 24584 | tf_op jit(solution)/shard_map/ppermute | solution.py:162
  14.2 2.4 %collective-permute-start = (s32[1,36]{1,0:T(1,128)S(1)}, s32[1,36]{1,0:T(1,128)S(1)}, u32[]{:S(2)}, u32[]{:S(2)}) collective-permute-start(s32[1,36]{1,0:T(1,128)S(1)} %get-tuple-element.38), channel_id=1, source_target_pairs={{0,1},{1,2},{2,3},{3,4},{4,5},{5,6},{6,7},{7,8},{8,9},{9,10},{10,1... | collective-permute-start | bytes 440 | tf_op jit(solution)/shard_map/ppermute | solution.py:162
  16.7 1.9 %collective-permute-start.1 = (s32[1,36]{1,0:T(1,128)S(1)}, s32[1,36]{1,0:T(1,128)S(1)}, u32[]{:S(2)}, u32[]{:S(2)}) collective-permute-start(s32[1,36]{1,0:T(1,128)S(1)} %get-tuple-element.37), channel_id=1, source_target_pairs={{1,0},{2,1},{3,2},{4,3},{5,4},{6,5},{7,6},{8,7},{9,8},{10,9},{11,1... | collective-permute-start | bytes 440 | tf_op jit(solution)/shard_map/ppermute | solution.py:163
  20.1 2.1 %copy.20 = bf16[3,256,256]{1,2,0:T(8,128)(2,1)} copy(bf16[3,256,256]{2,1,0:T(8,128)(2,1)} %param.8) | data formatting | bytes 786432 | tf_op args[3]
  26.9 2.0 %pad_maximum_fusion = bf16[1,2112,768]{2,1,0:T(8,128)(2,1)} fusion(bf16[1,2112,256]{2,1,0:T(8,128)(2,1)S(1)} %get-tuple-element.19, bf16[1,2112,256]{2,1,0:T(8,128)(2,1)S(1)} %get-tuple-element.20, bf16[1,2112,256]{2,1,0:T(8,128)(2,1)S(1)} %get-tuple-element.18), kind=kLoop, calls=%fused_computation.7 | loop fusion | flops 9732096 | bytes 6488064 | tf_op jit(solution)/shard_map/concatenate | solution.py:192
  30.7 2.4 %fusion.40 = (bf16[1,2112,256]{2,1,0:T(8,128)(2,1)S(1)}, f32[1,2112,256]{2,1,0:T(8,128)}) fusion(pred[2112]{0:T(1024)(128)(4,1)S(1)} %fusion.67, f32[1,2112,512]{2,1,0:T(8,128)S(1)} %convolution_bitcast_fusion.1), kind=kLoop, calls=%fused_computation.65 | loop fusion | flops 5947392 | bytes 7571520 | tf_op jit(solution)/shard_map/jit(_where)/select_n | solution.py:219
  42.4 4.1 %rev.20 = f32[128,768]{1,0:T(8,128)} reverse(f32[128,768]{1,0:T(8,128)} %slice.137), dimensions={0,1} | reverse | bytes 786432 | tf_op jit(solution)/shard_map/rev | solution.py:129
  52.1 4.1 %convolution_bitcast_fusion.2 = f32[1,2048,512]{2,1,0:T(8,128)S(1)} fusion(bf16[1,2048,256]{2,1,0:T(8,128)(2,1)} %get-tuple-element.25, bf16[1,2048,256]{2,1,0:T(8,128)(2,1)} %get-tuple-element.26, bf16[1,2048,256]{2,1,0:T(8,128)(2,1)} %get-tuple-element.24, bf16[768,256]{1,0:T(8,128)(2,1)} %bitcast.77, bf16[768,256]{1,0:T(8,128)(2,1)} %bitcast.76), kind=kOutput, calls=%fused_computation.5 | convolution fusion | flops 1621622784 | bytes 8126464 | tf_op jit(solution)/shard_map/dot_general | solution.py:40
  56.2 2.0 %fusion.4 = f32[256,768]{1,0:T(8,128)S(1)} fusion(bf16[1,2112,768]{2,1,0:T(8,128)(2,1)S(1)} %copy-done.1, f32[1,2048,512]{2,1,0:T(8,128)S(1)} %convolution_bitcast_fusion.2, f32[1,2112,256]{2,1,0:T(8,128)S(1)} %copy-done.2, bf16[1,2048,256]{2,1,0:T(8,128)(2,1)S(1)} %copy-done.4), kind=kOutput, calls=%fused_computation.12 | convolution fusion | flops 817364992 | bytes 11272192 | tf_op jit(solution)/shard_map/dot_general | solution.py:123
  59.9 4.1 %rev.21 = f32[128,768]{1,0:T(8,128)} reverse(f32[128,768]{1,0:T(8,128)} %slice.145), dimensions={0,1} | reverse | bytes 786432 | tf_op jit(solution)/shard_map/rev | solution.py:129
  69.5 1.9 %constant_dynamic-slice_fusion.5 = (f32[192,256]{1,0:T(8,128)}, f32[192,256]{1,0:T(8,128)}, f32[192,256]{1,0:T(8,128)}) fusion(f32[768,256]{1,0:T(8,128)} %constant_dynamic-update-slice_fusion, s32[]{:T(128)S(6)} %select_n.71, s32[]{:T(128)S(6)} %select_n.73, s32[]{:T(128)S(6)} %select_n.72), kind=kLoop, calls=%fused_computation.116 | loop fusion | bytes 1179660 | tf_op jit(solution)/shard_map/dynamic_slice | solution.py:98
  71.4 2.5 %collective-permute-start.6 = (f32[192,256]{1,0:T(8,128)}, f32[192,256]{1,0:T(8,128)S(1)}, u32[]{:S(2)}, u32[]{:S(2)}) collective-permute-start(f32[192,256]{1,0:T(8,128)} %get-tuple-element.32), channel_id=1, source_target_pairs={{0,48},{16,32},{32,16},{48,0},{64,112},{80,96},{96,80},{112,64},{1... | collective-permute-start | bytes 589832 | tf_op jit(solution)/shard_map/ppermute | solution.py:99
  74.7 7.8 %collective-permute-done.6 = f32[192,256]{1,0:T(8,128)S(1)} collective-permute-done((f32[192,256]{1,0:T(8,128)}, f32[192,256]{1,0:T(8,128)S(1)}, u32[]{:S(2)}, u32[]{:S(2)}) %collective-permute-start.6) | collective-permute-done | bytes 196640 | tf_op jit(solution)/shard_map/ppermute | solution.py:99
  85.4 3.2 %collective-permute-start.7 = (f32[48,256]{1,0:T(8,128)S(1)}, f32[48,256]{1,0:T(8,128)}, u32[]{:S(2)}, u32[]{:S(2)}) collective-permute-start(f32[48,256]{1,0:T(8,128)S(1)} %get-tuple-element.34), channel_id=1, source_target_pairs={{0,4},{1,5},{2,6},{3,7},{4,0},{5,1},{6,2},{7,3},{8,12},{9,13},{10,... | collective-permute-start | bytes 147464 | tf_op jit(solution)/shard_map/ppermute | solution.py:99
  91.6 2.7 %collective-permute-start.12 = (f32[48,256]{1,0:T(8,128)S(1)}, f32[48,256]{1,0:T(8,128)S(1)}, u32[]{:S(2)}, u32[]{:S(2)}) collective-permute-start(f32[48,256]{1,0:T(8,128)S(1)} %add_add_fusion.1), channel_id=1, source_target_pairs={{0,192},{16,208},{32,224},{48,240},{64,128},{80,144},{96,160},{112... | collective-permute-start | bytes 147464 | tf_op jit(solution)/shard_map/ppermute | solution.py:104
  98.2 10.3 %collective-permute-start.15 = (f32[48,256]{1,0:T(8,128)S(1)}, f32[48,256]{1,0:T(8,128)S(1)}, u32[]{:S(2)}, u32[]{:S(2)}) collective-permute-start(f32[48,256]{1,0:T(8,128)S(1)} %fusion.92), channel_id=1, source_target_pairs={{0,3},{1,2},{2,1},{3,0},{4,7},{5,6},{6,5},{7,4},{8,11},{9,10},{10,... | collective-permute-start | bytes 147464 | tf_op jit(solution)/shard_map/ppermute | solution.py:104
  108.5 2.3 %collective-permute-start.14 = (f32[48,256]{1,0:T(8,128)S(1)}, f32[48,256]{1,0:T(8,128)S(1)}, u32[]{:S(2)}, u32[]{:S(2)}) collective-permute-start(f32[48,256]{1,0:T(8,128)S(1)} %fusion.92), channel_id=1, source_target_pairs={{0,2},{1,3},{2,0},{3,1},{4,6},{5,7},{6,4},{7,5},{8,10},{9,11},{10,... | collective-permute-start | bytes 147464 | tf_op jit(solution)/shard_map/ppermute | solution.py:104
  110.8 4.7 %collective-permute-done.14 = f32[48,256]{1,0:T(8,128)S(1)} collective-permute-done((f32[48,256]{1,0:T(8,128)S(1)}, f32[48,256]{1,0:T(8,128)S(1)}, u32[]{:S(2)}, u32[]{:S(2)}) %collective-permute-start.14) | collective-permute-done | bytes 49184 | tf_op jit(solution)/shard_map/ppermute | solution.py:104
  117.1 2.5 %collective-permute-start.17 = (f32[48,256]{1,0:T(8,128)S(1)}, f32[48,256]{1,0:T(8,128)S(1)}, u32[]{:S(2)}, u32[]{:S(2)}) collective-permute-start(f32[48,256]{1,0:T(8,128)S(1)} %get-tuple-element.13), channel_id=1, source_target_pairs={{0,8},{1,9},{2,10},{3,11},{4,12},{5,13},{6,14},{7,15},{8,0},{9,1},... | collective-permute-start | bytes 147464 | tf_op jit(solution)/shard_map/ppermute | solution.py:115
  121.6 2.9 %collective-permute-done.18 = f32[48,256]{1,0:T(8,128)S(1)} collective-permute-done((f32[48,256]{1,0:T(8,128)S(1)}, f32[48,256]{1,0:T(8,128)S(1)}, u32[]{:S(2)}, u32[]{:S(2)}) %collective-permute-start.18) | collective-permute-done | bytes 49184 | tf_op jit(solution)/shard_map/ppermute | solution.py:115
  127.1 2.4 %collective-permute-start.20 = (f32[192,256]{1,0:T(8,128)S(1)}, f32[192,256]{1,0:T(8,128)S(1)}, u32[]{:S(2)}, u32[]{:S(2)}) collective-permute-start(f32[192,256]{1,0:T(8,128)S(1)} %constant_dynamic-update-slice_fusion.9), channel_id=1, source_target_pairs={{0,32},{16,48},{32,0},{48,16},{64,96},{80,112},{96,64},{112,80},{1... | collective-permute-start | bytes 589832 | tf_op jit(solution)/shard_map/ppermute | solution.py:115
  130.6 6.2 %collective-permute-done.20 = f32[192,256]{1,0:T(8,128)S(1)} collective-permute-done((f32[192,256]{1,0:T(8,128)S(1)}, f32[192,256]{1,0:T(8,128)S(1)}, u32[]{:S(2)}, u32[]{:S(2)}) %collective-permute-start.20) | collective-permute-done | bytes 196640 | tf_op jit(solution)/shard_map/ppermute | solution.py:115
  136.9 3.9 %collective-permute-done.21 = f32[192,256]{1,0:T(8,128)S(1)} collective-permute-done((f32[192,256]{1,0:T(8,128)S(1)}, f32[192,256]{1,0:T(8,128)S(1)}, u32[]{:S(2)}, u32[]{:S(2)}) %collective-permute-start.21) | collective-permute-done | bytes 196640 | tf_op jit(solution)/shard_map/ppermute | solution.py:115
  (114 shorter events, 54.6 us)
Async XLA Ops:
  0.6 25.2 %copy-start = (bf16[4,256]{1,0:T(4,128)(2,1)S(1)}, bf16[4,256]{1,0:T(4,128)(2,1)}, u32[]{:S(2)}) copy-start(bf16[4,256]{1,0:T(4,128)(2,1)} %param.6) | copy-start | bytes 6148
  0.6 25.0 %copy-start.11 = (s32[1,2048]{1,0:T(1,128)S(1)}, s32[1,2048]{1,0:T(1,128)}, u32[]{:S(2)}) copy-start(s32[1,2048]{1,0:T(1,128)} %param.5) | copy-start | bytes 24580
  1.4 34.9 %collective-permute-start.3 = (bf16[1,16,256]{2,1,0:T(8,128)(2,1)S(1)}, bf16[1,16,256]{2,1,0:T(8,128)(2,1)S(1)}, u32[]{:S(2)}, u32[]{:S(2)}) collective-permute-start(bf16[1,16,256]{2,1,0:T(8,128)(2,1)S(1)} %get-tuple-element.28), channel_id=1, source_target_pairs={{1,0},{2,1},{3,2},{4,3},{5,4},{6,5},{7,6},{8,7},{9,8},{10,9},{11,1... | collective-permute-start | bytes 24584 | tf_op jit(solution)/shard_map/ppermute | solution.py:163
  6.5 29.8 %collective-permute-start.2 = (bf16[1,16,256]{2,1,0:T(8,128)(2,1)S(1)}, bf16[1,16,256]{2,1,0:T(8,128)(2,1)S(1)}, u32[]{:S(2)}, u32[]{:S(2)}) collective-permute-start(bf16[1,16,256]{2,1,0:T(8,128)(2,1)S(1)} %get-tuple-element.27), channel_id=1, source_target_pairs={{0,1},{1,2},{2,3},{3,4},{4,5},{5,6},{6,7},{7,8},{8,9},{9,10},{10,1... | collective-permute-start | bytes 24584 | tf_op jit(solution)/shard_map/ppermute | solution.py:162
  14.2 10.4 %collective-permute-start = (s32[1,36]{1,0:T(1,128)S(1)}, s32[1,36]{1,0:T(1,128)S(1)}, u32[]{:S(2)}, u32[]{:S(2)}) collective-permute-start(s32[1,36]{1,0:T(1,128)S(1)} %get-tuple-element.38), channel_id=1, source_target_pairs={{0,1},{1,2},{2,3},{3,4},{4,5},{5,6},{6,7},{7,8},{8,9},{9,10},{10,1... | collective-permute-start | bytes 440 | tf_op jit(solution)/shard_map/ppermute | solution.py:162
  16.7 9.0 %collective-permute-start.1 = (s32[1,36]{1,0:T(1,128)S(1)}, s32[1,36]{1,0:T(1,128)S(1)}, u32[]{:S(2)}, u32[]{:S(2)}) collective-permute-start(s32[1,36]{1,0:T(1,128)S(1)} %get-tuple-element.37), channel_id=1, source_target_pairs={{1,0},{2,1},{3,2},{4,3},{5,4},{6,5},{7,6},{8,7},{9,8},{10,9},{11,1... | collective-permute-start | bytes 440 | tf_op jit(solution)/shard_map/ppermute | solution.py:163
  71.4 11.0 %collective-permute-start.6 = (f32[192,256]{1,0:T(8,128)}, f32[192,256]{1,0:T(8,128)S(1)}, u32[]{:S(2)}, u32[]{:S(2)}) collective-permute-start(f32[192,256]{1,0:T(8,128)} %get-tuple-element.32), channel_id=1, source_target_pairs={{0,48},{16,32},{32,16},{48,0},{64,112},{80,96},{96,80},{112,64},{1... | collective-permute-start | bytes 589832 | tf_op jit(solution)/shard_map/ppermute | solution.py:99
  73.9 8.6 %collective-permute-start.5 = (f32[192,256]{1,0:T(8,128)}, f32[192,256]{1,0:T(8,128)}, u32[]{:S(2)}, u32[]{:S(2)}) collective-permute-start(f32[192,256]{1,0:T(8,128)} %get-tuple-element.33), channel_id=1, source_target_pairs={{0,32},{16,48},{32,0},{48,16},{64,96},{80,112},{96,64},{112,80},{1... | collective-permute-start | bytes 589832 | tf_op jit(solution)/shard_map/ppermute | solution.py:99
  74.4 9.0 %collective-permute-start.4 = (f32[192,256]{1,0:T(8,128)}, f32[192,256]{1,0:T(8,128)}, u32[]{:S(2)}, u32[]{:S(2)}) collective-permute-start(f32[192,256]{1,0:T(8,128)} %get-tuple-element.31), channel_id=1, source_target_pairs={{0,16},{16,0},{32,48},{48,32},{64,80},{80,64},{96,112},{112,96},{1... | collective-permute-start | bytes 589832 | tf_op jit(solution)/shard_map/ppermute | solution.py:99
  85.4 5.0 %collective-permute-start.9 = (f32[48,256]{1,0:T(8,128)}, f32[48,256]{1,0:T(8,128)}, u32[]{:S(2)}, u32[]{:S(2)}) collective-permute-start(f32[48,256]{1,0:T(8,128)} %get-tuple-element.35), channel_id=1, source_target_pairs={{0,12},{1,13},{2,14},{3,15},{4,8},{5,9},{6,10},{7,11},{8,4},{9,5},... | collective-permute-start | bytes 147464 | tf_op jit(solution)/shard_map/ppermute | solution.py:99
  85.4 5.0 %collective-permute-start.8 = (f32[48,256]{1,0:T(8,128)S(1)}, f32[48,256]{1,0:T(8,128)}, u32[]{:S(2)}, u32[]{:S(2)}) collective-permute-start(f32[48,256]{1,0:T(8,128)S(1)} %get-tuple-element.36), channel_id=1, source_target_pairs={{0,8},{1,9},{2,10},{3,11},{4,12},{5,13},{6,14},{7,15},{8,0},{9,1},... | collective-permute-start | bytes 147464 | tf_op jit(solution)/shard_map/ppermute | solution.py:99
  85.4 5.4 %collective-permute-start.7 = (f32[48,256]{1,0:T(8,128)S(1)}, f32[48,256]{1,0:T(8,128)}, u32[]{:S(2)}, u32[]{:S(2)}) collective-permute-start(f32[48,256]{1,0:T(8,128)S(1)} %get-tuple-element.34), channel_id=1, source_target_pairs={{0,4},{1,5},{2,6},{3,7},{4,0},{5,1},{6,2},{7,3},{8,12},{9,13},{10,... | collective-permute-start | bytes 147464 | tf_op jit(solution)/shard_map/ppermute | solution.py:99
  91.6 5.2 %collective-permute-start.12 = (f32[48,256]{1,0:T(8,128)S(1)}, f32[48,256]{1,0:T(8,128)S(1)}, u32[]{:S(2)}, u32[]{:S(2)}) collective-permute-start(f32[48,256]{1,0:T(8,128)S(1)} %add_add_fusion.1), channel_id=1, source_target_pairs={{0,192},{16,208},{32,224},{48,240},{64,128},{80,144},{96,160},{112... | collective-permute-start | bytes 147464 | tf_op jit(solution)/shard_map/ppermute | solution.py:104
  94.3 3.8 %collective-permute-start.11 = (f32[48,256]{1,0:T(8,128)S(1)}, f32[48,256]{1,0:T(8,128)S(1)}, u32[]{:S(2)}, u32[]{:S(2)}) collective-permute-start(f32[48,256]{1,0:T(8,128)S(1)} %add_add_fusion.1), channel_id=1, source_target_pairs={{0,128},{16,144},{32,160},{48,176},{64,192},{80,208},{96,224},{112... | collective-permute-start | bytes 147464 | tf_op jit(solution)/shard_map/ppermute | solution.py:104
  94.3 3.8 %collective-permute-start.10 = (f32[48,256]{1,0:T(8,128)S(1)}, f32[48,256]{1,0:T(8,128)S(1)}, u32[]{:S(2)}, u32[]{:S(2)}) collective-permute-start(f32[48,256]{1,0:T(8,128)S(1)} %add_add_fusion.1), channel_id=1, source_target_pairs={{0,64},{16,80},{32,96},{48,112},{64,0},{80,16},{96,32},{112,48},{1... | collective-permute-start | bytes 147464 | tf_op jit(solution)/shard_map/ppermute | solution.py:104
  98.2 12.6 %collective-permute-start.15 = (f32[48,256]{1,0:T(8,128)S(1)}, f32[48,256]{1,0:T(8,128)S(1)}, u32[]{:S(2)}, u32[]{:S(2)}) collective-permute-start(f32[48,256]{1,0:T(8,128)S(1)} %fusion.92), channel_id=1, source_target_pairs={{0,3},{1,2},{2,1},{3,0},{4,7},{5,6},{6,5},{7,4},{8,11},{9,10},{10,... | collective-permute-start | bytes 147464 | tf_op jit(solution)/shard_map/ppermute | solution.py:104
  108.5 7.0 %collective-permute-start.14 = (f32[48,256]{1,0:T(8,128)S(1)}, f32[48,256]{1,0:T(8,128)S(1)}, u32[]{:S(2)}, u32[]{:S(2)}) collective-permute-start(f32[48,256]{1,0:T(8,128)S(1)} %fusion.92), channel_id=1, source_target_pairs={{0,2},{1,3},{2,0},{3,1},{4,6},{5,7},{6,4},{7,5},{8,10},{9,11},{10,... | collective-permute-start | bytes 147464 | tf_op jit(solution)/shard_map/ppermute | solution.py:104
  110.8 4.7 %collective-permute-start.13 = (f32[48,256]{1,0:T(8,128)S(1)}, f32[48,256]{1,0:T(8,128)S(1)}, u32[]{:S(2)}, u32[]{:S(2)}) collective-permute-start(f32[48,256]{1,0:T(8,128)S(1)} %fusion.92), channel_id=1, source_target_pairs={{0,1},{1,0},{2,3},{3,2},{4,5},{5,4},{6,7},{7,6},{8,9},{9,8},{10,11... | collective-permute-start | bytes 147464 | tf_op jit(solution)/shard_map/ppermute | solution.py:104
  115.6 4.6 %collective-permute-start.16 = (f32[48,256]{1,0:T(8,128)S(1)}, f32[48,256]{1,0:T(8,128)S(1)}, u32[]{:S(2)}, u32[]{:S(2)}) collective-permute-start(f32[48,256]{1,0:T(8,128)S(1)} %get-tuple-element.13), channel_id=1, source_target_pairs={{0,4},{1,5},{2,6},{3,7},{4,0},{5,1},{6,2},{7,3},{8,12},{9,13},{10,... | collective-permute-start | bytes 147464 | tf_op jit(solution)/shard_map/ppermute | solution.py:115
  117.1 4.5 %collective-permute-start.17 = (f32[48,256]{1,0:T(8,128)S(1)}, f32[48,256]{1,0:T(8,128)S(1)}, u32[]{:S(2)}, u32[]{:S(2)}) collective-permute-start(f32[48,256]{1,0:T(8,128)S(1)} %get-tuple-element.13), channel_id=1, source_target_pairs={{0,8},{1,9},{2,10},{3,11},{4,12},{5,13},{6,14},{7,15},{8,0},{9,1},... | collective-permute-start | bytes 147464 | tf_op jit(solution)/shard_map/ppermute | solution.py:115
  119.6 4.9 %collective-permute-start.18 = (f32[48,256]{1,0:T(8,128)S(1)}, f32[48,256]{1,0:T(8,128)S(1)}, u32[]{:S(2)}, u32[]{:S(2)}) collective-permute-start(f32[48,256]{1,0:T(8,128)S(1)} %get-tuple-element.13), channel_id=1, source_target_pairs={{0,12},{1,13},{2,14},{3,15},{4,8},{5,9},{6,10},{7,11},{8,4},{9,5},... | collective-permute-start | bytes 147464 | tf_op jit(solution)/shard_map/ppermute | solution.py:115
  124.5 6.1 %collective-permute-start.19 = (f32[192,256]{1,0:T(8,128)S(1)}, f32[192,256]{1,0:T(8,128)S(1)}, u32[]{:S(2)}, u32[]{:S(2)}) collective-permute-start(f32[192,256]{1,0:T(8,128)S(1)} %constant_dynamic-update-slice_fusion.9), channel_id=1, source_target_pairs={{0,16},{16,0},{32,48},{48,32},{64,80},{80,64},{96,112},{112,96},{1... | collective-permute-start | bytes 589832 | tf_op jit(solution)/shard_map/ppermute | solution.py:115
  127.1 9.8 %collective-permute-start.20 = (f32[192,256]{1,0:T(8,128)S(1)}, f32[192,256]{1,0:T(8,128)S(1)}, u32[]{:S(2)}, u32[]{:S(2)}) collective-permute-start(f32[192,256]{1,0:T(8,128)S(1)} %constant_dynamic-update-slice_fusion.9), channel_id=1, source_target_pairs={{0,32},{16,48},{32,0},{48,16},{64,96},{80,112},{96,64},{112,80},{1... | collective-permute-start | bytes 589832 | tf_op jit(solution)/shard_map/ppermute | solution.py:115
  129.5 11.3 %collective-permute-start.21 = (f32[192,256]{1,0:T(8,128)S(1)}, f32[192,256]{1,0:T(8,128)S(1)}, u32[]{:S(2)}, u32[]{:S(2)}) collective-permute-start(f32[192,256]{1,0:T(8,128)S(1)} %constant_dynamic-update-slice_fusion.9), channel_id=1, source_target_pairs={{0,48},{16,32},{32,16},{48,0},{64,112},{80,96},{96,80},{112,64},{1... | collective-permute-start | bytes 589832 | tf_op jit(solution)/shard_map/ppermute | solution.py:115
  (11 other events, 26.5 us)

commit v7 on v6

--- a/solution.py
+++ b/solution.py
@@ -118,6 +118,43 @@
     return rows
 
 
+def reversed_channels(value, keep=None):
+    anti = anti_diagonal(value.shape[-1])
+    if keep is not None:
+        anti = anti[:, :keep]
+    return jnp.einsum("btc,cd->btd", value, anti, preferred_element_type=jnp.float32).astype(value.dtype)
+
+
+def folded_half(value, grad, dilation, offset):
+    channels = grad.shape[-1]
+    half = channels // 2
+    panel = grad.shape[1]
+    mirror = reversed_channels(value)
+    grad_left = grad[0, :, :half]
+    grad_mirror = reversed_channels(grad, half)[0]
+    blocks = []
+    for k in range(3):
+        own = lax.slice_in_dim(value, offset + k * dilation, offset + k * dilation + panel, axis=1)[0]
+        other = lax.slice_in_dim(mirror, offset + (2 - k) * dilation, offset + (2 - k) * dilation + panel, axis=1)[0]
+        blocks.append(
+            jnp.dot(grad_left.T, own, preferred_element_type=jnp.float32)
+            + jnp.dot(grad_mirror.T, other, preferred_element_type=jnp.float32)
+        )
+    return jnp.concatenate(blocks, axis=0)
+
+
+def unfolded_halves(first, second):
+    rows, channels = first.shape
+    half = rows // 3
+    total = butterfly_sum(jnp.concatenate([first, second], axis=0))
+    outs = []
+    for i in range(2):
+        part = total[i * rows : (i + 1) * rows]
+        taps = [part[k * half : (k + 1) * half].T for k in range(3)]
+        outs.append(jnp.stack([jnp.concatenate([taps[k], taps[2 - k][::-1, ::-1]], axis=1) for k in range(3)]))
+    return outs
+
+
 def folded_term(stacked, grad):
     channels = grad.shape[-1]
     term = jnp.dot(
@@ -238,11 +275,9 @@
     first_grad = back_one(hidden_gradient)[0].astype(jnp.bfloat16)
 
     second_grad_own = lax.slice_in_dim(second_grad_wide, two, two + panel, axis=1)
-    second_weight_gradient = folded_term(lax.slice_in_dim(second_stack, two, two + panel, axis=1), second_grad_own)
-    first_weight_gradient = folded_term(
-        lax.slice_in_dim(first_stack, reach_hidden, reach_hidden + panel, axis=1), first_grad
-    )
-    second_weight_gradient, first_weight_gradient = unfolded_sums(second_weight_gradient, first_weight_gradient)
+    second_weight_gradient = folded_half(hidden, second_grad_own, two, reach_hidden - two)
+    first_weight_gradient = folded_half(features, first_grad, one, reach_codes - one)
+    second_weight_gradient, first_weight_gradient = unfolded_halves(second_weight_gradient, first_weight_gradient)
     return (block_out, first_weight_gradient, second_weight_gradient)
 
 

time: 147 us -> 126 us (0.86)
  local copies, waits for them, and re-layouts: 34.8 us -> 19.1 us
  waiting for transfers between devices: 34.1 us -> 24.3 us
  starting transfers between devices: 47 us -> 55.7 us
  other arithmetic: 14.8 us -> 8.92 us
    ppermute x6, waiting for transfers between devices: 15.2 us -> 5.62 us  [butterfly_sum(): got = lax.ppermute(rows, axis, partner_pairs(axis, shift, offset))]
    rev x6, local copies, waits for them, and re-layouts: 9.65 us -> 1.12 us  [unfolded_halves(): taps[2 - k][::-1, ::-1]]
    dynamic_update_slice x6, local copies, waits for them, and re-layouts: 0.07 us -> 8.53 us  [butterfly_sum(): lax.dynamic_update_slice_in_dim(full, got, (place ^ offset) * width, 0)]
    ppermute x2, starting transfers between devices: 9.4 us -> 17.7 us  [neighbour_halo(): lax.ppermute(tail, 'seq', [(i, i + 1) for i in range(count - 1)])]
    unnamed x30 -> x11, local copies, waits for them, and re-layouts: 9.57 us -> 3.35 us
    ppermute x6, starting transfers between devices: 6.51 us -> 12 us  [butterfly_sum(): total = total + lax.ppermute(sent, axis, partner_pairs(axis, shift, offset))]
    reshape x4 -> x0, local copies, waits for them, and re-layouts: 3.92 us -> none  [the longest x1 1.87 us: unfolded_sums(): first.reshape(rows, lanes)]
    add x2 -> x0, other arithmetic: 3.8 us -> none  [folded_term(): return term[:half] + term[half:][::-1, ::-1]]
  transfers between devices with their start and end apart: 22 -> 22, of which waited for: 13 -> 12; matrix products, arithmetic and copies ran while one was open for 13% -> 18% of each run, Pallas kernels for 0% -> 0%
where the time goes in v7:
time: 126 us; the launch traced here: 125 us
  starting transfers between devices  55.7 us (44%)
  waiting for transfers between devices  24.3 us (19%)
  local copies, waits for them, and re-layouts  19.1 us (15%)
  matrix products  15.5 us (12%)
  other arithmetic  8.92 us (7%)
  between operations  1.28 us (1%)
    ppermute x2, starting transfers between devices, neighbour_halo(): lax.ppermute(tail, 'seq', [(i, i + 1) for i in range(count - 1)])  17.7 us
    ppermute x6, starting transfers between devices, butterfly_sum(): lax.ppermute(rows, axis, partner_pairs(axis, shift, offset))  14.3 us
    ppermute x6, starting transfers between devices, butterfly_sum(): total = total + lax.ppermute(sent, axis, partner_pairs(axis, shift, offset))  12 us
    ppermute x6, waiting for transfers between devices, butterfly_sum(): total = total + lax.ppermute(sent, axis, partner_pairs(axis, shift, offset))  11.6 us
    dynamic_update_slice x6, local copies, waits for them, and re-layouts, butterfly_sum(): lax.dynamic_update_slice_in_dim(full, got, (place ^ offset) * width, 0)  8.53 us
    ppermute x6, starting transfers between devices, butterfly_sum(): got = lax.ppermute(rows, axis, partner_pairs(axis, shift, offset))  7.88 us
    ppermute x6, waiting for transfers between devices, butterfly_sum(): lax.ppermute(rows, axis, partner_pairs(axis, shift, offset))  7.11 us
    dot_general x4, matrix products, product(): jnp.dot(stacked.reshape(-1, shape_in[-1]), matrix, preferred_element_type...  6.28 us
  transfers between devices with their start and end apart: 22, of which 12 were waited for; matrix products, arithmetic and copies ran while one was open for 18% of the time, Pallas kernels for 0%

profile of v7, /device:TPU:1, one launch (start us, length us, event | category | flops | bytes accessed | tf_op | source)
XLA Modules:
  0.0 124.9 jit_solution(18103521651426483791)
XLA Ops:
  1.4 10.2 %collective-permute-start = (s32[1,36]{1,0:T(1,128)S(1)}, s32[1,36]{1,0:T(1,128)S(1)}, u32[]{:S(2)}, u32[]{:S(2)}) collective-permute-start(s32[1,36]{1,0:T(1,128)S(1)} %get-tuple-element.31), channel_id=1, source_target_pairs={{0,1},{1,2},{2,3},{3,4},{4,5},{5,6},{6,7},{7,8},{8,9},{9,10},{10,1... | collective-permute-start | bytes 440 | tf_op jit(solution)/shard_map/ppermute | solution.py:199
  11.6 1.9 %collective-permute-start.1 = (s32[1,36]{1,0:T(1,128)S(1)}, s32[1,36]{1,0:T(1,128)S(1)}, u32[]{:S(2)}, u32[]{:S(2)}) collective-permute-start(s32[1,36]{1,0:T(1,128)S(1)} %get-tuple-element.30), channel_id=1, source_target_pairs={{1,0},{2,1},{3,2},{4,3},{5,4},{6,5},{7,6},{8,7},{9,8},{10,9},{11,1... | collective-permute-start | bytes 440 | tf_op jit(solution)/shard_map/ppermute | solution.py:200
  14.3 7.5 %collective-permute-start.2 = (bf16[1,16,256]{2,1,0:T(8,128)(2,1)S(1)}, bf16[1,16,256]{2,1,0:T(8,128)(2,1)S(1)}, u32[]{:S(2)}, u32[]{:S(2)}) collective-permute-start(bf16[1,16,256]{2,1,0:T(8,128)(2,1)S(1)} %get-tuple-element.16), channel_id=1, source_target_pairs={{0,1},{1,2},{2,3},{3,4},{4,5},{5,6},{6,7},{7,8},{8,9},{9,10},{10,1... | collective-permute-start | bytes 24584 | tf_op jit(solution)/shard_map/ppermute | solution.py:199
  21.8 1.9 %collective-permute-start.3 = (bf16[1,16,256]{2,1,0:T(8,128)(2,1)S(1)}, bf16[1,16,256]{2,1,0:T(8,128)(2,1)S(1)}, u32[]{:S(2)}, u32[]{:S(2)}) collective-permute-start(bf16[1,16,256]{2,1,0:T(8,128)(2,1)S(1)} %get-tuple-element.17), channel_id=1, source_target_pairs={{1,0},{2,1},{3,2},{4,3},{5,4},{6,5},{7,6},{8,7},{9,8},{10,9},{11,1... | collective-permute-start | bytes 24584 | tf_op jit(solution)/shard_map/ppermute | solution.py:200
  30.5 1.9 %convolution_bitcast_fusion.1 = f32[1,2112,512]{2,1,0:T(8,128)S(1)} fusion(bf16[1,2112,256]{2,1,0:T(8,128)(2,1)S(1)} %get-tuple-element.8, bf16[1,2112,256]{2,1,0:T(8,128)(2,1)S(1)} %get-tuple-element.9, bf16[1,2112,256]{2,1,0:T(8,128)(2,1)S(1)} %get-tuple-element.7, bf16[768,256]{1,0:T(8,128)(2,1)S(1)} %bitcast.161, bf16[768,256]{1,0:T(8,128)(2,1)S(1)} %bitcast.160), kind=kOutput, calls=%fused_computation.1 | convolution fusion | flops 1672249344 | bytes 8355840 | tf_op jit(solution)/shard_map/dot_general | solution.py:40
  35.0 1.9 %convolution_bitcast_fusion = f32[1,2080,512]{2,1,0:T(8,128)S(1)} fusion(bf16[1,2080,256]{2,1,0:T(8,128)(2,1)S(1)} %get-tuple-element.11, bf16[1,2080,256]{2,1,0:T(8,128)(2,1)S(1)} %get-tuple-element.12, bf16[1,2080,256]{2,1,0:T(8,128)(2,1)S(1)} %get-tuple-element.10, bf16[768,256]{1,0:T(8,128)(2,1)S(1)} %bitcast.152, bf16[768,256]{1,0:T(8,128)(2,1)S(1)} %bitcast.148), kind=kOutput, calls=%fused_computation | convolution fusion | flops 1646936064 | bytes 8241152 | tf_op jit(solution)/shard_map/dot_general | solution.py:40
  43.9 2.8 %fusion.39 = (bf16[1,2048,256]{2,1,0:T(8,128)(2,1)S(1)}, bf16[1,2048,256]{2,1,0:T(8,128)(2,1)}) fusion(f32[1,2048,512]{2,1,0:T(8,128)S(1)} %convolution_bitcast_fusion.2, f32[1,2112,256]{2,1,0:T(8,128)S(1)} %get-tuple-element.6, bf16[1,2048,256]{2,1,0:T(8,128)(2,1)S(1)} %copy-done.1, f32[1,2080,256]{2,1,0:T(8,128)S(1)} %add_multiply_fusion, ...), kind=kLoop, calls=%fused_computation.59 | loop fusion | flops 14155776 | bytes 14680064 | tf_op jit(solution)/shard_map/convert_element_type | solution.py:275
  52.1 2.4 %collective-permute-start.5 = (f32[192,256]{1,0:T(8,128)S(1)}, f32[192,256]{1,0:T(8,128)S(1)}, u32[]{:S(2)}, u32[]{:S(2)}) collective-permute-start(f32[192,256]{1,0:T(8,128)S(1)} %get-tuple-element.26), channel_id=1, source_target_pairs={{0,32},{16,48},{32,0},{48,16},{64,96},{80,112},{96,64},{112,80},{1... | collective-permute-start | bytes 589832 | tf_op jit(solution)/shard_map/ppermute | solution.py:99
  55.7 4.1 %collective-permute-done.5 = f32[192,256]{1,0:T(8,128)S(1)} collective-permute-done((f32[192,256]{1,0:T(8,128)S(1)}, f32[192,256]{1,0:T(8,128)S(1)}, u32[]{:S(2)}, u32[]{:S(2)}) %collective-permute-start.5) | collective-permute-done | bytes 196640 | tf_op jit(solution)/shard_map/ppermute | solution.py:99
  59.8 2.0 %collective-permute-done.6 = f32[192,256]{1,0:T(8,128)S(1)} collective-permute-done((f32[192,256]{1,0:T(8,128)S(1)}, f32[192,256]{1,0:T(8,128)S(1)}, u32[]{:S(2)}, u32[]{:S(2)}) %collective-permute-start.6) | collective-permute-done | bytes 196640 | tf_op jit(solution)/shard_map/ppermute | solution.py:99
  61.9 5.4 %collective-permute-start.7 = (f32[48,256]{1,0:T(8,128)S(1)}, f32[48,256]{1,0:T(8,128)S(1)}, u32[]{:S(2)}, u32[]{:S(2)}) collective-permute-start(f32[48,256]{1,0:T(8,128)S(1)} %get-tuple-element.27), channel_id=1, source_target_pairs={{0,4},{1,5},{2,6},{3,7},{4,0},{5,1},{6,2},{7,3},{8,12},{9,13},{10,... | collective-permute-start | bytes 147464 | tf_op jit(solution)/shard_map/ppermute | solution.py:99
  67.3 2.6 %collective-permute-start.8 = (f32[48,256]{1,0:T(8,128)S(1)}, f32[48,256]{1,0:T(8,128)S(1)}, u32[]{:S(2)}, u32[]{:S(2)}) collective-permute-start(f32[48,256]{1,0:T(8,128)S(1)} %get-tuple-element.29), channel_id=1, source_target_pairs={{0,8},{1,9},{2,10},{3,11},{4,12},{5,13},{6,14},{7,15},{8,0},{9,1},... | collective-permute-start | bytes 147464 | tf_op jit(solution)/shard_map/ppermute | solution.py:99
  70.0 2.0 %collective-permute-done.8 = f32[48,256]{1,0:T(8,128)S(1)} collective-permute-done((f32[48,256]{1,0:T(8,128)S(1)}, f32[48,256]{1,0:T(8,128)S(1)}, u32[]{:S(2)}, u32[]{:S(2)}) %collective-permute-start.8) | collective-permute-done | bytes 49184 | tf_op jit(solution)/shard_map/ppermute | solution.py:99
  72.0 2.5 %collective-permute-done.9 = f32[48,256]{1,0:T(8,128)S(1)} collective-permute-done((f32[48,256]{1,0:T(8,128)S(1)}, f32[48,256]{1,0:T(8,128)S(1)}, u32[]{:S(2)}, u32[]{:S(2)}) %collective-permute-start.9) | collective-permute-done | bytes 49184 | tf_op jit(solution)/shard_map/ppermute | solution.py:99
  75.0 3.1 %collective-permute-start.12 = (f32[48,256]{1,0:T(8,128)S(1)}, f32[48,256]{1,0:T(8,128)S(1)}, u32[]{:S(2)}, u32[]{:S(2)}) collective-permute-start(f32[48,256]{1,0:T(8,128)S(1)} %add_add_fusion.1), channel_id=1, source_target_pairs={{0,192},{16,208},{32,224},{48,240},{64,128},{80,144},{96,160},{112... | collective-permute-start | bytes 147464 | tf_op jit(solution)/shard_map/ppermute | solution.py:104
  80.3 5.0 %collective-permute-start.13 = (f32[48,256]{1,0:T(8,128)S(1)}, f32[48,256]{1,0:T(8,128)S(1)}, u32[]{:S(2)}, u32[]{:S(2)}) collective-permute-start(f32[48,256]{1,0:T(8,128)S(1)} %fusion.110), channel_id=1, source_target_pairs={{0,1},{1,0},{2,3},{3,2},{4,5},{5,4},{6,7},{7,6},{8,9},{9,8},{10,11... | collective-permute-start | bytes 147464 | tf_op jit(solution)/shard_map/ppermute | solution.py:104
  85.3 2.0 %collective-permute-start.14 = (f32[48,256]{1,0:T(8,128)S(1)}, f32[48,256]{1,0:T(8,128)S(1)}, u32[]{:S(2)}, u32[]{:S(2)}) collective-permute-start(f32[48,256]{1,0:T(8,128)S(1)} %fusion.110), channel_id=1, source_target_pairs={{0,2},{1,3},{2,0},{3,1},{4,6},{5,7},{6,4},{7,5},{8,10},{9,11},{10,... | collective-permute-start | bytes 147464 | tf_op jit(solution)/shard_map/ppermute | solution.py:104
  87.3 3.7 %collective-permute-start.15 = (f32[48,256]{1,0:T(8,128)S(1)}, f32[48,256]{1,0:T(8,128)S(1)}, u32[]{:S(2)}, u32[]{:S(2)}) collective-permute-start(f32[48,256]{1,0:T(8,128)S(1)} %fusion.110), channel_id=1, source_target_pairs={{0,3},{1,2},{2,1},{3,0},{4,7},{5,6},{6,5},{7,4},{8,11},{9,10},{10,... | collective-permute-start | bytes 147464 | tf_op jit(solution)/shard_map/ppermute | solution.py:104
  92.7 3.3 %collective-permute-done.15 = f32[48,256]{1,0:T(8,128)S(1)} collective-permute-done((f32[48,256]{1,0:T(8,128)S(1)}, f32[48,256]{1,0:T(8,128)S(1)}, u32[]{:S(2)}, u32[]{:S(2)}) %collective-permute-start.15) | collective-permute-done | bytes 49184 | tf_op jit(solution)/shard_map/ppermute | solution.py:104
  97.5 2.5 %collective-permute-start.18 = (f32[48,256]{1,0:T(8,128)S(1)}, f32[48,256]{1,0:T(8,128)S(1)}, u32[]{:S(2)}, u32[]{:S(2)}) collective-permute-start(f32[48,256]{1,0:T(8,128)S(1)} %add_bitcast_fusion), channel_id=1, source_target_pairs={{0,12},{1,13},{2,14},{3,15},{4,8},{5,9},{6,10},{7,11},{8,4},{9,5},... | collective-permute-start | bytes 147464 | tf_op jit(solution)/shard_map/ppermute | solution.py:115
  106.9 2.1 %collective-permute-start.21 = (f32[192,256]{0,1:T(8,128)S(1)}, f32[192,256]{0,1:T(8,128)S(1)}, u32[]{:S(2)}, u32[]{:S(2)}) collective-permute-start(f32[192,256]{0,1:T(8,128)S(1)} %dynamic_update_slice.27), channel_id=1, source_target_pairs={{0,48},{16,32},{32,16},{48,0},{64,112},{80,96},{96,80},{112,64},{1... | collective-permute-start | bytes 589832 | tf_op jit(solution)/shard_map/ppermute | solution.py:115
  109.1 1.9 %dynamic_update_slice.28 = f32[768,256]{0,1:T(8,128)S(1)} dynamic-update-slice(f32[768,256]{0,1:T(8,128)S(1)} %broadcast_in_dim.28, f32[192,256]{0,1:T(8,128)S(1)} %dynamic_update_slice.27, s32[]{:T(128)S(6)} %select_n.70, s32[]{:T(128)} %constant.26.clone.1) | dynamic-update-slice | bytes 393220 | tf_op jit(solution)/shard_map/dynamic_update_slice | solution.py:113
  112.9 2.2 %dynamic_update_slice.29 = f32[768,256]{0,1:T(8,128)S(1)} dynamic-update-slice(f32[768,256]{0,1:T(8,128)S(1)} %dynamic_update_slice.28, f32[192,256]{0,1:T(8,128)S(1)} %collective-permute-done.19, s32[]{:T(128)S(6)} %select_n.71, s32[]{:T(128)} %constant.26.clone.1) | dynamic-update-slice | bytes 393220 | tf_op jit(solution)/shard_map/dynamic_update_slice | solution.py:116
  115.1 3.0 %collective-permute-done.20 = f32[192,256]{0,1:T(8,128)S(1)} collective-permute-done((f32[192,256]{0,1:T(8,128)S(1)}, f32[192,256]{0,1:T(8,128)S(1)}, u32[]{:S(2)}, u32[]{:S(2)}) %collective-permute-start.20) | collective-permute-done | bytes 196640 | tf_op jit(solution)/shard_map/ppermute | solution.py:115
  (106 shorter events, 45.5 us)
Async XLA Ops:
  0.6 27.7 %copy-start = (bf16[4,256]{1,0:T(4,128)(2,1)S(1)}, bf16[4,256]{1,0:T(4,128)(2,1)}, u32[]{:S(2)}) copy-start(bf16[4,256]{1,0:T(4,128)(2,1)} %param.6) | copy-start | bytes 6148
  0.6 27.5 %copy-start.3 = (s32[1,2048]{1,0:T(1,128)S(1)}, s32[1,2048]{1,0:T(1,128)}, u32[]{:S(2)}) copy-start(s32[1,2048]{1,0:T(1,128)} %param.5) | copy-start | bytes 24580
  1.4 26.7 %collective-permute-start = (s32[1,36]{1,0:T(1,128)S(1)}, s32[1,36]{1,0:T(1,128)S(1)}, u32[]{:S(2)}, u32[]{:S(2)}) collective-permute-start(s32[1,36]{1,0:T(1,128)S(1)} %get-tuple-element.31), channel_id=1, source_target_pairs={{0,1},{1,2},{2,3},{3,4},{4,5},{5,6},{6,7},{7,8},{8,9},{9,10},{10,1... | collective-permute-start | bytes 440 | tf_op jit(solution)/shard_map/ppermute | solution.py:199
  11.6 16.5 %collective-permute-start.1 = (s32[1,36]{1,0:T(1,128)S(1)}, s32[1,36]{1,0:T(1,128)S(1)}, u32[]{:S(2)}, u32[]{:S(2)}) collective-permute-start(s32[1,36]{1,0:T(1,128)S(1)} %get-tuple-element.30), channel_id=1, source_target_pairs={{1,0},{2,1},{3,2},{4,3},{5,4},{6,5},{7,6},{8,7},{9,8},{10,9},{11,1... | collective-permute-start | bytes 440 | tf_op jit(solution)/shard_map/ppermute | solution.py:200
  14.3 23.1 %collective-permute-start.2 = (bf16[1,16,256]{2,1,0:T(8,128)(2,1)S(1)}, bf16[1,16,256]{2,1,0:T(8,128)(2,1)S(1)}, u32[]{:S(2)}, u32[]{:S(2)}) collective-permute-start(bf16[1,16,256]{2,1,0:T(8,128)(2,1)S(1)} %get-tuple-element.16), channel_id=1, source_target_pairs={{0,1},{1,2},{2,3},{3,4},{4,5},{5,6},{6,7},{7,8},{8,9},{9,10},{10,1... | collective-permute-start | bytes 24584 | tf_op jit(solution)/shard_map/ppermute | solution.py:199
  21.8 15.6 %collective-permute-start.3 = (bf16[1,16,256]{2,1,0:T(8,128)(2,1)S(1)}, bf16[1,16,256]{2,1,0:T(8,128)(2,1)S(1)}, u32[]{:S(2)}, u32[]{:S(2)}) collective-permute-start(bf16[1,16,256]{2,1,0:T(8,128)(2,1)S(1)} %get-tuple-element.17), channel_id=1, source_target_pairs={{1,0},{2,1},{3,2},{4,3},{5,4},{6,5},{7,6},{8,7},{9,8},{10,9},{11,1... | collective-permute-start | bytes 24584 | tf_op jit(solution)/shard_map/ppermute | solution.py:200
  50.8 4.9 %collective-permute-start.4 = (f32[192,256]{1,0:T(8,128)S(1)}, f32[192,256]{1,0:T(8,128)S(1)}, u32[]{:S(2)}, u32[]{:S(2)}) collective-permute-start(f32[192,256]{1,0:T(8,128)S(1)} %get-tuple-element.24), channel_id=1, source_target_pairs={{0,16},{16,0},{32,48},{48,32},{64,80},{80,64},{96,112},{112,96},{1... | collective-permute-start | bytes 589832 | tf_op jit(solution)/shard_map/ppermute | solution.py:99
  52.1 7.7 %collective-permute-start.5 = (f32[192,256]{1,0:T(8,128)S(1)}, f32[192,256]{1,0:T(8,128)S(1)}, u32[]{:S(2)}, u32[]{:S(2)}) collective-permute-start(f32[192,256]{1,0:T(8,128)S(1)} %get-tuple-element.26), channel_id=1, source_target_pairs={{0,32},{16,48},{32,0},{48,16},{64,96},{80,112},{96,64},{112,80},{1... | collective-permute-start | bytes 589832 | tf_op jit(solution)/shard_map/ppermute | solution.py:99
  54.6 7.3 %collective-permute-start.6 = (f32[192,256]{1,0:T(8,128)S(1)}, f32[192,256]{1,0:T(8,128)S(1)}, u32[]{:S(2)}, u32[]{:S(2)}) collective-permute-start(f32[192,256]{1,0:T(8,128)S(1)} %get-tuple-element.25), channel_id=1, source_target_pairs={{0,48},{16,32},{32,16},{48,0},{64,112},{80,96},{96,80},{112,64},{1... | collective-permute-start | bytes 589832 | tf_op jit(solution)/shard_map/ppermute | solution.py:99
  61.9 8.1 %collective-permute-start.7 = (f32[48,256]{1,0:T(8,128)S(1)}, f32[48,256]{1,0:T(8,128)S(1)}, u32[]{:S(2)}, u32[]{:S(2)}) collective-permute-start(f32[48,256]{1,0:T(8,128)S(1)} %get-tuple-element.27), channel_id=1, source_target_pairs={{0,4},{1,5},{2,6},{3,7},{4,0},{5,1},{6,2},{7,3},{8,12},{9,13},{10,... | collective-permute-start | bytes 147464 | tf_op jit(solution)/shard_map/ppermute | solution.py:99
  67.3 4.6 %collective-permute-start.8 = (f32[48,256]{1,0:T(8,128)S(1)}, f32[48,256]{1,0:T(8,128)S(1)}, u32[]{:S(2)}, u32[]{:S(2)}) collective-permute-start(f32[48,256]{1,0:T(8,128)S(1)} %get-tuple-element.29), channel_id=1, source_target_pairs={{0,8},{1,9},{2,10},{3,11},{4,12},{5,13},{6,14},{7,15},{8,0},{9,1},... | collective-permute-start | bytes 147464 | tf_op jit(solution)/shard_map/ppermute | solution.py:99
  70.0 4.5 %collective-permute-start.9 = (f32[48,256]{1,0:T(8,128)S(1)}, f32[48,256]{1,0:T(8,128)S(1)}, u32[]{:S(2)}, u32[]{:S(2)}) collective-permute-start(f32[48,256]{1,0:T(8,128)S(1)} %get-tuple-element.28), channel_id=1, source_target_pairs={{0,12},{1,13},{2,14},{3,15},{4,8},{5,9},{6,10},{7,11},{8,4},{9,5},... | collective-permute-start | bytes 147464 | tf_op jit(solution)/shard_map/ppermute | solution.py:99
  74.5 3.6 %collective-permute-start.10 = (f32[48,256]{1,0:T(8,128)S(1)}, f32[48,256]{1,0:T(8,128)S(1)}, u32[]{:S(2)}, u32[]{:S(2)}) collective-permute-start(f32[48,256]{1,0:T(8,128)S(1)} %add_add_fusion.1), channel_id=1, source_target_pairs={{0,64},{16,80},{32,96},{48,112},{64,0},{80,16},{96,32},{112,48},{1... | collective-permute-start | bytes 147464 | tf_op jit(solution)/shard_map/ppermute | solution.py:104
  75.0 3.8 %collective-permute-start.11 = (f32[48,256]{1,0:T(8,128)S(1)}, f32[48,256]{1,0:T(8,128)S(1)}, u32[]{:S(2)}, u32[]{:S(2)}) collective-permute-start(f32[48,256]{1,0:T(8,128)S(1)} %add_add_fusion.1), channel_id=1, source_target_pairs={{0,128},{16,144},{32,160},{48,176},{64,192},{80,208},{96,224},{112... | collective-permute-start | bytes 147464 | tf_op jit(solution)/shard_map/ppermute | solution.py:104
  75.0 5.2 %collective-permute-start.12 = (f32[48,256]{1,0:T(8,128)S(1)}, f32[48,256]{1,0:T(8,128)S(1)}, u32[]{:S(2)}, u32[]{:S(2)}) collective-permute-start(f32[48,256]{1,0:T(8,128)S(1)} %add_add_fusion.1), channel_id=1, source_target_pairs={{0,192},{16,208},{32,224},{48,240},{64,128},{80,144},{96,160},{112... | collective-permute-start | bytes 147464 | tf_op jit(solution)/shard_map/ppermute | solution.py:104
  80.3 10.7 %collective-permute-start.13 = (f32[48,256]{1,0:T(8,128)S(1)}, f32[48,256]{1,0:T(8,128)S(1)}, u32[]{:S(2)}, u32[]{:S(2)}) collective-permute-start(f32[48,256]{1,0:T(8,128)S(1)} %fusion.110), channel_id=1, source_target_pairs={{0,1},{1,0},{2,3},{3,2},{4,5},{5,4},{6,7},{7,6},{8,9},{9,8},{10,11... | collective-permute-start | bytes 147464 | tf_op jit(solution)/shard_map/ppermute | solution.py:104
  85.3 7.4 %collective-permute-start.14 = (f32[48,256]{1,0:T(8,128)S(1)}, f32[48,256]{1,0:T(8,128)S(1)}, u32[]{:S(2)}, u32[]{:S(2)}) collective-permute-start(f32[48,256]{1,0:T(8,128)S(1)} %fusion.110), channel_id=1, source_target_pairs={{0,2},{1,3},{2,0},{3,1},{4,6},{5,7},{6,4},{7,5},{8,10},{9,11},{10,... | collective-permute-start | bytes 147464 | tf_op jit(solution)/shard_map/ppermute | solution.py:104
  87.3 8.7 %collective-permute-start.15 = (f32[48,256]{1,0:T(8,128)S(1)}, f32[48,256]{1,0:T(8,128)S(1)}, u32[]{:S(2)}, u32[]{:S(2)}) collective-permute-start(f32[48,256]{1,0:T(8,128)S(1)} %fusion.110), channel_id=1, source_target_pairs={{0,3},{1,2},{2,1},{3,0},{4,7},{5,6},{6,5},{7,4},{8,11},{9,10},{10,... | collective-permute-start | bytes 147464 | tf_op jit(solution)/shard_map/ppermute | solution.py:104
  96.0 5.2 %collective-permute-start.16 = (f32[48,256]{1,0:T(8,128)S(1)}, f32[48,256]{1,0:T(8,128)S(1)}, u32[]{:S(2)}, u32[]{:S(2)}) collective-permute-start(f32[48,256]{1,0:T(8,128)S(1)} %add_bitcast_fusion), channel_id=1, source_target_pairs={{0,4},{1,5},{2,6},{3,7},{4,0},{5,1},{6,2},{7,3},{8,12},{9,13},{10,... | collective-permute-start | bytes 147464 | tf_op jit(solution)/shard_map/ppermute | solution.py:115
  96.1 6.5 %collective-permute-start.17 = (f32[48,256]{1,0:T(8,128)S(1)}, f32[48,256]{1,0:T(8,128)S(1)}, u32[]{:S(2)}, u32[]{:S(2)}) collective-permute-start(f32[48,256]{1,0:T(8,128)S(1)} %add_bitcast_fusion), channel_id=1, source_target_pairs={{0,8},{1,9},{2,10},{3,11},{4,12},{5,13},{6,14},{7,15},{8,0},{9,1},... | collective-permute-start | bytes 147464 | tf_op jit(solution)/shard_map/ppermute | solution.py:115
  97.5 6.6 %collective-permute-start.18 = (f32[48,256]{1,0:T(8,128)S(1)}, f32[48,256]{1,0:T(8,128)S(1)}, u32[]{:S(2)}, u32[]{:S(2)}) collective-permute-start(f32[48,256]{1,0:T(8,128)S(1)} %add_bitcast_fusion), channel_id=1, source_target_pairs={{0,12},{1,13},{2,14},{3,15},{4,8},{5,9},{6,10},{7,11},{8,4},{9,5},... | collective-permute-start | bytes 147464 | tf_op jit(solution)/shard_map/ppermute | solution.py:115
  105.1 7.8 %collective-permute-start.19 = (f32[192,256]{0,1:T(8,128)S(1)}, f32[192,256]{0,1:T(8,128)S(1)}, u32[]{:S(2)}, u32[]{:S(2)}) collective-permute-start(f32[192,256]{0,1:T(8,128)S(1)} %dynamic_update_slice.27), channel_id=1, source_target_pairs={{0,16},{16,0},{32,48},{48,32},{64,80},{80,64},{96,112},{112,96},{1... | collective-permute-start | bytes 589832 | tf_op jit(solution)/shard_map/ppermute | solution.py:115
  105.2 12.9 %collective-permute-start.20 = (f32[192,256]{0,1:T(8,128)S(1)}, f32[192,256]{0,1:T(8,128)S(1)}, u32[]{:S(2)}, u32[]{:S(2)}) collective-permute-start(f32[192,256]{0,1:T(8,128)S(1)} %dynamic_update_slice.27), channel_id=1, source_target_pairs={{0,32},{16,48},{32,0},{48,16},{64,96},{80,112},{96,64},{112,80},{1... | collective-permute-start | bytes 589832 | tf_op jit(solution)/shard_map/ppermute | solution.py:115
  106.9 13.4 %collective-permute-start.21 = (f32[192,256]{0,1:T(8,128)S(1)}, f32[192,256]{0,1:T(8,128)S(1)}, u32[]{:S(2)}, u32[]{:S(2)}) collective-permute-start(f32[192,256]{0,1:T(8,128)S(1)} %dynamic_update_slice.27), channel_id=1, source_target_pairs={{0,48},{16,32},{32,16},{48,0},{64,112},{80,96},{96,80},{112,64},{1... | collective-permute-start | bytes 589832 | tf_op jit(solution)/shard_map/ppermute | solution.py:115
  (3 other events, 3.2 us)

commit v8 on v7

--- a/solution.py
+++ b/solution.py
@@ -236,8 +236,21 @@
     panel = codes.shape[1]
     reach_hidden = 2 * two
     reach_codes = reach_hidden + one
-    code_left, code_right = neighbour_halo(codes, reach_codes, 1)
-    cot_left, cot_right = neighbour_halo(cotangent, two, 1)
+    channels = cotangent.shape[2]
+    codes_row = codes.astype(cotangent.dtype)
+    head = jnp.concatenate(
+        [cotangent[:, :two], jnp.pad(codes_row[:, :reach_codes], ((0, 0), (0, channels - reach_codes)))[:, None]], axis=1
+    )
+    tail = jnp.concatenate(
+        [cotangent[:, panel - two :], jnp.pad(codes_row[:, panel - reach_codes :], ((0, 0), (0, channels - reach_codes)))[:, None]],
+        axis=1,
+    )
+    count = lax.axis_size("seq")
+    from_left = lax.ppermute(tail, "seq", [(i, i + 1) for i in range(count - 1)])
+    from_right = lax.ppermute(head, "seq", [(i + 1, i) for i in range(count - 1)])
+    cot_left, cot_right = from_left[:, :two], from_right[:, :two]
+    code_left = from_left[:, two, :reach_codes].astype(jnp.int32)
+    code_right = from_right[:, two, :reach_codes].astype(jnp.int32)
     codes_wide = jnp.concatenate([code_left, codes, code_right], axis=1)
     cot_wide = jnp.concatenate([cot_left, cotangent, cot_right], axis=1)
 

time: 126 us -> 118 us (0.937)
  starting transfers between devices: 55.7 us -> 43.8 us
  waiting for transfers between devices: 24.3 us -> 30 us
  local copies, waits for them, and re-layouts: 19.1 us -> 16 us
  other arithmetic: 8.92 us -> 10.3 us
    ppermute x4 -> x2, starting transfers between devices: 21.6 us -> 12.1 us  [the longest x1 10.2 us: local(): lax.ppermute(tail, 'seq', [(i, i + 1) for i in range(count - 1)])]
    ppermute x4 -> x2, waiting for transfers between devices: 0.01 us -> 3.55 us  [the longest x1 3.55 us: local(): lax.ppermute(head, 'seq', [(i + 1, i) for i in range(count - 1)])]
    ppermute x6, starting transfers between devices: 12 us -> 9.21 us  [butterfly_sum(): total = total + lax.ppermute(sent, axis, partner_pairs(axis, shift, offset))]
    unnamed x11, local copies, waits for them, and re-layouts: 3.35 us -> 0.84 us
    ppermute x6, waiting for transfers between devices: 7.11 us -> 9.21 us  [butterfly_sum(): lax.ppermute(rows, axis, partner_pairs(axis, shift, offset))]
  transfers between devices with their start and end apart: 22 -> 20, of which waited for: 12 -> 13; matrix products, arithmetic and copies ran while one was open for 18% -> 12% of each run, Pallas kernels for 0% -> 0%
where the time goes in v8:
time: 118 us; the launch traced here: 117 us
  starting transfers between devices  43.8 us (37%)
  waiting for transfers between devices  30 us (25%)
  local copies, waits for them, and re-layouts  16 us (14%)
  matrix products  15.5 us (13%)
  other arithmetic  10.3 us (9%)
  between operations  1.28 us (1%)
    ppermute x6, starting transfers between devices, butterfly_sum(): lax.ppermute(rows, axis, partner_pairs(axis, shift, offset))  14.6 us
    ppermute x6, waiting for transfers between devices, butterfly_sum(): total = total + lax.ppermute(sent, axis, partner_pairs(axis, shift, offset))  11.9 us
    ppermute x1, starting transfers between devices, local(): lax.ppermute(tail, 'seq', [(i, i + 1) for i in range(count - 1)])  10.2 us
    ppermute x6, starting transfers between devices, butterfly_sum(): total = total + lax.ppermute(sent, axis, partner_pairs(axis, shift, offset))  9.21 us
    ppermute x6, waiting for transfers between devices, butterfly_sum(): lax.ppermute(rows, axis, partner_pairs(axis, shift, offset))  9.21 us
    dynamic_update_slice x6, local copies, waits for them, and re-layouts, butterfly_sum(): lax.dynamic_update_slice_in_dim(full, got, (place ^ offset) * width, 0)  8.53 us
    ppermute x6, starting transfers between devices, butterfly_sum(): got = lax.ppermute(rows, axis, partner_pairs(axis, shift, offset))  7.88 us
    dot_general x4, matrix products, product(): jnp.dot(stacked.reshape(-1, shape_in[-1]), matrix, preferred_element_type...  6.19 us
  transfers between devices with their start and end apart: 20, of which 13 were waited for; matrix products, arithmetic and copies ran while one was open for 12% of the time, Pallas kernels for 0%

profile of v8, /device:TPU:1, one launch (start us, length us, event | category | flops | bytes accessed | tf_op | source)
XLA Modules:
  0.0 116.8 jit_solution(3684161447310028010)
XLA Ops:
  2.2 10.2 %collective-permute-start = (bf16[1,17,256]{2,1,0:T(8,128)(2,1)S(1)}, bf16[1,17,256]{2,1,0:T(8,128)(2,1)S(1)}, u32[]{:S(2)}, u32[]{:S(2)}) collective-permute-start(bf16[1,17,256]{2,1,0:T(8,128)(2,1)S(1)} %pad_maximum_fusion.4), channel_id=1, source_target_pairs={{0,1},{1,2},{2,3},{3,4},{4,5},{5,6},{6,7},{7,8},{8,9},{9,10},{10,1... | collective-permute-start | bytes 26120 | tf_op jit(solution)/shard_map/ppermute | solution.py:249
  13.1 1.9 %collective-permute-start.1 = (bf16[1,17,256]{2,1,0:T(8,128)(2,1)S(1)}, bf16[1,17,256]{2,1,0:T(8,128)(2,1)S(1)}, u32[]{:S(2)}, u32[]{:S(2)}) collective-permute-start(bf16[1,17,256]{2,1,0:T(8,128)(2,1)S(1)} %pad_maximum_fusion.5), channel_id=1, source_target_pairs={{1,0},{2,1},{3,2},{4,3},{5,4},{6,5},{7,6},{8,7},{9,8},{10,9},{11,1... | collective-permute-start | bytes 26120 | tf_op jit(solution)/shard_map/ppermute | solution.py:250
  18.5 3.5 %collective-permute-done.1 = bf16[1,17,256]{2,1,0:T(8,128)(2,1)S(1)} collective-permute-done((bf16[1,17,256]{2,1,0:T(8,128)(2,1)S(1)}, bf16[1,17,256]{2,1,0:T(8,128)(2,1)S(1)}, u32[]{:S(2)}, u32[]{:S(2)}) %collective-permute-start.1) | collective-permute-done | bytes 8736 | tf_op jit(solution)/shard_map/ppermute | solution.py:250
  23.9 1.8 %convolution_bitcast_fusion.1 = f32[1,2112,512]{2,1,0:T(8,128)S(1)} fusion(bf16[1,2112,256]{2,1,0:T(8,128)(2,1)S(1)} %get-tuple-element.8, bf16[1,2112,256]{2,1,0:T(8,128)(2,1)S(1)} %get-tuple-element.9, bf16[1,2112,256]{2,1,0:T(8,128)(2,1)S(1)} %get-tuple-element.7, bf16[768,256]{1,0:T(8,128)(2,1)S(1)} %bitcast.175, bf16[768,256]{1,0:T(8,128)(2,1)S(1)} %bitcast.174), kind=kOutput, calls=%fused_computation.1 | convolution fusion | flops 1672249344 | bytes 8355840 | tf_op jit(solution)/shard_map/dot_general | solution.py:40
  28.0 1.9 %convolution_bitcast_fusion = f32[1,2080,512]{2,1,0:T(8,128)S(1)} fusion(bf16[1,2080,256]{2,1,0:T(8,128)(2,1)S(1)} %get-tuple-element.11, bf16[1,2080,256]{2,1,0:T(8,128)(2,1)S(1)} %get-tuple-element.12, bf16[1,2080,256]{2,1,0:T(8,128)(2,1)S(1)} %get-tuple-element.10, bf16[768,256]{1,0:T(8,128)(2,1)S(1)} %bitcast.165, bf16[768,256]{1,0:T(8,128)(2,1)S(1)} %bitcast.162), kind=kOutput, calls=%fused_computation | convolution fusion | flops 1646936064 | bytes 8241152 | tf_op jit(solution)/shard_map/dot_general | solution.py:40
  35.8 2.8 %fusion.39 = (bf16[1,2048,256]{2,1,0:T(8,128)(2,1)S(1)}, bf16[1,2048,256]{2,1,0:T(8,128)(2,1)}) fusion(f32[1,2048,512]{2,1,0:T(8,128)S(1)} %convolution_bitcast_fusion.2, f32[1,2112,256]{2,1,0:T(8,128)S(1)} %get-tuple-element.6, bf16[1,2048,256]{2,1,0:T(8,128)(2,1)S(1)} %copy-done.1, f32[1,2080,256]{2,1,0:T(8,128)S(1)} %add_multiply_fusion, ...), kind=kLoop, calls=%fused_computation.59 | loop fusion | flops 14155776 | bytes 14680064 | tf_op jit(solution)/shard_map/convert_element_type | solution.py:288
  44.3 2.5 %collective-permute-start.3 = (f32[192,256]{1,0:T(8,128)S(1)}, f32[192,256]{1,0:T(8,128)S(1)}, u32[]{:S(2)}, u32[]{:S(2)}) collective-permute-start(f32[192,256]{1,0:T(8,128)S(1)} %get-tuple-element.26), channel_id=1, source_target_pairs={{0,32},{16,48},{32,0},{48,16},{64,96},{80,112},{96,64},{112,80},{1... | collective-permute-start | bytes 589832 | tf_op jit(solution)/shard_map/ppermute | solution.py:99
  48.0 4.1 %collective-permute-done.3 = f32[192,256]{1,0:T(8,128)S(1)} collective-permute-done((f32[192,256]{1,0:T(8,128)S(1)}, f32[192,256]{1,0:T(8,128)S(1)}, u32[]{:S(2)}, u32[]{:S(2)}) %collective-permute-start.3) | collective-permute-done | bytes 196640 | tf_op jit(solution)/shard_map/ppermute | solution.py:99
  52.1 2.0 %collective-permute-done.4 = f32[192,256]{1,0:T(8,128)S(1)} collective-permute-done((f32[192,256]{1,0:T(8,128)S(1)}, f32[192,256]{1,0:T(8,128)S(1)}, u32[]{:S(2)}, u32[]{:S(2)}) %collective-permute-start.4) | collective-permute-done | bytes 196640 | tf_op jit(solution)/shard_map/ppermute | solution.py:99
  54.1 2.3 %collective-permute-start.5 = (f32[48,256]{1,0:T(8,128)S(1)}, f32[48,256]{1,0:T(8,128)S(1)}, u32[]{:S(2)}, u32[]{:S(2)}) collective-permute-start(f32[48,256]{1,0:T(8,128)S(1)} %get-tuple-element.27), channel_id=1, source_target_pairs={{0,4},{1,5},{2,6},{3,7},{4,0},{5,1},{6,2},{7,3},{8,12},{9,13},{10,... | collective-permute-start | bytes 147464 | tf_op jit(solution)/shard_map/ppermute | solution.py:99
  56.4 2.9 %collective-permute-start.6 = (f32[48,256]{1,0:T(8,128)S(1)}, f32[48,256]{1,0:T(8,128)S(1)}, u32[]{:S(2)}, u32[]{:S(2)}) collective-permute-start(f32[48,256]{1,0:T(8,128)S(1)} %get-tuple-element.29), channel_id=1, source_target_pairs={{0,8},{1,9},{2,10},{3,11},{4,12},{5,13},{6,14},{7,15},{8,0},{9,1},... | collective-permute-start | bytes 147464 | tf_op jit(solution)/shard_map/ppermute | solution.py:99
  59.4 2.6 %collective-permute-done.6 = f32[48,256]{1,0:T(8,128)S(1)} collective-permute-done((f32[48,256]{1,0:T(8,128)S(1)}, f32[48,256]{1,0:T(8,128)S(1)}, u32[]{:S(2)}, u32[]{:S(2)}) %collective-permute-start.6) | collective-permute-done | bytes 49184 | tf_op jit(solution)/shard_map/ppermute | solution.py:99
  62.0 2.3 %collective-permute-done.7 = f32[48,256]{1,0:T(8,128)S(1)} collective-permute-done((f32[48,256]{1,0:T(8,128)S(1)}, f32[48,256]{1,0:T(8,128)S(1)}, u32[]{:S(2)}, u32[]{:S(2)}) %collective-permute-start.7) | collective-permute-done | bytes 49184 | tf_op jit(solution)/shard_map/ppermute | solution.py:99
  65.3 4.0 %collective-permute-start.9 = (f32[48,256]{1,0:T(8,128)S(1)}, f32[48,256]{1,0:T(8,128)S(1)}, u32[]{:S(2)}, u32[]{:S(2)}) collective-permute-start(f32[48,256]{1,0:T(8,128)S(1)} %add_add_fusion.1), channel_id=1, source_target_pairs={{0,128},{16,144},{32,160},{48,176},{64,192},{80,208},{96,224},{112... | collective-permute-start | bytes 147464 | tf_op jit(solution)/shard_map/ppermute | solution.py:104
  69.3 2.0 %collective-permute-done.9 = f32[48,256]{1,0:T(8,128)S(1)} collective-permute-done((f32[48,256]{1,0:T(8,128)S(1)}, f32[48,256]{1,0:T(8,128)S(1)}, u32[]{:S(2)}, u32[]{:S(2)}) %collective-permute-start.9) | collective-permute-done | bytes 49184 | tf_op jit(solution)/shard_map/ppermute | solution.py:104
  71.3 2.7 %collective-permute-done.10 = f32[48,256]{1,0:T(8,128)S(1)} collective-permute-done((f32[48,256]{1,0:T(8,128)S(1)}, f32[48,256]{1,0:T(8,128)S(1)}, u32[]{:S(2)}, u32[]{:S(2)}) %collective-permute-start.10) | collective-permute-done | bytes 49184 | tf_op jit(solution)/shard_map/ppermute | solution.py:104
  74.1 3.9 %collective-permute-start.11 = (f32[48,256]{1,0:T(8,128)S(1)}, f32[48,256]{1,0:T(8,128)S(1)}, u32[]{:S(2)}, u32[]{:S(2)}) collective-permute-start(f32[48,256]{1,0:T(8,128)S(1)} %fusion.112), channel_id=1, source_target_pairs={{0,1},{1,0},{2,3},{3,2},{4,5},{5,4},{6,7},{7,6},{8,9},{9,8},{10,11... | collective-permute-start | bytes 147464 | tf_op jit(solution)/shard_map/ppermute | solution.py:104
  79.7 3.9 %collective-permute-start.13 = (f32[48,256]{1,0:T(8,128)S(1)}, f32[48,256]{1,0:T(8,128)S(1)}, u32[]{:S(2)}, u32[]{:S(2)}) collective-permute-start(f32[48,256]{1,0:T(8,128)S(1)} %fusion.112), channel_id=1, source_target_pairs={{0,3},{1,2},{2,1},{3,0},{4,7},{5,6},{6,5},{7,4},{8,11},{9,10},{10,... | collective-permute-start | bytes 147464 | tf_op jit(solution)/shard_map/ppermute | solution.py:104
  84.8 3.3 %collective-permute-done.13 = f32[48,256]{1,0:T(8,128)S(1)} collective-permute-done((f32[48,256]{1,0:T(8,128)S(1)}, f32[48,256]{1,0:T(8,128)S(1)}, u32[]{:S(2)}, u32[]{:S(2)}) %collective-permute-start.13) | collective-permute-done | bytes 49184 | tf_op jit(solution)/shard_map/ppermute | solution.py:104
  90.1 2.0 %collective-permute-start.16 = (f32[48,256]{1,0:T(8,128)S(1)}, f32[48,256]{1,0:T(8,128)S(1)}, u32[]{:S(2)}, u32[]{:S(2)}) collective-permute-start(f32[48,256]{1,0:T(8,128)S(1)} %add_bitcast_fusion), channel_id=1, source_target_pairs={{0,12},{1,13},{2,14},{3,15},{4,8},{5,9},{6,10},{7,11},{8,4},{9,5},... | collective-permute-start | bytes 147464 | tf_op jit(solution)/shard_map/ppermute | solution.py:115
  98.8 2.4 %collective-permute-start.19 = (f32[192,256]{0,1:T(8,128)S(1)}, f32[192,256]{0,1:T(8,128)S(1)}, u32[]{:S(2)}, u32[]{:S(2)}) collective-permute-start(f32[192,256]{0,1:T(8,128)S(1)} %dynamic_update_slice.27), channel_id=1, source_target_pairs={{0,48},{16,32},{32,16},{48,0},{64,112},{80,96},{96,80},{112,64},{1... | collective-permute-start | bytes 589832 | tf_op jit(solution)/shard_map/ppermute | solution.py:115
  101.2 1.9 %dynamic_update_slice.28 = f32[768,256]{0,1:T(8,128)S(1)} dynamic-update-slice(f32[768,256]{0,1:T(8,128)S(1)} %broadcast_in_dim.56, f32[192,256]{0,1:T(8,128)S(1)} %dynamic_update_slice.27, s32[]{:T(128)S(6)} %select_n.70, s32[]{:T(128)} %constant.27.clone.1) | dynamic-update-slice | bytes 393220 | tf_op jit(solution)/shard_map/dynamic_update_slice | solution.py:113
  103.9 2.2 %dynamic_update_slice.29 = f32[768,256]{0,1:T(8,128)S(1)} dynamic-update-slice(f32[768,256]{0,1:T(8,128)S(1)} %dynamic_update_slice.28, f32[192,256]{0,1:T(8,128)S(1)} %collective-permute-done.17, s32[]{:T(128)S(6)} %select_n.71, s32[]{:T(128)} %constant.27.clone.1) | dynamic-update-slice | bytes 393220 | tf_op jit(solution)/shard_map/dynamic_update_slice | solution.py:116
  106.1 3.5 %collective-permute-done.18 = f32[192,256]{0,1:T(8,128)S(1)} collective-permute-done((f32[192,256]{0,1:T(8,128)S(1)}, f32[192,256]{0,1:T(8,128)S(1)}, u32[]{:S(2)}, u32[]{:S(2)}) %collective-permute-start.18) | collective-permute-done | bytes 196640 | tf_op jit(solution)/shard_map/ppermute | solution.py:115
  (111 shorter events, 43.0 us)
Async XLA Ops:
  0.6 21.6 %copy-start = (bf16[4,256]{1,0:T(4,128)(2,1)S(1)}, bf16[4,256]{1,0:T(4,128)(2,1)}, u32[]{:S(2)}) copy-start(bf16[4,256]{1,0:T(4,128)(2,1)} %param.6) | copy-start | bytes 6148
  0.6 21.4 %copy-start.3 = (s32[1,2048]{1,0:T(1,128)S(1)}, s32[1,2048]{1,0:T(1,128)}, u32[]{:S(2)}) copy-start(s32[1,2048]{1,0:T(1,128)} %param.5) | copy-start | bytes 24580
  0.7 17.4 %copy-start.2 = (bf16[3,256,256]{2,1,0:T(8,128)(2,1)S(1)}, bf16[3,256,256]{2,1,0:T(8,128)(2,1)}, u32[]{:S(2)}) copy-start(bf16[3,256,256]{2,1,0:T(8,128)(2,1)} %param.8) | copy-start | bytes 1179652
  2.2 16.3 %collective-permute-start = (bf16[1,17,256]{2,1,0:T(8,128)(2,1)S(1)}, bf16[1,17,256]{2,1,0:T(8,128)(2,1)S(1)}, u32[]{:S(2)}, u32[]{:S(2)}) collective-permute-start(bf16[1,17,256]{2,1,0:T(8,128)(2,1)S(1)} %pad_maximum_fusion.4), channel_id=1, source_target_pairs={{0,1},{1,2},{2,3},{3,4},{4,5},{5,6},{6,7},{7,8},{8,9},{9,10},{10,1... | collective-permute-start | bytes 26120 | tf_op jit(solution)/shard_map/ppermute | solution.py:249
  13.1 8.9 %collective-permute-start.1 = (bf16[1,17,256]{2,1,0:T(8,128)(2,1)S(1)}, bf16[1,17,256]{2,1,0:T(8,128)(2,1)S(1)}, u32[]{:S(2)}, u32[]{:S(2)}) collective-permute-start(bf16[1,17,256]{2,1,0:T(8,128)(2,1)S(1)} %pad_maximum_fusion.5), channel_id=1, source_target_pairs={{1,0},{2,1},{3,2},{4,3},{5,4},{6,5},{7,6},{8,7},{9,8},{10,9},{11,1... | collective-permute-start | bytes 26120 | tf_op jit(solution)/shard_map/ppermute | solution.py:250
  28.0 1.9 %copy-start.1 = (bf16[1,2048,256]{2,1,0:T(8,128)(2,1)S(1)}, bf16[1,2048,256]{2,1,0:T(8,128)(2,1)}, u32[]{:S(2)}) copy-start(bf16[1,2048,256]{2,1,0:T(8,128)(2,1)} %param.9) | copy-start | bytes 3145732
  43.1 4.9 %collective-permute-start.2 = (f32[192,256]{1,0:T(8,128)S(1)}, f32[192,256]{1,0:T(8,128)S(1)}, u32[]{:S(2)}, u32[]{:S(2)}) collective-permute-start(f32[192,256]{1,0:T(8,128)S(1)} %get-tuple-element.24), channel_id=1, source_target_pairs={{0,16},{16,0},{32,48},{48,32},{64,80},{80,64},{96,112},{112,96},{1... | collective-permute-start | bytes 589832 | tf_op jit(solution)/shard_map/ppermute | solution.py:99
  44.3 7.7 %collective-permute-start.3 = (f32[192,256]{1,0:T(8,128)S(1)}, f32[192,256]{1,0:T(8,128)S(1)}, u32[]{:S(2)}, u32[]{:S(2)}) collective-permute-start(f32[192,256]{1,0:T(8,128)S(1)} %get-tuple-element.26), channel_id=1, source_target_pairs={{0,32},{16,48},{32,0},{48,16},{64,96},{80,112},{96,64},{112,80},{1... | collective-permute-start | bytes 589832 | tf_op jit(solution)/shard_map/ppermute | solution.py:99
  46.8 7.3 %collective-permute-start.4 = (f32[192,256]{1,0:T(8,128)S(1)}, f32[192,256]{1,0:T(8,128)S(1)}, u32[]{:S(2)}, u32[]{:S(2)}) collective-permute-start(f32[192,256]{1,0:T(8,128)S(1)} %get-tuple-element.25), channel_id=1, source_target_pairs={{0,48},{16,32},{32,16},{48,0},{64,112},{80,96},{96,80},{112,64},{1... | collective-permute-start | bytes 589832 | tf_op jit(solution)/shard_map/ppermute | solution.py:99
  54.1 5.2 %collective-permute-start.5 = (f32[48,256]{1,0:T(8,128)S(1)}, f32[48,256]{1,0:T(8,128)S(1)}, u32[]{:S(2)}, u32[]{:S(2)}) collective-permute-start(f32[48,256]{1,0:T(8,128)S(1)} %get-tuple-element.27), channel_id=1, source_target_pairs={{0,4},{1,5},{2,6},{3,7},{4,0},{5,1},{6,2},{7,3},{8,12},{9,13},{10,... | collective-permute-start | bytes 147464 | tf_op jit(solution)/shard_map/ppermute | solution.py:99
  56.4 5.5 %collective-permute-start.6 = (f32[48,256]{1,0:T(8,128)S(1)}, f32[48,256]{1,0:T(8,128)S(1)}, u32[]{:S(2)}, u32[]{:S(2)}) collective-permute-start(f32[48,256]{1,0:T(8,128)S(1)} %get-tuple-element.29), channel_id=1, source_target_pairs={{0,8},{1,9},{2,10},{3,11},{4,12},{5,13},{6,14},{7,15},{8,0},{9,1},... | collective-permute-start | bytes 147464 | tf_op jit(solution)/shard_map/ppermute | solution.py:99
  59.4 4.9 %collective-permute-start.7 = (f32[48,256]{1,0:T(8,128)S(1)}, f32[48,256]{1,0:T(8,128)S(1)}, u32[]{:S(2)}, u32[]{:S(2)}) collective-permute-start(f32[48,256]{1,0:T(8,128)S(1)} %get-tuple-element.28), channel_id=1, source_target_pairs={{0,12},{1,13},{2,14},{3,15},{4,8},{5,9},{6,10},{7,11},{8,4},{9,5},... | collective-permute-start | bytes 147464 | tf_op jit(solution)/shard_map/ppermute | solution.py:99
  64.2 5.1 %collective-permute-start.8 = (f32[48,256]{1,0:T(8,128)S(1)}, f32[48,256]{1,0:T(8,128)S(1)}, u32[]{:S(2)}, u32[]{:S(2)}) collective-permute-start(f32[48,256]{1,0:T(8,128)S(1)} %add_add_fusion.1), channel_id=1, source_target_pairs={{0,64},{16,80},{32,96},{48,112},{64,0},{80,16},{96,32},{112,48},{1... | collective-permute-start | bytes 147464 | tf_op jit(solution)/shard_map/ppermute | solution.py:104
  65.3 6.0 %collective-permute-start.9 = (f32[48,256]{1,0:T(8,128)S(1)}, f32[48,256]{1,0:T(8,128)S(1)}, u32[]{:S(2)}, u32[]{:S(2)}) collective-permute-start(f32[48,256]{1,0:T(8,128)S(1)} %add_add_fusion.1), channel_id=1, source_target_pairs={{0,128},{16,144},{32,160},{48,176},{64,192},{80,208},{96,224},{112... | collective-permute-start | bytes 147464 | tf_op jit(solution)/shard_map/ppermute | solution.py:104
  69.3 4.7 %collective-permute-start.10 = (f32[48,256]{1,0:T(8,128)S(1)}, f32[48,256]{1,0:T(8,128)S(1)}, u32[]{:S(2)}, u32[]{:S(2)}) collective-permute-start(f32[48,256]{1,0:T(8,128)S(1)} %add_add_fusion.1), channel_id=1, source_target_pairs={{0,192},{16,208},{32,224},{48,240},{64,128},{80,144},{96,160},{112... | collective-permute-start | bytes 147464 | tf_op jit(solution)/shard_map/ppermute | solution.py:104
  74.1 9.6 %collective-permute-start.11 = (f32[48,256]{1,0:T(8,128)S(1)}, f32[48,256]{1,0:T(8,128)S(1)}, u32[]{:S(2)}, u32[]{:S(2)}) collective-permute-start(f32[48,256]{1,0:T(8,128)S(1)} %fusion.112), channel_id=1, source_target_pairs={{0,1},{1,0},{2,3},{3,2},{4,5},{5,4},{6,7},{7,6},{8,9},{9,8},{10,11... | collective-permute-start | bytes 147464 | tf_op jit(solution)/shard_map/ppermute | solution.py:104
  78.0 6.8 %collective-permute-start.12 = (f32[48,256]{1,0:T(8,128)S(1)}, f32[48,256]{1,0:T(8,128)S(1)}, u32[]{:S(2)}, u32[]{:S(2)}) collective-permute-start(f32[48,256]{1,0:T(8,128)S(1)} %fusion.112), channel_id=1, source_target_pairs={{0,2},{1,3},{2,0},{3,1},{4,6},{5,7},{6,4},{7,5},{8,10},{9,11},{10,... | collective-permute-start | bytes 147464 | tf_op jit(solution)/shard_map/ppermute | solution.py:104
  79.7 8.4 %collective-permute-start.13 = (f32[48,256]{1,0:T(8,128)S(1)}, f32[48,256]{1,0:T(8,128)S(1)}, u32[]{:S(2)}, u32[]{:S(2)}) collective-permute-start(f32[48,256]{1,0:T(8,128)S(1)} %fusion.112), channel_id=1, source_target_pairs={{0,3},{1,2},{2,1},{3,0},{4,7},{5,6},{6,5},{7,4},{8,11},{9,10},{10,... | collective-permute-start | bytes 147464 | tf_op jit(solution)/shard_map/ppermute | solution.py:104
  88.2 5.2 %collective-permute-start.14 = (f32[48,256]{1,0:T(8,128)S(1)}, f32[48,256]{1,0:T(8,128)S(1)}, u32[]{:S(2)}, u32[]{:S(2)}) collective-permute-start(f32[48,256]{1,0:T(8,128)S(1)} %add_bitcast_fusion), channel_id=1, source_target_pairs={{0,4},{1,5},{2,6},{3,7},{4,0},{5,1},{6,2},{7,3},{8,12},{9,13},{10,... | collective-permute-start | bytes 147464 | tf_op jit(solution)/shard_map/ppermute | solution.py:115
  88.3 6.5 %collective-permute-start.15 = (f32[48,256]{1,0:T(8,128)S(1)}, f32[48,256]{1,0:T(8,128)S(1)}, u32[]{:S(2)}, u32[]{:S(2)}) collective-permute-start(f32[48,256]{1,0:T(8,128)S(1)} %add_bitcast_fusion), channel_id=1, source_target_pairs={{0,8},{1,9},{2,10},{3,11},{4,12},{5,13},{6,14},{7,15},{8,0},{9,1},... | collective-permute-start | bytes 147464 | tf_op jit(solution)/shard_map/ppermute | solution.py:115
  90.1 6.1 %collective-permute-start.16 = (f32[48,256]{1,0:T(8,128)S(1)}, f32[48,256]{1,0:T(8,128)S(1)}, u32[]{:S(2)}, u32[]{:S(2)}) collective-permute-start(f32[48,256]{1,0:T(8,128)S(1)} %add_bitcast_fusion), channel_id=1, source_target_pairs={{0,12},{1,13},{2,14},{3,15},{4,8},{5,9},{6,10},{7,11},{8,4},{9,5},... | collective-permute-start | bytes 147464 | tf_op jit(solution)/shard_map/ppermute | solution.py:115
  97.2 6.7 %collective-permute-start.17 = (f32[192,256]{0,1:T(8,128)S(1)}, f32[192,256]{0,1:T(8,128)S(1)}, u32[]{:S(2)}, u32[]{:S(2)}) collective-permute-start(f32[192,256]{0,1:T(8,128)S(1)} %dynamic_update_slice.27), channel_id=1, source_target_pairs={{0,16},{16,0},{32,48},{48,32},{64,80},{80,64},{96,112},{112,96},{1... | collective-permute-start | bytes 589832 | tf_op jit(solution)/shard_map/ppermute | solution.py:115
  97.3 12.3 %collective-permute-start.18 = (f32[192,256]{0,1:T(8,128)S(1)}, f32[192,256]{0,1:T(8,128)S(1)}, u32[]{:S(2)}, u32[]{:S(2)}) collective-permute-start(f32[192,256]{0,1:T(8,128)S(1)} %dynamic_update_slice.27), channel_id=1, source_target_pairs={{0,32},{16,48},{32,0},{48,16},{64,96},{80,112},{96,64},{112,80},{1... | collective-permute-start | bytes 589832 | tf_op jit(solution)/shard_map/ppermute | solution.py:115
  98.8 13.4 %collective-permute-start.19 = (f32[192,256]{0,1:T(8,128)S(1)}, f32[192,256]{0,1:T(8,128)S(1)}, u32[]{:S(2)}, u32[]{:S(2)}) collective-permute-start(f32[192,256]{0,1:T(8,128)S(1)} %dynamic_update_slice.27), channel_id=1, source_target_pairs={{0,48},{16,32},{32,16},{48,0},{64,112},{80,96},{96,80},{112,64},{1... | collective-permute-start | bytes 589832 | tf_op jit(solution)/shard_map/ppermute | solution.py:115
  (1 other events, 1.0 us)

commit v9 on v8

--- a/solution.py
+++ b/solution.py
@@ -109,12 +109,9 @@
         rows = total
     for axis, shift, radix, place in reversed(kept):
         width = rows.shape[0]
-        full = jnp.zeros((width * radix,) + rows.shape[1:], rows.dtype)
-        full = lax.dynamic_update_slice_in_dim(full, rows, place * width, 0)
-        for offset in range(1, radix):
-            got = lax.ppermute(rows, axis, partner_pairs(axis, shift, offset))
-            full = lax.dynamic_update_slice_in_dim(full, got, (place ^ offset) * width, 0)
-        rows = full
+        pieces = [rows] + [lax.ppermute(rows, axis, partner_pairs(axis, shift, offset)) for offset in range(1, radix)]
+        order = jnp.arange(radix, dtype=jnp.int32) ^ place
+        rows = jnp.take(jnp.stack(pieces), order, axis=0).reshape((width * radix,) + rows.shape[1:])
     return rows
 
 

time: 118 us -> 112 us (0.949)
  local copies, waits for them, and re-layouts: 16 us -> 7.66 us
  waiting for transfers between devices: 30 us -> 34.1 us
  other arithmetic: 10.3 us -> 8.96 us
    dynamic_update_slice x8 -> x0, local copies, waits for them, and re-layouts: 11.5 us -> none  [the longest x6 8.53 us: butterfly_sum(): lax.dynamic_update_slice_in_dim(full, got, (place ^ offset) * width, 0)]
    ppermute x6 -> x12, waiting for transfers between devices: 9.21 us -> 18.9 us  [butterfly_sum(): lax.ppermute(rows, axis, partner_pairs(axis, shift, offset))]
    ppermute x6 -> x12, starting transfers between devices: 14.6 us -> 22.6 us  [butterfly_sum(): lax.ppermute(rows, axis, partner_pairs(axis, shift, offset))]
    ppermute x6 -> x0, starting transfers between devices: 7.88 us -> none  [butterfly_sum(): got = lax.ppermute(rows, axis, partner_pairs(axis, shift, offset))]
    ppermute x6 -> x0, waiting for transfers between devices: 5.39 us -> none  [butterfly_sum(): got = lax.ppermute(rows, axis, partner_pairs(axis, shift, offset))]
    unnamed x11 -> x13, local copies, waits for them, and re-layouts: 0.84 us -> 3.14 us
    another operation x8, other arithmetic: 2.02 us -> 0.26 us  [unfolded_halves(): jnp.stack([jnp.concatenate([taps[k], taps[2 - k][::-1, ::-1]], axis=1) fo...]
  transfers between devices with their start and end apart: 20 -> 20, of which waited for: 13 -> 15; matrix products, arithmetic and copies ran while one was open for 12% -> 4% of each run, Pallas kernels for 0% -> 0%
where the time goes in v9:
time: 112 us
  starting transfers between devices  43.9 us (39%)
  waiting for transfers between devices  34.1 us (30%)
  matrix products  15.4 us (14%)
  other arithmetic  8.96 us (8%)
  local copies, waits for them, and re-layouts  7.66 us (7%)
  between operations  1.35 us (1%)
    ppermute x12, starting transfers between devices, butterfly_sum(): lax.ppermute(rows, axis, partner_pairs(axis, shift, offset))  22.6 us
    ppermute x12, waiting for transfers between devices, butterfly_sum(): lax.ppermute(rows, axis, partner_pairs(axis, shift, offset))  18.9 us
    ppermute x6, waiting for transfers between devices, butterfly_sum(): total = total + lax.ppermute(sent, axis, partner_pairs(axis, shift, offset))  11.8 us
    ppermute x1, starting transfers between devices, local(): lax.ppermute(tail, 'seq', [(i, i + 1) for i in range(count - 1)])  10.2 us
    ppermute x6, starting transfers between devices, butterfly_sum(): total = total + lax.ppermute(sent, axis, partner_pairs(axis, shift, offset))  9.29 us
    dot_general x4, matrix products, product(): jnp.dot(stacked.reshape(-1, shape_in[-1]), matrix, preferred_element_type...  6.19 us
    ppermute x1, waiting for transfers between devices, local(): lax.ppermute(head, 'seq', [(i + 1, i) for i in range(count - 1)])  3.5 us
    unnamed x13, local copies, waits for them, and re-layouts  3.14 us
  transfers between devices with their start and end apart: 20, of which 15 were waited for; matrix products, arithmetic and copies ran while one was open for 4% of the time, Pallas kernels for 0%

profile of v9, /device:TPU:1, one launch (start us, length us, event | category | flops | bytes accessed | tf_op | source)
XLA Modules:
  0.0 111.5 jit_solution(8256471168383566116)
XLA Ops:
  2.2 10.2 %collective-permute-start = (bf16[1,17,256]{2,1,0:T(8,128)(2,1)S(1)}, bf16[1,17,256]{2,1,0:T(8,128)(2,1)S(1)}, u32[]{:S(2)}, u32[]{:S(2)}) collective-permute-start(bf16[1,17,256]{2,1,0:T(8,128)(2,1)S(1)} %pad_maximum_fusion.6), channel_id=1, source_target_pairs={{0,1},{1,2},{2,3},{3,4},{4,5},{5,6},{6,7},{7,8},{8,9},{9,10},{10,1... | collective-permute-start | bytes 26120 | tf_op jit(solution)/shard_map/ppermute | solution.py:246
  13.1 1.9 %collective-permute-start.1 = (bf16[1,17,256]{2,1,0:T(8,128)(2,1)S(1)}, bf16[1,17,256]{2,1,0:T(8,128)(2,1)S(1)}, u32[]{:S(2)}, u32[]{:S(2)}) collective-permute-start(bf16[1,17,256]{2,1,0:T(8,128)(2,1)S(1)} %pad_maximum_fusion.7), channel_id=1, source_target_pairs={{1,0},{2,1},{3,2},{4,3},{5,4},{6,5},{7,6},{8,7},{9,8},{10,9},{11,1... | collective-permute-start | bytes 26120 | tf_op jit(solution)/shard_map/ppermute | solution.py:247
  18.6 3.5 %collective-permute-done.1 = bf16[1,17,256]{2,1,0:T(8,128)(2,1)S(1)} collective-permute-done((bf16[1,17,256]{2,1,0:T(8,128)(2,1)S(1)}, bf16[1,17,256]{2,1,0:T(8,128)(2,1)S(1)}, u32[]{:S(2)}, u32[]{:S(2)}) %collective-permute-start.1) | collective-permute-done | bytes 8736 | tf_op jit(solution)/shard_map/ppermute | solution.py:247
  23.9 1.8 %convolution_bitcast_fusion.1 = f32[1,2112,512]{2,1,0:T(8,128)S(1)} fusion(bf16[1,2112,256]{2,1,0:T(8,128)(2,1)S(1)} %get-tuple-element.14, bf16[1,2112,256]{2,1,0:T(8,128)(2,1)S(1)} %get-tuple-element.15, bf16[1,2112,256]{2,1,0:T(8,128)(2,1)S(1)} %get-tuple-element.13, bf16[768,256]{1,0:T(8,128)(2,1)S(1)} %bitcast.201, bf16[768,256]{1,0:T(8,128)(2,1)S(1)} %bitcast.200), kind=kOutput, calls=%fused_computation.3 | convolution fusion | flops 1672249344 | bytes 8355840 | tf_op jit(solution)/shard_map/dot_general | solution.py:40
  28.0 1.9 %convolution_bitcast_fusion = f32[1,2080,512]{2,1,0:T(8,128)S(1)} fusion(bf16[1,2080,256]{2,1,0:T(8,128)(2,1)S(1)} %get-tuple-element.17, bf16[1,2080,256]{2,1,0:T(8,128)(2,1)S(1)} %get-tuple-element.18, bf16[1,2080,256]{2,1,0:T(8,128)(2,1)S(1)} %get-tuple-element.16, bf16[768,256]{1,0:T(8,128)(2,1)S(1)} %bitcast.185, bf16[768,256]{1,0:T(8,128)(2,1)S(1)} %bitcast.182), kind=kOutput, calls=%fused_computation.2 | convolution fusion | flops 1646936064 | bytes 8241152 | tf_op jit(solution)/shard_map/dot_general | solution.py:40
  34.0 1.8 %convolution_bitcast_fusion.2 = f32[1,2048,512]{2,1,0:T(8,128)S(1)} fusion(bf16[1,2048,256]{2,1,0:T(8,128)(2,1)S(1)} %get-tuple-element.20, bf16[1,2048,256]{2,1,0:T(8,128)(2,1)S(1)} %get-tuple-element.21, bf16[1,2048,256]{2,1,0:T(8,128)(2,1)S(1)} %get-tuple-element.19, bf16[768,256]{1,0:T(8,128)(2,1)S(1)} %bitcast.186, bf16[768,256]{1,0:T(8,128)(2,1)S(1)} %bitcast.183), kind=kOutput, calls=%fused_computation.10 | convolution fusion | flops 1621622784 | bytes 8126464 | tf_op jit(solution)/shard_map/dot_general | solution.py:40
  35.8 2.8 %fusion.39 = (bf16[1,2048,256]{2,1,0:T(8,128)(2,1)S(1)}, bf16[1,2048,256]{2,1,0:T(8,128)(2,1)}) fusion(f32[1,2048,512]{2,1,0:T(8,128)S(1)} %convolution_bitcast_fusion.2, f32[1,2112,256]{2,1,0:T(8,128)S(1)} %get-tuple-element.12, bf16[1,2048,256]{2,1,0:T(8,128)(2,1)S(1)} %copy-done.1, f32[1,2080,256]{2,1,0:T(8,128)S(1)} %add_multiply_fusion, ...), kind=kLoop, calls=%fused_computation.61 | loop fusion | flops 14155776 | bytes 14680064 | tf_op jit(solution)/shard_map/convert_element_type | solution.py:285
  44.3 2.5 %collective-permute-start.3 = (f32[192,256]{1,0:T(8,128)S(1)}, f32[192,256]{1,0:T(8,128)S(1)}, u32[]{:S(2)}, u32[]{:S(2)}) collective-permute-start(f32[192,256]{1,0:T(8,128)S(1)} %get-tuple-element.28), channel_id=1, source_target_pairs={{0,32},{16,48},{32,0},{48,16},{64,96},{80,112},{96,64},{112,80},{1... | collective-permute-start | bytes 589832 | tf_op jit(solution)/shard_map/ppermute | solution.py:99
  48.0 4.1 %collective-permute-done.3 = f32[192,256]{1,0:T(8,128)S(1)} collective-permute-done((f32[192,256]{1,0:T(8,128)S(1)}, f32[192,256]{1,0:T(8,128)S(1)}, u32[]{:S(2)}, u32[]{:S(2)}) %collective-permute-start.3) | collective-permute-done | bytes 196640 | tf_op jit(solution)/shard_map/ppermute | solution.py:99
  52.1 2.0 %collective-permute-done.4 = f32[192,256]{1,0:T(8,128)S(1)} collective-permute-done((f32[192,256]{1,0:T(8,128)S(1)}, f32[192,256]{1,0:T(8,128)S(1)}, u32[]{:S(2)}, u32[]{:S(2)}) %collective-permute-start.4) | collective-permute-done | bytes 196640 | tf_op jit(solution)/shard_map/ppermute | solution.py:99
  54.1 2.3 %collective-permute-start.5 = (f32[48,256]{1,0:T(8,128)S(1)}, f32[48,256]{1,0:T(8,128)S(1)}, u32[]{:S(2)}, u32[]{:S(2)}) collective-permute-start(f32[48,256]{1,0:T(8,128)S(1)} %get-tuple-element.35), channel_id=1, source_target_pairs={{0,4},{1,5},{2,6},{3,7},{4,0},{5,1},{6,2},{7,3},{8,12},{9,13},{10,... | collective-permute-start | bytes 147464 | tf_op jit(solution)/shard_map/ppermute | solution.py:99
  56.5 3.0 %collective-permute-start.6 = (f32[48,256]{1,0:T(8,128)S(1)}, f32[48,256]{1,0:T(8,128)S(1)}, u32[]{:S(2)}, u32[]{:S(2)}) collective-permute-start(f32[48,256]{1,0:T(8,128)S(1)} %get-tuple-element.37), channel_id=1, source_target_pairs={{0,8},{1,9},{2,10},{3,11},{4,12},{5,13},{6,14},{7,15},{8,0},{9,1},... | collective-permute-start | bytes 147464 | tf_op jit(solution)/shard_map/ppermute | solution.py:99
  59.5 2.7 %collective-permute-done.6 = f32[48,256]{1,0:T(8,128)S(1)} collective-permute-done((f32[48,256]{1,0:T(8,128)S(1)}, f32[48,256]{1,0:T(8,128)S(1)}, u32[]{:S(2)}, u32[]{:S(2)}) %collective-permute-start.6) | collective-permute-done | bytes 49184 | tf_op jit(solution)/shard_map/ppermute | solution.py:99
  62.1 2.1 %collective-permute-done.7 = f32[48,256]{1,0:T(8,128)S(1)} collective-permute-done((f32[48,256]{1,0:T(8,128)S(1)}, f32[48,256]{1,0:T(8,128)S(1)}, u32[]{:S(2)}, u32[]{:S(2)}) %collective-permute-start.7) | collective-permute-done | bytes 49184 | tf_op jit(solution)/shard_map/ppermute | solution.py:99
  65.4 4.0 %collective-permute-start.9 = (f32[48,256]{1,0:T(8,128)S(1)}, f32[48,256]{1,0:T(8,128)S(1)}, u32[]{:S(2)}, u32[]{:S(2)}) collective-permute-start(f32[48,256]{1,0:T(8,128)S(1)} %add_add_fusion.1), channel_id=1, source_target_pairs={{0,128},{16,144},{32,160},{48,176},{64,192},{80,208},{96,224},{112... | collective-permute-start | bytes 147464 | tf_op jit(solution)/shard_map/ppermute | solution.py:104
  71.4 2.7 %collective-permute-done.10 = f32[48,256]{1,0:T(8,128)S(1)} collective-permute-done((f32[48,256]{1,0:T(8,128)S(1)}, f32[48,256]{1,0:T(8,128)S(1)}, u32[]{:S(2)}, u32[]{:S(2)}) %collective-permute-start.10) | collective-permute-done | bytes 49184 | tf_op jit(solution)/shard_map/ppermute | solution.py:104
  74.2 3.9 %collective-permute-start.11 = (f32[48,256]{1,0:T(8,128)S(1)}, f32[48,256]{1,0:T(8,128)S(1)}, u32[]{:S(2)}, u32[]{:S(2)}) collective-permute-start(f32[48,256]{1,0:T(8,128)S(1)} %fusion.116), channel_id=1, source_target_pairs={{0,1},{1,0},{2,3},{3,2},{4,5},{5,4},{6,7},{7,6},{8,9},{9,8},{10,11... | collective-permute-start | bytes 147464 | tf_op jit(solution)/shard_map/ppermute | solution.py:104
  79.7 4.0 %collective-permute-start.13 = (f32[48,256]{1,0:T(8,128)S(1)}, f32[48,256]{1,0:T(8,128)S(1)}, u32[]{:S(2)}, u32[]{:S(2)}) collective-permute-start(f32[48,256]{1,0:T(8,128)S(1)} %fusion.116), channel_id=1, source_target_pairs={{0,3},{1,2},{2,1},{3,0},{4,7},{5,6},{6,5},{7,4},{8,11},{9,10},{10,... | collective-permute-start | bytes 147464 | tf_op jit(solution)/shard_map/ppermute | solution.py:104
  84.9 3.1 %collective-permute-done.13 = f32[48,256]{1,0:T(8,128)S(1)} collective-permute-done((f32[48,256]{1,0:T(8,128)S(1)}, f32[48,256]{1,0:T(8,128)S(1)}, u32[]{:S(2)}, u32[]{:S(2)}) %collective-permute-start.13) | collective-permute-done | bytes 49184 | tf_op jit(solution)/shard_map/ppermute | solution.py:104
  88.2 2.0 %collective-permute-start.15 = (f32[48,256]{1,0:T(8,128)S(1)}, f32[48,256]{1,0:T(8,128)S(1)}, u32[]{:S(2)}, u32[]{:S(2)}) collective-permute-start(f32[48,256]{1,0:T(8,128)S(1)} %fusion.115), channel_id=1, source_target_pairs={{0,8},{1,9},{2,10},{3,11},{4,12},{5,13},{6,14},{7,15},{8,0},{9,1},... | collective-permute-start | bytes 147464 | tf_op jit(solution)/shard_map/ppermute | solution.py:112
  90.2 1.9 %collective-permute-start.16 = (f32[48,256]{1,0:T(8,128)S(1)}, f32[48,256]{1,0:T(8,128)S(1)}, u32[]{:S(2)}, u32[]{:S(2)}) collective-permute-start(f32[48,256]{1,0:T(8,128)S(1)} %fusion.115), channel_id=1, source_target_pairs={{0,12},{1,13},{2,14},{3,15},{4,8},{5,9},{6,10},{7,11},{8,4},{9,5},... | collective-permute-start | bytes 147464 | tf_op jit(solution)/shard_map/ppermute | solution.py:112
  96.5 2.5 %collective-permute-start.19 = (f32[192,256]{1,0:T(8,128)S(1)}, f32[192,256]{1,0:T(8,128)S(1)}, u32[]{:S(2)}, u32[]{:S(2)}) collective-permute-start(f32[192,256]{1,0:T(8,128)S(1)} %bitcast_select_fusion), channel_id=1, source_target_pairs={{0,48},{16,32},{32,16},{48,0},{64,112},{80,96},{96,80},{112,64},{1... | collective-permute-start | bytes 589832 | tf_op jit(solution)/shard_map/ppermute | solution.py:112
  99.6 3.8 %collective-permute-done.18 = f32[192,256]{1,0:T(8,128)S(1)} collective-permute-done((f32[192,256]{1,0:T(8,128)S(1)}, f32[192,256]{1,0:T(8,128)S(1)}, u32[]{:S(2)}, u32[]{:S(2)}) %collective-permute-start.18) | collective-permute-done | bytes 196640 | tf_op jit(solution)/shard_map/ppermute | solution.py:112
  103.4 3.5 %collective-permute-done.19 = f32[192,256]{1,0:T(8,128)S(1)} collective-permute-done((f32[192,256]{1,0:T(8,128)S(1)}, f32[192,256]{1,0:T(8,128)S(1)}, u32[]{:S(2)}, u32[]{:S(2)}) %collective-permute-start.19) | collective-permute-done | bytes 196640 | tf_op jit(solution)/shard_map/ppermute | solution.py:112
  (116 shorter events, 36.4 us)
Async XLA Ops:
  0.6 21.6 %copy-start = (bf16[4,256]{1,0:T(4,128)(2,1)S(1)}, bf16[4,256]{1,0:T(4,128)(2,1)}, u32[]{:S(2)}) copy-start(bf16[4,256]{1,0:T(4,128)(2,1)} %param.6) | copy-start | bytes 6148
  0.6 21.4 %copy-start.3 = (s32[1,2048]{1,0:T(1,128)S(1)}, s32[1,2048]{1,0:T(1,128)}, u32[]{:S(2)}) copy-start(s32[1,2048]{1,0:T(1,128)} %param.5) | copy-start | bytes 24580
  0.7 17.4 %copy-start.2 = (bf16[3,256,256]{2,1,0:T(8,128)(2,1)S(1)}, bf16[3,256,256]{2,1,0:T(8,128)(2,1)}, u32[]{:S(2)}) copy-start(bf16[3,256,256]{2,1,0:T(8,128)(2,1)} %param.8) | copy-start | bytes 1179652
  2.2 16.3 %collective-permute-start = (bf16[1,17,256]{2,1,0:T(8,128)(2,1)S(1)}, bf16[1,17,256]{2,1,0:T(8,128)(2,1)S(1)}, u32[]{:S(2)}, u32[]{:S(2)}) collective-permute-start(bf16[1,17,256]{2,1,0:T(8,128)(2,1)S(1)} %pad_maximum_fusion.6), channel_id=1, source_target_pairs={{0,1},{1,2},{2,3},{3,4},{4,5},{5,6},{6,7},{7,8},{8,9},{9,10},{10,1... | collective-permute-start | bytes 26120 | tf_op jit(solution)/shard_map/ppermute | solution.py:246
  13.1 8.9 %collective-permute-start.1 = (bf16[1,17,256]{2,1,0:T(8,128)(2,1)S(1)}, bf16[1,17,256]{2,1,0:T(8,128)(2,1)S(1)}, u32[]{:S(2)}, u32[]{:S(2)}) collective-permute-start(bf16[1,17,256]{2,1,0:T(8,128)(2,1)S(1)} %pad_maximum_fusion.7), channel_id=1, source_target_pairs={{1,0},{2,1},{3,2},{4,3},{5,4},{6,5},{7,6},{8,7},{9,8},{10,9},{11,1... | collective-permute-start | bytes 26120 | tf_op jit(solution)/shard_map/ppermute | solution.py:247
  28.0 1.9 %copy-start.1 = (bf16[1,2048,256]{2,1,0:T(8,128)(2,1)S(1)}, bf16[1,2048,256]{2,1,0:T(8,128)(2,1)}, u32[]{:S(2)}) copy-start(bf16[1,2048,256]{2,1,0:T(8,128)(2,1)} %param.9) | copy-start | bytes 3145732
  43.1 4.9 %collective-permute-start.2 = (f32[192,256]{1,0:T(8,128)S(1)}, f32[192,256]{1,0:T(8,128)S(1)}, u32[]{:S(2)}, u32[]{:S(2)}) collective-permute-start(f32[192,256]{1,0:T(8,128)S(1)} %get-tuple-element.26), channel_id=1, source_target_pairs={{0,16},{16,0},{32,48},{48,32},{64,80},{80,64},{96,112},{112,96},{1... | collective-permute-start | bytes 589832 | tf_op jit(solution)/shard_map/ppermute | solution.py:99
  44.3 7.7 %collective-permute-start.3 = (f32[192,256]{1,0:T(8,128)S(1)}, f32[192,256]{1,0:T(8,128)S(1)}, u32[]{:S(2)}, u32[]{:S(2)}) collective-permute-start(f32[192,256]{1,0:T(8,128)S(1)} %get-tuple-element.28), channel_id=1, source_target_pairs={{0,32},{16,48},{32,0},{48,16},{64,96},{80,112},{96,64},{112,80},{1... | collective-permute-start | bytes 589832 | tf_op jit(solution)/shard_map/ppermute | solution.py:99
  46.8 7.3 %collective-permute-start.4 = (f32[192,256]{1,0:T(8,128)S(1)}, f32[192,256]{1,0:T(8,128)S(1)}, u32[]{:S(2)}, u32[]{:S(2)}) collective-permute-start(f32[192,256]{1,0:T(8,128)S(1)} %get-tuple-element.27), channel_id=1, source_target_pairs={{0,48},{16,32},{32,16},{48,0},{64,112},{80,96},{96,80},{112,64},{1... | collective-permute-start | bytes 589832 | tf_op jit(solution)/shard_map/ppermute | solution.py:99
  54.1 5.3 %collective-permute-start.5 = (f32[48,256]{1,0:T(8,128)S(1)}, f32[48,256]{1,0:T(8,128)S(1)}, u32[]{:S(2)}, u32[]{:S(2)}) collective-permute-start(f32[48,256]{1,0:T(8,128)S(1)} %get-tuple-element.35), channel_id=1, source_target_pairs={{0,4},{1,5},{2,6},{3,7},{4,0},{5,1},{6,2},{7,3},{8,12},{9,13},{10,... | collective-permute-start | bytes 147464 | tf_op jit(solution)/shard_map/ppermute | solution.py:99
  56.5 5.7 %collective-permute-start.6 = (f32[48,256]{1,0:T(8,128)S(1)}, f32[48,256]{1,0:T(8,128)S(1)}, u32[]{:S(2)}, u32[]{:S(2)}) collective-permute-start(f32[48,256]{1,0:T(8,128)S(1)} %get-tuple-element.37), channel_id=1, source_target_pairs={{0,8},{1,9},{2,10},{3,11},{4,12},{5,13},{6,14},{7,15},{8,0},{9,1},... | collective-permute-start | bytes 147464 | tf_op jit(solution)/shard_map/ppermute | solution.py:99
  59.4 4.8 %collective-permute-start.7 = (f32[48,256]{1,0:T(8,128)S(1)}, f32[48,256]{1,0:T(8,128)S(1)}, u32[]{:S(2)}, u32[]{:S(2)}) collective-permute-start(f32[48,256]{1,0:T(8,128)S(1)} %get-tuple-element.36), channel_id=1, source_target_pairs={{0,12},{1,13},{2,14},{3,15},{4,8},{5,9},{6,10},{7,11},{8,4},{9,5},... | collective-permute-start | bytes 147464 | tf_op jit(solution)/shard_map/ppermute | solution.py:99
  64.2 5.3 %collective-permute-start.8 = (f32[48,256]{1,0:T(8,128)S(1)}, f32[48,256]{1,0:T(8,128)S(1)}, u32[]{:S(2)}, u32[]{:S(2)}) collective-permute-start(f32[48,256]{1,0:T(8,128)S(1)} %add_add_fusion.1), channel_id=1, source_target_pairs={{0,64},{16,80},{32,96},{48,112},{64,0},{80,16},{96,32},{112,48},{1... | collective-permute-start | bytes 147464 | tf_op jit(solution)/shard_map/ppermute | solution.py:104
  65.4 6.0 %collective-permute-start.9 = (f32[48,256]{1,0:T(8,128)S(1)}, f32[48,256]{1,0:T(8,128)S(1)}, u32[]{:S(2)}, u32[]{:S(2)}) collective-permute-start(f32[48,256]{1,0:T(8,128)S(1)} %add_add_fusion.1), channel_id=1, source_target_pairs={{0,128},{16,144},{32,160},{48,176},{64,192},{80,208},{96,224},{112... | collective-permute-start | bytes 147464 | tf_op jit(solution)/shard_map/ppermute | solution.py:104
  69.4 4.7 %collective-permute-start.10 = (f32[48,256]{1,0:T(8,128)S(1)}, f32[48,256]{1,0:T(8,128)S(1)}, u32[]{:S(2)}, u32[]{:S(2)}) collective-permute-start(f32[48,256]{1,0:T(8,128)S(1)} %add_add_fusion.1), channel_id=1, source_target_pairs={{0,192},{16,208},{32,224},{48,240},{64,128},{80,144},{96,160},{112... | collective-permute-start | bytes 147464 | tf_op jit(solution)/shard_map/ppermute | solution.py:104
  74.2 9.6 %collective-permute-start.11 = (f32[48,256]{1,0:T(8,128)S(1)}, f32[48,256]{1,0:T(8,128)S(1)}, u32[]{:S(2)}, u32[]{:S(2)}) collective-permute-start(f32[48,256]{1,0:T(8,128)S(1)} %fusion.116), channel_id=1, source_target_pairs={{0,1},{1,0},{2,3},{3,2},{4,5},{5,4},{6,7},{7,6},{8,9},{9,8},{10,11... | collective-permute-start | bytes 147464 | tf_op jit(solution)/shard_map/ppermute | solution.py:104
  78.1 6.8 %collective-permute-start.12 = (f32[48,256]{1,0:T(8,128)S(1)}, f32[48,256]{1,0:T(8,128)S(1)}, u32[]{:S(2)}, u32[]{:S(2)}) collective-permute-start(f32[48,256]{1,0:T(8,128)S(1)} %fusion.116), channel_id=1, source_target_pairs={{0,2},{1,3},{2,0},{3,1},{4,6},{5,7},{6,4},{7,5},{8,10},{9,11},{10,... | collective-permute-start | bytes 147464 | tf_op jit(solution)/shard_map/ppermute | solution.py:104
  79.7 8.4 %collective-permute-start.13 = (f32[48,256]{1,0:T(8,128)S(1)}, f32[48,256]{1,0:T(8,128)S(1)}, u32[]{:S(2)}, u32[]{:S(2)}) collective-permute-start(f32[48,256]{1,0:T(8,128)S(1)} %fusion.116), channel_id=1, source_target_pairs={{0,3},{1,2},{2,1},{3,0},{4,7},{5,6},{6,5},{7,4},{8,11},{9,10},{10,... | collective-permute-start | bytes 147464 | tf_op jit(solution)/shard_map/ppermute | solution.py:104
  88.1 4.0 %collective-permute-start.14 = (f32[48,256]{1,0:T(8,128)S(1)}, f32[48,256]{1,0:T(8,128)S(1)}, u32[]{:S(2)}, u32[]{:S(2)}) collective-permute-start(f32[48,256]{1,0:T(8,128)S(1)} %fusion.115), channel_id=1, source_target_pairs={{0,4},{1,5},{2,6},{3,7},{4,0},{5,1},{6,2},{7,3},{8,12},{9,13},{10,... | collective-permute-start | bytes 147464 | tf_op jit(solution)/shard_map/ppermute | solution.py:112
  88.2 4.8 %collective-permute-start.15 = (f32[48,256]{1,0:T(8,128)S(1)}, f32[48,256]{1,0:T(8,128)S(1)}, u32[]{:S(2)}, u32[]{:S(2)}) collective-permute-start(f32[48,256]{1,0:T(8,128)S(1)} %fusion.115), channel_id=1, source_target_pairs={{0,8},{1,9},{2,10},{3,11},{4,12},{5,13},{6,14},{7,15},{8,0},{9,1},... | collective-permute-start | bytes 147464 | tf_op jit(solution)/shard_map/ppermute | solution.py:112
  90.2 4.2 %collective-permute-start.16 = (f32[48,256]{1,0:T(8,128)S(1)}, f32[48,256]{1,0:T(8,128)S(1)}, u32[]{:S(2)}, u32[]{:S(2)}) collective-permute-start(f32[48,256]{1,0:T(8,128)S(1)} %fusion.115), channel_id=1, source_target_pairs={{0,12},{1,13},{2,14},{3,15},{4,8},{5,9},{6,10},{7,11},{8,4},{9,5},... | collective-permute-start | bytes 147464 | tf_op jit(solution)/shard_map/ppermute | solution.py:112
  95.0 4.6 %collective-permute-start.17 = (f32[192,256]{1,0:T(8,128)S(1)}, f32[192,256]{1,0:T(8,128)S(1)}, u32[]{:S(2)}, u32[]{:S(2)}) collective-permute-start(f32[192,256]{1,0:T(8,128)S(1)} %bitcast_select_fusion), channel_id=1, source_target_pairs={{0,16},{16,0},{32,48},{48,32},{64,80},{80,64},{96,112},{112,96},{1... | collective-permute-start | bytes 589832 | tf_op jit(solution)/shard_map/ppermute | solution.py:112
  95.1 8.3 %collective-permute-start.18 = (f32[192,256]{1,0:T(8,128)S(1)}, f32[192,256]{1,0:T(8,128)S(1)}, u32[]{:S(2)}, u32[]{:S(2)}) collective-permute-start(f32[192,256]{1,0:T(8,128)S(1)} %bitcast_select_fusion), channel_id=1, source_target_pairs={{0,32},{16,48},{32,0},{48,16},{64,96},{80,112},{96,64},{112,80},{1... | collective-permute-start | bytes 589832 | tf_op jit(solution)/shard_map/ppermute | solution.py:112
  96.5 10.3 %collective-permute-start.19 = (f32[192,256]{1,0:T(8,128)S(1)}, f32[192,256]{1,0:T(8,128)S(1)}, u32[]{:S(2)}, u32[]{:S(2)}) collective-permute-start(f32[192,256]{1,0:T(8,128)S(1)} %bitcast_select_fusion), channel_id=1, source_target_pairs={{0,48},{16,32},{32,16},{48,0},{64,112},{80,96},{96,80},{112,64},{1... | collective-permute-start | bytes 589832 | tf_op jit(solution)/shard_map/ppermute | solution.py:112
  (1 other events, 1.0 us)

commit v10 on v9

--- a/solution.py
+++ b/solution.py
@@ -76,7 +76,7 @@
 
 def exchange_groups():
     groups = []
-    for axis, shift, radix in (("dp", 0, 4), ("seq", 2, 4), ("dp", 2, 4), ("seq", 0, 4)):
+    for axis, shift, radix in (("dp", 0, 4), ("seq", 2, 4), ("dp", 2, 4), ("seq", 0, 2), ("seq", 1, 2)):
         if (radix << shift) <= lax.axis_size(axis):
             groups.append((axis, shift, radix))
     return groups

time: 112 us -> 111 us (level)
  starting transfers between devices: 43.9 us -> 40 us
  waiting for transfers between devices: 34.1 us -> 36.8 us
    ppermute x12 -> x11, starting transfers between devices: 22.6 us -> 18.6 us  [butterfly_sum(): lax.ppermute(rows, axis, partner_pairs(axis, shift, offset))]
    ppermute x12 -> x11, waiting for transfers between devices: 18.9 us -> 21.4 us  [butterfly_sum(): lax.ppermute(rows, axis, partner_pairs(axis, shift, offset))]
  transfers between devices with their start and end apart: 20 -> 19, of which waited for: 15 -> 15; matrix products, arithmetic and copies ran while one was open for 4% -> 4% of each run, Pallas kernels for 0% -> 0%
where the time goes in v10:
time: 111 us; the launch traced here: 110 us
  starting transfers between devices  40 us (36%)
  waiting for transfers between devices  36.8 us (33%)
  matrix products  15.5 us (14%)
  other arithmetic  8.96 us (8%)
  local copies, waits for them, and re-layouts  7.67 us (7%)
  between operations  1.25 us (1%)
    ppermute x11, waiting for transfers between devices, butterfly_sum(): lax.ppermute(rows, axis, partner_pairs(axis, shift, offset))  21.4 us
    ppermute x11, starting transfers between devices, butterfly_sum(): lax.ppermute(rows, axis, partner_pairs(axis, shift, offset))  18.6 us
    ppermute x6, waiting for transfers between devices, butterfly_sum(): total = total + lax.ppermute(sent, axis, partner_pairs(axis, shift, offset))  11.8 us
    ppermute x1, starting transfers between devices, local(): lax.ppermute(tail, 'seq', [(i, i + 1) for i in range(count - 1)])  10.2 us
    ppermute x6, starting transfers between devices, butterfly_sum(): total = total + lax.ppermute(sent, axis, partner_pairs(axis, shift, offset))  9.21 us
    dot_general x4, matrix products, product(): jnp.dot(stacked.reshape(-1, shape_in[-1]), matrix, preferred_element_type...  6.19 us
    ppermute x1, waiting for transfers between devices, local(): lax.ppermute(head, 'seq', [(i + 1, i) for i in range(count - 1)])  3.55 us
    unnamed x13, local copies, waits for them, and re-layouts  3.14 us
  transfers between devices with their start and end apart: 19, of which 15 were waited for; matrix products, arithmetic and copies ran while one was open for 4% of the time, Pallas kernels for 0%

profile of v10, /device:TPU:1, one launch (start us, length us, event | category | flops | bytes accessed | tf_op | source)
XLA Modules:
  0.0 110.1 jit_solution(16243392986175327052)
XLA Ops:
  2.2 10.2 %collective-permute-start = (bf16[1,17,256]{2,1,0:T(8,128)(2,1)S(1)}, bf16[1,17,256]{2,1,0:T(8,128)(2,1)S(1)}, u32[]{:S(2)}, u32[]{:S(2)}) collective-permute-start(bf16[1,17,256]{2,1,0:T(8,128)(2,1)S(1)} %pad_maximum_fusion.5), channel_id=1, source_target_pairs={{0,1},{1,2},{2,3},{3,4},{4,5},{5,6},{6,7},{7,8},{8,9},{9,10},{10,1... | collective-permute-start | bytes 26120 | tf_op jit(solution)/shard_map/ppermute | solution.py:246
  13.1 1.9 %collective-permute-start.1 = (bf16[1,17,256]{2,1,0:T(8,128)(2,1)S(1)}, bf16[1,17,256]{2,1,0:T(8,128)(2,1)S(1)}, u32[]{:S(2)}, u32[]{:S(2)}) collective-permute-start(bf16[1,17,256]{2,1,0:T(8,128)(2,1)S(1)} %pad_maximum_fusion.6), channel_id=1, source_target_pairs={{1,0},{2,1},{3,2},{4,3},{5,4},{6,5},{7,6},{8,7},{9,8},{10,9},{11,1... | collective-permute-start | bytes 26120 | tf_op jit(solution)/shard_map/ppermute | solution.py:247
  18.5 3.5 %collective-permute-done.1 = bf16[1,17,256]{2,1,0:T(8,128)(2,1)S(1)} collective-permute-done((bf16[1,17,256]{2,1,0:T(8,128)(2,1)S(1)}, bf16[1,17,256]{2,1,0:T(8,128)(2,1)S(1)}, u32[]{:S(2)}, u32[]{:S(2)}) %collective-permute-start.1) | collective-permute-done | bytes 8736 | tf_op jit(solution)/shard_map/ppermute | solution.py:247
  23.9 1.8 %convolution_bitcast_fusion.1 = f32[1,2112,512]{2,1,0:T(8,128)S(1)} fusion(bf16[1,2112,256]{2,1,0:T(8,128)(2,1)S(1)} %get-tuple-element.14, bf16[1,2112,256]{2,1,0:T(8,128)(2,1)S(1)} %get-tuple-element.15, bf16[1,2112,256]{2,1,0:T(8,128)(2,1)S(1)} %get-tuple-element.13, bf16[768,256]{1,0:T(8,128)(2,1)S(1)} %bitcast.203, bf16[768,256]{1,0:T(8,128)(2,1)S(1)} %bitcast.202), kind=kOutput, calls=%fused_computation.3 | convolution fusion | flops 1672249344 | bytes 8355840 | tf_op jit(solution)/shard_map/dot_general | solution.py:40
  28.0 1.9 %convolution_bitcast_fusion = f32[1,2080,512]{2,1,0:T(8,128)S(1)} fusion(bf16[1,2080,256]{2,1,0:T(8,128)(2,1)S(1)} %get-tuple-element.17, bf16[1,2080,256]{2,1,0:T(8,128)(2,1)S(1)} %get-tuple-element.18, bf16[1,2080,256]{2,1,0:T(8,128)(2,1)S(1)} %get-tuple-element.16, bf16[768,256]{1,0:T(8,128)(2,1)S(1)} %bitcast.184, bf16[768,256]{1,0:T(8,128)(2,1)S(1)} %bitcast.181), kind=kOutput, calls=%fused_computation.2 | convolution fusion | flops 1646936064 | bytes 8241152 | tf_op jit(solution)/shard_map/dot_general | solution.py:40
  34.0 1.8 %convolution_bitcast_fusion.2 = f32[1,2048,512]{2,1,0:T(8,128)S(1)} fusion(bf16[1,2048,256]{2,1,0:T(8,128)(2,1)S(1)} %get-tuple-element.20, bf16[1,2048,256]{2,1,0:T(8,128)(2,1)S(1)} %get-tuple-element.21, bf16[1,2048,256]{2,1,0:T(8,128)(2,1)S(1)} %get-tuple-element.19, bf16[768,256]{1,0:T(8,128)(2,1)S(1)} %bitcast.185, bf16[768,256]{1,0:T(8,128)(2,1)S(1)} %bitcast.182), kind=kOutput, calls=%fused_computation.10 | convolution fusion | flops 1621622784 | bytes 8126464 | tf_op jit(solution)/shard_map/dot_general | solution.py:40
  35.8 2.8 %fusion.39 = (bf16[1,2048,256]{2,1,0:T(8,128)(2,1)S(1)}, bf16[1,2048,256]{2,1,0:T(8,128)(2,1)}) fusion(f32[1,2048,512]{2,1,0:T(8,128)S(1)} %convolution_bitcast_fusion.2, f32[1,2112,256]{2,1,0:T(8,128)S(1)} %get-tuple-element.12, bf16[1,2048,256]{2,1,0:T(8,128)(2,1)S(1)} %copy-done.1, f32[1,2080,256]{2,1,0:T(8,128)S(1)} %add_multiply_fusion, ...), kind=kLoop, calls=%fused_computation.61 | loop fusion | flops 14155776 | bytes 14680064 | tf_op jit(solution)/shard_map/convert_element_type | solution.py:285
  44.3 2.5 %collective-permute-start.3 = (f32[192,256]{1,0:T(8,128)S(1)}, f32[192,256]{1,0:T(8,128)S(1)}, u32[]{:S(2)}, u32[]{:S(2)}) collective-permute-start(f32[192,256]{1,0:T(8,128)S(1)} %get-tuple-element.28), channel_id=1, source_target_pairs={{0,32},{16,48},{32,0},{48,16},{64,96},{80,112},{96,64},{112,80},{1... | collective-permute-start | bytes 589832 | tf_op jit(solution)/shard_map/ppermute | solution.py:99
  48.0 4.1 %collective-permute-done.3 = f32[192,256]{1,0:T(8,128)S(1)} collective-permute-done((f32[192,256]{1,0:T(8,128)S(1)}, f32[192,256]{1,0:T(8,128)S(1)}, u32[]{:S(2)}, u32[]{:S(2)}) %collective-permute-start.3) | collective-permute-done | bytes 196640 | tf_op jit(solution)/shard_map/ppermute | solution.py:99
  52.1 2.0 %collective-permute-done.4 = f32[192,256]{1,0:T(8,128)S(1)} collective-permute-done((f32[192,256]{1,0:T(8,128)S(1)}, f32[192,256]{1,0:T(8,128)S(1)}, u32[]{:S(2)}, u32[]{:S(2)}) %collective-permute-start.4) | collective-permute-done | bytes 196640 | tf_op jit(solution)/shard_map/ppermute | solution.py:99
  54.1 2.3 %collective-permute-start.5 = (f32[48,256]{1,0:T(8,128)S(1)}, f32[48,256]{1,0:T(8,128)S(1)}, u32[]{:S(2)}, u32[]{:S(2)}) collective-permute-start(f32[48,256]{1,0:T(8,128)S(1)} %get-tuple-element.35), channel_id=1, source_target_pairs={{0,4},{1,5},{2,6},{3,7},{4,0},{5,1},{6,2},{7,3},{8,12},{9,13},{10,... | collective-permute-start | bytes 147464 | tf_op jit(solution)/shard_map/ppermute | solution.py:99
  56.4 2.9 %collective-permute-start.6 = (f32[48,256]{1,0:T(8,128)S(1)}, f32[48,256]{1,0:T(8,128)S(1)}, u32[]{:S(2)}, u32[]{:S(2)}) collective-permute-start(f32[48,256]{1,0:T(8,128)S(1)} %get-tuple-element.37), channel_id=1, source_target_pairs={{0,8},{1,9},{2,10},{3,11},{4,12},{5,13},{6,14},{7,15},{8,0},{9,1},... | collective-permute-start | bytes 147464 | tf_op jit(solution)/shard_map/ppermute | solution.py:99
  59.4 2.6 %collective-permute-done.6 = f32[48,256]{1,0:T(8,128)S(1)} collective-permute-done((f32[48,256]{1,0:T(8,128)S(1)}, f32[48,256]{1,0:T(8,128)S(1)}, u32[]{:S(2)}, u32[]{:S(2)}) %collective-permute-start.6) | collective-permute-done | bytes 49184 | tf_op jit(solution)/shard_map/ppermute | solution.py:99
  62.0 2.3 %collective-permute-done.7 = f32[48,256]{1,0:T(8,128)S(1)} collective-permute-done((f32[48,256]{1,0:T(8,128)S(1)}, f32[48,256]{1,0:T(8,128)S(1)}, u32[]{:S(2)}, u32[]{:S(2)}) %collective-permute-start.7) | collective-permute-done | bytes 49184 | tf_op jit(solution)/shard_map/ppermute | solution.py:99
  65.3 4.0 %collective-permute-start.9 = (f32[48,256]{1,0:T(8,128)S(1)}, f32[48,256]{1,0:T(8,128)S(1)}, u32[]{:S(2)}, u32[]{:S(2)}) collective-permute-start(f32[48,256]{1,0:T(8,128)S(1)} %add_add_fusion.1), channel_id=1, source_target_pairs={{0,128},{16,144},{32,160},{48,176},{64,192},{80,208},{96,224},{112... | collective-permute-start | bytes 147464 | tf_op jit(solution)/shard_map/ppermute | solution.py:104
  69.3 2.0 %collective-permute-done.9 = f32[48,256]{1,0:T(8,128)S(1)} collective-permute-done((f32[48,256]{1,0:T(8,128)S(1)}, f32[48,256]{1,0:T(8,128)S(1)}, u32[]{:S(2)}, u32[]{:S(2)}) %collective-permute-start.9) | collective-permute-done | bytes 49184 | tf_op jit(solution)/shard_map/ppermute | solution.py:104
  71.3 2.7 %collective-permute-done.10 = f32[48,256]{1,0:T(8,128)S(1)} collective-permute-done((f32[48,256]{1,0:T(8,128)S(1)}, f32[48,256]{1,0:T(8,128)S(1)}, u32[]{:S(2)}, u32[]{:S(2)}) %collective-permute-start.10) | collective-permute-done | bytes 49184 | tf_op jit(solution)/shard_map/ppermute | solution.py:104
  74.1 3.9 %collective-permute-start.11 = (f32[48,256]{1,0:T(8,128)S(1)}, f32[48,256]{1,0:T(8,128)S(1)}, u32[]{:S(2)}, u32[]{:S(2)}) collective-permute-start(f32[48,256]{1,0:T(8,128)S(1)} %fusion.121), channel_id=1, source_target_pairs={{0,1},{1,0},{2,3},{3,2},{4,5},{5,4},{6,7},{7,6},{8,9},{9,8},{10,11... | collective-permute-start | bytes 147464 | tf_op jit(solution)/shard_map/ppermute | solution.py:104
  80.7 5.1 %collective-permute-done.12 = f32[48,256]{1,0:T(8,128)S(1)} collective-permute-done((f32[48,256]{1,0:T(8,128)S(1)}, f32[48,256]{1,0:T(8,128)S(1)}, u32[]{:S(2)}, u32[]{:S(2)}) %collective-permute-start.12) | collective-permute-done | bytes 49184 | tf_op jit(solution)/shard_map/ppermute | solution.py:104
  86.0 2.4 %collective-permute-start.14 = (f32[48,256]{1,0:T(8,128)S(1)}, f32[48,256]{1,0:T(8,128)S(1)}, u32[]{:S(2)}, u32[]{:S(2)}) collective-permute-start(f32[48,256]{1,0:T(8,128)S(1)} %bitcast.190), channel_id=1, source_target_pairs={{0,8},{1,9},{2,10},{3,11},{4,12},{5,13},{6,14},{7,15},{8,0},{9,1},... | collective-permute-start | bytes 147464 | tf_op jit(solution)/shard_map/ppermute | solution.py:112
  90.6 2.4 %collective-permute-done.15 = f32[48,256]{1,0:T(8,128)S(1)} collective-permute-done((f32[48,256]{1,0:T(8,128)S(1)}, f32[48,256]{1,0:T(8,128)S(1)}, u32[]{:S(2)}, u32[]{:S(2)}) %collective-permute-start.15) | collective-permute-done | bytes 49184 | tf_op jit(solution)/shard_map/ppermute | solution.py:112
  95.1 2.6 %collective-permute-start.18 = (f32[192,256]{1,0:T(8,128)S(1)}, f32[192,256]{1,0:T(8,128)S(1)}, u32[]{:S(2)}, u32[]{:S(2)}) collective-permute-start(f32[192,256]{1,0:T(8,128)S(1)} %bitcast_select_fusion), channel_id=1, source_target_pairs={{0,48},{16,32},{32,16},{48,0},{64,112},{80,96},{96,80},{112,64},{1... | collective-permute-start | bytes 589832 | tf_op jit(solution)/shard_map/ppermute | solution.py:112
  98.3 3.7 %collective-permute-done.17 = f32[192,256]{1,0:T(8,128)S(1)} collective-permute-done((f32[192,256]{1,0:T(8,128)S(1)}, f32[192,256]{1,0:T(8,128)S(1)}, u32[]{:S(2)}, u32[]{:S(2)}) %collective-permute-start.17) | collective-permute-done | bytes 196640 | tf_op jit(solution)/shard_map/ppermute | solution.py:112
  101.9 3.5 %collective-permute-done.18 = f32[192,256]{1,0:T(8,128)S(1)} collective-permute-done((f32[192,256]{1,0:T(8,128)S(1)}, f32[192,256]{1,0:T(8,128)S(1)}, u32[]{:S(2)}, u32[]{:S(2)}) %collective-permute-start.18) | collective-permute-done | bytes 196640 | tf_op jit(solution)/shard_map/ppermute | solution.py:112
  (113 shorter events, 34.1 us)
Async XLA Ops:
  0.6 21.6 %copy-start = (bf16[4,256]{1,0:T(4,128)(2,1)S(1)}, bf16[4,256]{1,0:T(4,128)(2,1)}, u32[]{:S(2)}) copy-start(bf16[4,256]{1,0:T(4,128)(2,1)} %param.6) | copy-start | bytes 6148
  0.6 21.4 %copy-start.3 = (s32[1,2048]{1,0:T(1,128)S(1)}, s32[1,2048]{1,0:T(1,128)}, u32[]{:S(2)}) copy-start(s32[1,2048]{1,0:T(1,128)} %param.5) | copy-start | bytes 24580
  0.7 17.4 %copy-start.2 = (bf16[3,256,256]{2,1,0:T(8,128)(2,1)S(1)}, bf16[3,256,256]{2,1,0:T(8,128)(2,1)}, u32[]{:S(2)}) copy-start(bf16[3,256,256]{2,1,0:T(8,128)(2,1)} %param.8) | copy-start | bytes 1179652
  2.2 16.3 %collective-permute-start = (bf16[1,17,256]{2,1,0:T(8,128)(2,1)S(1)}, bf16[1,17,256]{2,1,0:T(8,128)(2,1)S(1)}, u32[]{:S(2)}, u32[]{:S(2)}) collective-permute-start(bf16[1,17,256]{2,1,0:T(8,128)(2,1)S(1)} %pad_maximum_fusion.5), channel_id=1, source_target_pairs={{0,1},{1,2},{2,3},{3,4},{4,5},{5,6},{6,7},{7,8},{8,9},{9,10},{10,1... | collective-permute-start | bytes 26120 | tf_op jit(solution)/shard_map/ppermute | solution.py:246
  13.1 8.9 %collective-permute-start.1 = (bf16[1,17,256]{2,1,0:T(8,128)(2,1)S(1)}, bf16[1,17,256]{2,1,0:T(8,128)(2,1)S(1)}, u32[]{:S(2)}, u32[]{:S(2)}) collective-permute-start(bf16[1,17,256]{2,1,0:T(8,128)(2,1)S(1)} %pad_maximum_fusion.6), channel_id=1, source_target_pairs={{1,0},{2,1},{3,2},{4,3},{5,4},{6,5},{7,6},{8,7},{9,8},{10,9},{11,1... | collective-permute-start | bytes 26120 | tf_op jit(solution)/shard_map/ppermute | solution.py:247
  22.9 1.0 copy-start.4
  28.0 1.9 %copy-start.1 = (bf16[1,2048,256]{2,1,0:T(8,128)(2,1)S(1)}, bf16[1,2048,256]{2,1,0:T(8,128)(2,1)}, u32[]{:S(2)}) copy-start(bf16[1,2048,256]{2,1,0:T(8,128)(2,1)} %param.9) | copy-start | bytes 3145732
  43.1 4.9 %collective-permute-start.2 = (f32[192,256]{1,0:T(8,128)S(1)}, f32[192,256]{1,0:T(8,128)S(1)}, u32[]{:S(2)}, u32[]{:S(2)}) collective-permute-start(f32[192,256]{1,0:T(8,128)S(1)} %get-tuple-element.26), channel_id=1, source_target_pairs={{0,16},{16,0},{32,48},{48,32},{64,80},{80,64},{96,112},{112,96},{1... | collective-permute-start | bytes 589832 | tf_op jit(solution)/shard_map/ppermute | solution.py:99
  44.3 7.7 %collective-permute-start.3 = (f32[192,256]{1,0:T(8,128)S(1)}, f32[192,256]{1,0:T(8,128)S(1)}, u32[]{:S(2)}, u32[]{:S(2)}) collective-permute-start(f32[192,256]{1,0:T(8,128)S(1)} %get-tuple-element.28), channel_id=1, source_target_pairs={{0,32},{16,48},{32,0},{48,16},{64,96},{80,112},{96,64},{112,80},{1... | collective-permute-start | bytes 589832 | tf_op jit(solution)/shard_map/ppermute | solution.py:99
  46.8 7.3 %collective-permute-start.4 = (f32[192,256]{1,0:T(8,128)S(1)}, f32[192,256]{1,0:T(8,128)S(1)}, u32[]{:S(2)}, u32[]{:S(2)}) collective-permute-start(f32[192,256]{1,0:T(8,128)S(1)} %get-tuple-element.27), channel_id=1, source_target_pairs={{0,48},{16,32},{32,16},{48,0},{64,112},{80,96},{96,80},{112,64},{1... | collective-permute-start | bytes 589832 | tf_op jit(solution)/shard_map/ppermute | solution.py:99
  54.1 5.2 %collective-permute-start.5 = (f32[48,256]{1,0:T(8,128)S(1)}, f32[48,256]{1,0:T(8,128)S(1)}, u32[]{:S(2)}, u32[]{:S(2)}) collective-permute-start(f32[48,256]{1,0:T(8,128)S(1)} %get-tuple-element.35), channel_id=1, source_target_pairs={{0,4},{1,5},{2,6},{3,7},{4,0},{5,1},{6,2},{7,3},{8,12},{9,13},{10,... | collective-permute-start | bytes 147464 | tf_op jit(solution)/shard_map/ppermute | solution.py:99
  56.4 5.5 %collective-permute-start.6 = (f32[48,256]{1,0:T(8,128)S(1)}, f32[48,256]{1,0:T(8,128)S(1)}, u32[]{:S(2)}, u32[]{:S(2)}) collective-permute-start(f32[48,256]{1,0:T(8,128)S(1)} %get-tuple-element.37), channel_id=1, source_target_pairs={{0,8},{1,9},{2,10},{3,11},{4,12},{5,13},{6,14},{7,15},{8,0},{9,1},... | collective-permute-start | bytes 147464 | tf_op jit(solution)/shard_map/ppermute | solution.py:99
  59.4 4.9 %collective-permute-start.7 = (f32[48,256]{1,0:T(8,128)S(1)}, f32[48,256]{1,0:T(8,128)S(1)}, u32[]{:S(2)}, u32[]{:S(2)}) collective-permute-start(f32[48,256]{1,0:T(8,128)S(1)} %get-tuple-element.36), channel_id=1, source_target_pairs={{0,12},{1,13},{2,14},{3,15},{4,8},{5,9},{6,10},{7,11},{8,4},{9,5},... | collective-permute-start | bytes 147464 | tf_op jit(solution)/shard_map/ppermute | solution.py:99
  64.2 5.1 %collective-permute-start.8 = (f32[48,256]{1,0:T(8,128)S(1)}, f32[48,256]{1,0:T(8,128)S(1)}, u32[]{:S(2)}, u32[]{:S(2)}) collective-permute-start(f32[48,256]{1,0:T(8,128)S(1)} %add_add_fusion.1), channel_id=1, source_target_pairs={{0,64},{16,80},{32,96},{48,112},{64,0},{80,16},{96,32},{112,48},{1... | collective-permute-start | bytes 147464 | tf_op jit(solution)/shard_map/ppermute | solution.py:104
  65.3 6.0 %collective-permute-start.9 = (f32[48,256]{1,0:T(8,128)S(1)}, f32[48,256]{1,0:T(8,128)S(1)}, u32[]{:S(2)}, u32[]{:S(2)}) collective-permute-start(f32[48,256]{1,0:T(8,128)S(1)} %add_add_fusion.1), channel_id=1, source_target_pairs={{0,128},{16,144},{32,160},{48,176},{64,192},{80,208},{96,224},{112... | collective-permute-start | bytes 147464 | tf_op jit(solution)/shard_map/ppermute | solution.py:104
  69.3 4.7 %collective-permute-start.10 = (f32[48,256]{1,0:T(8,128)S(1)}, f32[48,256]{1,0:T(8,128)S(1)}, u32[]{:S(2)}, u32[]{:S(2)}) collective-permute-start(f32[48,256]{1,0:T(8,128)S(1)} %add_add_fusion.1), channel_id=1, source_target_pairs={{0,192},{16,208},{32,224},{48,240},{64,128},{80,144},{96,160},{112... | collective-permute-start | bytes 147464 | tf_op jit(solution)/shard_map/ppermute | solution.py:104
  74.1 4.8 %collective-permute-start.11 = (f32[48,256]{1,0:T(8,128)S(1)}, f32[48,256]{1,0:T(8,128)S(1)}, u32[]{:S(2)}, u32[]{:S(2)}) collective-permute-start(f32[48,256]{1,0:T(8,128)S(1)} %fusion.121), channel_id=1, source_target_pairs={{0,1},{1,0},{2,3},{3,2},{4,5},{5,4},{6,7},{7,6},{8,9},{9,8},{10,11... | collective-permute-start | bytes 147464 | tf_op jit(solution)/shard_map/ppermute | solution.py:104
  78.9 6.9 %collective-permute-start.12 = (f32[48,256]{1,0:T(8,128)S(1)}, f32[48,256]{1,0:T(8,128)S(1)}, u32[]{:S(2)}, u32[]{:S(2)}) collective-permute-start(f32[48,256]{1,0:T(8,128)S(1)} %bitcast.193), channel_id=1, source_target_pairs={{0,2},{1,3},{2,0},{3,1},{4,6},{5,7},{6,4},{7,5},{8,10},{9,11},{10,... | collective-permute-start | bytes 147464 | tf_op jit(solution)/shard_map/ppermute | solution.py:104
  85.9 4.1 %collective-permute-start.13 = (f32[48,256]{1,0:T(8,128)S(1)}, f32[48,256]{1,0:T(8,128)S(1)}, u32[]{:S(2)}, u32[]{:S(2)}) collective-permute-start(f32[48,256]{1,0:T(8,128)S(1)} %bitcast.189), channel_id=1, source_target_pairs={{0,4},{1,5},{2,6},{3,7},{4,0},{5,1},{6,2},{7,3},{8,12},{9,13},{10,... | collective-permute-start | bytes 147464 | tf_op jit(solution)/shard_map/ppermute | solution.py:112
  86.0 4.6 %collective-permute-start.14 = (f32[48,256]{1,0:T(8,128)S(1)}, f32[48,256]{1,0:T(8,128)S(1)}, u32[]{:S(2)}, u32[]{:S(2)}) collective-permute-start(f32[48,256]{1,0:T(8,128)S(1)} %bitcast.190), channel_id=1, source_target_pairs={{0,8},{1,9},{2,10},{3,11},{4,12},{5,13},{6,14},{7,15},{8,0},{9,1},... | collective-permute-start | bytes 147464 | tf_op jit(solution)/shard_map/ppermute | solution.py:112
  88.3 4.7 %collective-permute-start.15 = (f32[48,256]{1,0:T(8,128)S(1)}, f32[48,256]{1,0:T(8,128)S(1)}, u32[]{:S(2)}, u32[]{:S(2)}) collective-permute-start(f32[48,256]{1,0:T(8,128)S(1)} %bitcast.191), channel_id=1, source_target_pairs={{0,12},{1,13},{2,14},{3,15},{4,8},{5,9},{6,10},{7,11},{8,4},{9,5},... | collective-permute-start | bytes 147464 | tf_op jit(solution)/shard_map/ppermute | solution.py:112
  93.7 4.6 %collective-permute-start.16 = (f32[192,256]{1,0:T(8,128)S(1)}, f32[192,256]{1,0:T(8,128)S(1)}, u32[]{:S(2)}, u32[]{:S(2)}) collective-permute-start(f32[192,256]{1,0:T(8,128)S(1)} %bitcast_select_fusion), channel_id=1, source_target_pairs={{0,16},{16,0},{32,48},{48,32},{64,80},{80,64},{96,112},{112,96},{1... | collective-permute-start | bytes 589832 | tf_op jit(solution)/shard_map/ppermute | solution.py:112
  93.8 8.2 %collective-permute-start.17 = (f32[192,256]{1,0:T(8,128)S(1)}, f32[192,256]{1,0:T(8,128)S(1)}, u32[]{:S(2)}, u32[]{:S(2)}) collective-permute-start(f32[192,256]{1,0:T(8,128)S(1)} %bitcast_select_fusion), channel_id=1, source_target_pairs={{0,32},{16,48},{32,0},{48,16},{64,96},{80,112},{96,64},{112,80},{1... | collective-permute-start | bytes 589832 | tf_op jit(solution)/shard_map/ppermute | solution.py:112
  95.1 10.4 %collective-permute-start.18 = (f32[192,256]{1,0:T(8,128)S(1)}, f32[192,256]{1,0:T(8,128)S(1)}, u32[]{:S(2)}, u32[]{:S(2)}) collective-permute-start(f32[192,256]{1,0:T(8,128)S(1)} %bitcast_select_fusion), channel_id=1, source_target_pairs={{0,48},{16,32},{32,16},{48,0},{64,112},{80,96},{96,80},{112,64},{1... | collective-permute-start | bytes 589832 | tf_op jit(solution)/shard_map/ppermute | solution.py:112

commit v11 on v10

--- a/solution.py
+++ b/solution.py
@@ -143,10 +143,10 @@
 def unfolded_halves(first, second):
     rows, channels = first.shape
     half = rows // 3
-    total = butterfly_sum(jnp.concatenate([first, second], axis=0))
+    totals = [butterfly_sum(first), butterfly_sum(second)]
     outs = []
     for i in range(2):
-        part = total[i * rows : (i + 1) * rows]
+        part = totals[i]
         taps = [part[k * half : (k + 1) * half].T for k in range(3)]
         outs.append(jnp.stack([jnp.concatenate([taps[k], taps[2 - k][::-1, ::-1]], axis=1) for k in range(3)]))
     return outs

time: 111 us -> 115 us (1.036)
  starting transfers between devices: 40 us -> 63.2 us
  waiting for transfers between devices: 36.8 us -> 16 us
    ppermute x11 -> x22, starting transfers between devices: 18.6 us -> 35.3 us  [butterfly_sum(): lax.ppermute(rows, axis, partner_pairs(axis, shift, offset))]
    ppermute x11 -> x22, waiting for transfers between devices: 21.4 us -> 10.4 us  [butterfly_sum(): lax.ppermute(rows, axis, partner_pairs(axis, shift, offset))]
    ppermute x6 -> x12, waiting for transfers between devices: 11.8 us -> 2.21 us  [butterfly_sum(): total = total + lax.ppermute(sent, axis, partner_pairs(axis, shift, offset))]
    ppermute x6 -> x12, starting transfers between devices: 9.21 us -> 15.8 us  [butterfly_sum(): total = total + lax.ppermute(sent, axis, partner_pairs(axis, shift, offset))]
  transfers between devices with their start and end apart: 19 -> 36, of which waited for: 15 -> 10; matrix products, arithmetic and copies ran while one was open for 4% -> 6% of each run, Pallas kernels for 0% -> 0%
where the time goes in v11:
time: 115 us; the launch traced here: 114 us
  starting transfers between devices  63.2 us (55%)
  waiting for transfers between devices  16 us (14%)
  matrix products  15.3 us (13%)
  other arithmetic  9.06 us (8%)
  local copies, waits for them, and re-layouts  8.57 us (7%)
  between operations  1.48 us (1%)
    ppermute x22, starting transfers between devices, butterfly_sum(): lax.ppermute(rows, axis, partner_pairs(axis, shift, offset))  35.3 us
    ppermute x12, starting transfers between devices, butterfly_sum(): total = total + lax.ppermute(sent, axis, partner_pairs(axis, shift, offset))  15.8 us
    ppermute x22, waiting for transfers between devices, butterfly_sum(): lax.ppermute(rows, axis, partner_pairs(axis, shift, offset))  10.4 us
    ppermute x1, starting transfers between devices, local(): lax.ppermute(tail, 'seq', [(i, i + 1) for i in range(count - 1)])  10.2 us
    dot_general x4, matrix products, product(): jnp.dot(stacked.reshape(-1, shape_in[-1]), matrix, preferred_element_type...  6.25 us
    ppermute x1, waiting for transfers between devices, local(): lax.ppermute(head, 'seq', [(i + 1, i) for i in range(count - 1)])  3.39 us
    unnamed x13, local copies, waits for them, and re-layouts  3.14 us
    dot_general x2, matrix products, mirrored_taps(): jnp.einsum('kab,bc->kac', left, anti, preferred_element_type=jnp.float32)  2.93 us
  transfers between devices with their start and end apart: 36, of which 10 were waited for; matrix products, arithmetic and copies ran while one was open for 6% of the time, Pallas kernels for 0%

profile of v11, /device:TPU:1, one launch (start us, length us, event | category | flops | bytes accessed | tf_op | source)
XLA Modules:
  0.0 113.7 jit_solution(9085800255698807754)
XLA Ops:
  2.2 10.2 %collective-permute-start = (bf16[1,17,256]{2,1,0:T(8,128)(2,1)S(1)}, bf16[1,17,256]{2,1,0:T(8,128)(2,1)S(1)}, u32[]{:S(2)}, u32[]{:S(2)}) collective-permute-start(bf16[1,17,256]{2,1,0:T(8,128)(2,1)S(1)} %pad_maximum_fusion.10), channel_id=1, source_target_pairs={{0,1},{1,2},{2,3},{3,4},{4,5},{5,6},{6,7},{7,8},{8,9},{9,10},{10,1... | collective-permute-start | bytes 26120 | tf_op jit(solution)/shard_map/ppermute | solution.py:246
  13.1 1.9 %collective-permute-start.1 = (bf16[1,17,256]{2,1,0:T(8,128)(2,1)S(1)}, bf16[1,17,256]{2,1,0:T(8,128)(2,1)S(1)}, u32[]{:S(2)}, u32[]{:S(2)}) collective-permute-start(bf16[1,17,256]{2,1,0:T(8,128)(2,1)S(1)} %pad_maximum_fusion.11), channel_id=1, source_target_pairs={{1,0},{2,1},{3,2},{4,3},{5,4},{6,5},{7,6},{8,7},{9,8},{10,9},{11,1... | collective-permute-start | bytes 26120 | tf_op jit(solution)/shard_map/ppermute | solution.py:247
  18.7 3.4 %collective-permute-done.1 = bf16[1,17,256]{2,1,0:T(8,128)(2,1)S(1)} collective-permute-done((bf16[1,17,256]{2,1,0:T(8,128)(2,1)S(1)}, bf16[1,17,256]{2,1,0:T(8,128)(2,1)S(1)}, u32[]{:S(2)}, u32[]{:S(2)}) %collective-permute-start.1) | collective-permute-done | bytes 8736 | tf_op jit(solution)/shard_map/ppermute | solution.py:247
  28.1 2.0 %convolution_bitcast_fusion = f32[1,2080,512]{2,1,0:T(8,128)S(1)} fusion(bf16[1,2080,256]{2,1,0:T(8,128)(2,1)S(1)} %get-tuple-element.19, bf16[1,2080,256]{2,1,0:T(8,128)(2,1)S(1)} %get-tuple-element.20, bf16[1,2080,256]{2,1,0:T(8,128)(2,1)S(1)} %get-tuple-element.18, bf16[768,256]{1,0:T(8,128)(2,1)S(1)} %bitcast.193, bf16[768,256]{1,0:T(8,128)(2,1)S(1)} %bitcast.191), kind=kOutput, calls=%fused_computation.4 | convolution fusion | flops 1646936064 | bytes 8241152 | tf_op jit(solution)/shard_map/dot_general | solution.py:40
  34.3 2.8 %fusion.39 = (bf16[1,2048,256]{2,1,0:T(8,128)(2,1)S(1)}, bf16[1,2048,256]{2,1,0:T(8,128)(2,1)}) fusion(f32[1,2048,512]{2,1,0:T(8,128)S(1)} %convolution_bitcast_fusion.2, f32[1,2112,256]{2,1,0:T(8,128)S(1)} %get-tuple-element.14, bf16[1,2048,256]{2,1,0:T(8,128)(2,1)S(1)} %copy-done.1, f32[1,2080,256]{2,1,0:T(8,128)S(1)} %add_multiply_fusion, ...), kind=kLoop, calls=%fused_computation.63 | loop fusion | flops 14155776 | bytes 14680064 | tf_op jit(solution)/shard_map/convert_element_type | solution.py:285
  43.2 2.4 %collective-permute-start.3 = (f32[96,256]{1,0:T(8,128)S(1)}, f32[96,256]{1,0:T(8,128)S(1)}, u32[]{:S(2)}, u32[]{:S(2)}) collective-permute-start(f32[96,256]{1,0:T(8,128)S(1)} %get-tuple-element.37), channel_id=1, source_target_pairs={{0,32},{16,48},{32,0},{48,16},{64,96},{80,112},{96,64},{112,80},{1... | collective-permute-start | bytes 294920 | tf_op jit(solution)/shard_map/ppermute | solution.py:99
  47.1 3.6 %collective-permute-start.20 = (f32[96,256]{1,0:T(8,128)S(1)}, f32[96,256]{1,0:T(8,128)S(1)}, u32[]{:S(2)}, u32[]{:S(2)}) collective-permute-start(f32[96,256]{1,0:T(8,128)S(1)} %get-tuple-element.31), channel_id=1, source_target_pairs={{0,32},{16,48},{32,0},{48,16},{64,96},{80,112},{96,64},{112,80},{1... | collective-permute-start | bytes 294920 | tf_op jit(solution)/shard_map/ppermute | solution.py:99
  51.0 2.2 %collective-permute-done.4 = f32[96,256]{1,0:T(8,128)S(1)} collective-permute-done((f32[96,256]{1,0:T(8,128)S(1)}, f32[96,256]{1,0:T(8,128)S(1)}, u32[]{:S(2)}, u32[]{:S(2)}) %collective-permute-start.4) | collective-permute-done | bytes 98336 | tf_op jit(solution)/shard_map/ppermute | solution.py:99
  53.3 1.9 %collective-permute-start.6 = (f32[24,256]{1,0:T(8,128)S(1)}, f32[24,256]{1,0:T(8,128)S(1)}, u32[]{:S(2)}, u32[]{:S(2)}) collective-permute-start(f32[24,256]{1,0:T(8,128)S(1)} %get-tuple-element.43), channel_id=1, source_target_pairs={{0,8},{1,9},{2,10},{3,11},{4,12},{5,13},{6,14},{7,15},{8,0},{9,1},... | collective-permute-start | bytes 73736 | tf_op jit(solution)/shard_map/ppermute | solution.py:99
  55.2 2.0 %collective-permute-start.7 = (f32[24,256]{1,0:T(8,128)S(1)}, f32[24,256]{1,0:T(8,128)S(1)}, u32[]{:S(2)}, u32[]{:S(2)}) collective-permute-start(f32[24,256]{1,0:T(8,128)S(1)} %get-tuple-element.42), channel_id=1, source_target_pairs={{0,12},{1,13},{2,14},{3,15},{4,8},{5,9},{6,10},{7,11},{8,4},{9,5},... | collective-permute-start | bytes 73736 | tf_op jit(solution)/shard_map/ppermute | solution.py:99
  57.3 2.8 %collective-permute-start.23 = (f32[24,256]{1,0:T(8,128)S(1)}, f32[24,256]{1,0:T(8,128)S(1)}, u32[]{:S(2)}, u32[]{:S(2)}) collective-permute-start(f32[24,256]{1,0:T(8,128)S(1)} %get-tuple-element.40), channel_id=1, source_target_pairs={{0,8},{1,9},{2,10},{3,11},{4,12},{5,13},{6,14},{7,15},{8,0},{9,1},... | collective-permute-start | bytes 73736 | tf_op jit(solution)/shard_map/ppermute | solution.py:99
  62.0 2.3 %collective-permute-start.9 = (f32[24,256]{1,0:T(8,128)S(1)}, f32[24,256]{1,0:T(8,128)S(1)}, u32[]{:S(2)}, u32[]{:S(2)}) collective-permute-start(f32[24,256]{1,0:T(8,128)S(1)} %add_add_fusion.3), channel_id=1, source_target_pairs={{0,128},{16,144},{32,160},{48,176},{64,192},{80,208},{96,224},{112... | collective-permute-start | bytes 73736 | tf_op jit(solution)/shard_map/ppermute | solution.py:104
  65.7 2.5 %collective-permute-start.26 = (f32[24,256]{1,0:T(8,128)S(1)}, f32[24,256]{1,0:T(8,128)S(1)}, u32[]{:S(2)}, u32[]{:S(2)}) collective-permute-start(f32[24,256]{1,0:T(8,128)S(1)} %add_add_fusion.2), channel_id=1, source_target_pairs={{0,128},{16,144},{32,160},{48,176},{64,192},{80,208},{96,224},{112... | collective-permute-start | bytes 73736 | tf_op jit(solution)/shard_map/ppermute | solution.py:104
  68.9 2.9 %collective-permute-start.11 = (f32[24,256]{1,0:T(8,128)S(1)}, f32[24,256]{1,0:T(8,128)S(1)}, u32[]{:S(2)}, u32[]{:S(2)}) collective-permute-start(f32[24,256]{1,0:T(8,128)S(1)} %fusion.118), channel_id=1, source_target_pairs={{0,1},{1,0},{2,3},{3,2},{4,5},{5,4},{6,7},{7,6},{8,9},{9,8},{10,11... | collective-permute-start | bytes 73736 | tf_op jit(solution)/shard_map/ppermute | solution.py:104
  72.7 4.0 %collective-permute-start.28 = (f32[24,256]{1,0:T(8,128)S(1)}, f32[24,256]{1,0:T(8,128)S(1)}, u32[]{:S(2)}, u32[]{:S(2)}) collective-permute-start(f32[24,256]{1,0:T(8,128)S(1)} %fusion.119), channel_id=1, source_target_pairs={{0,1},{1,0},{2,3},{3,2},{4,5},{5,4},{6,7},{7,6},{8,9},{9,8},{10,11... | collective-permute-start | bytes 73736 | tf_op jit(solution)/shard_map/ppermute | solution.py:104
  76.8 2.8 %collective-permute-start.12 = (f32[24,256]{1,0:T(8,128)S(1)}, f32[24,256]{1,0:T(8,128)S(1)}, u32[]{:S(2)}, u32[]{:S(2)}) collective-permute-start(f32[24,256]{1,0:T(8,128)S(1)} %bitcast.219), channel_id=1, source_target_pairs={{0,2},{1,3},{2,0},{3,1},{4,6},{5,7},{6,4},{7,5},{8,10},{9,11},{10,... | collective-permute-start | bytes 73736 | tf_op jit(solution)/shard_map/ppermute | solution.py:104
  79.6 2.7 %collective-permute-start.29 = (f32[24,256]{1,0:T(8,128)S(1)}, f32[24,256]{1,0:T(8,128)S(1)}, u32[]{:S(2)}, u32[]{:S(2)}) collective-permute-start(f32[24,256]{1,0:T(8,128)S(1)} %bitcast.218), channel_id=1, source_target_pairs={{0,2},{1,3},{2,0},{3,1},{4,6},{5,7},{6,4},{7,5},{8,10},{9,11},{10,... | collective-permute-start | bytes 73736 | tf_op jit(solution)/shard_map/ppermute | solution.py:104
  83.9 3.2 %collective-permute-start.14 = (f32[24,256]{1,0:T(8,128)S(1)}, f32[24,256]{1,0:T(8,128)S(1)}, u32[]{:S(2)}, u32[]{:S(2)}) collective-permute-start(f32[24,256]{1,0:T(8,128)S(1)} %bitcast.211), channel_id=1, source_target_pairs={{0,8},{1,9},{2,10},{3,11},{4,12},{5,13},{6,14},{7,15},{8,0},{9,1},... | collective-permute-start | bytes 73736 | tf_op jit(solution)/shard_map/ppermute | solution.py:112
  87.5 3.6 %collective-permute-start.31 = (f32[24,256]{1,0:T(8,128)S(1)}, f32[24,256]{1,0:T(8,128)S(1)}, u32[]{:S(2)}, u32[]{:S(2)}) collective-permute-start(f32[24,256]{1,0:T(8,128)S(1)} %bitcast.214), channel_id=1, source_target_pairs={{0,8},{1,9},{2,10},{3,11},{4,12},{5,13},{6,14},{7,15},{8,0},{9,1},... | collective-permute-start | bytes 73736 | tf_op jit(solution)/shard_map/ppermute | solution.py:112
  92.6 2.8 %collective-permute-done.32 = f32[24,256]{1,0:T(8,128)S(1)} collective-permute-done((f32[24,256]{1,0:T(8,128)S(1)}, f32[24,256]{1,0:T(8,128)S(1)}, u32[]{:S(2)}, u32[]{:S(2)}) %collective-permute-start.32) | collective-permute-done | bytes 24608 | tf_op jit(solution)/shard_map/ppermute | solution.py:112
  97.9 2.1 %collective-permute-start.18 = (f32[96,256]{1,0:T(8,128)S(1)}, f32[96,256]{1,0:T(8,128)S(1)}, u32[]{:S(2)}, u32[]{:S(2)}) collective-permute-start(f32[96,256]{1,0:T(8,128)S(1)} %bitcast.202), channel_id=1, source_target_pairs={{0,48},{16,32},{32,16},{48,0},{64,112},{80,96},{96,80},{112,64},{1... | collective-permute-start | bytes 294920 | tf_op jit(solution)/shard_map/ppermute | solution.py:112
  101.8 2.1 %collective-permute-start.35 = (f32[96,256]{1,0:T(8,128)S(1)}, f32[96,256]{1,0:T(8,128)S(1)}, u32[]{:S(2)}, u32[]{:S(2)}) collective-permute-start(f32[96,256]{1,0:T(8,128)S(1)} %bitcast.198), channel_id=1, source_target_pairs={{0,48},{16,32},{32,16},{48,0},{64,112},{80,96},{96,80},{112,64},{1... | collective-permute-start | bytes 294920 | tf_op jit(solution)/shard_map/ppermute | solution.py:112
  104.8 2.0 %collective-permute-done.34 = f32[96,256]{1,0:T(8,128)S(1)} collective-permute-done((f32[96,256]{1,0:T(8,128)S(1)}, f32[96,256]{1,0:T(8,128)S(1)}, u32[]{:S(2)}, u32[]{:S(2)}) %collective-permute-start.34) | collective-permute-done | bytes 98336 | tf_op jit(solution)/shard_map/ppermute | solution.py:112
  106.8 2.3 %collective-permute-done.35 = f32[96,256]{1,0:T(8,128)S(1)} collective-permute-done((f32[96,256]{1,0:T(8,128)S(1)}, f32[96,256]{1,0:T(8,128)S(1)}, u32[]{:S(2)}, u32[]{:S(2)}) %collective-permute-start.35) | collective-permute-done | bytes 98336 | tf_op jit(solution)/shard_map/ppermute | solution.py:112
  (158 shorter events, 41.6 us)
Async XLA Ops:
  2.2 16.4 %collective-permute-start = (bf16[1,17,256]{2,1,0:T(8,128)(2,1)S(1)}, bf16[1,17,256]{2,1,0:T(8,128)(2,1)S(1)}, u32[]{:S(2)}, u32[]{:S(2)}) collective-permute-start(bf16[1,17,256]{2,1,0:T(8,128)(2,1)S(1)} %pad_maximum_fusion.10), channel_id=1, source_target_pairs={{0,1},{1,2},{2,3},{3,4},{4,5},{5,6},{6,7},{7,8},{8,9},{9,10},{10,1... | collective-permute-start | bytes 26120 | tf_op jit(solution)/shard_map/ppermute | solution.py:246
  13.1 8.9 %collective-permute-start.1 = (bf16[1,17,256]{2,1,0:T(8,128)(2,1)S(1)}, bf16[1,17,256]{2,1,0:T(8,128)(2,1)S(1)}, u32[]{:S(2)}, u32[]{:S(2)}) collective-permute-start(bf16[1,17,256]{2,1,0:T(8,128)(2,1)S(1)} %pad_maximum_fusion.11), channel_id=1, source_target_pairs={{1,0},{2,1},{3,2},{4,3},{5,4},{6,5},{7,6},{8,7},{9,8},{10,9},{11,1... | collective-permute-start | bytes 26120 | tf_op jit(solution)/shard_map/ppermute | solution.py:247
  41.9 8.8 %collective-permute-start.2 = (f32[96,256]{1,0:T(8,128)S(1)}, f32[96,256]{1,0:T(8,128)S(1)}, u32[]{:S(2)}, u32[]{:S(2)}) collective-permute-start(f32[96,256]{1,0:T(8,128)S(1)} %get-tuple-element.35), channel_id=1, source_target_pairs={{0,16},{16,0},{32,48},{48,32},{64,80},{80,64},{96,112},{112,96},{1... | collective-permute-start | bytes 294920 | tf_op jit(solution)/shard_map/ppermute | solution.py:99
  43.2 7.7 %collective-permute-start.3 = (f32[96,256]{1,0:T(8,128)S(1)}, f32[96,256]{1,0:T(8,128)S(1)}, u32[]{:S(2)}, u32[]{:S(2)}) collective-permute-start(f32[96,256]{1,0:T(8,128)S(1)} %get-tuple-element.37), channel_id=1, source_target_pairs={{0,32},{16,48},{32,0},{48,16},{64,96},{80,112},{96,64},{112,80},{1... | collective-permute-start | bytes 294920 | tf_op jit(solution)/shard_map/ppermute | solution.py:99
  45.7 7.5 %collective-permute-start.4 = (f32[96,256]{1,0:T(8,128)S(1)}, f32[96,256]{1,0:T(8,128)S(1)}, u32[]{:S(2)}, u32[]{:S(2)}) collective-permute-start(f32[96,256]{1,0:T(8,128)S(1)} %get-tuple-element.36), channel_id=1, source_target_pairs={{0,48},{16,32},{32,16},{48,0},{64,112},{80,96},{96,80},{112,64},{1... | collective-permute-start | bytes 294920 | tf_op jit(solution)/shard_map/ppermute | solution.py:99
  47.0 8.1 %collective-permute-start.19 = (f32[96,256]{1,0:T(8,128)S(1)}, f32[96,256]{1,0:T(8,128)S(1)}, u32[]{:S(2)}, u32[]{:S(2)}) collective-permute-start(f32[96,256]{1,0:T(8,128)S(1)} %get-tuple-element.29), channel_id=1, source_target_pairs={{0,16},{16,0},{32,48},{48,32},{64,80},{80,64},{96,112},{112,96},{1... | collective-permute-start | bytes 294920 | tf_op jit(solution)/shard_map/ppermute | solution.py:99
  47.1 10.0 %collective-permute-start.20 = (f32[96,256]{1,0:T(8,128)S(1)}, f32[96,256]{1,0:T(8,128)S(1)}, u32[]{:S(2)}, u32[]{:S(2)}) collective-permute-start(f32[96,256]{1,0:T(8,128)S(1)} %get-tuple-element.31), channel_id=1, source_target_pairs={{0,32},{16,48},{32,0},{48,16},{64,96},{80,112},{96,64},{112,80},{1... | collective-permute-start | bytes 294920 | tf_op jit(solution)/shard_map/ppermute | solution.py:99
  50.8 6.4 %collective-permute-start.21 = (f32[96,256]{1,0:T(8,128)S(1)}, f32[96,256]{1,0:T(8,128)S(1)}, u32[]{:S(2)}, u32[]{:S(2)}) collective-permute-start(f32[96,256]{1,0:T(8,128)S(1)} %get-tuple-element.30), channel_id=1, source_target_pairs={{0,48},{16,32},{32,16},{48,0},{64,112},{80,96},{96,80},{112,64},{1... | collective-permute-start | bytes 294920 | tf_op jit(solution)/shard_map/ppermute | solution.py:99
  53.2 6.9 %collective-permute-start.5 = (f32[24,256]{1,0:T(8,128)S(1)}, f32[24,256]{1,0:T(8,128)S(1)}, u32[]{:S(2)}, u32[]{:S(2)}) collective-permute-start(f32[24,256]{1,0:T(8,128)S(1)} %get-tuple-element.41), channel_id=1, source_target_pairs={{0,4},{1,5},{2,6},{3,7},{4,0},{5,1},{6,2},{7,3},{8,12},{9,13},{10,... | collective-permute-start | bytes 73736 | tf_op jit(solution)/shard_map/ppermute | solution.py:99
  53.3 7.9 %collective-permute-start.6 = (f32[24,256]{1,0:T(8,128)S(1)}, f32[24,256]{1,0:T(8,128)S(1)}, u32[]{:S(2)}, u32[]{:S(2)}) collective-permute-start(f32[24,256]{1,0:T(8,128)S(1)} %get-tuple-element.43), channel_id=1, source_target_pairs={{0,8},{1,9},{2,10},{3,11},{4,12},{5,13},{6,14},{7,15},{8,0},{9,1},... | collective-permute-start | bytes 73736 | tf_op jit(solution)/shard_map/ppermute | solution.py:99
  57.2 7.1 %collective-permute-start.22 = (f32[24,256]{1,0:T(8,128)S(1)}, f32[24,256]{1,0:T(8,128)S(1)}, u32[]{:S(2)}, u32[]{:S(2)}) collective-permute-start(f32[24,256]{1,0:T(8,128)S(1)} %get-tuple-element.38), channel_id=1, source_target_pairs={{0,4},{1,5},{2,6},{3,7},{4,0},{5,1},{6,2},{7,3},{8,12},{9,13},{10,... | collective-permute-start | bytes 73736 | tf_op jit(solution)/shard_map/ppermute | solution.py:99
  57.3 7.5 %collective-permute-start.23 = (f32[24,256]{1,0:T(8,128)S(1)}, f32[24,256]{1,0:T(8,128)S(1)}, u32[]{:S(2)}, u32[]{:S(2)}) collective-permute-start(f32[24,256]{1,0:T(8,128)S(1)} %get-tuple-element.40), channel_id=1, source_target_pairs={{0,8},{1,9},{2,10},{3,11},{4,12},{5,13},{6,14},{7,15},{8,0},{9,1},... | collective-permute-start | bytes 73736 | tf_op jit(solution)/shard_map/ppermute | solution.py:99
  61.2 7.0 %collective-permute-start.8 = (f32[24,256]{1,0:T(8,128)S(1)}, f32[24,256]{1,0:T(8,128)S(1)}, u32[]{:S(2)}, u32[]{:S(2)}) collective-permute-start(f32[24,256]{1,0:T(8,128)S(1)} %add_add_fusion.3), channel_id=1, source_target_pairs={{0,64},{16,80},{32,96},{48,112},{64,0},{80,16},{96,32},{112,48},{1... | collective-permute-start | bytes 73736 | tf_op jit(solution)/shard_map/ppermute | solution.py:104
  62.0 6.5 %collective-permute-start.9 = (f32[24,256]{1,0:T(8,128)S(1)}, f32[24,256]{1,0:T(8,128)S(1)}, u32[]{:S(2)}, u32[]{:S(2)}) collective-permute-start(f32[24,256]{1,0:T(8,128)S(1)} %add_add_fusion.3), channel_id=1, source_target_pairs={{0,128},{16,144},{32,160},{48,176},{64,192},{80,208},{96,224},{112... | collective-permute-start | bytes 73736 | tf_op jit(solution)/shard_map/ppermute | solution.py:104
  64.8 6.9 %collective-permute-start.25 = (f32[24,256]{1,0:T(8,128)S(1)}, f32[24,256]{1,0:T(8,128)S(1)}, u32[]{:S(2)}, u32[]{:S(2)}) collective-permute-start(f32[24,256]{1,0:T(8,128)S(1)} %add_add_fusion.2), channel_id=1, source_target_pairs={{0,64},{16,80},{32,96},{48,112},{64,0},{80,16},{96,32},{112,48},{1... | collective-permute-start | bytes 73736 | tf_op jit(solution)/shard_map/ppermute | solution.py:104
  68.9 7.8 %collective-permute-start.11 = (f32[24,256]{1,0:T(8,128)S(1)}, f32[24,256]{1,0:T(8,128)S(1)}, u32[]{:S(2)}, u32[]{:S(2)}) collective-permute-start(f32[24,256]{1,0:T(8,128)S(1)} %fusion.118), channel_id=1, source_target_pairs={{0,1},{1,0},{2,3},{3,2},{4,5},{5,4},{6,7},{7,6},{8,9},{9,8},{10,11... | collective-permute-start | bytes 73736 | tf_op jit(solution)/shard_map/ppermute | solution.py:104
  72.7 6.8 %collective-permute-start.28 = (f32[24,256]{1,0:T(8,128)S(1)}, f32[24,256]{1,0:T(8,128)S(1)}, u32[]{:S(2)}, u32[]{:S(2)}) collective-permute-start(f32[24,256]{1,0:T(8,128)S(1)} %fusion.119), channel_id=1, source_target_pairs={{0,1},{1,0},{2,3},{3,2},{4,5},{5,4},{6,7},{7,6},{8,9},{9,8},{10,11... | collective-permute-start | bytes 73736 | tf_op jit(solution)/shard_map/ppermute | solution.py:104
  76.8 6.7 %collective-permute-start.12 = (f32[24,256]{1,0:T(8,128)S(1)}, f32[24,256]{1,0:T(8,128)S(1)}, u32[]{:S(2)}, u32[]{:S(2)}) collective-permute-start(f32[24,256]{1,0:T(8,128)S(1)} %bitcast.219), channel_id=1, source_target_pairs={{0,2},{1,3},{2,0},{3,1},{4,6},{5,7},{6,4},{7,5},{8,10},{9,11},{10,... | collective-permute-start | bytes 73736 | tf_op jit(solution)/shard_map/ppermute | solution.py:104
  79.6 7.8 %collective-permute-start.29 = (f32[24,256]{1,0:T(8,128)S(1)}, f32[24,256]{1,0:T(8,128)S(1)}, u32[]{:S(2)}, u32[]{:S(2)}) collective-permute-start(f32[24,256]{1,0:T(8,128)S(1)} %bitcast.218), channel_id=1, source_target_pairs={{0,2},{1,3},{2,0},{3,1},{4,6},{5,7},{6,4},{7,5},{8,10},{9,11},{10,... | collective-permute-start | bytes 73736 | tf_op jit(solution)/shard_map/ppermute | solution.py:104
  83.5 7.7 %collective-permute-start.13 = (f32[24,256]{1,0:T(8,128)S(1)}, f32[24,256]{1,0:T(8,128)S(1)}, u32[]{:S(2)}, u32[]{:S(2)}) collective-permute-start(f32[24,256]{1,0:T(8,128)S(1)} %bitcast.210), channel_id=1, source_target_pairs={{0,4},{1,5},{2,6},{3,7},{4,0},{5,1},{6,2},{7,3},{8,12},{9,13},{10,... | collective-permute-start | bytes 73736 | tf_op jit(solution)/shard_map/ppermute | solution.py:112
  83.9 7.5 %collective-permute-start.14 = (f32[24,256]{1,0:T(8,128)S(1)}, f32[24,256]{1,0:T(8,128)S(1)}, u32[]{:S(2)}, u32[]{:S(2)}) collective-permute-start(f32[24,256]{1,0:T(8,128)S(1)} %bitcast.211), channel_id=1, source_target_pairs={{0,8},{1,9},{2,10},{3,11},{4,12},{5,13},{6,14},{7,15},{8,0},{9,1},... | collective-permute-start | bytes 73736 | tf_op jit(solution)/shard_map/ppermute | solution.py:112
  96.1 7.7 %collective-permute-start.17 = (f32[96,256]{1,0:T(8,128)S(1)}, f32[96,256]{1,0:T(8,128)S(1)}, u32[]{:S(2)}, u32[]{:S(2)}) collective-permute-start(f32[96,256]{1,0:T(8,128)S(1)} %bitcast.201), channel_id=1, source_target_pairs={{0,32},{16,48},{32,0},{48,16},{64,96},{80,112},{96,64},{112,80},{1... | collective-permute-start | bytes 294920 | tf_op jit(solution)/shard_map/ppermute | solution.py:112
  100.0 6.8 %collective-permute-start.34 = (f32[96,256]{1,0:T(8,128)S(1)}, f32[96,256]{1,0:T(8,128)S(1)}, u32[]{:S(2)}, u32[]{:S(2)}) collective-permute-start(f32[96,256]{1,0:T(8,128)S(1)} %bitcast.197), channel_id=1, source_target_pairs={{0,32},{16,48},{32,0},{48,16},{64,96},{80,112},{96,64},{112,80},{1... | collective-permute-start | bytes 294920 | tf_op jit(solution)/shard_map/ppermute | solution.py:112
  101.8 7.3 %collective-permute-start.35 = (f32[96,256]{1,0:T(8,128)S(1)}, f32[96,256]{1,0:T(8,128)S(1)}, u32[]{:S(2)}, u32[]{:S(2)}) collective-permute-start(f32[96,256]{1,0:T(8,128)S(1)} %bitcast.198), channel_id=1, source_target_pairs={{0,48},{16,32},{32,16},{48,0},{64,112},{80,96},{96,80},{112,64},{1... | collective-permute-start | bytes 294920 | tf_op jit(solution)/shard_map/ppermute | solution.py:112
  (17 other events, 123.9 us)

commit v12 on v10

--- a/solution.py
+++ b/solution.py
@@ -102,10 +102,12 @@
     for axis, shift, radix in groups[scattered:]:
         place = (lax.axis_index(axis) >> shift) & (radix - 1)
         pieces = [rows] + [lax.ppermute(rows, axis, partner_pairs(axis, shift, offset)) for offset in range(1, radix)]
-        stacked = jnp.stack(pieces)
-        total = stacked[place]
-        for position in range(1, radix):
-            total = total + stacked[place ^ position]
+        total = None
+        for position in range(radix):
+            chosen = pieces[0]
+            for offset in range(1, radix):
+                chosen = jnp.where((position ^ place) == offset, pieces[offset], chosen)
+            total = chosen if total is None else total + chosen
         rows = total
     for axis, shift, radix, place in reversed(kept):
         width = rows.shape[0]

time: 111 us -> 110 us (level)
  starting transfers between devices: 40 us -> 38.4 us
  waiting for transfers between devices: 36.8 us -> 38 us
    ppermute x11, starting transfers between devices: 18.6 us -> 17.1 us  [butterfly_sum(): lax.ppermute(rows, axis, partner_pairs(axis, shift, offset))]
    ppermute x11, waiting for transfers between devices: 21.4 us -> 22.6 us  [butterfly_sum(): lax.ppermute(rows, axis, partner_pairs(axis, shift, offset))]
where the time goes in v12:
time: 110 us
  starting transfers between devices  38.4 us (35%)
  waiting for transfers between devices  38 us (35%)
  matrix products  15.5 us (14%)
  other arithmetic  8.91 us (8%)
  local copies, waits for them, and re-layouts  7.67 us (7%)
  between operations  1.23 us (1%)
    ppermute x11, waiting for transfers between devices, butterfly_sum(): lax.ppermute(rows, axis, partner_pairs(axis, shift, offset))  22.6 us
    ppermute x11, starting transfers between devices, butterfly_sum(): lax.ppermute(rows, axis, partner_pairs(axis, shift, offset))  17.1 us
    ppermute x6, waiting for transfers between devices, butterfly_sum(): total = total + lax.ppermute(sent, axis, partner_pairs(axis, shift, offset))  11.9 us
    ppermute x1, starting transfers between devices, local(): lax.ppermute(tail, 'seq', [(i, i + 1) for i in range(count - 1)])  10.2 us
    ppermute x6, starting transfers between devices, butterfly_sum(): total = total + lax.ppermute(sent, axis, partner_pairs(axis, shift, offset))  9.21 us
    dot_general x4, matrix products, product(): jnp.dot(stacked.reshape(-1, shape_in[-1]), matrix, preferred_element_type...  6.19 us
    ppermute x1, waiting for transfers between devices, local(): lax.ppermute(head, 'seq', [(i + 1, i) for i in range(count - 1)])  3.55 us
    unnamed x13, local copies, waits for them, and re-layouts  3.14 us
  transfers between devices with their start and end apart: 19, of which 15 were waited for; matrix products, arithmetic and copies ran while one was open for 4% of the time, Pallas kernels for 0%

profile of v12, /device:TPU:1, one launch (start us, length us, event | category | flops | bytes accessed | tf_op | source)
XLA Modules:
  0.0 109.7 jit_solution(3203999921752452040)
XLA Ops:
  2.2 10.2 %collective-permute-start = (bf16[1,17,256]{2,1,0:T(8,128)(2,1)S(1)}, bf16[1,17,256]{2,1,0:T(8,128)(2,1)S(1)}, u32[]{:S(2)}, u32[]{:S(2)}) collective-permute-start(bf16[1,17,256]{2,1,0:T(8,128)(2,1)S(1)} %pad_maximum_fusion.4), channel_id=1, source_target_pairs={{0,1},{1,2},{2,3},{3,4},{4,5},{5,6},{6,7},{7,8},{8,9},{9,10},{10,1... | collective-permute-start | bytes 26120 | tf_op jit(solution)/shard_map/ppermute | solution.py:248
  13.1 1.9 %collective-permute-start.1 = (bf16[1,17,256]{2,1,0:T(8,128)(2,1)S(1)}, bf16[1,17,256]{2,1,0:T(8,128)(2,1)S(1)}, u32[]{:S(2)}, u32[]{:S(2)}) collective-permute-start(bf16[1,17,256]{2,1,0:T(8,128)(2,1)S(1)} %pad_maximum_fusion.5), channel_id=1, source_target_pairs={{1,0},{2,1},{3,2},{4,3},{5,4},{6,5},{7,6},{8,7},{9,8},{10,9},{11,1... | collective-permute-start | bytes 26120 | tf_op jit(solution)/shard_map/ppermute | solution.py:249
  18.5 3.5 %collective-permute-done.1 = bf16[1,17,256]{2,1,0:T(8,128)(2,1)S(1)} collective-permute-done((bf16[1,17,256]{2,1,0:T(8,128)(2,1)S(1)}, bf16[1,17,256]{2,1,0:T(8,128)(2,1)S(1)}, u32[]{:S(2)}, u32[]{:S(2)}) %collective-permute-start.1) | collective-permute-done | bytes 8736 | tf_op jit(solution)/shard_map/ppermute | solution.py:249
  23.9 1.8 %convolution_bitcast_fusion.1 = f32[1,2112,512]{2,1,0:T(8,128)S(1)} fusion(bf16[1,2112,256]{2,1,0:T(8,128)(2,1)S(1)} %get-tuple-element.14, bf16[1,2112,256]{2,1,0:T(8,128)(2,1)S(1)} %get-tuple-element.15, bf16[1,2112,256]{2,1,0:T(8,128)(2,1)S(1)} %get-tuple-element.13, bf16[768,256]{1,0:T(8,128)(2,1)S(1)} %bitcast.185, bf16[768,256]{1,0:T(8,128)(2,1)S(1)} %bitcast.184), kind=kOutput, calls=%fused_computation.3 | convolution fusion | flops 1672249344 | bytes 8355840 | tf_op jit(solution)/shard_map/dot_general | solution.py:40
  28.0 1.9 %convolution_bitcast_fusion = f32[1,2080,512]{2,1,0:T(8,128)S(1)} fusion(bf16[1,2080,256]{2,1,0:T(8,128)(2,1)S(1)} %get-tuple-element.17, bf16[1,2080,256]{2,1,0:T(8,128)(2,1)S(1)} %get-tuple-element.18, bf16[1,2080,256]{2,1,0:T(8,128)(2,1)S(1)} %get-tuple-element.16, bf16[768,256]{1,0:T(8,128)(2,1)S(1)} %bitcast.175, bf16[768,256]{1,0:T(8,128)(2,1)S(1)} %bitcast.172), kind=kOutput, calls=%fused_computation.2 | convolution fusion | flops 1646936064 | bytes 8241152 | tf_op jit(solution)/shard_map/dot_general | solution.py:40
  34.0 1.8 %convolution_bitcast_fusion.2 = f32[1,2048,512]{2,1,0:T(8,128)S(1)} fusion(bf16[1,2048,256]{2,1,0:T(8,128)(2,1)S(1)} %get-tuple-element.20, bf16[1,2048,256]{2,1,0:T(8,128)(2,1)S(1)} %get-tuple-element.21, bf16[1,2048,256]{2,1,0:T(8,128)(2,1)S(1)} %get-tuple-element.19, bf16[768,256]{1,0:T(8,128)(2,1)S(1)} %bitcast.176, bf16[768,256]{1,0:T(8,128)(2,1)S(1)} %bitcast.173), kind=kOutput, calls=%fused_computation.10 | convolution fusion | flops 1621622784 | bytes 8126464 | tf_op jit(solution)/shard_map/dot_general | solution.py:40
  35.8 2.8 %fusion.39 = (bf16[1,2048,256]{2,1,0:T(8,128)(2,1)S(1)}, bf16[1,2048,256]{2,1,0:T(8,128)(2,1)}) fusion(f32[1,2048,512]{2,1,0:T(8,128)S(1)} %convolution_bitcast_fusion.2, f32[1,2112,256]{2,1,0:T(8,128)S(1)} %get-tuple-element.12, bf16[1,2048,256]{2,1,0:T(8,128)(2,1)S(1)} %copy-done.1, f32[1,2080,256]{2,1,0:T(8,128)S(1)} %add_multiply_fusion, ...), kind=kLoop, calls=%fused_computation.61 | loop fusion | flops 14155776 | bytes 14680064 | tf_op jit(solution)/shard_map/convert_element_type | solution.py:287
  44.3 2.5 %collective-permute-start.3 = (f32[192,256]{1,0:T(8,128)S(1)}, f32[192,256]{1,0:T(8,128)S(1)}, u32[]{:S(2)}, u32[]{:S(2)}) collective-permute-start(f32[192,256]{1,0:T(8,128)S(1)} %get-tuple-element.28), channel_id=1, source_target_pairs={{0,32},{16,48},{32,0},{48,16},{64,96},{80,112},{96,64},{112,80},{1... | collective-permute-start | bytes 589832 | tf_op jit(solution)/shard_map/ppermute | solution.py:99
  48.0 4.1 %collective-permute-done.3 = f32[192,256]{1,0:T(8,128)S(1)} collective-permute-done((f32[192,256]{1,0:T(8,128)S(1)}, f32[192,256]{1,0:T(8,128)S(1)}, u32[]{:S(2)}, u32[]{:S(2)}) %collective-permute-start.3) | collective-permute-done | bytes 196640 | tf_op jit(solution)/shard_map/ppermute | solution.py:99
  52.1 2.0 %collective-permute-done.4 = f32[192,256]{1,0:T(8,128)S(1)} collective-permute-done((f32[192,256]{1,0:T(8,128)S(1)}, f32[192,256]{1,0:T(8,128)S(1)}, u32[]{:S(2)}, u32[]{:S(2)}) %collective-permute-start.4) | collective-permute-done | bytes 196640 | tf_op jit(solution)/shard_map/ppermute | solution.py:99
  54.1 2.3 %collective-permute-start.5 = (f32[48,256]{1,0:T(8,128)S(1)}, f32[48,256]{1,0:T(8,128)S(1)}, u32[]{:S(2)}, u32[]{:S(2)}) collective-permute-start(f32[48,256]{1,0:T(8,128)S(1)} %get-tuple-element.35), channel_id=1, source_target_pairs={{0,4},{1,5},{2,6},{3,7},{4,0},{5,1},{6,2},{7,3},{8,12},{9,13},{10,... | collective-permute-start | bytes 147464 | tf_op jit(solution)/shard_map/ppermute | solution.py:99
  56.4 2.9 %collective-permute-start.6 = (f32[48,256]{1,0:T(8,128)S(1)}, f32[48,256]{1,0:T(8,128)S(1)}, u32[]{:S(2)}, u32[]{:S(2)}) collective-permute-start(f32[48,256]{1,0:T(8,128)S(1)} %get-tuple-element.37), channel_id=1, source_target_pairs={{0,8},{1,9},{2,10},{3,11},{4,12},{5,13},{6,14},{7,15},{8,0},{9,1},... | collective-permute-start | bytes 147464 | tf_op jit(solution)/shard_map/ppermute | solution.py:99
  59.4 2.6 %collective-permute-done.6 = f32[48,256]{1,0:T(8,128)S(1)} collective-permute-done((f32[48,256]{1,0:T(8,128)S(1)}, f32[48,256]{1,0:T(8,128)S(1)}, u32[]{:S(2)}, u32[]{:S(2)}) %collective-permute-start.6) | collective-permute-done | bytes 49184 | tf_op jit(solution)/shard_map/ppermute | solution.py:99
  62.0 2.3 %collective-permute-done.7 = f32[48,256]{1,0:T(8,128)S(1)} collective-permute-done((f32[48,256]{1,0:T(8,128)S(1)}, f32[48,256]{1,0:T(8,128)S(1)}, u32[]{:S(2)}, u32[]{:S(2)}) %collective-permute-start.7) | collective-permute-done | bytes 49184 | tf_op jit(solution)/shard_map/ppermute | solution.py:99
  65.3 3.8 %collective-permute-start.8 = (f32[48,256]{1,0:T(8,128)S(1)}, f32[48,256]{1,0:T(8,128)S(1)}, u32[]{:S(2)}, u32[]{:S(2)}) collective-permute-start(f32[48,256]{1,0:T(8,128)S(1)} %add_add_fusion.1), channel_id=1, source_target_pairs={{0,192},{16,208},{32,224},{48,240},{64,128},{80,144},{96,160},{112... | collective-permute-start | bytes 147464 | tf_op jit(solution)/shard_map/ppermute | solution.py:104
  69.3 1.8 %collective-permute-done.8 = f32[48,256]{1,0:T(8,128)S(1)} collective-permute-done((f32[48,256]{1,0:T(8,128)S(1)}, f32[48,256]{1,0:T(8,128)S(1)}, u32[]{:S(2)}, u32[]{:S(2)}) %collective-permute-start.8) | collective-permute-done | bytes 49184 | tf_op jit(solution)/shard_map/ppermute | solution.py:104
  71.1 3.1 %collective-permute-done.9 = f32[48,256]{1,0:T(8,128)S(1)} collective-permute-done((f32[48,256]{1,0:T(8,128)S(1)}, f32[48,256]{1,0:T(8,128)S(1)}, u32[]{:S(2)}, u32[]{:S(2)}) %collective-permute-start.9) | collective-permute-done | bytes 49184 | tf_op jit(solution)/shard_map/ppermute | solution.py:104
  74.3 2.3 %collective-permute-start.11 = (f32[48,256]{1,0:T(8,128)S(1)}, f32[48,256]{1,0:T(8,128)S(1)}, u32[]{:S(2)}, u32[]{:S(2)}) collective-permute-start(f32[48,256]{1,0:T(8,128)S(1)} %select_add_fusion.2), channel_id=1, source_target_pairs={{0,1},{1,0},{2,3},{3,2},{4,5},{5,4},{6,7},{7,6},{8,9},{9,8},{10,11... | collective-permute-start | bytes 147464 | tf_op jit(solution)/shard_map/ppermute | solution.py:104
  77.5 1.8 %collective-permute-start.12 = (f32[48,256]{1,0:T(8,128)S(1)}, f32[48,256]{1,0:T(8,128)S(1)}, u32[]{:S(2)}, u32[]{:S(2)}) collective-permute-start(f32[48,256]{1,0:T(8,128)S(1)} %select_add_fusion.1), channel_id=1, source_target_pairs={{0,2},{1,3},{2,0},{3,1},{4,6},{5,7},{6,4},{7,5},{8,10},{9,11},{10,... | collective-permute-start | bytes 147464 | tf_op jit(solution)/shard_map/ppermute | solution.py:104
  79.3 6.4 %collective-permute-done.12 = f32[48,256]{1,0:T(8,128)S(1)} collective-permute-done((f32[48,256]{1,0:T(8,128)S(1)}, f32[48,256]{1,0:T(8,128)S(1)}, u32[]{:S(2)}, u32[]{:S(2)}) %collective-permute-start.12) | collective-permute-done | bytes 49184 | tf_op jit(solution)/shard_map/ppermute | solution.py:104
  86.1 3.6 %collective-permute-start.15 = (f32[48,256]{1,0:T(8,128)S(1)}, f32[48,256]{1,0:T(8,128)S(1)}, u32[]{:S(2)}, u32[]{:S(2)}) collective-permute-start(f32[48,256]{1,0:T(8,128)S(1)} %select_add_fusion), channel_id=1, source_target_pairs={{0,12},{1,13},{2,14},{3,15},{4,8},{5,9},{6,10},{7,11},{8,4},{9,5},... | collective-permute-start | bytes 147464 | tf_op jit(solution)/shard_map/ppermute | solution.py:114
  94.1 2.4 %collective-permute-start.18 = (f32[192,256]{1,0:T(8,128)S(1)}, f32[192,256]{1,0:T(8,128)S(1)}, u32[]{:S(2)}, u32[]{:S(2)}) collective-permute-start(f32[192,256]{1,0:T(8,128)S(1)} %bitcast_select_fusion), channel_id=1, source_target_pairs={{0,48},{16,32},{32,16},{48,0},{64,112},{80,96},{96,80},{112,64},{1... | collective-permute-start | bytes 589832 | tf_op jit(solution)/shard_map/ppermute | solution.py:114
  97.6 4.2 %collective-permute-done.17 = f32[192,256]{1,0:T(8,128)S(1)} collective-permute-done((f32[192,256]{1,0:T(8,128)S(1)}, f32[192,256]{1,0:T(8,128)S(1)}, u32[]{:S(2)}, u32[]{:S(2)}) %collective-permute-start.17) | collective-permute-done | bytes 196640 | tf_op jit(solution)/shard_map/ppermute | solution.py:114
  101.8 3.2 %collective-permute-done.18 = f32[192,256]{1,0:T(8,128)S(1)} collective-permute-done((f32[192,256]{1,0:T(8,128)S(1)}, f32[192,256]{1,0:T(8,128)S(1)}, u32[]{:S(2)}, u32[]{:S(2)}) %collective-permute-start.18) | collective-permute-done | bytes 196640 | tf_op jit(solution)/shard_map/ppermute | solution.py:114
  (111 shorter events, 33.2 us)
Async XLA Ops:
  0.6 21.6 %copy-start = (bf16[4,256]{1,0:T(4,128)(2,1)S(1)}, bf16[4,256]{1,0:T(4,128)(2,1)}, u32[]{:S(2)}) copy-start(bf16[4,256]{1,0:T(4,128)(2,1)} %param.6) | copy-start | bytes 6148
  0.6 21.4 %copy-start.3 = (s32[1,2048]{1,0:T(1,128)S(1)}, s32[1,2048]{1,0:T(1,128)}, u32[]{:S(2)}) copy-start(s32[1,2048]{1,0:T(1,128)} %param.5) | copy-start | bytes 24580
  0.7 17.4 %copy-start.2 = (bf16[3,256,256]{2,1,0:T(8,128)(2,1)S(1)}, bf16[3,256,256]{2,1,0:T(8,128)(2,1)}, u32[]{:S(2)}) copy-start(bf16[3,256,256]{2,1,0:T(8,128)(2,1)} %param.8) | copy-start | bytes 1179652
  2.2 16.3 %collective-permute-start = (bf16[1,17,256]{2,1,0:T(8,128)(2,1)S(1)}, bf16[1,17,256]{2,1,0:T(8,128)(2,1)S(1)}, u32[]{:S(2)}, u32[]{:S(2)}) collective-permute-start(bf16[1,17,256]{2,1,0:T(8,128)(2,1)S(1)} %pad_maximum_fusion.4), channel_id=1, source_target_pairs={{0,1},{1,2},{2,3},{3,4},{4,5},{5,6},{6,7},{7,8},{8,9},{9,10},{10,1... | collective-permute-start | bytes 26120 | tf_op jit(solution)/shard_map/ppermute | solution.py:248
  13.1 8.9 %collective-permute-start.1 = (bf16[1,17,256]{2,1,0:T(8,128)(2,1)S(1)}, bf16[1,17,256]{2,1,0:T(8,128)(2,1)S(1)}, u32[]{:S(2)}, u32[]{:S(2)}) collective-permute-start(bf16[1,17,256]{2,1,0:T(8,128)(2,1)S(1)} %pad_maximum_fusion.5), channel_id=1, source_target_pairs={{1,0},{2,1},{3,2},{4,3},{5,4},{6,5},{7,6},{8,7},{9,8},{10,9},{11,1... | collective-permute-start | bytes 26120 | tf_op jit(solution)/shard_map/ppermute | solution.py:249
  22.9 1.0 copy-start.4
  28.0 1.9 %copy-start.1 = (bf16[1,2048,256]{2,1,0:T(8,128)(2,1)S(1)}, bf16[1,2048,256]{2,1,0:T(8,128)(2,1)}, u32[]{:S(2)}) copy-start(bf16[1,2048,256]{2,1,0:T(8,128)(2,1)} %param.9) | copy-start | bytes 3145732
  43.1 4.9 %collective-permute-start.2 = (f32[192,256]{1,0:T(8,128)S(1)}, f32[192,256]{1,0:T(8,128)S(1)}, u32[]{:S(2)}, u32[]{:S(2)}) collective-permute-start(f32[192,256]{1,0:T(8,128)S(1)} %get-tuple-element.26), channel_id=1, source_target_pairs={{0,16},{16,0},{32,48},{48,32},{64,80},{80,64},{96,112},{112,96},{1... | collective-permute-start | bytes 589832 | tf_op jit(solution)/shard_map/ppermute | solution.py:99
  44.3 7.7 %collective-permute-start.3 = (f32[192,256]{1,0:T(8,128)S(1)}, f32[192,256]{1,0:T(8,128)S(1)}, u32[]{:S(2)}, u32[]{:S(2)}) collective-permute-start(f32[192,256]{1,0:T(8,128)S(1)} %get-tuple-element.28), channel_id=1, source_target_pairs={{0,32},{16,48},{32,0},{48,16},{64,96},{80,112},{96,64},{112,80},{1... | collective-permute-start | bytes 589832 | tf_op jit(solution)/shard_map/ppermute | solution.py:99
  46.8 7.3 %collective-permute-start.4 = (f32[192,256]{1,0:T(8,128)S(1)}, f32[192,256]{1,0:T(8,128)S(1)}, u32[]{:S(2)}, u32[]{:S(2)}) collective-permute-start(f32[192,256]{1,0:T(8,128)S(1)} %get-tuple-element.27), channel_id=1, source_target_pairs={{0,48},{16,32},{32,16},{48,0},{64,112},{80,96},{96,80},{112,64},{1... | collective-permute-start | bytes 589832 | tf_op jit(solution)/shard_map/ppermute | solution.py:99
  54.1 5.2 %collective-permute-start.5 = (f32[48,256]{1,0:T(8,128)S(1)}, f32[48,256]{1,0:T(8,128)S(1)}, u32[]{:S(2)}, u32[]{:S(2)}) collective-permute-start(f32[48,256]{1,0:T(8,128)S(1)} %get-tuple-element.35), channel_id=1, source_target_pairs={{0,4},{1,5},{2,6},{3,7},{4,0},{5,1},{6,2},{7,3},{8,12},{9,13},{10,... | collective-permute-start | bytes 147464 | tf_op jit(solution)/shard_map/ppermute | solution.py:99
  56.4 5.5 %collective-permute-start.6 = (f32[48,256]{1,0:T(8,128)S(1)}, f32[48,256]{1,0:T(8,128)S(1)}, u32[]{:S(2)}, u32[]{:S(2)}) collective-permute-start(f32[48,256]{1,0:T(8,128)S(1)} %get-tuple-element.37), channel_id=1, source_target_pairs={{0,8},{1,9},{2,10},{3,11},{4,12},{5,13},{6,14},{7,15},{8,0},{9,1},... | collective-permute-start | bytes 147464 | tf_op jit(solution)/shard_map/ppermute | solution.py:99
  59.4 4.9 %collective-permute-start.7 = (f32[48,256]{1,0:T(8,128)S(1)}, f32[48,256]{1,0:T(8,128)S(1)}, u32[]{:S(2)}, u32[]{:S(2)}) collective-permute-start(f32[48,256]{1,0:T(8,128)S(1)} %get-tuple-element.36), channel_id=1, source_target_pairs={{0,12},{1,13},{2,14},{3,15},{4,8},{5,9},{6,10},{7,11},{8,4},{9,5},... | collective-permute-start | bytes 147464 | tf_op jit(solution)/shard_map/ppermute | solution.py:99
  64.2 5.1 %collective-permute-start.10 = (f32[48,256]{1,0:T(8,128)S(1)}, f32[48,256]{1,0:T(8,128)S(1)}, u32[]{:S(2)}, u32[]{:S(2)}) collective-permute-start(f32[48,256]{1,0:T(8,128)S(1)} %add_add_fusion.1), channel_id=1, source_target_pairs={{0,64},{16,80},{32,96},{48,112},{64,0},{80,16},{96,32},{112,48},{1... | collective-permute-start | bytes 147464 | tf_op jit(solution)/shard_map/ppermute | solution.py:104
  65.3 5.8 %collective-permute-start.8 = (f32[48,256]{1,0:T(8,128)S(1)}, f32[48,256]{1,0:T(8,128)S(1)}, u32[]{:S(2)}, u32[]{:S(2)}) collective-permute-start(f32[48,256]{1,0:T(8,128)S(1)} %add_add_fusion.1), channel_id=1, source_target_pairs={{0,192},{16,208},{32,224},{48,240},{64,128},{80,144},{96,160},{112... | collective-permute-start | bytes 147464 | tf_op jit(solution)/shard_map/ppermute | solution.py:104
  69.1 5.1 %collective-permute-start.9 = (f32[48,256]{1,0:T(8,128)S(1)}, f32[48,256]{1,0:T(8,128)S(1)}, u32[]{:S(2)}, u32[]{:S(2)}) collective-permute-start(f32[48,256]{1,0:T(8,128)S(1)} %add_add_fusion.1), channel_id=1, source_target_pairs={{0,128},{16,144},{32,160},{48,176},{64,192},{80,208},{96,224},{112... | collective-permute-start | bytes 147464 | tf_op jit(solution)/shard_map/ppermute | solution.py:104
  74.3 3.2 %collective-permute-start.11 = (f32[48,256]{1,0:T(8,128)S(1)}, f32[48,256]{1,0:T(8,128)S(1)}, u32[]{:S(2)}, u32[]{:S(2)}) collective-permute-start(f32[48,256]{1,0:T(8,128)S(1)} %select_add_fusion.2), channel_id=1, source_target_pairs={{0,1},{1,0},{2,3},{3,2},{4,5},{5,4},{6,7},{7,6},{8,9},{9,8},{10,11... | collective-permute-start | bytes 147464 | tf_op jit(solution)/shard_map/ppermute | solution.py:104
  77.5 8.2 %collective-permute-start.12 = (f32[48,256]{1,0:T(8,128)S(1)}, f32[48,256]{1,0:T(8,128)S(1)}, u32[]{:S(2)}, u32[]{:S(2)}) collective-permute-start(f32[48,256]{1,0:T(8,128)S(1)} %select_add_fusion.1), channel_id=1, source_target_pairs={{0,2},{1,3},{2,0},{3,1},{4,6},{5,7},{6,4},{7,5},{8,10},{9,11},{10,... | collective-permute-start | bytes 147464 | tf_op jit(solution)/shard_map/ppermute | solution.py:104
  85.8 4.1 %collective-permute-start.13 = (f32[48,256]{1,0:T(8,128)S(1)}, f32[48,256]{1,0:T(8,128)S(1)}, u32[]{:S(2)}, u32[]{:S(2)}) collective-permute-start(f32[48,256]{1,0:T(8,128)S(1)} %select_add_fusion), channel_id=1, source_target_pairs={{0,4},{1,5},{2,6},{3,7},{4,0},{5,1},{6,2},{7,3},{8,12},{9,13},{10,... | collective-permute-start | bytes 147464 | tf_op jit(solution)/shard_map/ppermute | solution.py:114
  85.9 4.5 %collective-permute-start.14 = (f32[48,256]{1,0:T(8,128)S(1)}, f32[48,256]{1,0:T(8,128)S(1)}, u32[]{:S(2)}, u32[]{:S(2)}) collective-permute-start(f32[48,256]{1,0:T(8,128)S(1)} %select_add_fusion), channel_id=1, source_target_pairs={{0,8},{1,9},{2,10},{3,11},{4,12},{5,13},{6,14},{7,15},{8,0},{9,1},... | collective-permute-start | bytes 147464 | tf_op jit(solution)/shard_map/ppermute | solution.py:114
  86.1 5.7 %collective-permute-start.15 = (f32[48,256]{1,0:T(8,128)S(1)}, f32[48,256]{1,0:T(8,128)S(1)}, u32[]{:S(2)}, u32[]{:S(2)}) collective-permute-start(f32[48,256]{1,0:T(8,128)S(1)} %select_add_fusion), channel_id=1, source_target_pairs={{0,12},{1,13},{2,14},{3,15},{4,8},{5,9},{6,10},{7,11},{8,4},{9,5},... | collective-permute-start | bytes 147464 | tf_op jit(solution)/shard_map/ppermute | solution.py:114
  92.5 5.1 %collective-permute-start.16 = (f32[192,256]{1,0:T(8,128)S(1)}, f32[192,256]{1,0:T(8,128)S(1)}, u32[]{:S(2)}, u32[]{:S(2)}) collective-permute-start(f32[192,256]{1,0:T(8,128)S(1)} %bitcast_select_fusion), channel_id=1, source_target_pairs={{0,16},{16,0},{32,48},{48,32},{64,80},{80,64},{96,112},{112,96},{1... | collective-permute-start | bytes 589832 | tf_op jit(solution)/shard_map/ppermute | solution.py:114
  92.6 9.2 %collective-permute-start.17 = (f32[192,256]{1,0:T(8,128)S(1)}, f32[192,256]{1,0:T(8,128)S(1)}, u32[]{:S(2)}, u32[]{:S(2)}) collective-permute-start(f32[192,256]{1,0:T(8,128)S(1)} %bitcast_select_fusion), channel_id=1, source_target_pairs={{0,32},{16,48},{32,0},{48,16},{64,96},{80,112},{96,64},{112,80},{1... | collective-permute-start | bytes 589832 | tf_op jit(solution)/shard_map/ppermute | solution.py:114
  94.1 10.9 %collective-permute-start.18 = (f32[192,256]{1,0:T(8,128)S(1)}, f32[192,256]{1,0:T(8,128)S(1)}, u32[]{:S(2)}, u32[]{:S(2)}) collective-permute-start(f32[192,256]{1,0:T(8,128)S(1)} %bitcast_select_fusion), channel_id=1, source_target_pairs={{0,48},{16,32},{32,16},{48,0},{64,112},{80,96},{96,80},{112,64},{1... | collective-permute-start | bytes 589832 | tf_op jit(solution)/shard_map/ppermute | solution.py:114

commit v13 on v12

--- a/solution.py
+++ b/solution.py
@@ -93,9 +93,17 @@
     for axis, shift, radix in groups[:scattered]:
         place = (lax.axis_index(axis) >> shift) & (radix - 1)
         width = rows.shape[0] // radix
-        total = lax.dynamic_slice_in_dim(rows, place * width, width)
+        quarters = [rows[q * width : (q + 1) * width] for q in range(radix)]
+
+        def pick(index, choices=quarters):
+            chosen = choices[0]
+            for q in range(1, radix):
+                chosen = jnp.where(index == q, choices[q], chosen)
+            return chosen
+
+        total = pick(place)
         for offset in range(1, radix):
-            sent = lax.dynamic_slice_in_dim(rows, (place ^ offset) * width, width)
+            sent = pick(place ^ offset)
             total = total + lax.ppermute(sent, axis, partner_pairs(axis, shift, offset))
         rows = total
         kept.append((axis, shift, radix, place))
@@ -112,8 +120,13 @@
     for axis, shift, radix, place in reversed(kept):
         width = rows.shape[0]
         pieces = [rows] + [lax.ppermute(rows, axis, partner_pairs(axis, shift, offset)) for offset in range(1, radix)]
-        order = jnp.arange(radix, dtype=jnp.int32) ^ place
-        rows = jnp.take(jnp.stack(pieces), order, axis=0).reshape((width * radix,) + rows.shape[1:])
+        slots = []
+        for position in range(radix):
+            chosen = pieces[0]
+            for offset in range(1, radix):
+                chosen = jnp.where((position ^ place) == offset, pieces[offset], chosen)
+            slots.append(chosen)
+        rows = jnp.concatenate(slots, axis=0)
     return rows
 
 

time: 110 us -> 108 us (0.982)
  local copies, waits for them, and re-layouts: 7.67 us -> 6.16 us
    gather x2 -> x0, local copies, waits for them, and re-layouts: 1.16 us -> none  [butterfly_sum(): jnp.take(jnp.stack(pieces), order, axis=0)]
  transfers between devices with their start and end apart: 19 -> 19, of which waited for: 15 -> 13; matrix products, arithmetic and copies ran while one was open for 4% -> 4% of each run, Pallas kernels for 0% -> 0%
where the time goes in v13:
time: 108 us
  starting transfers between devices  38.3 us (35%)
  waiting for transfers between devices  37.8 us (35%)
  matrix products  15.2 us (14%)
  other arithmetic  8.93 us (8%)
  local copies, waits for them, and re-layouts  6.16 us (6%)
  between operations  1.22 us (1%)
    ppermute x11, waiting for transfers between devices, butterfly_sum(): lax.ppermute(rows, axis, partner_pairs(axis, shift, offset))  23 us
    ppermute x11, starting transfers between devices, butterfly_sum(): lax.ppermute(rows, axis, partner_pairs(axis, shift, offset))  16.3 us
    ppermute x6, waiting for transfers between devices, butterfly_sum(): total = total + lax.ppermute(sent, axis, partner_pairs(axis, shift, offset))  11.3 us
    ppermute x1, starting transfers between devices, local(): lax.ppermute(tail, 'seq', [(i, i + 1) for i in range(count - 1)])  10.2 us
    ppermute x6, starting transfers between devices, butterfly_sum(): total = total + lax.ppermute(sent, axis, partner_pairs(axis, shift, offset))  9.88 us
    dot_general x4, matrix products, product(): jnp.dot(stacked.reshape(-1, shape_in[-1]), matrix, preferred_element_type...  6.19 us
    ppermute x1, waiting for transfers between devices, local(): lax.ppermute(head, 'seq', [(i + 1, i) for i in range(count - 1)])  3.56 us
    unnamed x13, local copies, waits for them, and re-layouts  3.14 us
  transfers between devices with their start and end apart: 19, of which 13 were waited for; matrix products, arithmetic and copies ran while one was open for 4% of the time, Pallas kernels for 0%

profile of v13, /device:TPU:1, one launch (start us, length us, event | category | flops | bytes accessed | tf_op | source)
XLA Modules:
  0.0 107.7 jit_solution(14992161393194702703)
XLA Ops:
  2.2 10.2 %collective-permute-start = (bf16[1,17,256]{2,1,0:T(8,128)(2,1)S(1)}, bf16[1,17,256]{2,1,0:T(8,128)(2,1)S(1)}, u32[]{:S(2)}, u32[]{:S(2)}) collective-permute-start(bf16[1,17,256]{2,1,0:T(8,128)(2,1)S(1)} %pad_maximum_fusion.9), channel_id=1, source_target_pairs={{0,1},{1,2},{2,3},{3,4},{4,5},{5,6},{6,7},{7,8},{8,9},{9,10},{10,1... | collective-permute-start | bytes 26120 | tf_op jit(solution)/shard_map/ppermute | solution.py:261
  13.1 1.9 %collective-permute-start.1 = (bf16[1,17,256]{2,1,0:T(8,128)(2,1)S(1)}, bf16[1,17,256]{2,1,0:T(8,128)(2,1)S(1)}, u32[]{:S(2)}, u32[]{:S(2)}) collective-permute-start(bf16[1,17,256]{2,1,0:T(8,128)(2,1)S(1)} %pad_maximum_fusion.10), channel_id=1, source_target_pairs={{1,0},{2,1},{3,2},{4,3},{5,4},{6,5},{7,6},{8,7},{9,8},{10,9},{11,1... | collective-permute-start | bytes 26120 | tf_op jit(solution)/shard_map/ppermute | solution.py:262
  18.5 3.6 %collective-permute-done.1 = bf16[1,17,256]{2,1,0:T(8,128)(2,1)S(1)} collective-permute-done((bf16[1,17,256]{2,1,0:T(8,128)(2,1)S(1)}, bf16[1,17,256]{2,1,0:T(8,128)(2,1)S(1)}, u32[]{:S(2)}, u32[]{:S(2)}) %collective-permute-start.1) | collective-permute-done | bytes 8736 | tf_op jit(solution)/shard_map/ppermute | solution.py:262
  23.9 1.8 %convolution_bitcast_fusion.1 = f32[1,2112,512]{2,1,0:T(8,128)S(1)} fusion(bf16[1,2112,256]{2,1,0:T(8,128)(2,1)S(1)} %get-tuple-element.17, bf16[1,2112,256]{2,1,0:T(8,128)(2,1)S(1)} %get-tuple-element.18, bf16[1,2112,256]{2,1,0:T(8,128)(2,1)S(1)} %get-tuple-element.16, bf16[768,256]{1,0:T(8,128)(2,1)S(1)} %bitcast.157, bf16[768,256]{1,0:T(8,128)(2,1)S(1)} %bitcast.156), kind=kOutput, calls=%fused_computation.1 | convolution fusion | flops 1672249344 | bytes 8355840 | tf_op jit(solution)/shard_map/dot_general | solution.py:40
  28.0 1.9 %convolution_bitcast_fusion = f32[1,2080,512]{2,1,0:T(8,128)S(1)} fusion(bf16[1,2080,256]{2,1,0:T(8,128)(2,1)S(1)} %get-tuple-element.20, bf16[1,2080,256]{2,1,0:T(8,128)(2,1)S(1)} %get-tuple-element.21, bf16[1,2080,256]{2,1,0:T(8,128)(2,1)S(1)} %get-tuple-element.19, bf16[768,256]{1,0:T(8,128)(2,1)S(1)} %bitcast.154, bf16[768,256]{1,0:T(8,128)(2,1)S(1)} %bitcast.151), kind=kOutput, calls=%fused_computation | convolution fusion | flops 1646936064 | bytes 8241152 | tf_op jit(solution)/shard_map/dot_general | solution.py:40
  30.0 1.7 %fusion.25 = (bf16[1,2080,256]{2,1,0:T(8,128)(2,1)S(1)}, f32[1,2080,256]{2,1,0:T(8,128)S(1)}) fusion(bf16[1,16,256]{2,1,0:T(8,128)(2,1)S(1)} %slice.255, bf16[1,2048,256]{2,1,0:T(8,128)(2,1)S(1)} %copy-done.1, bf16[1,16,256]{2,1,0:T(8,128)(2,1)S(1)} %slice.254, f32[1,2080,512]{2,1,0:T(8,128)S(1)} %convolution_bitcast_fusion), kind=kLoop, calls=%fused_computation.44 | loop fusion | flops 14376960 | bytes 8519680 | tf_op jit(solution)/shard_map/convert_element_type | solution.py:291
  34.0 1.8 %convolution_bitcast_fusion.2 = f32[1,2048,512]{2,1,0:T(8,128)S(1)} fusion(bf16[1,2048,256]{2,1,0:T(8,128)(2,1)S(1)} %get-tuple-element.23, bf16[1,2048,256]{2,1,0:T(8,128)(2,1)S(1)} %get-tuple-element.24, bf16[1,2048,256]{2,1,0:T(8,128)(2,1)S(1)} %get-tuple-element.22, bf16[768,256]{1,0:T(8,128)(2,1)S(1)} %bitcast.155, bf16[768,256]{1,0:T(8,128)(2,1)S(1)} %bitcast.152), kind=kOutput, calls=%fused_computation.8 | convolution fusion | flops 1621622784 | bytes 8126464 | tf_op jit(solution)/shard_map/dot_general | solution.py:40
  35.8 2.8 %fusion.39 = (bf16[1,2048,256]{2,1,0:T(8,128)(2,1)S(1)}, bf16[1,2048,256]{2,1,0:T(8,128)(2,1)}) fusion(f32[1,2048,512]{2,1,0:T(8,128)S(1)} %convolution_bitcast_fusion.2, f32[1,2112,256]{2,1,0:T(8,128)S(1)} %get-tuple-element.15, bf16[1,2048,256]{2,1,0:T(8,128)(2,1)S(1)} %copy-done.1, f32[1,2080,256]{2,1,0:T(8,128)S(1)} %add_multiply_fusion, ...), kind=kLoop, calls=%fused_computation.59 | loop fusion | flops 14155776 | bytes 14680064 | tf_op jit(solution)/shard_map/convert_element_type | solution.py:300
  44.2 2.8 %collective-permute-start.3 = (f32[192,256]{1,0:T(8,128)S(1)}, f32[192,256]{1,0:T(8,128)S(1)}, u32[]{:S(2)}, u32[]{:S(2)}) collective-permute-start(f32[192,256]{1,0:T(8,128)S(1)} %select_select_fusion.5), channel_id=1, source_target_pairs={{0,32},{16,48},{32,0},{48,16},{64,96},{80,112},{96,64},{112,80},{1... | collective-permute-start | bytes 589832 | tf_op jit(solution)/shard_map/ppermute | solution.py:107
  47.7 4.1 %collective-permute-done.3 = f32[192,256]{1,0:T(8,128)S(1)} collective-permute-done((f32[192,256]{1,0:T(8,128)S(1)}, f32[192,256]{1,0:T(8,128)S(1)}, u32[]{:S(2)}, u32[]{:S(2)}) %collective-permute-start.3) | collective-permute-done | bytes 196640 | tf_op jit(solution)/shard_map/ppermute | solution.py:107
  51.9 2.0 %collective-permute-done.4 = f32[192,256]{1,0:T(8,128)S(1)} collective-permute-done((f32[192,256]{1,0:T(8,128)S(1)}, f32[192,256]{1,0:T(8,128)S(1)}, u32[]{:S(2)}, u32[]{:S(2)}) %collective-permute-start.4) | collective-permute-done | bytes 196640 | tf_op jit(solution)/shard_map/ppermute | solution.py:107
  54.0 2.4 %collective-permute-start.5 = (f32[48,256]{1,0:T(8,128)S(1)}, f32[48,256]{1,0:T(8,128)S(1)}, u32[]{:S(2)}, u32[]{:S(2)}) collective-permute-start(f32[48,256]{1,0:T(8,128)S(1)} %get-tuple-element.41), channel_id=1, source_target_pairs={{0,4},{1,5},{2,6},{3,7},{4,0},{5,1},{6,2},{7,3},{8,12},{9,13},{10,... | collective-permute-start | bytes 147464 | tf_op jit(solution)/shard_map/ppermute | solution.py:107
  56.4 3.0 %collective-permute-start.6 = (f32[48,256]{1,0:T(8,128)S(1)}, f32[48,256]{1,0:T(8,128)S(1)}, u32[]{:S(2)}, u32[]{:S(2)}) collective-permute-start(f32[48,256]{1,0:T(8,128)S(1)} %get-tuple-element.42), channel_id=1, source_target_pairs={{0,8},{1,9},{2,10},{3,11},{4,12},{5,13},{6,14},{7,15},{8,0},{9,1},... | collective-permute-start | bytes 147464 | tf_op jit(solution)/shard_map/ppermute | solution.py:107
  59.6 2.2 %collective-permute-done.6 = f32[48,256]{1,0:T(8,128)S(1)} collective-permute-done((f32[48,256]{1,0:T(8,128)S(1)}, f32[48,256]{1,0:T(8,128)S(1)}, u32[]{:S(2)}, u32[]{:S(2)}) %collective-permute-start.6) | collective-permute-done | bytes 49184 | tf_op jit(solution)/shard_map/ppermute | solution.py:107
  61.8 2.5 %collective-permute-done.7 = f32[48,256]{1,0:T(8,128)S(1)} collective-permute-done((f32[48,256]{1,0:T(8,128)S(1)}, f32[48,256]{1,0:T(8,128)S(1)}, u32[]{:S(2)}, u32[]{:S(2)}) %collective-permute-start.7) | collective-permute-done | bytes 49184 | tf_op jit(solution)/shard_map/ppermute | solution.py:107
  65.5 4.0 %collective-permute-start.8 = (f32[48,256]{1,0:T(8,128)S(1)}, f32[48,256]{1,0:T(8,128)S(1)}, u32[]{:S(2)}, u32[]{:S(2)}) collective-permute-start(f32[48,256]{1,0:T(8,128)S(1)} %add_add_fusion.1), channel_id=1, source_target_pairs={{0,192},{16,208},{32,224},{48,240},{64,128},{80,144},{96,160},{112... | collective-permute-start | bytes 147464 | tf_op jit(solution)/shard_map/ppermute | solution.py:112
  69.7 1.8 %collective-permute-done.8 = f32[48,256]{1,0:T(8,128)S(1)} collective-permute-done((f32[48,256]{1,0:T(8,128)S(1)}, f32[48,256]{1,0:T(8,128)S(1)}, u32[]{:S(2)}, u32[]{:S(2)}) %collective-permute-start.8) | collective-permute-done | bytes 49184 | tf_op jit(solution)/shard_map/ppermute | solution.py:112
  71.5 3.1 %collective-permute-done.9 = f32[48,256]{1,0:T(8,128)S(1)} collective-permute-done((f32[48,256]{1,0:T(8,128)S(1)}, f32[48,256]{1,0:T(8,128)S(1)}, u32[]{:S(2)}, u32[]{:S(2)}) %collective-permute-start.9) | collective-permute-done | bytes 49184 | tf_op jit(solution)/shard_map/ppermute | solution.py:112
  74.7 2.3 %collective-permute-start.11 = (f32[48,256]{1,0:T(8,128)S(1)}, f32[48,256]{1,0:T(8,128)S(1)}, u32[]{:S(2)}, u32[]{:S(2)}) collective-permute-start(f32[48,256]{1,0:T(8,128)S(1)} %select_add_fusion.2), channel_id=1, source_target_pairs={{0,1},{1,0},{2,3},{3,2},{4,5},{5,4},{6,7},{7,6},{8,9},{9,8},{10,11... | collective-permute-start | bytes 147464 | tf_op jit(solution)/shard_map/ppermute | solution.py:112
  77.9 1.9 %collective-permute-start.12 = (f32[48,256]{1,0:T(8,128)S(1)}, f32[48,256]{1,0:T(8,128)S(1)}, u32[]{:S(2)}, u32[]{:S(2)}) collective-permute-start(f32[48,256]{1,0:T(8,128)S(1)} %select_add_fusion.1), channel_id=1, source_target_pairs={{0,2},{1,3},{2,0},{3,1},{4,6},{5,7},{6,4},{7,5},{8,10},{9,11},{10,... | collective-permute-start | bytes 147464 | tf_op jit(solution)/shard_map/ppermute | solution.py:112
  79.8 6.4 %collective-permute-done.12 = f32[48,256]{1,0:T(8,128)S(1)} collective-permute-done((f32[48,256]{1,0:T(8,128)S(1)}, f32[48,256]{1,0:T(8,128)S(1)}, u32[]{:S(2)}, u32[]{:S(2)}) %collective-permute-start.12) | collective-permute-done | bytes 49184 | tf_op jit(solution)/shard_map/ppermute | solution.py:112
  86.4 3.1 %collective-permute-start.15 = (f32[48,256]{1,0:T(8,128)S(1)}, f32[48,256]{1,0:T(8,128)S(1)}, u32[]{:S(2)}, u32[]{:S(2)}) collective-permute-start(f32[48,256]{1,0:T(8,128)S(1)} %select_add_fusion), channel_id=1, source_target_pairs={{0,4},{1,5},{2,6},{3,7},{4,0},{5,1},{6,2},{7,3},{8,12},{9,13},{10,... | collective-permute-start | bytes 147464 | tf_op jit(solution)/shard_map/ppermute | solution.py:122
  92.5 2.7 %collective-permute-start.18 = (f32[192,256]{1,0:T(8,128)S(1)}, f32[192,256]{1,0:T(8,128)S(1)}, u32[]{:S(2)}, u32[]{:S(2)}) collective-permute-start(f32[192,256]{1,0:T(8,128)S(1)} %pad_maximum_fusion.6), channel_id=1, source_target_pairs={{0,16},{16,0},{32,48},{48,32},{64,80},{80,64},{96,112},{112,96},{1... | collective-permute-start | bytes 589832 | tf_op jit(solution)/shard_map/ppermute | solution.py:122
  95.2 8.5 %collective-permute-done.16 = f32[192,256]{1,0:T(8,128)S(1)} collective-permute-done((f32[192,256]{1,0:T(8,128)S(1)}, f32[192,256]{1,0:T(8,128)S(1)}, u32[]{:S(2)}, u32[]{:S(2)}) %collective-permute-start.16) | collective-permute-done | bytes 196640 | tf_op jit(solution)/shard_map/ppermute | solution.py:122
  (103 shorter events, 27.9 us)
Async XLA Ops:
  0.6 21.6 %copy-start = (bf16[4,256]{1,0:T(4,128)(2,1)S(1)}, bf16[4,256]{1,0:T(4,128)(2,1)}, u32[]{:S(2)}) copy-start(bf16[4,256]{1,0:T(4,128)(2,1)} %param.6) | copy-start | bytes 6148
  0.6 21.4 %copy-start.3 = (s32[1,2048]{1,0:T(1,128)S(1)}, s32[1,2048]{1,0:T(1,128)}, u32[]{:S(2)}) copy-start(s32[1,2048]{1,0:T(1,128)} %param.5) | copy-start | bytes 24580
  0.7 17.4 %copy-start.2 = (bf16[3,256,256]{2,1,0:T(8,128)(2,1)S(1)}, bf16[3,256,256]{2,1,0:T(8,128)(2,1)}, u32[]{:S(2)}) copy-start(bf16[3,256,256]{2,1,0:T(8,128)(2,1)} %param.8) | copy-start | bytes 1179652
  2.2 16.2 %collective-permute-start = (bf16[1,17,256]{2,1,0:T(8,128)(2,1)S(1)}, bf16[1,17,256]{2,1,0:T(8,128)(2,1)S(1)}, u32[]{:S(2)}, u32[]{:S(2)}) collective-permute-start(bf16[1,17,256]{2,1,0:T(8,128)(2,1)S(1)} %pad_maximum_fusion.9), channel_id=1, source_target_pairs={{0,1},{1,2},{2,3},{3,4},{4,5},{5,6},{6,7},{7,8},{8,9},{9,10},{10,1... | collective-permute-start | bytes 26120 | tf_op jit(solution)/shard_map/ppermute | solution.py:261
  13.1 8.9 %collective-permute-start.1 = (bf16[1,17,256]{2,1,0:T(8,128)(2,1)S(1)}, bf16[1,17,256]{2,1,0:T(8,128)(2,1)S(1)}, u32[]{:S(2)}, u32[]{:S(2)}) collective-permute-start(bf16[1,17,256]{2,1,0:T(8,128)(2,1)S(1)} %pad_maximum_fusion.10), channel_id=1, source_target_pairs={{1,0},{2,1},{3,2},{4,3},{5,4},{6,5},{7,6},{8,7},{9,8},{10,9},{11,1... | collective-permute-start | bytes 26120 | tf_op jit(solution)/shard_map/ppermute | solution.py:262
  22.9 1.0 copy-start.4
  28.0 1.9 %copy-start.1 = (bf16[1,2048,256]{2,1,0:T(8,128)(2,1)S(1)}, bf16[1,2048,256]{2,1,0:T(8,128)(2,1)}, u32[]{:S(2)}) copy-start(bf16[1,2048,256]{2,1,0:T(8,128)(2,1)} %param.9) | copy-start | bytes 3145732
  42.8 4.9 %collective-permute-start.2 = (f32[192,256]{1,0:T(8,128)S(1)}, f32[192,256]{1,0:T(8,128)S(1)}, u32[]{:S(2)}, u32[]{:S(2)}) collective-permute-start(f32[192,256]{1,0:T(8,128)S(1)} %select_select_fusion.6), channel_id=1, source_target_pairs={{0,16},{16,0},{32,48},{48,32},{64,80},{80,64},{96,112},{112,96},{1... | collective-permute-start | bytes 589832 | tf_op jit(solution)/shard_map/ppermute | solution.py:107
  44.2 7.7 %collective-permute-start.3 = (f32[192,256]{1,0:T(8,128)S(1)}, f32[192,256]{1,0:T(8,128)S(1)}, u32[]{:S(2)}, u32[]{:S(2)}) collective-permute-start(f32[192,256]{1,0:T(8,128)S(1)} %select_select_fusion.5), channel_id=1, source_target_pairs={{0,32},{16,48},{32,0},{48,16},{64,96},{80,112},{96,64},{112,80},{1... | collective-permute-start | bytes 589832 | tf_op jit(solution)/shard_map/ppermute | solution.py:107
  47.0 6.9 %collective-permute-start.4 = (f32[192,256]{1,0:T(8,128)S(1)}, f32[192,256]{1,0:T(8,128)S(1)}, u32[]{:S(2)}, u32[]{:S(2)}) collective-permute-start(f32[192,256]{1,0:T(8,128)S(1)} %select_select_fusion.4), channel_id=1, source_target_pairs={{0,48},{16,32},{32,16},{48,0},{64,112},{80,96},{96,80},{112,64},{1... | collective-permute-start | bytes 589832 | tf_op jit(solution)/shard_map/ppermute | solution.py:107
  54.0 5.6 %collective-permute-start.5 = (f32[48,256]{1,0:T(8,128)S(1)}, f32[48,256]{1,0:T(8,128)S(1)}, u32[]{:S(2)}, u32[]{:S(2)}) collective-permute-start(f32[48,256]{1,0:T(8,128)S(1)} %get-tuple-element.41), channel_id=1, source_target_pairs={{0,4},{1,5},{2,6},{3,7},{4,0},{5,1},{6,2},{7,3},{8,12},{9,13},{10,... | collective-permute-start | bytes 147464 | tf_op jit(solution)/shard_map/ppermute | solution.py:107
  56.4 5.4 %collective-permute-start.6 = (f32[48,256]{1,0:T(8,128)S(1)}, f32[48,256]{1,0:T(8,128)S(1)}, u32[]{:S(2)}, u32[]{:S(2)}) collective-permute-start(f32[48,256]{1,0:T(8,128)S(1)} %get-tuple-element.42), channel_id=1, source_target_pairs={{0,8},{1,9},{2,10},{3,11},{4,12},{5,13},{6,14},{7,15},{8,0},{9,1},... | collective-permute-start | bytes 147464 | tf_op jit(solution)/shard_map/ppermute | solution.py:107
  59.4 4.8 %collective-permute-start.7 = (f32[48,256]{1,0:T(8,128)S(1)}, f32[48,256]{1,0:T(8,128)S(1)}, u32[]{:S(2)}, u32[]{:S(2)}) collective-permute-start(f32[48,256]{1,0:T(8,128)S(1)} %select_select_fusion.11), channel_id=1, source_target_pairs={{0,12},{1,13},{2,14},{3,15},{4,8},{5,9},{6,10},{7,11},{8,4},{9,5},... | collective-permute-start | bytes 147464 | tf_op jit(solution)/shard_map/ppermute | solution.py:107
  64.3 5.4 %collective-permute-start.10 = (f32[48,256]{1,0:T(8,128)S(1)}, f32[48,256]{1,0:T(8,128)S(1)}, u32[]{:S(2)}, u32[]{:S(2)}) collective-permute-start(f32[48,256]{1,0:T(8,128)S(1)} %add_add_fusion.1), channel_id=1, source_target_pairs={{0,64},{16,80},{32,96},{48,112},{64,0},{80,16},{96,32},{112,48},{1... | collective-permute-start | bytes 147464 | tf_op jit(solution)/shard_map/ppermute | solution.py:112
  65.5 6.0 %collective-permute-start.8 = (f32[48,256]{1,0:T(8,128)S(1)}, f32[48,256]{1,0:T(8,128)S(1)}, u32[]{:S(2)}, u32[]{:S(2)}) collective-permute-start(f32[48,256]{1,0:T(8,128)S(1)} %add_add_fusion.1), channel_id=1, source_target_pairs={{0,192},{16,208},{32,224},{48,240},{64,128},{80,144},{96,160},{112... | collective-permute-start | bytes 147464 | tf_op jit(solution)/shard_map/ppermute | solution.py:112
  69.5 5.1 %collective-permute-start.9 = (f32[48,256]{1,0:T(8,128)S(1)}, f32[48,256]{1,0:T(8,128)S(1)}, u32[]{:S(2)}, u32[]{:S(2)}) collective-permute-start(f32[48,256]{1,0:T(8,128)S(1)} %add_add_fusion.1), channel_id=1, source_target_pairs={{0,128},{16,144},{32,160},{48,176},{64,192},{80,208},{96,224},{112... | collective-permute-start | bytes 147464 | tf_op jit(solution)/shard_map/ppermute | solution.py:112
  74.7 3.2 %collective-permute-start.11 = (f32[48,256]{1,0:T(8,128)S(1)}, f32[48,256]{1,0:T(8,128)S(1)}, u32[]{:S(2)}, u32[]{:S(2)}) collective-permute-start(f32[48,256]{1,0:T(8,128)S(1)} %select_add_fusion.2), channel_id=1, source_target_pairs={{0,1},{1,0},{2,3},{3,2},{4,5},{5,4},{6,7},{7,6},{8,9},{9,8},{10,11... | collective-permute-start | bytes 147464 | tf_op jit(solution)/shard_map/ppermute | solution.py:112
  77.9 8.3 %collective-permute-start.12 = (f32[48,256]{1,0:T(8,128)S(1)}, f32[48,256]{1,0:T(8,128)S(1)}, u32[]{:S(2)}, u32[]{:S(2)}) collective-permute-start(f32[48,256]{1,0:T(8,128)S(1)} %select_add_fusion.1), channel_id=1, source_target_pairs={{0,2},{1,3},{2,0},{3,1},{4,6},{5,7},{6,4},{7,5},{8,10},{9,11},{10,... | collective-permute-start | bytes 147464 | tf_op jit(solution)/shard_map/ppermute | solution.py:112
  86.2 4.8 %collective-permute-start.13 = (f32[48,256]{1,0:T(8,128)S(1)}, f32[48,256]{1,0:T(8,128)S(1)}, u32[]{:S(2)}, u32[]{:S(2)}) collective-permute-start(f32[48,256]{1,0:T(8,128)S(1)} %select_add_fusion), channel_id=1, source_target_pairs={{0,12},{1,13},{2,14},{3,15},{4,8},{5,9},{6,10},{7,11},{8,4},{9,5},... | collective-permute-start | bytes 147464 | tf_op jit(solution)/shard_map/ppermute | solution.py:122
  86.3 4.7 %collective-permute-start.14 = (f32[48,256]{1,0:T(8,128)S(1)}, f32[48,256]{1,0:T(8,128)S(1)}, u32[]{:S(2)}, u32[]{:S(2)}) collective-permute-start(f32[48,256]{1,0:T(8,128)S(1)} %select_add_fusion), channel_id=1, source_target_pairs={{0,8},{1,9},{2,10},{3,11},{4,12},{5,13},{6,14},{7,15},{8,0},{9,1},... | collective-permute-start | bytes 147464 | tf_op jit(solution)/shard_map/ppermute | solution.py:122
  86.4 5.4 %collective-permute-start.15 = (f32[48,256]{1,0:T(8,128)S(1)}, f32[48,256]{1,0:T(8,128)S(1)}, u32[]{:S(2)}, u32[]{:S(2)}) collective-permute-start(f32[48,256]{1,0:T(8,128)S(1)} %select_add_fusion), channel_id=1, source_target_pairs={{0,4},{1,5},{2,6},{3,7},{4,0},{5,1},{6,2},{7,3},{8,12},{9,13},{10,... | collective-permute-start | bytes 147464 | tf_op jit(solution)/shard_map/ppermute | solution.py:122
  91.9 11.8 %collective-permute-start.16 = (f32[192,256]{1,0:T(8,128)S(1)}, f32[192,256]{1,0:T(8,128)S(1)}, u32[]{:S(2)}, u32[]{:S(2)}) collective-permute-start(f32[192,256]{1,0:T(8,128)S(1)} %pad_maximum_fusion.6), channel_id=1, source_target_pairs={{0,48},{16,32},{32,16},{48,0},{64,112},{80,96},{96,80},{112,64},{1... | collective-permute-start | bytes 589832 | tf_op jit(solution)/shard_map/ppermute | solution.py:122
  92.2 11.6 %collective-permute-start.17 = (f32[192,256]{1,0:T(8,128)S(1)}, f32[192,256]{1,0:T(8,128)S(1)}, u32[]{:S(2)}, u32[]{:S(2)}) collective-permute-start(f32[192,256]{1,0:T(8,128)S(1)} %pad_maximum_fusion.6), channel_id=1, source_target_pairs={{0,32},{16,48},{32,0},{48,16},{64,96},{80,112},{96,64},{112,80},{1... | collective-permute-start | bytes 589832 | tf_op jit(solution)/shard_map/ppermute | solution.py:122
  92.5 11.2 %collective-permute-start.18 = (f32[192,256]{1,0:T(8,128)S(1)}, f32[192,256]{1,0:T(8,128)S(1)}, u32[]{:S(2)}, u32[]{:S(2)}) collective-permute-start(f32[192,256]{1,0:T(8,128)S(1)} %pad_maximum_fusion.6), channel_id=1, source_target_pairs={{0,16},{16,0},{32,48},{48,32},{64,80},{80,64},{96,112},{112,96},{1... | collective-permute-start | bytes 589832 | tf_op jit(solution)/shard_map/ppermute | solution.py:122
